TPU v7x, 256 devices: a whole 4x4x8 slice. The times are simulated.
256 devices in a mesh: region: 8 (over x, core), dp: 32 (over y, z).
Axes of the slice: x: 4, y: 4, z: 8, core: 2. Of those that a mesh axis runs over, the one named last changes fastest.
Arguments:
- cells: bfloat16 [32, 131072, 256], P('dp', 'region'), may hold values from -12 to 12
- cell_weight: float32 [32, 131072], P('dp', 'region'), may hold values from 0.1 to 10
- cell_cluster: int32 [32, 131072], P('dp', 'region'), may hold values from -1 to 2047, as said below
- cluster_edges: int32 [32, 2048, 8], P('dp', 'region'), may hold values from 0 to 2047, as said below
- labels: int32 [32, 2048], P('dp', 'region'), may hold values from 0 to 7
- w_self: bfloat16 [256, 1024], replicated, may hold values from -0.375 to 0.375
- w_nbr: bfloat16 [256, 1024], replicated, may hold values from -0.375 to 0.375
- w_out: bfloat16 [1024, 8], replicated, may hold values from -0.1875 to 0.1875
Outputs:
- logits: float32 [32, 2048, 8], P('dp', 'region')
- grad_self: float32 [256, 1024], replicated
- grad_nbr: float32 [256, 1024], replicated
- grad_out: float32 [1024, 8], replicated
Inputs may be any that keep to these rules, and one draw needn't show every extreme that they name: `cell_cluster`: clusters (r) * 256 to ((r) + 1) * 256 - 1 belong to region r; a cell's cluster belongs to the cell's own region or an adjacent one; every cluster has at least one cell. `cluster_edges`: A cluster's neighbours belong to its own region or an adjacent one; every cluster is listed by some cluster.
All inputs are finite; a program needn't handle non-finite values.
Results may differ from a plain program's by a relative error of at most 0.0051.
Values may be sent and summed in bfloat16 or wider, within the bound.
No kernel may reach another device: no remote copies, remote signals or barrier semaphores. Data moves between devices by JAX's collectives and lax.ppermute only.
A program may use at most 64 MiB of HBM per device.

v0:
```python
import jax
import jax.numpy as jnp
from jax import lax
from jax.sharding import PartitionSpec as P


def passed_along(value, axis, steps):
    count = lax.axis_size(axis)
    initial, last = (max(0, -steps), min(count, count - steps))
    return lax.ppermute(value, axis, [(source, source + steps) for source in range(initial, last)])


def padded(block, sides, width):
    for axis, dim in sides:
        count = lax.axis_size(axis)
        forward = [(i, i + 1) for i in range(count - 1)]
        backward = [(target, source) for source, target in forward]
        low = lax.ppermute(
            lax.slice_in_dim(block, block.shape[dim] - width, None, axis=dim), axis, forward
        )
        high = lax.ppermute(lax.slice_in_dim(block, 0, width, axis=dim), axis, backward)
        block = jnp.concatenate([low, block, high], axis=dim)
    return block


def accumulate(cluster_ids, weighted, weights, width):
    events, length, feats = weighted.shape
    block = min(512, length)
    slots = jnp.arange(width, dtype=jnp.int32)

    def add_block(index, carry):
        numer, denom = carry
        start = index * block
        ids = lax.dynamic_slice_in_dim(cluster_ids, start, block, 1)
        rows = lax.dynamic_slice_in_dim(weighted, start, block, 1)
        scale = lax.dynamic_slice_in_dim(weights, start, block, 1)
        member = ids[:, None, :] == slots[None, :, None]
        numer = numer + jnp.einsum(
            "ekb,ebf->ekf", member.astype(jnp.bfloat16), rows, preferred_element_type=jnp.float32
        )
        denom = denom + jnp.einsum(
            "ekb,eb->ek", member.astype(jnp.float32), scale, precision=lax.Precision.HIGHEST
        )
        return (numer, denom)

    start_sums = (
        jnp.zeros((events, width, feats), jnp.float32),
        jnp.zeros((events, width), jnp.float32),
    )
    return lax.fori_loop(0, length // block, add_block, start_sums)


def local(cells, cell_weight, cell_cluster, cluster_edges, labels, w_self, w_nbr, w_out):
    region = lax.axis_index("region")
    owned = cluster_edges.shape[1]
    degree = cluster_edges.shape[2]
    weighted = (cell_weight[..., None] * cells.astype(jnp.float32)).astype(jnp.bfloat16)
    relative = cell_cluster - (region - 1) * owned
    numer_three, denom_three = accumulate(relative, weighted, cell_weight, 3 * owned)
    above_numer, above_denom = passed_along(
        (numer_three[:, :owned], denom_three[:, :owned]), "region", -1
    )
    below_numer, below_denom = passed_along(
        (numer_three[:, 2 * owned :], denom_three[:, 2 * owned :]), "region", 1
    )
    numer = numer_three[:, owned : 2 * owned] + above_numer + below_numer
    denom = denom_three[:, owned : 2 * owned] + above_denom + below_denom
    pooled = (numer / denom[..., None]).astype(jnp.bfloat16)
    table = padded(pooled, (("region", 1),), owned)
    targets = cluster_edges - (region - 1) * owned
    width = 3 * owned
    slots = jnp.arange(width, dtype=jnp.int32)
    tally = jnp.zeros((pooled.shape[0], owned, width), jnp.float32)
    for which in range(degree):
        tally = tally + (targets[:, :, which, None] == slots[None, None, :]).astype(jnp.float32)
    agg = (
        jnp.einsum(
            "ekj,ejf->ekf", tally.astype(jnp.bfloat16), table, preferred_element_type=jnp.float32
        )
        / degree
    ).astype(jnp.bfloat16)
    zval = jnp.einsum("ekf,fh->ekh", pooled, w_self, preferred_element_type=jnp.float32)
    zval = zval + jnp.einsum("ekf,fh->ekh", agg, w_nbr, preferred_element_type=jnp.float32)
    sig = jax.nn.sigmoid(zval)
    units = (zval * sig).astype(jnp.bfloat16)
    scores = jnp.einsum("ekh,hc->ekc", units, w_out, preferred_element_type=jnp.float32)
    events = lax.axis_size("dp") * cells.shape[0]
    classes = jnp.arange(w_out.shape[1], dtype=jnp.int32)
    target = (labels[..., None] == classes[None, None, :]).astype(jnp.float32)
    d_logits = ((jax.nn.sigmoid(scores) - target) / events).astype(jnp.bfloat16)
    grad_head = jnp.einsum("ekh,ekc->hc", units, d_logits, preferred_element_type=jnp.float32)
    d_units = jnp.einsum("ekc,hc->ekh", d_logits, w_out, preferred_element_type=jnp.float32)
    d_z = (d_units * sig * (1.0 + zval * (1.0 - sig))).astype(jnp.bfloat16)
    grad_own = jnp.einsum("ekf,ekh->fh", pooled, d_z, preferred_element_type=jnp.float32)
    grad_side = jnp.einsum("ekf,ekh->fh", agg, d_z, preferred_element_type=jnp.float32)
    grad_own, grad_side, grad_head = lax.psum((grad_own, grad_side, grad_head), ("region", "dp"))
    return (scores, grad_own, grad_side, grad_head)


def solution(mesh):
    return jax.shard_map(
        local,
        mesh=mesh,
        in_specs=(
            P("dp", "region", None),
            P("dp", "region"),
            P("dp", "region"),
            P("dp", "region", None),
            P("dp", "region"),
            P(),
            P(),
            P(),
        ),
        out_specs=(P("dp", "region", None), P(), P(), P()),
        check_vma=False,
    )
```

profile of v0, /device:TPU:1, one launch (start us, length us, event | category | flops | bytes accessed | tf_op | source)
XLA Modules:
  0.0 420.6 jit_solution(15747265865628729639)
XLA Ops:
  8.2 7.9 %multiply_convert_fusion = bf16[1,16384,256]{2,1,0:T(8,128)(2,1)} fusion(bf16[1,16384,256]{2,1,0:T(8,128)(2,1)} %param.10, f32[16384]{0:T(1024)} %bitcast.57), kind=kLoop, calls=%fused_computation.17 | loop fusion | flops 12582912 | bytes 16842752 | tf_op jit(solution)/shard_map/convert_element_type | solution.py:57
  16.1 95.4 %while.16 = (s32[]{:T(128)}, f32[1,768,256]{2,1,0:T(8,128)S(1)}, f32[1,768]{1,0:T(1,128)S(1)}, s32[1,16384]{1,0:T(1,128)S(1)}, bf16[1,16384,256]{2,1,0:T(8,128)(...) while((s32[]{:T(128)}, f32[1,768,256]{2,1,0:T(8,128)S(1)}, ...), condition=%wide.region_1.0_spmd.clone, body=%wide.region_0.0_spmd.clone.sunk | while | flops 207226368 | bytes 1851562 | solution.py:50
  16.1 1.5 fusion.59
  17.7 1.5 fusion.60
  19.2 1.5 fusion.59
  20.7 1.5 fusion.60
  22.1 1.5 fusion.59
  23.6 1.5 fusion.60
  25.1 1.5 fusion.59
  26.6 1.5 fusion.60
  28.1 1.5 fusion.59
  31.1 1.5 fusion.59
  34.1 1.5 fusion.59
  35.6 1.5 fusion.60
  37.0 1.5 fusion.59
  38.5 1.5 fusion.60
  40.0 1.5 fusion.59
  41.5 1.5 fusion.60
  43.0 1.5 fusion.59
  44.5 1.5 fusion.60
  46.0 1.5 fusion.59
  47.5 1.5 fusion.60
  49.0 1.5 fusion.59
  50.5 1.5 fusion.60
  52.0 1.5 fusion.59
  53.5 1.5 fusion.60
  54.9 1.5 fusion.59
  56.4 1.5 fusion.60
  57.9 1.5 fusion.59
  59.4 1.5 fusion.60
  60.9 1.5 fusion.59
  62.4 1.5 fusion.60
  63.9 1.5 fusion.59
  65.4 1.5 fusion.60
  66.9 1.5 fusion.59
  68.4 1.5 fusion.60
  69.8 1.5 fusion.59
  71.3 1.5 fusion.60
  72.8 1.5 fusion.59
  74.3 1.5 fusion.60
  75.8 1.5 fusion.59
  78.8 1.5 fusion.59
  81.8 1.5 fusion.59
  84.7 1.5 fusion.59
  87.7 1.5 fusion.59
  90.7 1.5 fusion.59
  93.7 1.5 fusion.59
  96.7 1.5 fusion.59
  99.6 1.5 fusion.59
  102.6 1.5 fusion.59
  105.6 1.5 fusion.59
  108.6 1.5 fusion.59
  111.6 5.2 %collective-permute-start.2 = (f32[1,256]{1,0:T(1,128)S(1)}, f32[1,256]{1,0:T(1,128)S(1)}, u32[]{:S(2)}, u32[]{:S(2)}) collective-permute-start(f32[1,256]{1,0:T(1,128)S(1)} %get-tuple-element.178), channel_id=1, source_target_pairs={{32,0},{64,32},{96,64},{128,96},{160,128},{192,160},{224,192},{33,... | collective-permute-start | bytes 3080 | tf_op jit(solution)/shard_map/ppermute | solution.py:10
  116.9 1.9 collective-permute-start.3
  118.8 2.4 collective-permute-start
  121.2 3.2 collective-permute-start.1
  124.5 2.1 collective-permute-done
  127.8 4.4 %collective-permute-start.4 = (bf16[1,256,256]{2,1,0:T(8,128)(2,1)S(1)}, bf16[1,256,256]{2,1,0:T(8,128)(2,1)S(1)}, u32[]{:S(2)}, u32[]{:S(2)}) collective-permute-start(bf16[1,256,256]{2,1,0:T(8,128)(2,1)S(1)} %divide_convert_fusion), channel_id=1, source_target_pairs={{0,32},{32,64},{64,96},{96,128},{128,160},{160,192},{192,224},{1,3... | collective-permute-start | bytes 393224 | tf_op jit(solution)/shard_map/ppermute | solution.py:18
  132.2 1.9 collective-permute-start.5
  134.2 4.3 %collective-permute-done.5 = bf16[1,256,256]{2,1,0:T(8,128)(2,1)S(1)} collective-permute-done((bf16[1,256,256]{2,1,0:T(8,128)(2,1)S(1)}, bf16[1,256,256]{2,1,0:T(8,128)(2,1)S(1)}, u32[]{:S(2)}, u32[]{:S(2)}) %collective-permute-start.5) | collective-permute-done | bytes 131104 | tf_op jit(solution)/shard_map/ppermute | solution.py:21
  143.9 78.9 %psum.23 = f32[1024,8]{0,1:T(8,128)} all-reduce(f32[1024,8]{0,1:T(8,128)S(1)} %fusion.36), channel_id=1, replica_groups=mesh['region'=8,'dp'=32] {'region','dp'}, use_global_device_ids=true, to_apply=%region_4.0 | all-reduce | flops 8192 | bytes 65536 | tf_op jit(solution)/shard_map/psum | solution.py:96
  222.8 186.3 %all-reduce.3.cloned.1.call-done = (f32[256,1024]{1,0:T(8,128)}, f32[256,1024]{1,0:T(8,128)}) async-done(((f32[256,1024]{1,0:T(8,128)}, f32[256,1024]{1,0:T(8,128)}), (f32[256,1024]{1,0:T(8,128)}, f32[256,1024]{1,0:T(8,128)})) %all-reduce.3.cloned.1.call-update) | async-done | bytes 2097168 | tf_op jit(solution)/shard_map/psum | solution.py:96
  409.1 2.3 copy.23
  411.5 2.3 copy.24
  (81 shorter events, 28.4 us)
Async XLA Ops:
  7.2 132.6 %copy-start = (bf16[256,1024]{1,0:T(8,128)(2,1)S(1)}, bf16[256,1024]{1,0:T(8,128)(2,1)}, u32[]{:S(2)}) copy-start(bf16[256,1024]{1,0:T(8,128)(2,1)} %param.15) | copy-start | bytes 1572868
  7.2 402.0 %all-reduce.3.cloned.1.call-start = ((), (), s32[]{:S(2)}) async-start(), calls=%async_computation | async-start | bytes 4194304 | tf_op jit(solution)/shard_map/psum | solution.py:96
  16.1 108.3 %copy-start.4 = (s32[1,256,8]{1,2,0:T(8,128)S(1)}, s32[1,256,8]{1,2,0:T(8,128)}, u32[]{:S(2)}) copy-start(s32[1,256,8]{1,2,0:T(8,128)} %param.13) | copy-start | bytes 24580
  16.1 123.4 %copy-start.1 = (bf16[256,1024]{1,0:T(8,128)(2,1)S(1)}, bf16[256,1024]{1,0:T(8,128)(2,1)}, u32[]{:S(2)}) copy-start(bf16[256,1024]{1,0:T(8,128)(2,1)} %param.16) | copy-start | bytes 1572868
  111.6 28.7 %copy-start.3 = (bf16[1024,8]{0,1:T(8,128)(2,1)S(1)}, bf16[1024,8]{0,1:T(8,128)(2,1)}, u32[]{:S(2)}) copy-start(bf16[1024,8]{0,1:T(8,128)(2,1)} %param.17) | copy-start | bytes 49156
  111.6 29.0 %copy-start.5 = (s32[1,256]{1,0:T(1,128)S(1)}, s32[1,256]{1,0:T(1,128)}, u32[]{:S(2)}) copy-start(s32[1,256]{1,0:T(1,128)} %param.14) | copy-start | bytes 3076
  111.6 12.8 %collective-permute-start.2 = (f32[1,256]{1,0:T(1,128)S(1)}, f32[1,256]{1,0:T(1,128)S(1)}, u32[]{:S(2)}, u32[]{:S(2)}) collective-permute-start(f32[1,256]{1,0:T(1,128)S(1)} %get-tuple-element.178), channel_id=1, source_target_pairs={{32,0},{64,32},{96,64},{128,96},{160,128},{192,160},{224,192},{33,... | collective-permute-start | bytes 3080 | tf_op jit(solution)/shard_map/ppermute | solution.py:10
  116.9 7.6 %collective-permute-start.3 = (f32[1,256]{1,0:T(1,128)S(1)}, f32[1,256]{1,0:T(1,128)S(1)}, u32[]{:S(2)}, u32[]{:S(2)}) collective-permute-start(f32[1,256]{1,0:T(1,128)S(1)} %get-tuple-element.179), channel_id=1, source_target_pairs={{0,32},{32,64},{64,96},{96,128},{128,160},{160,192},{192,224},{1,3... | collective-permute-start | bytes 3080 | tf_op jit(solution)/shard_map/ppermute | solution.py:10
  118.8 7.7 %collective-permute-start = (f32[1,256,256]{2,1,0:T(8,128)S(1)}, f32[1,256,256]{2,1,0:T(8,128)S(1)}, u32[]{:S(2)}, u32[]{:S(2)}) collective-permute-start(f32[1,256,256]{2,1,0:T(8,128)S(1)} %get-tuple-element.168), channel_id=1, source_target_pairs={{32,0},{64,32},{96,64},{128,96},{160,128},{192,160},{224,192},{33,... | collective-permute-start | bytes 786440 | tf_op jit(solution)/shard_map/ppermute | solution.py:10
  121.2 6.5 %collective-permute-start.1 = (f32[1,256,256]{2,1,0:T(8,128)S(1)}, f32[1,256,256]{2,1,0:T(8,128)S(1)}, u32[]{:S(2)}, u32[]{:S(2)}) collective-permute-start(f32[1,256,256]{2,1,0:T(8,128)S(1)} %get-tuple-element.169), channel_id=1, source_target_pairs={{0,32},{32,64},{64,96},{96,128},{128,160},{160,192},{192,224},{1,3... | collective-permute-start | bytes 786440 | tf_op jit(solution)/shard_map/ppermute | solution.py:10
  127.8 6.3 %collective-permute-start.4 = (bf16[1,256,256]{2,1,0:T(8,128)(2,1)S(1)}, bf16[1,256,256]{2,1,0:T(8,128)(2,1)S(1)}, u32[]{:S(2)}, u32[]{:S(2)}) collective-permute-start(bf16[1,256,256]{2,1,0:T(8,128)(2,1)S(1)} %divide_convert_fusion), channel_id=1, source_target_pairs={{0,32},{32,64},{64,96},{96,128},{128,160},{160,192},{192,224},{1,3... | collective-permute-start | bytes 393224 | tf_op jit(solution)/shard_map/ppermute | solution.py:18
  132.2 6.3 %collective-permute-start.5 = (bf16[1,256,256]{2,1,0:T(8,128)(2,1)S(1)}, bf16[1,256,256]{2,1,0:T(8,128)(2,1)S(1)}, u32[]{:S(2)}, u32[]{:S(2)}) collective-permute-start(bf16[1,256,256]{2,1,0:T(8,128)(2,1)S(1)} %divide_convert_fusion), channel_id=1, source_target_pairs={{32,0},{64,32},{96,64},{128,96},{160,128},{192,160},{224,192},{33,... | collective-permute-start | bytes 393224 | tf_op jit(solution)/shard_map/ppermute | solution.py:21
  140.5 273.2 %copy-start.2 = (f32[256,8]{0,1:T(8,128)}, f32[256,8]{0,1:T(8,128)S(1)}, u32[]{:S(2)}) copy-start(f32[256,8]{0,1:T(8,128)S(1)} %fusion.41) | copy-start | bytes 24580
Sparse Core Ops, SparseCore 0:
  143.8 265.2 all-reduce.2
where the time goes:
time: 424 us; the launch traced here: 421 us
  waiting for transfers between devices  194 us (46%)
  matrix products  100 us (24%)
  blocking collectives  78.9 us (19%)
  starting transfers between devices  19.1 us (5%)
  between operations  14.3 us (3%)
  other arithmetic  9 us (2%)
  local copies, waits for them, and re-layouts  4.75 us (1%)
    psum x1, waiting for transfers between devices, local(): lax.psum((grad_own, grad_side, grad_head), ('region', 'dp'))  186 us
    psum x1, blocking collectives, local(): lax.psum((grad_own, grad_side, grad_head), ('region', 'dp'))  78.9 us
    dot_general x32, matrix products, add_block(): jnp.einsum('ekb,ebf->ekf', member.astype(jnp.bfloat16), rows, preferred_e...  47.9 us
    dot_general x32, matrix products, add_block(): jnp.einsum('ekb,eb->ek', member.astype(jnp.float32), scale, precision=lax...  47.2 us
    ppermute x4, starting transfers between devices, passed_along(): lax.ppermute(value, axis, [(source, source + steps) for source in range(i...  12.7 us
  transfers between devices with their start and end apart: 7, of which 4 were waited for; matrix products, arithmetic and copies ran while one was open for 0% of the time, Pallas kernels for 0%

commit v1 on v0

--- a/solution.py
+++ b/solution.py
@@ -50,6 +50,48 @@
     return lax.fori_loop(0, length // block, add_block, start_sums)
 
 
+def halving_plan(sizes):
+    core = [("region", 1)]
+    first = [("region", 2), ("dp", 8), ("dp", 1), ("region", 4), ("dp", 16), ("dp", 2), ("dp", 4)]
+    second = [("dp", 8), ("dp", 1), ("region", 2), ("dp", 16), ("dp", 2), ("region", 4), ("dp", 4)]
+    width = sizes["dp"]
+    steps = []
+    for flip0, flip1 in zip(core + first, core + second):
+        perm, bits = [], []
+        for device in range(sizes["region"] * width):
+            at = {"region": device // width, "dp": device % width}
+            axis, bit = flip1 if at["region"] & 1 else flip0
+            bits.append(1 if at[axis] & bit else 0)
+            at[axis] ^= bit
+            perm.append((device, at["region"] * width + at["dp"]))
+        steps.append((perm, bits))
+    return steps
+
+
+def all_sum(buffers, sizes):
+    axes = ("region", "dp")
+    me = lax.axis_index("region") * sizes["dp"] + lax.axis_index("dp")
+    steps = halving_plan(sizes)
+    for perm, bits in steps:
+        upper = jnp.asarray(bits, jnp.int32)[me] == 1
+        keeps, sends = [], []
+        for value in buffers:
+            half = value.shape[0] // 2
+            low, high = value[:half], value[half:]
+            keeps.append(jnp.where(upper, high, low))
+            sends.append(jnp.where(upper, low, high))
+        got = lax.ppermute(tuple(sends), axes, perm)
+        buffers = tuple(k + g for k, g in zip(keeps, got))
+    for perm, bits in reversed(steps):
+        upper = jnp.asarray(bits, jnp.int32)[me] == 1
+        got = lax.ppermute(buffers, axes, perm)
+        buffers = tuple(
+            jnp.concatenate([jnp.where(upper, g, v), jnp.where(upper, v, g)], axis=0)
+            for v, g in zip(buffers, got)
+        )
+    return buffers
+
+
 def local(cells, cell_weight, cell_cluster, cluster_edges, labels, w_self, w_nbr, w_out):
     region = lax.axis_index("region")
     owned = cluster_edges.shape[1]
@@ -88,12 +130,18 @@
     classes = jnp.arange(w_out.shape[1], dtype=jnp.int32)
     target = (labels[..., None] == classes[None, None, :]).astype(jnp.float32)
     d_logits = ((jax.nn.sigmoid(scores) - target) / events).astype(jnp.bfloat16)
-    grad_head = jnp.einsum("ekh,ekc->hc", units, d_logits, preferred_element_type=jnp.float32)
+    grad_head = jnp.einsum("ekh,ekc->ch", units, d_logits, preferred_element_type=jnp.float32)
     d_units = jnp.einsum("ekc,hc->ekh", d_logits, w_out, preferred_element_type=jnp.float32)
     d_z = (d_units * sig * (1.0 + zval * (1.0 - sig))).astype(jnp.bfloat16)
     grad_own = jnp.einsum("ekf,ekh->fh", pooled, d_z, preferred_element_type=jnp.float32)
     grad_side = jnp.einsum("ekf,ekh->fh", agg, d_z, preferred_element_type=jnp.float32)
-    grad_own, grad_side, grad_head = lax.psum((grad_own, grad_side, grad_head), ("region", "dp"))
+    sizes = {"region": lax.axis_size("region"), "dp": lax.axis_size("dp")}
+    hid = grad_own.shape[1]
+    grads, head = all_sum(
+        (jnp.concatenate([grad_own, grad_side], axis=0), grad_head.reshape(-1)), sizes
+    )
+    grad_own, grad_side = grads[: pooled.shape[2]], grads[pooled.shape[2] :]
+    grad_head = head.reshape(-1, hid).T
     return (scores, grad_own, grad_side, grad_head)
 
 

time: 424 us -> 251 us (0.59)
  waiting for transfers between devices: 194 us -> 43.8 us
  blocking collectives: 78.9 us -> 0 us
  starting transfers between devices: 19.1 us -> 81.1 us
  between operations: 14.3 us -> 6.48 us
  other arithmetic: 9 us -> 13.9 us
    psum x1 -> x0, waiting for transfers between devices: 186 us -> none  [local(): lax.psum((grad_own, grad_side, grad_head), ('region', 'dp'))]
    psum x1 -> x0, blocking collectives: 78.9 us -> none  [local(): lax.psum((grad_own, grad_side, grad_head), ('region', 'dp'))]
    ppermute x0 -> x32, starting transfers between devices: none -> 62.1 us  [the longest x16 37.5 us: all_sum(): got = lax.ppermute(buffers, axes, perm)]
    ppermute x0 -> x32, waiting for transfers between devices: none -> 37.4 us  [the longest x16 21.1 us: all_sum(): got = lax.ppermute(buffers, axes, perm)]
    dynamic_slice x0 -> x8, local copies, waits for them, and re-layouts: none -> 4.69 us  [all_sum(): upper = jnp.asarray(bits, jnp.int32)[me] == 1]
    unnamed x14 -> x29, local copies, waits for them, and re-layouts: 4.65 us -> 0.1 us
  transfers between devices with their start and end apart: 7 -> 38, of which waited for: 4 -> 24; matrix products, arithmetic and copies ran while one was open for 0% -> 3% of each run, Pallas kernels for 0% -> 0%
where the time goes in v1:
time: 251 us; the launch traced here: 249 us
  matrix products  98.4 us (39%)
  starting transfers between devices  81.1 us (32%)
  waiting for transfers between devices  43.8 us (17%)
  other arithmetic  13.9 us (6%)
  between operations  6.48 us (3%)
  local copies, waits for them, and re-layouts  4.93 us (2%)
    dot_general x32, matrix products, add_block(): jnp.einsum('ekb,ebf->ekf', member.astype(jnp.bfloat16), rows, preferred_e...  47.9 us
    dot_general x32, matrix products, add_block(): jnp.einsum('ekb,eb->ek', member.astype(jnp.float32), scale, precision=lax...  47.2 us
    ppermute x16, starting transfers between devices, all_sum(): got = lax.ppermute(buffers, axes, perm)  37.5 us
    ppermute x16, starting transfers between devices, all_sum(): got = lax.ppermute(tuple(sends), axes, perm)  24.6 us
    ppermute x16, waiting for transfers between devices, all_sum(): got = lax.ppermute(buffers, axes, perm)  21.1 us
    ppermute x16, waiting for transfers between devices, all_sum(): got = lax.ppermute(tuple(sends), axes, perm)  16.3 us
    ppermute x4, starting transfers between devices, passed_along(): lax.ppermute(value, axis, [(source, source + steps) for source in range(i...  12.7 us
    convert_element_type x1, other arithmetic, local(): (cell_weight[..., None] * cells.astype(jnp.float32)).astype(jnp.bfloat16)  7.98 us
  transfers between devices with their start and end apart: 38, of which 24 were waited for; matrix products, arithmetic and copies ran while one was open for 3% of the time, Pallas kernels for 0%

profile of v1, /device:TPU:1, one launch (start us, length us, event | category | flops | bytes accessed | tf_op | source)
XLA Modules:
  0.0 248.9 jit_solution(5386342132935175194)
XLA Ops:
  1.6 8.0 %multiply_convert_fusion = bf16[1,16384,256]{2,1,0:T(8,128)(2,1)} fusion(bf16[1,16384,256]{2,1,0:T(8,128)(2,1)} %param.26, f32[16384]{0:T(1024)} %bitcast.78), kind=kLoop, calls=%fused_computation.17 | loop fusion | flops 12582912 | bytes 16842752 | tf_op jit(solution)/shard_map/convert_element_type | solution.py:99
  9.6 95.5 %while.16 = (s32[]{:T(128)}, f32[1,768,256]{2,1,0:T(8,128)S(1)}, f32[1,768]{1,0:T(1,128)S(1)}, s32[1,16384]{1,0:T(1,128)S(1)}, bf16[1,16384,256]{2,1,0:T(8,128)(...) while((s32[]{:T(128)}, f32[1,768,256]{2,1,0:T(8,128)S(1)}, ...), condition=%wide.region_1.0_spmd.clone, body=%wide.region_0.0_spmd.clone.sunk | while | flops 207226368 | bytes 1851562 | solution.py:50
  9.6 1.5 fusion.62
  12.7 1.5 fusion.62
  15.7 1.5 fusion.62
  18.6 1.5 fusion.62
  21.6 1.5 fusion.62
  24.6 1.5 fusion.62
  27.6 1.5 fusion.62
  30.6 1.5 fusion.62
  33.5 1.5 fusion.62
  36.5 1.5 fusion.62
  39.5 1.5 fusion.62
  42.5 1.5 fusion.62
  45.5 1.5 fusion.62
  48.4 1.5 fusion.62
  51.4 1.5 fusion.62
  54.4 1.5 fusion.62
  60.4 1.5 fusion.62
  63.4 1.5 fusion.62
  66.3 1.5 fusion.62
  69.3 1.5 fusion.62
  72.3 1.5 fusion.62
  75.3 1.5 fusion.62
  78.3 1.5 fusion.62
  81.2 1.5 fusion.62
  84.2 1.5 fusion.62
  87.2 1.5 fusion.62
  90.2 1.5 fusion.62
  96.1 1.5 fusion.62
  99.1 1.5 fusion.62
  102.1 1.5 fusion.62
  105.1 5.2 %collective-permute-start.2 = (f32[1,256]{1,0:T(1,128)S(1)}, f32[1,256]{1,0:T(1,128)S(1)}, u32[]{:S(2)}, u32[]{:S(2)}) collective-permute-start(f32[1,256]{1,0:T(1,128)S(1)} %get-tuple-element.202), channel_id=1, source_target_pairs={{32,0},{64,32},{96,64},{128,96},{160,128},{192,160},{224,192},{33,... | collective-permute-start | bytes 3080 | tf_op jit(solution)/shard_map/ppermute | solution.py:10
  110.4 1.9 collective-permute-start.3
  112.3 2.4 collective-permute-start
  114.7 3.2 %collective-permute-start.1 = (f32[1,256,256]{2,1,0:T(8,128)S(1)}, f32[1,256,256]{2,1,0:T(8,128)S(1)}, u32[]{:S(2)}, u32[]{:S(2)}) collective-permute-start(f32[1,256,256]{2,1,0:T(8,128)S(1)} %get-tuple-element.171), channel_id=1, source_target_pairs={{0,32},{32,64},{64,96},{96,128},{128,160},{160,192},{192,224},{1,3... | collective-permute-start | bytes 786440 | tf_op jit(solution)/shard_map/ppermute | solution.py:10
  121.3 4.4 %collective-permute-start.4 = (bf16[1,256,256]{2,1,0:T(8,128)(2,1)S(1)}, bf16[1,256,256]{2,1,0:T(8,128)(2,1)S(1)}, u32[]{:S(2)}, u32[]{:S(2)}) collective-permute-start(bf16[1,256,256]{2,1,0:T(8,128)(2,1)S(1)} %divide_convert_fusion), channel_id=1, source_target_pairs={{0,32},{32,64},{64,96},{96,128},{128,160},{160,192},{192,224},{1,3... | collective-permute-start | bytes 393224 | tf_op jit(solution)/shard_map/ppermute | solution.py:18
  125.7 1.9 collective-permute-start.5
  127.7 4.3 %collective-permute-done.5 = bf16[1,256,256]{2,1,0:T(8,128)(2,1)S(1)} collective-permute-done((bf16[1,256,256]{2,1,0:T(8,128)(2,1)S(1)}, bf16[1,256,256]{2,1,0:T(8,128)(2,1)S(1)}, u32[]{:S(2)}, u32[]{:S(2)}) %collective-permute-start.5) | collective-permute-done | bytes 131104 | tf_op jit(solution)/shard_map/ppermute | solution.py:21
  141.9 1.6 collective-permute-start.24
  152.4 2.7 %collective-permute-start.26 = (f32[256]{0:T(256)S(1)}, f32[256]{0:T(256)S(1)}, u32[]{:S(2)}, u32[]{:S(2)}) collective-permute-start(f32[256]{0:T(256)S(1)} %broadcast_select_fusion.37), channel_id=1, source_target_pairs={{0,128},{1,129},{2,130},{3,131},{4,132},{5,133},{6,134},{7,135},{8... | collective-permute-start | bytes 3080 | tf_op jit(solution)/shard_map/ppermute | solution.py:83
  155.1 1.8 collective-permute-done.8
  157.3 3.5 %collective-permute-done.9 = f32[32,1024]{1,0:T(8,128)S(1)} collective-permute-done((f32[32,1024]{1,0:T(8,128)S(1)}, f32[32,1024]{1,0:T(8,128)S(1)}, u32[]{:S(2)}, u32[]{:S(2)}) %collective-permute-start.9) | collective-permute-done | bytes 131104 | tf_op jit(solution)/shard_map/ppermute | solution.py:83
  160.9 2.7 %collective-permute-start.10 = (f32[16,1024]{1,0:T(8,128)S(1)}, f32[16,1024]{1,0:T(8,128)S(1)}, u32[]{:S(2)}, u32[]{:S(2)}) collective-permute-start(f32[16,1024]{1,0:T(8,128)S(1)} %slice_select_fusion.3), channel_id=1, source_target_pairs={{0,128},{1,129},{2,130},{3,131},{4,132},{5,133},{6,134},{7,135},{8... | collective-permute-start | bytes 196616 | tf_op jit(solution)/shard_map/ppermute | solution.py:83
  163.6 3.0 %collective-permute-start.27 = (f32[128]{0:T(128)S(1)}, f32[128]{0:T(128)S(1)}, u32[]{:S(2)}, u32[]{:S(2)}) collective-permute-start(f32[128]{0:T(128)S(1)} %broadcast_select_fusion.33), channel_id=1, source_target_pairs={{0,16},{1,17},{2,18},{3,19},{4,20},{5,21},{6,22},{7,23},{8,24},{9,... | collective-permute-start | bytes 1544 | tf_op jit(solution)/shard_map/ppermute | solution.py:83
  166.7 2.1 collective-permute-start.11
  168.8 2.3 collective-permute-done.11
  172.1 2.1 collective-permute-start.28
  175.3 4.5 %collective-permute-start.13 = (f32[2,1024]{1,0:T(2,128)S(1)}, f32[2,1024]{1,0:T(2,128)S(1)}, u32[]{:S(2)}, u32[]{:S(2)}) collective-permute-start(f32[2,1024]{1,0:T(2,128)S(1)} %broadcast_select_fusion.16), channel_id=1, source_target_pairs={{0,4},{1,5},{2,6},{3,7},{4,0},{5,1},{6,2},{7,3},{8,12},{9,13},{10,... | collective-permute-start | bytes 24584 | tf_op jit(solution)/shard_map/ppermute | solution.py:83
  179.8 2.0 collective-permute-done.13
  181.8 4.5 %collective-permute-start.14 = (f32[2,1024]{1,0:T(2,128)S(1)}, f32[2,1024]{1,0:T(2,128)S(1)}, u32[]{:S(2)}, u32[]{:S(2)}) collective-permute-start(f32[2,1024]{1,0:T(2,128)S(1)} %select_add_fusion.8), channel_id=1, source_target_pairs={{0,4},{1,5},{2,6},{3,7},{4,0},{5,1},{6,2},{7,3},{8,12},{9,13},{10,... | collective-permute-start | bytes 24584 | tf_op jit(solution)/shard_map/ppermute | solution.py:87
  189.3 3.4 %collective-permute-done.29 = f32[32]{0:T(128)S(1)} collective-permute-done((f32[32]{0:T(128)S(1)}, f32[32]{0:T(128)S(1)}, u32[]{:S(2)}, u32[]{:S(2)}) %collective-permute-start.29) | collective-permute-done | bytes 160 | tf_op jit(solution)/shard_map/ppermute | solution.py:83
  192.8 2.0 collective-permute-start.30
  196.1 3.1 %collective-permute-done.30 = f32[32]{0:T(128)S(1)} collective-permute-done((f32[32]{0:T(128)S(1)}, f32[32]{0:T(128)S(1)}, u32[]{:S(2)}, u32[]{:S(2)}) %collective-permute-start.30) | collective-permute-done | bytes 160 | tf_op jit(solution)/shard_map/ppermute | solution.py:87
  199.2 2.7 %collective-permute-start.17 = (f32[16,1024]{1,0:T(8,128)S(1)}, f32[16,1024]{1,0:T(8,128)S(1)}, u32[]{:S(2)}, u32[]{:S(2)}) collective-permute-start(f32[16,1024]{1,0:T(8,128)S(1)} %pad_maximum_fusion.4), channel_id=1, source_target_pairs={{0,128},{1,129},{2,130},{3,131},{4,132},{5,133},{6,134},{7,135},{8... | collective-permute-start | bytes 196616 | tf_op jit(solution)/shard_map/ppermute | solution.py:87
  202.0 1.8 collective-permute-start.31
  209.8 1.9 collective-permute-start.33
  211.7 1.8 collective-permute-done.19
  214.9 1.6 collective-permute-done.34
  216.5 5.5 %collective-permute-done.20 = f32[128,1024]{1,0:T(8,128)S(1)} collective-permute-done((f32[128,1024]{1,0:T(8,128)S(1)}, f32[128,1024]{1,0:T(8,128)S(1)}, u32[]{:S(2)}, u32[]{:S(2)}) %collective-permute-start.20) | collective-permute-done | bytes 524320 | tf_op jit(solution)/shard_map/ppermute | solution.py:87
  223.1 15.3 %collective-permute-start.21 = (f32[256,1024]{1,0:T(8,128)}, f32[256,1024]{1,0:T(8,128)S(1)}, u32[]{:S(2)}, u32[]{:S(2)}) collective-permute-start(f32[256,1024]{1,0:T(8,128)} %pad_maximum_fusion), channel_id=1, source_target_pairs={{0,32},{1,33},{2,34},{3,35},{4,36},{5,37},{6,38},{7,39},{8,40},{9,... | collective-permute-start | bytes 3145736 | tf_op jit(solution)/shard_map/ppermute | solution.py:87
  239.1 1.8 collective-permute-done.35
  241.1 2.3 collective-permute-done.36
  243.5 2.5 collective-permute-start.37
  (228 shorter events, 87.4 us)
Async XLA Ops:
  0.6 132.7 %copy-start = (bf16[256,1024]{1,0:T(8,128)(2,1)S(1)}, bf16[256,1024]{1,0:T(8,128)(2,1)}, u32[]{:S(2)}) copy-start(bf16[256,1024]{1,0:T(8,128)(2,1)} %param.31) | copy-start | bytes 1572868
  9.6 108.3 %copy-start.4 = (s32[1,256,8]{1,2,0:T(8,128)S(1)}, s32[1,256,8]{1,2,0:T(8,128)}, u32[]{:S(2)}) copy-start(s32[1,256,8]{1,2,0:T(8,128)} %param.29) | copy-start | bytes 24580
  9.6 108.3 %copy-start.13 = (s32[256]{0:T(256)S(1)}, s32[256]{0:T(256)}, u32[]{:S(2)}) copy-start(s32[256]{0:T(256)} %constant.91.clone) | copy-start | bytes 3076
  9.6 123.4 %copy-start.1 = (bf16[256,1024]{1,0:T(8,128)(2,1)S(1)}, bf16[256,1024]{1,0:T(8,128)(2,1)}, u32[]{:S(2)}) copy-start(bf16[256,1024]{1,0:T(8,128)(2,1)} %param.32) | copy-start | bytes 1572868
  105.1 28.7 %copy-start.3 = (bf16[1024,8]{0,1:T(8,128)(2,1)S(1)}, bf16[1024,8]{0,1:T(8,128)(2,1)}, u32[]{:S(2)}) copy-start(bf16[1024,8]{0,1:T(8,128)(2,1)} %param.33) | copy-start | bytes 49156
  105.1 29.0 %copy-start.5 = (s32[1,256]{1,0:T(1,128)S(1)}, s32[1,256]{1,0:T(1,128)}, u32[]{:S(2)}) copy-start(s32[1,256]{1,0:T(1,128)} %param.30) | copy-start | bytes 3076
  105.1 14.1 %collective-permute-start.2 = (f32[1,256]{1,0:T(1,128)S(1)}, f32[1,256]{1,0:T(1,128)S(1)}, u32[]{:S(2)}, u32[]{:S(2)}) collective-permute-start(f32[1,256]{1,0:T(1,128)S(1)} %get-tuple-element.202), channel_id=1, source_target_pairs={{32,0},{64,32},{96,64},{128,96},{160,128},{192,160},{224,192},{33,... | collective-permute-start | bytes 3080 | tf_op jit(solution)/shard_map/ppermute | solution.py:10
  110.4 8.8 %collective-permute-start.3 = (f32[1,256]{1,0:T(1,128)S(1)}, f32[1,256]{1,0:T(1,128)S(1)}, u32[]{:S(2)}, u32[]{:S(2)}) collective-permute-start(f32[1,256]{1,0:T(1,128)S(1)} %get-tuple-element.203), channel_id=1, source_target_pairs={{0,32},{32,64},{64,96},{96,128},{128,160},{160,192},{192,224},{1,3... | collective-permute-start | bytes 3080 | tf_op jit(solution)/shard_map/ppermute | solution.py:10
  112.3 7.7 %collective-permute-start = (f32[1,256,256]{2,1,0:T(8,128)S(1)}, f32[1,256,256]{2,1,0:T(8,128)S(1)}, u32[]{:S(2)}, u32[]{:S(2)}) collective-permute-start(f32[1,256,256]{2,1,0:T(8,128)S(1)} %get-tuple-element.170), channel_id=1, source_target_pairs={{32,0},{64,32},{96,64},{128,96},{160,128},{192,160},{224,192},{33,... | collective-permute-start | bytes 786440 | tf_op jit(solution)/shard_map/ppermute | solution.py:10
  114.7 6.5 %collective-permute-start.1 = (f32[1,256,256]{2,1,0:T(8,128)S(1)}, f32[1,256,256]{2,1,0:T(8,128)S(1)}, u32[]{:S(2)}, u32[]{:S(2)}) collective-permute-start(f32[1,256,256]{2,1,0:T(8,128)S(1)} %get-tuple-element.171), channel_id=1, source_target_pairs={{0,32},{32,64},{64,96},{96,128},{128,160},{160,192},{192,224},{1,3... | collective-permute-start | bytes 786440 | tf_op jit(solution)/shard_map/ppermute | solution.py:10
  121.3 6.3 %collective-permute-start.4 = (bf16[1,256,256]{2,1,0:T(8,128)(2,1)S(1)}, bf16[1,256,256]{2,1,0:T(8,128)(2,1)S(1)}, u32[]{:S(2)}, u32[]{:S(2)}) collective-permute-start(bf16[1,256,256]{2,1,0:T(8,128)(2,1)S(1)} %divide_convert_fusion), channel_id=1, source_target_pairs={{0,32},{32,64},{64,96},{96,128},{128,160},{160,192},{192,224},{1,3... | collective-permute-start | bytes 393224 | tf_op jit(solution)/shard_map/ppermute | solution.py:18
  125.7 6.3 %collective-permute-start.5 = (bf16[1,256,256]{2,1,0:T(8,128)(2,1)S(1)}, bf16[1,256,256]{2,1,0:T(8,128)(2,1)S(1)}, u32[]{:S(2)}, u32[]{:S(2)}) collective-permute-start(bf16[1,256,256]{2,1,0:T(8,128)(2,1)S(1)} %divide_convert_fusion), channel_id=1, source_target_pairs={{32,0},{64,32},{96,64},{128,96},{160,128},{192,160},{224,192},{33,... | collective-permute-start | bytes 393224 | tf_op jit(solution)/shard_map/ppermute | solution.py:21
  133.3 2.9 %copy-start.12 = (s32[256]{0:T(256)S(1)}, s32[256]{0:T(256)}, u32[]{:S(2)}) copy-start(s32[256]{0:T(256)} %constant.92.clone) | copy-start | bytes 3076
  133.3 5.6 %copy-start.11 = (s32[256]{0:T(256)S(1)}, s32[256]{0:T(256)}, u32[]{:S(2)}) copy-start(s32[256]{0:T(256)} %constant.93.clone) | copy-start | bytes 3076
  134.0 7.1 %copy-start.2 = (f32[256,8]{0,1:T(8,128)}, f32[256,8]{0,1:T(8,128)S(1)}, u32[]{:S(2)}) copy-start(f32[256,8]{0,1:T(8,128)S(1)} %fusion.44) | copy-start | bytes 24580
  134.0 9.5 %copy-start.10 = (s32[256]{0:T(256)S(1)}, s32[256]{0:T(256)}, u32[]{:S(2)}) copy-start(s32[256]{0:T(256)} %constant.94.clone) | copy-start | bytes 3076
  134.1 10.7 %copy-start.9 = (s32[256]{0:T(256)S(1)}, s32[256]{0:T(256)}, u32[]{:S(2)}) copy-start(s32[256]{0:T(256)} %constant.95.clone) | copy-start | bytes 3076
  134.1 12.0 %copy-start.8 = (s32[256]{0:T(256)S(1)}, s32[256]{0:T(256)}, u32[]{:S(2)}) copy-start(s32[256]{0:T(256)} %constant.96.clone) | copy-start | bytes 3076
  134.1 13.2 %copy-start.7 = (s32[256]{0:T(256)S(1)}, s32[256]{0:T(256)}, u32[]{:S(2)}) copy-start(s32[256]{0:T(256)} %constant.97.clone) | copy-start | bytes 3076
  134.1 14.4 %copy-start.6 = (s32[256]{0:T(256)S(1)}, s32[256]{0:T(256)}, u32[]{:S(2)}) copy-start(s32[256]{0:T(256)} %constant.98.clone) | copy-start | bytes 3076
  135.3 5.4 %collective-permute-start.6 = (f32[256,1024]{1,0:T(8,128)S(1)}, f32[256,1024]{1,0:T(8,128)S(1)}, u32[]{:S(2)}, u32[]{:S(2)}) collective-permute-start(f32[256,1024]{1,0:T(8,128)S(1)} %get-tuple-element.214), channel_id=1, source_target_pairs={{0,32},{1,33},{2,34},{3,35},{4,36},{5,37},{6,38},{7,39},{8,40},{9,... | collective-permute-start | bytes 3145736 | tf_op jit(solution)/shard_map/ppermute | solution.py:83
  135.6 2.5 collective-permute-start.22
  138.1 2.6 %collective-permute-start.23 = (f32[2048]{0:T(1024)S(1)}, f32[2048]{0:T(1024)S(1)}, u32[]{:S(2)}, u32[]{:S(2)}) collective-permute-start(f32[2048]{0:T(1024)S(1)} %slice_select_fusion.6), channel_id=1, source_target_pairs={{0,64},{1,65},{2,66},{3,67},{4,68},{5,69},{6,70},{7,71},{8,72},{9,... | collective-permute-start | bytes 24584 | tf_op jit(solution)/shard_map/ppermute | solution.py:83
  141.1 10.0 %collective-permute-start.7 = (f32[128,1024]{1,0:T(8,128)S(1)}, f32[128,1024]{1,0:T(8,128)S(1)}, u32[]{:S(2)}, u32[]{:S(2)}) collective-permute-start(f32[128,1024]{1,0:T(8,128)S(1)} %slice_select_fusion), channel_id=1, source_target_pairs={{0,64},{1,65},{2,66},{3,67},{4,68},{5,69},{6,70},{7,71},{8,72},{9,... | collective-permute-start | bytes 1572872 | tf_op jit(solution)/shard_map/ppermute | solution.py:83
  141.9 7.9 %collective-permute-start.24 = (f32[1024]{0:T(1024)S(1)}, f32[1024]{0:T(1024)S(1)}, u32[]{:S(2)}, u32[]{:S(2)}) collective-permute-start(f32[1024]{0:T(1024)S(1)} %slice_select_fusion.7), channel_id=1, source_target_pairs={{0,8},{1,9},{2,10},{3,11},{4,12},{5,13},{6,14},{7,15},{8,0},{9,1},... | collective-permute-start | bytes 12296 | tf_op jit(solution)/shard_map/ppermute | solution.py:83
  149.8 2.5 %collective-permute-start.25 = (f32[512]{0:T(512)S(1)}, f32[512]{0:T(512)S(1)}, u32[]{:S(2)}, u32[]{:S(2)}) collective-permute-start(f32[512]{0:T(512)S(1)} %slice_select_fusion.8), channel_id=1, source_target_pairs={{0,1},{1,0},{2,3},{3,2},{4,5},{5,4},{6,7},{7,6},{8,9},{9,8},{10,11... | collective-permute-start | bytes 6152 | tf_op jit(solution)/shard_map/ppermute | solution.py:83
  151.3 5.6 %collective-permute-start.8 = (f32[64,1024]{1,0:T(8,128)S(1)}, f32[64,1024]{1,0:T(8,128)S(1)}, u32[]{:S(2)}, u32[]{:S(2)}) collective-permute-start(f32[64,1024]{1,0:T(8,128)S(1)} %slice_select_fusion.1), channel_id=1, source_target_pairs={{0,8},{1,9},{2,10},{3,11},{4,12},{5,13},{6,14},{7,15},{8,0},{9,1},... | collective-permute-start | bytes 786440 | tf_op jit(solution)/shard_map/ppermute | solution.py:83
  152.4 5.0 %collective-permute-start.26 = (f32[256]{0:T(256)S(1)}, f32[256]{0:T(256)S(1)}, u32[]{:S(2)}, u32[]{:S(2)}) collective-permute-start(f32[256]{0:T(256)S(1)} %broadcast_select_fusion.37), channel_id=1, source_target_pairs={{0,128},{1,129},{2,130},{3,131},{4,132},{5,133},{6,134},{7,135},{8... | collective-permute-start | bytes 3080 | tf_op jit(solution)/shard_map/ppermute | solution.py:83
  157.0 3.9 %collective-permute-start.9 = (f32[32,1024]{1,0:T(8,128)S(1)}, f32[32,1024]{1,0:T(8,128)S(1)}, u32[]{:S(2)}, u32[]{:S(2)}) collective-permute-start(f32[32,1024]{1,0:T(8,128)S(1)} %slice_select_fusion.2), channel_id=1, source_target_pairs={{0,1},{1,0},{2,3},{3,2},{4,5},{5,4},{6,7},{7,6},{8,9},{9,8},{10,11... | collective-permute-start | bytes 393224 | tf_op jit(solution)/shard_map/ppermute | solution.py:83
  160.9 5.7 %collective-permute-start.10 = (f32[16,1024]{1,0:T(8,128)S(1)}, f32[16,1024]{1,0:T(8,128)S(1)}, u32[]{:S(2)}, u32[]{:S(2)}) collective-permute-start(f32[16,1024]{1,0:T(8,128)S(1)} %slice_select_fusion.3), channel_id=1, source_target_pairs={{0,128},{1,129},{2,130},{3,131},{4,132},{5,133},{6,134},{7,135},{8... | collective-permute-start | bytes 196616 | tf_op jit(solution)/shard_map/ppermute | solution.py:83
  163.6 5.1 %collective-permute-start.27 = (f32[128]{0:T(128)S(1)}, f32[128]{0:T(128)S(1)}, u32[]{:S(2)}, u32[]{:S(2)}) collective-permute-start(f32[128]{0:T(128)S(1)} %broadcast_select_fusion.33), channel_id=1, source_target_pairs={{0,16},{1,17},{2,18},{3,19},{4,20},{5,21},{6,22},{7,23},{8,24},{9,... | collective-permute-start | bytes 1544 | tf_op jit(solution)/shard_map/ppermute | solution.py:83
  166.7 4.4 %collective-permute-start.11 = (f32[8,1024]{1,0:T(8,128)S(1)}, f32[8,1024]{1,0:T(8,128)S(1)}, u32[]{:S(2)}, u32[]{:S(2)}) collective-permute-start(f32[8,1024]{1,0:T(8,128)S(1)} %slice_select_fusion.4), channel_id=1, source_target_pairs={{0,16},{1,17},{2,18},{3,19},{4,20},{5,21},{6,22},{7,23},{8,24},{9,... | collective-permute-start | bytes 98312 | tf_op jit(solution)/shard_map/ppermute | solution.py:83
  171.1 4.2 %collective-permute-start.12 = (f32[4,1024]{1,0:T(4,128)S(1)}, f32[4,1024]{1,0:T(4,128)S(1)}, u32[]{:S(2)}, u32[]{:S(2)}) collective-permute-start(f32[4,1024]{1,0:T(4,128)S(1)} %slice_select_fusion.5), channel_id=1, source_target_pairs={{0,2},{1,3},{2,0},{3,1},{4,6},{5,7},{6,4},{7,5},{8,10},{9,11},{10,... | collective-permute-start | bytes 49160 | tf_op jit(solution)/shard_map/ppermute | solution.py:83
  172.1 7.6 %collective-permute-start.28 = (f32[64]{0:T(128)S(1)}, f32[64]{0:T(128)S(1)}, u32[]{:S(2)}, u32[]{:S(2)}) collective-permute-start(f32[64]{0:T(128)S(1)} %broadcast_select_fusion.29), channel_id=1, source_target_pairs={{0,2},{1,3},{2,0},{3,1},{4,6},{5,7},{6,4},{7,5},{8,10},{9,11},{10,... | collective-permute-start | bytes 776 | tf_op jit(solution)/shard_map/ppermute | solution.py:83
  175.3 6.5 %collective-permute-start.13 = (f32[2,1024]{1,0:T(2,128)S(1)}, f32[2,1024]{1,0:T(2,128)S(1)}, u32[]{:S(2)}, u32[]{:S(2)}) collective-permute-start(f32[2,1024]{1,0:T(2,128)S(1)} %broadcast_select_fusion.16), channel_id=1, source_target_pairs={{0,4},{1,5},{2,6},{3,7},{4,0},{5,1},{6,2},{7,3},{8,12},{9,13},{10,... | collective-permute-start | bytes 24584 | tf_op jit(solution)/shard_map/ppermute | solution.py:83
  181.8 6.5 %collective-permute-start.14 = (f32[2,1024]{1,0:T(2,128)S(1)}, f32[2,1024]{1,0:T(2,128)S(1)}, u32[]{:S(2)}, u32[]{:S(2)}) collective-permute-start(f32[2,1024]{1,0:T(2,128)S(1)} %select_add_fusion.8), channel_id=1, source_target_pairs={{0,4},{1,5},{2,6},{3,7},{4,0},{5,1},{6,2},{7,3},{8,12},{9,13},{10,... | collective-permute-start | bytes 24584 | tf_op jit(solution)/shard_map/ppermute | solution.py:87
  186.4 6.3 %collective-permute-start.29 = (f32[32]{0:T(128)S(1)}, f32[32]{0:T(128)S(1)}, u32[]{:S(2)}, u32[]{:S(2)}) collective-permute-start(f32[32]{0:T(128)S(1)} %broadcast_select_fusion.25), channel_id=1, source_target_pairs={{0,4},{1,5},{2,6},{3,7},{4,0},{5,1},{6,2},{7,3},{8,12},{9,13},{10,... | collective-permute-start | bytes 392 | tf_op jit(solution)/shard_map/ppermute | solution.py:83
  188.3 6.5 %collective-permute-start.15 = (f32[4,1024]{1,0:T(4,128)S(1)}, f32[4,1024]{1,0:T(4,128)S(1)}, u32[]{:S(2)}, u32[]{:S(2)}) collective-permute-start(f32[4,1024]{1,0:T(4,128)S(1)} %pad_maximum_fusion.6), channel_id=1, source_target_pairs={{0,2},{1,3},{2,0},{3,1},{4,6},{5,7},{6,4},{7,5},{8,10},{9,11},{10,... | collective-permute-start | bytes 49160 | tf_op jit(solution)/shard_map/ppermute | solution.py:87
  192.8 6.3 %collective-permute-start.30 = (f32[32]{0:T(128)S(1)}, f32[32]{0:T(128)S(1)}, u32[]{:S(2)}, u32[]{:S(2)}) collective-permute-start(f32[32]{0:T(128)S(1)} %fusion.37), channel_id=1, source_target_pairs={{0,4},{1,5},{2,6},{3,7},{4,0},{5,1},{6,2},{7,3},{8,12},{9,13},{10,... | collective-permute-start | bytes 392 | tf_op jit(solution)/shard_map/ppermute | solution.py:87
  194.8 4.3 %collective-permute-start.16 = (f32[8,1024]{1,0:T(8,128)S(1)}, f32[8,1024]{1,0:T(8,128)S(1)}, u32[]{:S(2)}, u32[]{:S(2)}) collective-permute-start(f32[8,1024]{1,0:T(8,128)S(1)} %pad_maximum_fusion.5), channel_id=1, source_target_pairs={{0,16},{1,17},{2,18},{3,19},{4,20},{5,21},{6,22},{7,23},{8,24},{9,... | collective-permute-start | bytes 98312 | tf_op jit(solution)/shard_map/ppermute | solution.py:87
  199.2 4.7 %collective-permute-start.17 = (f32[16,1024]{1,0:T(8,128)S(1)}, f32[16,1024]{1,0:T(8,128)S(1)}, u32[]{:S(2)}, u32[]{:S(2)}) collective-permute-start(f32[16,1024]{1,0:T(8,128)S(1)} %pad_maximum_fusion.4), channel_id=1, source_target_pairs={{0,128},{1,129},{2,130},{3,131},{4,132},{5,133},{6,134},{7,135},{8... | collective-permute-start | bytes 196616 | tf_op jit(solution)/shard_map/ppermute | solution.py:87
  202.0 3.9 %collective-permute-start.31 = (f32[64]{0:T(128)S(1)}, f32[64]{0:T(128)S(1)}, u32[]{:S(2)}, u32[]{:S(2)}) collective-permute-start(f32[64]{0:T(128)S(1)} %pad_maximum_fusion.12), channel_id=1, source_target_pairs={{0,2},{1,3},{2,0},{3,1},{4,6},{5,7},{6,4},{7,5},{8,10},{9,11},{10,... | collective-permute-start | bytes 776 | tf_op jit(solution)/shard_map/ppermute | solution.py:87
  203.9 4.2 %collective-permute-start.18 = (f32[32,1024]{1,0:T(8,128)S(1)}, f32[32,1024]{1,0:T(8,128)S(1)}, u32[]{:S(2)}, u32[]{:S(2)}) collective-permute-start(f32[32,1024]{1,0:T(8,128)S(1)} %pad_maximum_fusion.3), channel_id=1, source_target_pairs={{0,1},{1,0},{2,3},{3,2},{4,5},{5,4},{6,7},{7,6},{8,9},{9,8},{10,11... | collective-permute-start | bytes 393224 | tf_op jit(solution)/shard_map/ppermute | solution.py:87
  206.0 3.6 %collective-permute-start.32 = (f32[128]{0:T(128)S(1)}, f32[128]{0:T(128)S(1)}, u32[]{:S(2)}, u32[]{:S(2)}) collective-permute-start(f32[128]{0:T(128)S(1)} %pad_maximum_fusion.13), channel_id=1, source_target_pairs={{0,16},{1,17},{2,18},{3,19},{4,20},{5,21},{6,22},{7,23},{8,24},{9,... | collective-permute-start | bytes 1544 | tf_op jit(solution)/shard_map/ppermute | solution.py:87
  208.2 5.3 %collective-permute-start.19 = (f32[64,1024]{1,0:T(8,128)S(1)}, f32[64,1024]{1,0:T(8,128)S(1)}, u32[]{:S(2)}, u32[]{:S(2)}) collective-permute-start(f32[64,1024]{1,0:T(8,128)S(1)} %pad_maximum_fusion.2), channel_id=1, source_target_pairs={{0,8},{1,9},{2,10},{3,11},{4,12},{5,13},{6,14},{7,15},{8,0},{9,1},... | collective-permute-start | bytes 786440 | tf_op jit(solution)/shard_map/ppermute | solution.py:87
  209.8 4.2 %collective-permute-start.33 = (f32[256]{0:T(256)S(1)}, f32[256]{0:T(256)S(1)}, u32[]{:S(2)}, u32[]{:S(2)}) collective-permute-start(f32[256]{0:T(256)S(1)} %pad_maximum_fusion.11), channel_id=1, source_target_pairs={{0,128},{1,129},{2,130},{3,131},{4,132},{5,133},{6,134},{7,135},{8... | collective-permute-start | bytes 3080 | tf_op jit(solution)/shard_map/ppermute | solution.py:87
  213.6 8.4 %collective-permute-start.20 = (f32[128,1024]{1,0:T(8,128)S(1)}, f32[128,1024]{1,0:T(8,128)S(1)}, u32[]{:S(2)}, u32[]{:S(2)}) collective-permute-start(f32[128,1024]{1,0:T(8,128)S(1)} %pad_maximum_fusion.1), channel_id=1, source_target_pairs={{0,64},{1,65},{2,66},{3,67},{4,68},{5,69},{6,70},{7,71},{8,72},{9,... | collective-permute-start | bytes 1572872 | tf_op jit(solution)/shard_map/ppermute | solution.py:87
  214.0 2.5 %collective-permute-start.34 = (f32[512]{0:T(512)S(1)}, f32[512]{0:T(512)S(1)}, u32[]{:S(2)}, u32[]{:S(2)}) collective-permute-start(f32[512]{0:T(512)S(1)} %pad_maximum_fusion.10), channel_id=1, source_target_pairs={{0,1},{1,0},{2,3},{3,2},{4,5},{5,4},{6,7},{7,6},{8,9},{9,8},{10,11... | collective-permute-start | bytes 6152 | tf_op jit(solution)/shard_map/ppermute | solution.py:87
  223.1 24.3 %collective-permute-start.21 = (f32[256,1024]{1,0:T(8,128)}, f32[256,1024]{1,0:T(8,128)S(1)}, u32[]{:S(2)}, u32[]{:S(2)}) collective-permute-start(f32[256,1024]{1,0:T(8,128)} %pad_maximum_fusion), channel_id=1, source_target_pairs={{0,32},{1,33},{2,34},{3,35},{4,36},{5,37},{6,38},{7,39},{8,40},{9,... | collective-permute-start | bytes 3145736 | tf_op jit(solution)/shard_map/ppermute | solution.py:87
  238.4 2.5 collective-permute-start.35
  240.9 2.6 %collective-permute-start.36 = (f32[2048]{0:T(1024)S(1)}, f32[2048]{0:T(1024)S(1)}, u32[]{:S(2)}, u32[]{:S(2)}) collective-permute-start(f32[2048]{0:T(1024)S(1)} %pad_maximum_fusion.8), channel_id=1, source_target_pairs={{0,64},{1,65},{2,66},{3,67},{4,68},{5,69},{6,70},{7,71},{8,72},{9,... | collective-permute-start | bytes 24584 | tf_op jit(solution)/shard_map/ppermute | solution.py:87
  243.5 3.3 %collective-permute-start.37 = (f32[4096]{0:T(1024)S(1)}, f32[4096]{0:T(1024)S(1)}, u32[]{:S(2)}, u32[]{:S(2)}) collective-permute-start(f32[4096]{0:T(1024)S(1)} %pad_maximum_fusion.7), channel_id=1, source_target_pairs={{0,32},{1,33},{2,34},{3,35},{4,36},{5,37},{6,38},{7,39},{8,40},{9,... | collective-permute-start | bytes 49160 | tf_op jit(solution)/shard_map/ppermute | solution.py:87

commit v2 on v1

--- a/solution.py
+++ b/solution.py
@@ -1,6 +1,7 @@
 import jax
 import jax.numpy as jnp
 from jax import lax
+from jax.experimental import pallas as pl
 from jax.sharding import PartitionSpec as P
 
 
@@ -23,31 +24,48 @@
     return block
 
 
+def pooled_sums_kernel(ids_ref, rows_ref, sums_ref):
+    @pl.when(pl.program_id(0) == 0)
+    def _():
+        sums_ref[...] = jnp.zeros_like(sums_ref)
+
+    width = sums_ref.shape[0]
+    slots = lax.broadcasted_iota(jnp.int32, (width, ids_ref.shape[1]), 0)
+    member = (ids_ref[...] == slots).astype(jnp.bfloat16)
+    sums_ref[...] += jnp.dot(member, rows_ref[...], preferred_element_type=jnp.float32)
+
+
 def accumulate(cluster_ids, weighted, weights, width):
-    events, length, feats = weighted.shape
-    block = min(512, length)
-    slots = jnp.arange(width, dtype=jnp.int32)
-
-    def add_block(index, carry):
-        numer, denom = carry
-        start = index * block
-        ids = lax.dynamic_slice_in_dim(cluster_ids, start, block, 1)
-        rows = lax.dynamic_slice_in_dim(weighted, start, block, 1)
-        scale = lax.dynamic_slice_in_dim(weights, start, block, 1)
-        member = ids[:, None, :] == slots[None, :, None]
-        numer = numer + jnp.einsum(
-            "ekb,ebf->ekf", member.astype(jnp.bfloat16), rows, preferred_element_type=jnp.float32
-        )
-        denom = denom + jnp.einsum(
-            "ekb,eb->ek", member.astype(jnp.float32), scale, precision=lax.Precision.HIGHEST
-        )
-        return (numer, denom)
-
-    start_sums = (
-        jnp.zeros((events, width, feats), jnp.float32),
-        jnp.zeros((events, width), jnp.float32),
+    length, feats = weighted.shape
+    high = weights.astype(jnp.bfloat16)
+    rest = weights - high.astype(jnp.float32)
+    middle = rest.astype(jnp.bfloat16)
+    low = (rest - middle.astype(jnp.float32)).astype(jnp.bfloat16)
+    lanes = 128
+    parts = jnp.stack([high, middle, low], axis=-1)
+    rows = jnp.concatenate(
+        [weighted, parts, jnp.zeros((length, lanes - 3), jnp.bfloat16)], axis=-1
     )
-    return lax.fori_loop(0, length // block, add_block, start_sums)
+    block = min(1024, length)
+    total = feats + lanes
+    sums = pl.pallas_call(
+        pooled_sums_kernel,
+        grid=(length // block,),
+        in_specs=[
+            pl.BlockSpec((1, block), lambda i: (0, i)),
+            pl.BlockSpec((block, total), lambda i: (i, 0)),
+        ],
+        out_specs=pl.BlockSpec((width, total), lambda i: (0, 0)),
+        out_shape=jax.ShapeDtypeStruct((width, total), jnp.float32),
+        cost_estimate=pl.CostEstimate(
+            flops=2 * width * length * total,
+            bytes_accessed=length * total * 2 + length * 4 + width * total * 4,
+            transcendentals=0,
+        ),
+    )(cluster_ids.reshape(1, length), rows)
+    numer = sums[:, :feats]
+    denom = sums[:, feats] + sums[:, feats + 1] + sums[:, feats + 2]
+    return numer[None], denom[None]
 
 
 def halving_plan(sizes):
@@ -98,7 +116,7 @@
     degree = cluster_edges.shape[2]
     weighted = (cell_weight[..., None] * cells.astype(jnp.float32)).astype(jnp.bfloat16)
     relative = cell_cluster - (region - 1) * owned
-    numer_three, denom_three = accumulate(relative, weighted, cell_weight, 3 * owned)
+    numer_three, denom_three = accumulate(relative[0], weighted[0], cell_weight[0], 3 * owned)
     above_numer, above_denom = passed_along(
         (numer_three[:, :owned], denom_three[:, :owned]), "region", -1
     )

time: 251 us -> 232 us (0.924)
  matrix products: 98.4 us -> 3.33 us
  local copies, waits for them, and re-layouts: 4.93 us -> 49.8 us
  Pallas kernels: 0 us -> 19.4 us
  other arithmetic: 13.9 us -> 26.5 us
    dot_general x64 -> x0, matrix products: 95.1 us -> none  [the longest x32 47.9 us: add_block(): jnp.einsum('ekb,ebf->ekf', member.astype(jnp.bfloat16), rows, preferred_e...]
    concatenate x0 -> x1, local copies, waits for them, and re-layouts: none -> 28.2 us  [accumulate(): jnp.concatenate([weighted, parts, jnp.zeros((length, lanes - 3), jnp.bflo...]
    pallas_call x0 -> x1, Pallas kernels: none -> 19.4 us  [accumulate(): pl.pallas_call(pooled_sums_kernel, grid=(length // block,), in_specs=[pl....]
    convert_element_type x0 -> x2, local copies, waits for them, and re-layouts: none -> 8.29 us  [the longest x1 4.81 us: accumulate(): rest = weights - high.astype(jnp.float32)]
    squeeze x0 -> x1, other arithmetic: none -> 7.94 us  [local(): weighted[0]]
    squeeze x0 -> x1, local copies, waits for them, and re-layouts: none -> 4.87 us  [local(): cell_weight[0]]
    broadcast_in_dim x0 -> x2, local copies, waits for them, and re-layouts: none -> 3.53 us  [the longest x1 2.35 us: accumulate(): jnp.zeros((length, lanes - 3), jnp.bfloat16)]
    convert_element_type x1 -> x2, other arithmetic: 7.98 us -> 11.1 us  [the longest x1 10.1 us: accumulate(): low = (rest - middle.astype(jnp.float32)).astype(jnp.bfloat16)]
where the time goes in v2:
time: 232 us; the launch traced here: 231 us
  starting transfers between devices  81 us (35%)
  local copies, waits for them, and re-layouts  49.8 us (21%)
  waiting for transfers between devices  44.2 us (19%)
  other arithmetic  26.5 us (11%)
  Pallas kernels  19.4 us (8%)
  between operations  6.48 us (3%)
  matrix products  3.33 us (1%)
    ppermute x16, starting transfers between devices, all_sum(): got = lax.ppermute(buffers, axes, perm)  37.3 us
    concatenate x1, local copies, waits for them, and re-layouts, accumulate(): jnp.concatenate([weighted, parts, jnp.zeros((length, lanes - 3), jnp.bflo...  28.2 us
    ppermute x16, starting transfers between devices, all_sum(): got = lax.ppermute(tuple(sends), axes, perm)  24.8 us
    ppermute x16, waiting for transfers between devices, all_sum(): got = lax.ppermute(buffers, axes, perm)  21.6 us
    pallas_call x1, Pallas kernels, accumulate(): pl.pallas_call(pooled_sums_kernel, grid=(length // block,), in_specs=[pl....  19.4 us
    ppermute x16, waiting for transfers between devices, all_sum(): got = lax.ppermute(tuple(sends), axes, perm)  16.3 us
    ppermute x4, starting transfers between devices, passed_along(): lax.ppermute(value, axis, [(source, source + steps) for source in range(i...  12.6 us
    convert_element_type x1, other arithmetic, accumulate(): low = (rest - middle.astype(jnp.float32)).astype(jnp.bfloat16)  10.1 us
  transfers between devices with their start and end apart: 38, of which 24 were waited for; matrix products, arithmetic and copies ran while one was open for 3% of the time, Pallas kernels for 0%

profile of v2, /device:TPU:1, one launch (start us, length us, event | category | flops | bytes accessed | tf_op | source)
XLA Modules:
  0.0 230.6 jit_solution(16425387328254862454)
XLA Ops:
  0.7 1.0 fusion.30
  1.6 4.8 %copy.31 = f32[16384,1]{1,0:T(8,128)} copy(f32[16384,1]{0,1:T(1,128)S(1)} %get-tuple-element.20) | data formatting | bytes 131072 | tf_op jit(solution)/shard_map/convert_element_type | solution.py:41
  6.5 4.9 %copy.30 = f32[16384,1]{1,0:T(8,128)} copy(f32[16384,1]{0,1:T(1,128)S(1)} %bitcast.64) | data formatting | bytes 131072 | tf_op jit(solution)/shard_map/squeeze | solution.py:119
  11.3 3.5 %copy.32 = bf16[16384,1]{1,0:T(8,128)(2,1)} copy(bf16[16384,1]{0,1:T(2,128)(2,1)S(1)} %get-tuple-element.21) | data formatting | bytes 65536 | tf_op jit(solution)/shard_map/convert_element_type | solution.py:40
  14.8 10.1 %subtract_convert_fusion = (bf16[16384,1]{1,0:T(8,128)(2,1)}, bf16[16384,1]{1,0:T(8,128)(2,1)}) fusion(f32[16384,1]{1,0:T(8,128)} %copy.30, f32[16384,1]{1,0:T(8,128)} %copy.31), kind=kLoop, calls=%fused_computation.2 | loop fusion | flops 81920 | bytes 196608 | tf_op jit(solution)/shard_map/convert_element_type | solution.py:43
  24.9 7.9 %fusion = bf16[16384,256]{1,0:T(8,128)(2,1)} fusion(bf16[1,16384,256]{2,1,0:T(8,128)(2,1)} %param.24, f32[16384]{0:T(1024)S(1)} %bitcast.65), kind=kLoop, calls=%fused_computation.1 | loop fusion | flops 12582912 | bytes 16842752 | tf_op jit(solution)/shard_map/squeeze | solution.py:119
  33.6 2.3 %broadcast_in_dim.4 = bf16[16384,125]{1,0:T(8,128)(2,1)} broadcast(bf16[]{:T(256)} %constant.54.clone.1), dimensions={} | broadcast | bytes 4096002 | tf_op jit(solution)/shard_map/broadcast_in_dim | solution.py:47
  35.9 28.2 %concatenate.56.rows_ref = bf16[16384,384]{1,0:T(8,128)(2,1)} concatenate(bf16[16384,256]{1,0:T(8,128)(2,1)} %fusion, bf16[16384,1]{1,0:T(8,128)(2,1)} %copy.32, bf16[16384,1]{1,0:T(8,128)(2,1)} %get-tuple-element.5, bf16[16384,1]{1,0:T(8,128)(2,1)} %get-tuple-element.4, bf16[16384,125]{1,0:T(8,128)(2,1)} %broadcast_in_dim.4), dimensions={1} | concatenate | bytes 25165824 | tf_op jit(solution)/shard_map/concatenate | solution.py:46
  64.1 19.4 %shard_map.255 = f32[768,384]{1,0:T(8,128)} custom-call(s32[1,16384]{1,0:T(1,128)} %broadcast_subtract_fusion.ids_ref, bf16[16384,384]{1,0:T(8,128)(2,1)} %concatenate.56.rows_ref), custom_call_target="tpu_custom_call" | custom-call | flops 9663676416 | bytes 13828096 | tf_op jit(solution)/shard_map/pallas_call | solution.py:51
  83.5 1.8 fusion.6
  85.4 5.1 %collective-permute-start.2 = (f32[1,256]{1,0:T(1,128)S(1)}, f32[1,256]{1,0:T(1,128)S(1)}, u32[]{:S(2)}, u32[]{:S(2)}) collective-permute-start(f32[1,256]{1,0:T(1,128)S(1)} %get-tuple-element.44), channel_id=1, source_target_pairs={{32,0},{64,32},{96,64},{128,96},{160,128},{192,160},{224,192},{33,... | collective-permute-start | bytes 3080 | tf_op jit(solution)/shard_map/ppermute | solution.py:11
  90.5 1.9 collective-permute-start.3
  92.4 1.2 slice_bitcast_fusion
  93.6 2.4 %collective-permute-start = (f32[1,256,256]{2,1,0:T(8,128)S(1)}, f32[1,256,256]{2,1,0:T(8,128)S(1)}, u32[]{:S(2)}, u32[]{:S(2)}) collective-permute-start(f32[1,256,256]{2,1,0:T(8,128)S(1)} %get-tuple-element.10), channel_id=1, source_target_pairs={{32,0},{64,32},{96,64},{128,96},{160,128},{192,160},{224,192},{33,... | collective-permute-start | bytes 786440 | tf_op jit(solution)/shard_map/ppermute | solution.py:11
  96.0 3.2 %collective-permute-start.1 = (f32[1,256,256]{2,1,0:T(8,128)S(1)}, f32[1,256,256]{2,1,0:T(8,128)S(1)}, u32[]{:S(2)}, u32[]{:S(2)}) collective-permute-start(f32[1,256,256]{2,1,0:T(8,128)S(1)} %get-tuple-element.11), channel_id=1, source_target_pairs={{0,32},{32,64},{64,96},{96,128},{128,160},{160,192},{192,224},{1,3... | collective-permute-start | bytes 786440 | tf_op jit(solution)/shard_map/ppermute | solution.py:11
  100.5 0.8 collective-permute-done
  101.3 1.2 collective-permute-done.1
  102.6 4.4 %collective-permute-start.4 = (bf16[1,256,256]{2,1,0:T(8,128)(2,1)S(1)}, bf16[1,256,256]{2,1,0:T(8,128)(2,1)S(1)}, u32[]{:S(2)}, u32[]{:S(2)}) collective-permute-start(bf16[1,256,256]{2,1,0:T(8,128)(2,1)S(1)} %fusion.21), channel_id=1, source_target_pairs={{0,32},{32,64},{64,96},{96,128},{128,160},{160,192},{192,224},{1,3... | collective-permute-start | bytes 393224 | tf_op jit(solution)/shard_map/ppermute | solution.py:19
  107.0 1.9 collective-permute-start.5
  109.0 4.3 %collective-permute-done.5 = bf16[1,256,256]{2,1,0:T(8,128)(2,1)S(1)} collective-permute-done((bf16[1,256,256]{2,1,0:T(8,128)(2,1)S(1)}, bf16[1,256,256]{2,1,0:T(8,128)(2,1)S(1)}, u32[]{:S(2)}, u32[]{:S(2)}) %collective-permute-start.5) | collective-permute-done | bytes 131104 | tf_op jit(solution)/shard_map/ppermute | solution.py:22
  113.3 1.0 fusion.3
  119.4 0.8 collective-permute-start.23
  122.4 0.8 collective-permute-start.7
  123.2 1.6 collective-permute-start.24
  131.1 1.5 collective-permute-start.25
  132.8 1.0 collective-permute-done.25
  133.8 2.7 %collective-permute-start.26 = (f32[256]{0:T(256)S(1)}, f32[256]{0:T(256)S(1)}, u32[]{:S(2)}, u32[]{:S(2)}) collective-permute-start(f32[256]{0:T(256)S(1)} %broadcast_select_fusion.36), channel_id=1, source_target_pairs={{0,128},{1,129},{2,130},{3,131},{4,132},{5,133},{6,134},{7,135},{8... | collective-permute-start | bytes 3080 | tf_op jit(solution)/shard_map/ppermute | solution.py:101
  136.5 1.8 collective-permute-done.8
  138.8 3.5 %collective-permute-done.9 = f32[32,1024]{1,0:T(8,128)S(1)} collective-permute-done((f32[32,1024]{1,0:T(8,128)S(1)}, f32[32,1024]{1,0:T(8,128)S(1)}, u32[]{:S(2)}, u32[]{:S(2)}) %collective-permute-start.9) | collective-permute-done | bytes 131104 | tf_op jit(solution)/shard_map/ppermute | solution.py:101
  142.4 2.7 %collective-permute-start.10 = (f32[16,1024]{1,0:T(8,128)S(1)}, f32[16,1024]{1,0:T(8,128)S(1)}, u32[]{:S(2)}, u32[]{:S(2)}) collective-permute-start(f32[16,1024]{1,0:T(8,128)S(1)} %slice_select_fusion.3), channel_id=1, source_target_pairs={{0,128},{1,129},{2,130},{3,131},{4,132},{5,133},{6,134},{7,135},{8... | collective-permute-start | bytes 196616 | tf_op jit(solution)/shard_map/ppermute | solution.py:101
  145.1 3.0 %collective-permute-start.27 = (f32[128]{0:T(128)S(1)}, f32[128]{0:T(128)S(1)}, u32[]{:S(2)}, u32[]{:S(2)}) collective-permute-start(f32[128]{0:T(128)S(1)} %broadcast_select_fusion.32), channel_id=1, source_target_pairs={{0,16},{1,17},{2,18},{3,19},{4,20},{5,21},{6,22},{7,23},{8,24},{9,... | collective-permute-start | bytes 1544 | tf_op jit(solution)/shard_map/ppermute | solution.py:101
  148.1 2.1 collective-permute-start.11
  150.2 2.3 %collective-permute-done.11 = f32[8,1024]{1,0:T(8,128)S(1)} collective-permute-done((f32[8,1024]{1,0:T(8,128)S(1)}, f32[8,1024]{1,0:T(8,128)S(1)}, u32[]{:S(2)}, u32[]{:S(2)}) %collective-permute-start.11) | collective-permute-done | bytes 32800 | tf_op jit(solution)/shard_map/ppermute | solution.py:101
  152.6 1.0 collective-permute-start.12
  153.6 2.1 collective-permute-start.28
  155.7 1.1 collective-permute-done.12
  156.8 4.5 %collective-permute-start.13 = (f32[2,1024]{1,0:T(2,128)S(1)}, f32[2,1024]{1,0:T(2,128)S(1)}, u32[]{:S(2)}, u32[]{:S(2)}) collective-permute-start(f32[2,1024]{1,0:T(2,128)S(1)} %broadcast_select_fusion.15), channel_id=1, source_target_pairs={{0,4},{1,5},{2,6},{3,7},{4,0},{5,1},{6,2},{7,3},{8,12},{9,13},{10,... | collective-permute-start | bytes 24584 | tf_op jit(solution)/shard_map/ppermute | solution.py:101
  161.3 2.0 collective-permute-done.13
  163.3 4.5 %collective-permute-start.14 = (f32[2,1024]{1,0:T(2,128)S(1)}, f32[2,1024]{1,0:T(2,128)S(1)}, u32[]{:S(2)}, u32[]{:S(2)}) collective-permute-start(f32[2,1024]{1,0:T(2,128)S(1)} %select_add_fusion.8), channel_id=1, source_target_pairs={{0,4},{1,5},{2,6},{3,7},{4,0},{5,1},{6,2},{7,3},{8,12},{9,13},{10,... | collective-permute-start | bytes 24584 | tf_op jit(solution)/shard_map/ppermute | solution.py:105
  167.9 0.9 collective-permute-start.29
  168.8 1.0 collective-permute-done.14
  169.8 1.0 collective-permute-start.15
  170.8 3.4 %collective-permute-done.29 = f32[32]{0:T(128)S(1)} collective-permute-done((f32[32]{0:T(128)S(1)}, f32[32]{0:T(128)S(1)}, u32[]{:S(2)}, u32[]{:S(2)}) %collective-permute-start.29) | collective-permute-done | bytes 160 | tf_op jit(solution)/shard_map/ppermute | solution.py:101
  174.3 2.0 collective-permute-start.30
  176.3 1.2 collective-permute-start.16
  177.5 3.1 %collective-permute-done.30 = f32[32]{0:T(128)S(1)} collective-permute-done((f32[32]{0:T(128)S(1)}, f32[32]{0:T(128)S(1)}, u32[]{:S(2)}, u32[]{:S(2)}) %collective-permute-start.30) | collective-permute-done | bytes 160 | tf_op jit(solution)/shard_map/ppermute | solution.py:105
  180.6 2.7 %collective-permute-start.17 = (f32[16,1024]{1,0:T(8,128)S(1)}, f32[16,1024]{1,0:T(8,128)S(1)}, u32[]{:S(2)}, u32[]{:S(2)}) collective-permute-start(f32[16,1024]{1,0:T(8,128)S(1)} %pad_maximum_fusion.4), channel_id=1, source_target_pairs={{0,128},{1,129},{2,130},{3,131},{4,132},{5,133},{6,134},{7,135},{8... | collective-permute-start | bytes 196616 | tf_op jit(solution)/shard_map/ppermute | solution.py:105
  183.4 1.6 collective-permute-start.31
  185.9 1.4 collective-permute-done.31
  187.5 1.1 collective-permute-start.32
  188.7 0.9 collective-permute-done.18
  190.4 0.8 collective-permute-done.32
  191.2 1.9 collective-permute-start.33
  193.2 1.8 collective-permute-done.19
  195.6 0.8 collective-permute-start.34
  196.4 1.7 collective-permute-done.34
  198.1 5.5 %collective-permute-done.20 = f32[128,1024]{1,0:T(8,128)S(1)} collective-permute-done((f32[128,1024]{1,0:T(8,128)S(1)}, f32[128,1024]{1,0:T(8,128)S(1)}, u32[]{:S(2)}, u32[]{:S(2)}) %collective-permute-start.20) | collective-permute-done | bytes 524320 | tf_op jit(solution)/shard_map/ppermute | solution.py:105
  203.8 1.0 pad_maximum_fusion
  204.8 15.3 %collective-permute-start.21 = (f32[256,1024]{1,0:T(8,128)}, f32[256,1024]{1,0:T(8,128)S(1)}, u32[]{:S(2)}, u32[]{:S(2)}) collective-permute-start(f32[256,1024]{1,0:T(8,128)} %pad_maximum_fusion), channel_id=1, source_target_pairs={{0,32},{1,33},{2,34},{3,35},{4,36},{5,37},{6,38},{7,39},{8,40},{9,... | collective-permute-start | bytes 3145736 | tf_op jit(solution)/shard_map/ppermute | solution.py:105
  220.7 1.8 collective-permute-done.35
  222.8 2.3 %collective-permute-done.36 = f32[2048]{0:T(1024)S(1)} collective-permute-done((f32[2048]{0:T(1024)S(1)}, f32[2048]{0:T(1024)S(1)}, u32[]{:S(2)}, u32[]{:S(2)}) %collective-permute-start.36) | collective-permute-done | bytes 8224 | tf_op jit(solution)/shard_map/ppermute | solution.py:105
  225.2 2.5 %collective-permute-start.37 = (f32[4096]{0:T(1024)S(1)}, f32[4096]{0:T(1024)S(1)}, u32[]{:S(2)}, u32[]{:S(2)}) collective-permute-start(f32[4096]{0:T(1024)S(1)} %pad_maximum_fusion.7), channel_id=1, source_target_pairs={{0,32},{1,33},{2,34},{3,35},{4,36},{5,37},{6,38},{7,39},{8,40},{9,... | collective-permute-start | bytes 49160 | tf_op jit(solution)/shard_map/ppermute | solution.py:105
  227.6 0.8 collective-permute-done.37
  229.1 1.5 broadcast_select_fusion.1
  (144 shorter events, 15.8 us)
Async XLA Ops:
  0.6 114.0 %copy-start = (bf16[256,1024]{1,0:T(8,128)(2,1)S(1)}, bf16[256,1024]{1,0:T(8,128)(2,1)}, u32[]{:S(2)}) copy-start(bf16[256,1024]{1,0:T(8,128)(2,1)} %param.29) | copy-start | bytes 1572868
  0.6 5.8 %copy-start.1 = (f32[1,16384]{1,0:T(1,128)S(1)}, f32[1,16384]{1,0:T(1,128)}, u32[]{:S(2)}) copy-start(f32[1,16384]{1,0:T(1,128)} %param.25) | copy-start | bytes 196612
  24.9 7.9 %copy-start.3 = (s32[1,16384]{1,0:T(1,128)S(1)}, s32[1,16384]{1,0:T(1,128)}, u32[]{:S(2)}) copy-start(s32[1,16384]{1,0:T(1,128)} %param.26) | copy-start | bytes 196612
  64.1 35.1 %copy-start.6 = (s32[1,256,8]{1,2,0:T(8,128)S(1)}, s32[1,256,8]{1,2,0:T(8,128)}, u32[]{:S(2)}) copy-start(s32[1,256,8]{1,2,0:T(8,128)} %param.27) | copy-start | bytes 24580
  64.1 35.1 %copy-start.15 = (s32[256]{0:T(256)S(1)}, s32[256]{0:T(256)}, u32[]{:S(2)}) copy-start(s32[256]{0:T(256)} %constant.62.clone) | copy-start | bytes 3076
  83.5 30.7 %copy-start.2 = (bf16[256,1024]{1,0:T(8,128)(2,1)S(1)}, bf16[256,1024]{1,0:T(8,128)(2,1)}, u32[]{:S(2)}) copy-start(bf16[256,1024]{1,0:T(8,128)(2,1)} %param.30) | copy-start | bytes 1572868
  83.5 31.5 %copy-start.5 = (bf16[1024,8]{0,1:T(8,128)(2,1)S(1)}, bf16[1024,8]{0,1:T(8,128)(2,1)}, u32[]{:S(2)}) copy-start(bf16[1024,8]{0,1:T(8,128)(2,1)} %param.31) | copy-start | bytes 49156
  83.5 31.8 %copy-start.7 = (s32[1,256]{1,0:T(1,128)S(1)}, s32[1,256]{1,0:T(1,128)}, u32[]{:S(2)}) copy-start(s32[1,256]{1,0:T(1,128)} %param.28) | copy-start | bytes 3076
  85.4 15.1 %collective-permute-start.2 = (f32[1,256]{1,0:T(1,128)S(1)}, f32[1,256]{1,0:T(1,128)S(1)}, u32[]{:S(2)}, u32[]{:S(2)}) collective-permute-start(f32[1,256]{1,0:T(1,128)S(1)} %get-tuple-element.44), channel_id=1, source_target_pairs={{32,0},{64,32},{96,64},{128,96},{160,128},{192,160},{224,192},{33,... | collective-permute-start | bytes 3080 | tf_op jit(solution)/shard_map/ppermute | solution.py:11
  90.5 10.0 %collective-permute-start.3 = (f32[1,256]{1,0:T(1,128)S(1)}, f32[1,256]{1,0:T(1,128)S(1)}, u32[]{:S(2)}, u32[]{:S(2)}) collective-permute-start(f32[1,256]{1,0:T(1,128)S(1)} %get-tuple-element.45), channel_id=1, source_target_pairs={{0,32},{32,64},{64,96},{96,128},{128,160},{160,192},{192,224},{1,3... | collective-permute-start | bytes 3080 | tf_op jit(solution)/shard_map/ppermute | solution.py:11
  93.6 7.7 %collective-permute-start = (f32[1,256,256]{2,1,0:T(8,128)S(1)}, f32[1,256,256]{2,1,0:T(8,128)S(1)}, u32[]{:S(2)}, u32[]{:S(2)}) collective-permute-start(f32[1,256,256]{2,1,0:T(8,128)S(1)} %get-tuple-element.10), channel_id=1, source_target_pairs={{32,0},{64,32},{96,64},{128,96},{160,128},{192,160},{224,192},{33,... | collective-permute-start | bytes 786440 | tf_op jit(solution)/shard_map/ppermute | solution.py:11
  96.0 6.5 %collective-permute-start.1 = (f32[1,256,256]{2,1,0:T(8,128)S(1)}, f32[1,256,256]{2,1,0:T(8,128)S(1)}, u32[]{:S(2)}, u32[]{:S(2)}) collective-permute-start(f32[1,256,256]{2,1,0:T(8,128)S(1)} %get-tuple-element.11), channel_id=1, source_target_pairs={{0,32},{32,64},{64,96},{96,128},{128,160},{160,192},{192,224},{1,3... | collective-permute-start | bytes 786440 | tf_op jit(solution)/shard_map/ppermute | solution.py:11
  102.6 6.3 %collective-permute-start.4 = (bf16[1,256,256]{2,1,0:T(8,128)(2,1)S(1)}, bf16[1,256,256]{2,1,0:T(8,128)(2,1)S(1)}, u32[]{:S(2)}, u32[]{:S(2)}) collective-permute-start(bf16[1,256,256]{2,1,0:T(8,128)(2,1)S(1)} %fusion.21), channel_id=1, source_target_pairs={{0,32},{32,64},{64,96},{96,128},{128,160},{160,192},{192,224},{1,3... | collective-permute-start | bytes 393224 | tf_op jit(solution)/shard_map/ppermute | solution.py:19
  107.0 6.3 %collective-permute-start.5 = (bf16[1,256,256]{2,1,0:T(8,128)(2,1)S(1)}, bf16[1,256,256]{2,1,0:T(8,128)(2,1)S(1)}, u32[]{:S(2)}, u32[]{:S(2)}) collective-permute-start(bf16[1,256,256]{2,1,0:T(8,128)(2,1)S(1)} %fusion.21), channel_id=1, source_target_pairs={{32,0},{64,32},{96,64},{128,96},{160,128},{192,160},{224,192},{33,... | collective-permute-start | bytes 393224 | tf_op jit(solution)/shard_map/ppermute | solution.py:22
  114.6 2.9 %copy-start.14 = (s32[256]{0:T(256)S(1)}, s32[256]{0:T(256)}, u32[]{:S(2)}) copy-start(s32[256]{0:T(256)} %constant.63.clone) | copy-start | bytes 3076
  114.6 5.6 %copy-start.13 = (s32[256]{0:T(256)S(1)}, s32[256]{0:T(256)}, u32[]{:S(2)}) copy-start(s32[256]{0:T(256)} %constant.64.clone) | copy-start | bytes 3076
  115.3 7.1 %copy-start.4 = (f32[256,8]{0,1:T(8,128)}, f32[256,8]{0,1:T(8,128)S(1)}, u32[]{:S(2)}) copy-start(f32[256,8]{0,1:T(8,128)S(1)} %fusion.36) | copy-start | bytes 24580
  115.3 9.5 %copy-start.12 = (s32[256]{0:T(256)S(1)}, s32[256]{0:T(256)}, u32[]{:S(2)}) copy-start(s32[256]{0:T(256)} %constant.65.clone) | copy-start | bytes 3076
  115.3 10.7 %copy-start.11 = (s32[256]{0:T(256)S(1)}, s32[256]{0:T(256)}, u32[]{:S(2)}) copy-start(s32[256]{0:T(256)} %constant.66.clone) | copy-start | bytes 3076
  115.4 12.0 %copy-start.10 = (s32[256]{0:T(256)S(1)}, s32[256]{0:T(256)}, u32[]{:S(2)}) copy-start(s32[256]{0:T(256)} %constant.67.clone) | copy-start | bytes 3076
  115.4 13.2 %copy-start.9 = (s32[256]{0:T(256)S(1)}, s32[256]{0:T(256)}, u32[]{:S(2)}) copy-start(s32[256]{0:T(256)} %constant.68.clone) | copy-start | bytes 3076
  115.4 14.4 %copy-start.8 = (s32[256]{0:T(256)S(1)}, s32[256]{0:T(256)}, u32[]{:S(2)}) copy-start(s32[256]{0:T(256)} %constant.69.clone) | copy-start | bytes 3076
  116.6 5.4 %collective-permute-start.6 = (f32[256,1024]{1,0:T(8,128)S(1)}, f32[256,1024]{1,0:T(8,128)S(1)}, u32[]{:S(2)}, u32[]{:S(2)}) collective-permute-start(f32[256,1024]{1,0:T(8,128)S(1)} %get-tuple-element.56), channel_id=1, source_target_pairs={{0,32},{1,33},{2,34},{3,35},{4,36},{5,37},{6,38},{7,39},{8,40},{9,... | collective-permute-start | bytes 3145736 | tf_op jit(solution)/shard_map/ppermute | solution.py:101
  116.9 2.5 %collective-permute-start.22 = (f32[4096]{0:T(1024)S(1)}, f32[4096]{0:T(1024)S(1)}, u32[]{:S(2)}, u32[]{:S(2)}) collective-permute-start(f32[4096]{0:T(1024)S(1)} %bitcast.67), channel_id=1, source_target_pairs={{0,32},{1,33},{2,34},{3,35},{4,36},{5,37},{6,38},{7,39},{8,40},{9,... | collective-permute-start | bytes 49160 | tf_op jit(solution)/shard_map/ppermute | solution.py:101
  119.4 2.6 %collective-permute-start.23 = (f32[2048]{0:T(1024)S(1)}, f32[2048]{0:T(1024)S(1)}, u32[]{:S(2)}, u32[]{:S(2)}) collective-permute-start(f32[2048]{0:T(1024)S(1)} %slice_select_fusion.6), channel_id=1, source_target_pairs={{0,64},{1,65},{2,66},{3,67},{4,68},{5,69},{6,70},{7,71},{8,72},{9,... | collective-permute-start | bytes 24584 | tf_op jit(solution)/shard_map/ppermute | solution.py:101
  122.4 10.2 %collective-permute-start.7 = (f32[128,1024]{1,0:T(8,128)S(1)}, f32[128,1024]{1,0:T(8,128)S(1)}, u32[]{:S(2)}, u32[]{:S(2)}) collective-permute-start(f32[128,1024]{1,0:T(8,128)S(1)} %slice_select_fusion), channel_id=1, source_target_pairs={{0,64},{1,65},{2,66},{3,67},{4,68},{5,69},{6,70},{7,71},{8,72},{9,... | collective-permute-start | bytes 1572872 | tf_op jit(solution)/shard_map/ppermute | solution.py:101
  123.2 7.9 %collective-permute-start.24 = (f32[1024]{0:T(1024)S(1)}, f32[1024]{0:T(1024)S(1)}, u32[]{:S(2)}, u32[]{:S(2)}) collective-permute-start(f32[1024]{0:T(1024)S(1)} %slice_select_fusion.7), channel_id=1, source_target_pairs={{0,8},{1,9},{2,10},{3,11},{4,12},{5,13},{6,14},{7,15},{8,0},{9,1},... | collective-permute-start | bytes 12296 | tf_op jit(solution)/shard_map/ppermute | solution.py:101
  131.1 2.7 %collective-permute-start.25 = (f32[512]{0:T(512)S(1)}, f32[512]{0:T(512)S(1)}, u32[]{:S(2)}, u32[]{:S(2)}) collective-permute-start(f32[512]{0:T(512)S(1)} %slice_select_fusion.8), channel_id=1, source_target_pairs={{0,1},{1,0},{2,3},{3,2},{4,5},{5,4},{6,7},{7,6},{8,9},{9,8},{10,11... | collective-permute-start | bytes 6152 | tf_op jit(solution)/shard_map/ppermute | solution.py:101
  132.7 5.6 %collective-permute-start.8 = (f32[64,1024]{1,0:T(8,128)S(1)}, f32[64,1024]{1,0:T(8,128)S(1)}, u32[]{:S(2)}, u32[]{:S(2)}) collective-permute-start(f32[64,1024]{1,0:T(8,128)S(1)} %slice_select_fusion.1), channel_id=1, source_target_pairs={{0,8},{1,9},{2,10},{3,11},{4,12},{5,13},{6,14},{7,15},{8,0},{9,1},... | collective-permute-start | bytes 786440 | tf_op jit(solution)/shard_map/ppermute | solution.py:101
  133.8 5.0 %collective-permute-start.26 = (f32[256]{0:T(256)S(1)}, f32[256]{0:T(256)S(1)}, u32[]{:S(2)}, u32[]{:S(2)}) collective-permute-start(f32[256]{0:T(256)S(1)} %broadcast_select_fusion.36), channel_id=1, source_target_pairs={{0,128},{1,129},{2,130},{3,131},{4,132},{5,133},{6,134},{7,135},{8... | collective-permute-start | bytes 3080 | tf_op jit(solution)/shard_map/ppermute | solution.py:101
  138.4 3.9 %collective-permute-start.9 = (f32[32,1024]{1,0:T(8,128)S(1)}, f32[32,1024]{1,0:T(8,128)S(1)}, u32[]{:S(2)}, u32[]{:S(2)}) collective-permute-start(f32[32,1024]{1,0:T(8,128)S(1)} %slice_select_fusion.2), channel_id=1, source_target_pairs={{0,1},{1,0},{2,3},{3,2},{4,5},{5,4},{6,7},{7,6},{8,9},{9,8},{10,11... | collective-permute-start | bytes 393224 | tf_op jit(solution)/shard_map/ppermute | solution.py:101
  142.4 5.7 %collective-permute-start.10 = (f32[16,1024]{1,0:T(8,128)S(1)}, f32[16,1024]{1,0:T(8,128)S(1)}, u32[]{:S(2)}, u32[]{:S(2)}) collective-permute-start(f32[16,1024]{1,0:T(8,128)S(1)} %slice_select_fusion.3), channel_id=1, source_target_pairs={{0,128},{1,129},{2,130},{3,131},{4,132},{5,133},{6,134},{7,135},{8... | collective-permute-start | bytes 196616 | tf_op jit(solution)/shard_map/ppermute | solution.py:101
  145.1 5.1 %collective-permute-start.27 = (f32[128]{0:T(128)S(1)}, f32[128]{0:T(128)S(1)}, u32[]{:S(2)}, u32[]{:S(2)}) collective-permute-start(f32[128]{0:T(128)S(1)} %broadcast_select_fusion.32), channel_id=1, source_target_pairs={{0,16},{1,17},{2,18},{3,19},{4,20},{5,21},{6,22},{7,23},{8,24},{9,... | collective-permute-start | bytes 1544 | tf_op jit(solution)/shard_map/ppermute | solution.py:101
  148.1 4.4 %collective-permute-start.11 = (f32[8,1024]{1,0:T(8,128)S(1)}, f32[8,1024]{1,0:T(8,128)S(1)}, u32[]{:S(2)}, u32[]{:S(2)}) collective-permute-start(f32[8,1024]{1,0:T(8,128)S(1)} %slice_select_fusion.4), channel_id=1, source_target_pairs={{0,16},{1,17},{2,18},{3,19},{4,20},{5,21},{6,22},{7,23},{8,24},{9,... | collective-permute-start | bytes 98312 | tf_op jit(solution)/shard_map/ppermute | solution.py:101
  152.6 4.2 %collective-permute-start.12 = (f32[4,1024]{1,0:T(4,128)S(1)}, f32[4,1024]{1,0:T(4,128)S(1)}, u32[]{:S(2)}, u32[]{:S(2)}) collective-permute-start(f32[4,1024]{1,0:T(4,128)S(1)} %slice_select_fusion.5), channel_id=1, source_target_pairs={{0,2},{1,3},{2,0},{3,1},{4,6},{5,7},{6,4},{7,5},{8,10},{9,11},{10,... | collective-permute-start | bytes 49160 | tf_op jit(solution)/shard_map/ppermute | solution.py:101
  153.6 7.6 %collective-permute-start.28 = (f32[64]{0:T(128)S(1)}, f32[64]{0:T(128)S(1)}, u32[]{:S(2)}, u32[]{:S(2)}) collective-permute-start(f32[64]{0:T(128)S(1)} %broadcast_select_fusion.28), channel_id=1, source_target_pairs={{0,2},{1,3},{2,0},{3,1},{4,6},{5,7},{6,4},{7,5},{8,10},{9,11},{10,... | collective-permute-start | bytes 776 | tf_op jit(solution)/shard_map/ppermute | solution.py:101
  156.8 6.5 %collective-permute-start.13 = (f32[2,1024]{1,0:T(2,128)S(1)}, f32[2,1024]{1,0:T(2,128)S(1)}, u32[]{:S(2)}, u32[]{:S(2)}) collective-permute-start(f32[2,1024]{1,0:T(2,128)S(1)} %broadcast_select_fusion.15), channel_id=1, source_target_pairs={{0,4},{1,5},{2,6},{3,7},{4,0},{5,1},{6,2},{7,3},{8,12},{9,13},{10,... | collective-permute-start | bytes 24584 | tf_op jit(solution)/shard_map/ppermute | solution.py:101
  163.3 6.5 %collective-permute-start.14 = (f32[2,1024]{1,0:T(2,128)S(1)}, f32[2,1024]{1,0:T(2,128)S(1)}, u32[]{:S(2)}, u32[]{:S(2)}) collective-permute-start(f32[2,1024]{1,0:T(2,128)S(1)} %select_add_fusion.8), channel_id=1, source_target_pairs={{0,4},{1,5},{2,6},{3,7},{4,0},{5,1},{6,2},{7,3},{8,12},{9,13},{10,... | collective-permute-start | bytes 24584 | tf_op jit(solution)/shard_map/ppermute | solution.py:105
  167.9 6.3 %collective-permute-start.29 = (f32[32]{0:T(128)S(1)}, f32[32]{0:T(128)S(1)}, u32[]{:S(2)}, u32[]{:S(2)}) collective-permute-start(f32[32]{0:T(128)S(1)} %broadcast_select_fusion.24), channel_id=1, source_target_pairs={{0,4},{1,5},{2,6},{3,7},{4,0},{5,1},{6,2},{7,3},{8,12},{9,13},{10,... | collective-permute-start | bytes 392 | tf_op jit(solution)/shard_map/ppermute | solution.py:101
  169.8 6.4 %collective-permute-start.15 = (f32[4,1024]{1,0:T(4,128)S(1)}, f32[4,1024]{1,0:T(4,128)S(1)}, u32[]{:S(2)}, u32[]{:S(2)}) collective-permute-start(f32[4,1024]{1,0:T(4,128)S(1)} %pad_maximum_fusion.6), channel_id=1, source_target_pairs={{0,2},{1,3},{2,0},{3,1},{4,6},{5,7},{6,4},{7,5},{8,10},{9,11},{10,... | collective-permute-start | bytes 49160 | tf_op jit(solution)/shard_map/ppermute | solution.py:105
  174.3 6.3 %collective-permute-start.30 = (f32[32]{0:T(128)S(1)}, f32[32]{0:T(128)S(1)}, u32[]{:S(2)}, u32[]{:S(2)}) collective-permute-start(f32[32]{0:T(128)S(1)} %fusion.28), channel_id=1, source_target_pairs={{0,4},{1,5},{2,6},{3,7},{4,0},{5,1},{6,2},{7,3},{8,12},{9,13},{10,... | collective-permute-start | bytes 392 | tf_op jit(solution)/shard_map/ppermute | solution.py:105
  176.3 4.3 %collective-permute-start.16 = (f32[8,1024]{1,0:T(8,128)S(1)}, f32[8,1024]{1,0:T(8,128)S(1)}, u32[]{:S(2)}, u32[]{:S(2)}) collective-permute-start(f32[8,1024]{1,0:T(8,128)S(1)} %pad_maximum_fusion.5), channel_id=1, source_target_pairs={{0,16},{1,17},{2,18},{3,19},{4,20},{5,21},{6,22},{7,23},{8,24},{9,... | collective-permute-start | bytes 98312 | tf_op jit(solution)/shard_map/ppermute | solution.py:105
  180.6 4.7 %collective-permute-start.17 = (f32[16,1024]{1,0:T(8,128)S(1)}, f32[16,1024]{1,0:T(8,128)S(1)}, u32[]{:S(2)}, u32[]{:S(2)}) collective-permute-start(f32[16,1024]{1,0:T(8,128)S(1)} %pad_maximum_fusion.4), channel_id=1, source_target_pairs={{0,128},{1,129},{2,130},{3,131},{4,132},{5,133},{6,134},{7,135},{8... | collective-permute-start | bytes 196616 | tf_op jit(solution)/shard_map/ppermute | solution.py:105
  183.4 3.9 %collective-permute-start.31 = (f32[64]{0:T(128)S(1)}, f32[64]{0:T(128)S(1)}, u32[]{:S(2)}, u32[]{:S(2)}) collective-permute-start(f32[64]{0:T(128)S(1)} %pad_maximum_fusion.12), channel_id=1, source_target_pairs={{0,2},{1,3},{2,0},{3,1},{4,6},{5,7},{6,4},{7,5},{8,10},{9,11},{10,... | collective-permute-start | bytes 776 | tf_op jit(solution)/shard_map/ppermute | solution.py:105
  185.4 4.2 %collective-permute-start.18 = (f32[32,1024]{1,0:T(8,128)S(1)}, f32[32,1024]{1,0:T(8,128)S(1)}, u32[]{:S(2)}, u32[]{:S(2)}) collective-permute-start(f32[32,1024]{1,0:T(8,128)S(1)} %pad_maximum_fusion.3), channel_id=1, source_target_pairs={{0,1},{1,0},{2,3},{3,2},{4,5},{5,4},{6,7},{7,6},{8,9},{9,8},{10,11... | collective-permute-start | bytes 393224 | tf_op jit(solution)/shard_map/ppermute | solution.py:105
  187.5 3.6 %collective-permute-start.32 = (f32[128]{0:T(128)S(1)}, f32[128]{0:T(128)S(1)}, u32[]{:S(2)}, u32[]{:S(2)}) collective-permute-start(f32[128]{0:T(128)S(1)} %pad_maximum_fusion.13), channel_id=1, source_target_pairs={{0,16},{1,17},{2,18},{3,19},{4,20},{5,21},{6,22},{7,23},{8,24},{9,... | collective-permute-start | bytes 1544 | tf_op jit(solution)/shard_map/ppermute | solution.py:105
  189.6 5.3 %collective-permute-start.19 = (f32[64,1024]{1,0:T(8,128)S(1)}, f32[64,1024]{1,0:T(8,128)S(1)}, u32[]{:S(2)}, u32[]{:S(2)}) collective-permute-start(f32[64,1024]{1,0:T(8,128)S(1)} %pad_maximum_fusion.2), channel_id=1, source_target_pairs={{0,8},{1,9},{2,10},{3,11},{4,12},{5,13},{6,14},{7,15},{8,0},{9,1},... | collective-permute-start | bytes 786440 | tf_op jit(solution)/shard_map/ppermute | solution.py:105
  191.2 4.3 %collective-permute-start.33 = (f32[256]{0:T(256)S(1)}, f32[256]{0:T(256)S(1)}, u32[]{:S(2)}, u32[]{:S(2)}) collective-permute-start(f32[256]{0:T(256)S(1)} %pad_maximum_fusion.11), channel_id=1, source_target_pairs={{0,128},{1,129},{2,130},{3,131},{4,132},{5,133},{6,134},{7,135},{8... | collective-permute-start | bytes 3080 | tf_op jit(solution)/shard_map/ppermute | solution.py:105
  195.0 8.6 %collective-permute-start.20 = (f32[128,1024]{1,0:T(8,128)S(1)}, f32[128,1024]{1,0:T(8,128)S(1)}, u32[]{:S(2)}, u32[]{:S(2)}) collective-permute-start(f32[128,1024]{1,0:T(8,128)S(1)} %pad_maximum_fusion.1), channel_id=1, source_target_pairs={{0,64},{1,65},{2,66},{3,67},{4,68},{5,69},{6,70},{7,71},{8,72},{9,... | collective-permute-start | bytes 1572872 | tf_op jit(solution)/shard_map/ppermute | solution.py:105
  195.6 2.5 %collective-permute-start.34 = (f32[512]{0:T(512)S(1)}, f32[512]{0:T(512)S(1)}, u32[]{:S(2)}, u32[]{:S(2)}) collective-permute-start(f32[512]{0:T(512)S(1)} %pad_maximum_fusion.10), channel_id=1, source_target_pairs={{0,1},{1,0},{2,3},{3,2},{4,5},{5,4},{6,7},{7,6},{8,9},{9,8},{10,11... | collective-permute-start | bytes 6152 | tf_op jit(solution)/shard_map/ppermute | solution.py:105
  204.8 24.3 %collective-permute-start.21 = (f32[256,1024]{1,0:T(8,128)}, f32[256,1024]{1,0:T(8,128)S(1)}, u32[]{:S(2)}, u32[]{:S(2)}) collective-permute-start(f32[256,1024]{1,0:T(8,128)} %pad_maximum_fusion), channel_id=1, source_target_pairs={{0,32},{1,33},{2,34},{3,35},{4,36},{5,37},{6,38},{7,39},{8,40},{9,... | collective-permute-start | bytes 3145736 | tf_op jit(solution)/shard_map/ppermute | solution.py:105
  220.1 2.5 %collective-permute-start.35 = (f32[1024]{0:T(1024)S(1)}, f32[1024]{0:T(1024)S(1)}, u32[]{:S(2)}, u32[]{:S(2)}) collective-permute-start(f32[1024]{0:T(1024)S(1)} %pad_maximum_fusion.9), channel_id=1, source_target_pairs={{0,8},{1,9},{2,10},{3,11},{4,12},{5,13},{6,14},{7,15},{8,0},{9,1},... | collective-permute-start | bytes 12296 | tf_op jit(solution)/shard_map/ppermute | solution.py:105
  222.6 2.6 %collective-permute-start.36 = (f32[2048]{0:T(1024)S(1)}, f32[2048]{0:T(1024)S(1)}, u32[]{:S(2)}, u32[]{:S(2)}) collective-permute-start(f32[2048]{0:T(1024)S(1)} %pad_maximum_fusion.8), channel_id=1, source_target_pairs={{0,64},{1,65},{2,66},{3,67},{4,68},{5,69},{6,70},{7,71},{8,72},{9,... | collective-permute-start | bytes 24584 | tf_op jit(solution)/shard_map/ppermute | solution.py:105
  225.2 3.3 %collective-permute-start.37 = (f32[4096]{0:T(1024)S(1)}, f32[4096]{0:T(1024)S(1)}, u32[]{:S(2)}, u32[]{:S(2)}) collective-permute-start(f32[4096]{0:T(1024)S(1)} %pad_maximum_fusion.7), channel_id=1, source_target_pairs={{0,32},{1,33},{2,34},{3,35},{4,36},{5,37},{6,38},{7,39},{8,40},{9,... | collective-permute-start | bytes 49160 | tf_op jit(solution)/shard_map/ppermute | solution.py:105

commit v3 on v2

--- a/solution.py
+++ b/solution.py
@@ -24,48 +24,62 @@
     return block
 
 
-def pooled_sums_kernel(ids_ref, rows_ref, sums_ref):
+def pooled_sums_kernel(ids_ref, split_ref, cells_ref, numer_ref, denom_ref):
     @pl.when(pl.program_id(0) == 0)
     def _():
-        sums_ref[...] = jnp.zeros_like(sums_ref)
+        numer_ref[...] = jnp.zeros_like(numer_ref)
+        denom_ref[...] = jnp.zeros_like(denom_ref)
 
-    width = sums_ref.shape[0]
-    slots = lax.broadcasted_iota(jnp.int32, (width, ids_ref.shape[1]), 0)
+    width = numer_ref.shape[0]
+    block = ids_ref.shape[1]
+    lanes = denom_ref.shape[1]
+    slots = lax.broadcasted_iota(jnp.int32, (width, block), 0)
     member = (ids_ref[...] == slots).astype(jnp.bfloat16)
-    sums_ref[...] += jnp.dot(member, rows_ref[...], preferred_element_type=jnp.float32)
+    split = split_ref[...]
+    pad = jnp.zeros((lanes - split.shape[0], block), jnp.float32)
+    columns = jnp.concatenate([split, pad], axis=0).T
+    lane = lax.broadcasted_iota(jnp.int32, (block, lanes), 1)
+    parts = jnp.where(lane < 3, columns, 0.0).astype(jnp.bfloat16)
+    weight = columns[:, 3:4]
+    weighted = (weight * cells_ref[...].astype(jnp.float32)).astype(jnp.bfloat16)
+    numer_ref[...] += jnp.dot(member, weighted, preferred_element_type=jnp.float32)
+    denom_ref[...] += jnp.dot(member, parts, preferred_element_type=jnp.float32)
 
 
-def accumulate(cluster_ids, weighted, weights, width):
-    length, feats = weighted.shape
-    high = weights.astype(jnp.bfloat16)
-    rest = weights - high.astype(jnp.float32)
-    middle = rest.astype(jnp.bfloat16)
-    low = (rest - middle.astype(jnp.float32)).astype(jnp.bfloat16)
+def accumulate(cluster_ids, cells, weights, width):
+    length, feats = cells.shape
+    high = lax.reduce_precision(weights, exponent_bits=8, mantissa_bits=7)
+    rest = weights - high
+    middle = lax.reduce_precision(rest, exponent_bits=8, mantissa_bits=7)
+    low = rest - middle
+    zero = jnp.zeros_like(weights)
+    split = jnp.stack([high, middle, low, weights, zero, zero, zero, zero], axis=0)
+    block = min(1024, length)
     lanes = 128
-    parts = jnp.stack([high, middle, low], axis=-1)
-    rows = jnp.concatenate(
-        [weighted, parts, jnp.zeros((length, lanes - 3), jnp.bfloat16)], axis=-1
-    )
-    block = min(1024, length)
-    total = feats + lanes
-    sums = pl.pallas_call(
+    numer, denom = pl.pallas_call(
         pooled_sums_kernel,
         grid=(length // block,),
         in_specs=[
             pl.BlockSpec((1, block), lambda i: (0, i)),
-            pl.BlockSpec((block, total), lambda i: (i, 0)),
+            pl.BlockSpec((8, block), lambda i: (0, i)),
+            pl.BlockSpec((block, feats), lambda i: (i, 0)),
         ],
-        out_specs=pl.BlockSpec((width, total), lambda i: (0, 0)),
-        out_shape=jax.ShapeDtypeStruct((width, total), jnp.float32),
+        out_specs=[
+            pl.BlockSpec((width, feats), lambda i: (0, 0)),
+            pl.BlockSpec((width, lanes), lambda i: (0, 0)),
+        ],
+        out_shape=[
+            jax.ShapeDtypeStruct((width, feats), jnp.float32),
+            jax.ShapeDtypeStruct((width, lanes), jnp.float32),
+        ],
         cost_estimate=pl.CostEstimate(
-            flops=2 * width * length * total,
-            bytes_accessed=length * total * 2 + length * 4 + width * total * 4,
+            flops=2 * width * length * (feats + lanes),
+            bytes_accessed=length * (feats * 2 + 36) + width * (feats + lanes) * 4,
             transcendentals=0,
         ),
-    )(cluster_ids.reshape(1, length), rows)
-    numer = sums[:, :feats]
-    denom = sums[:, feats] + sums[:, feats + 1] + sums[:, feats + 2]
-    return numer[None], denom[None]
+    )(cluster_ids.reshape(1, length), split, cells)
+    total = denom[:, 0] + denom[:, 1] + denom[:, 2]
+    return numer[None], total[None]
 
 
 def halving_plan(sizes):
@@ -114,9 +128,8 @@
     region = lax.axis_index("region")
     owned = cluster_edges.shape[1]
     degree = cluster_edges.shape[2]
-    weighted = (cell_weight[..., None] * cells.astype(jnp.float32)).astype(jnp.bfloat16)
     relative = cell_cluster - (region - 1) * owned
-    numer_three, denom_three = accumulate(relative[0], weighted[0], cell_weight[0], 3 * owned)
+    numer_three, denom_three = accumulate(relative[0], cells[0], cell_weight[0], 3 * owned)
     above_numer, above_denom = passed_along(
         (numer_three[:, :owned], denom_three[:, :owned]), "region", -1
     )

time: 232 us -> 174 us (0.75)
  local copies, waits for them, and re-layouts: 49.8 us -> 7.85 us
  other arithmetic: 26.5 us -> 10.2 us
  waiting for transfers between devices: 44.2 us -> 40.3 us
  Pallas kernels: 19.4 us -> 21.8 us
    concatenate x1 -> x0, local copies, waits for them, and re-layouts: 28.2 us -> none  [accumulate(): jnp.concatenate([weighted, parts, jnp.zeros((length, lanes - 3), jnp.bflo...]
    convert_element_type x2 -> x0, other arithmetic: 11.1 us -> none  [the longest x1 10.1 us: accumulate(): low = (rest - middle.astype(jnp.float32)).astype(jnp.bfloat16)]
    convert_element_type x2 -> x0, local copies, waits for them, and re-layouts: 8.29 us -> none  [the longest x1 4.81 us: accumulate(): rest = weights - high.astype(jnp.float32)]
    squeeze x1 -> x0, other arithmetic: 7.94 us -> none  [local(): weighted[0]]
    squeeze x1 -> x0, local copies, waits for them, and re-layouts: 4.87 us -> none  [local(): cell_weight[0]]
    ppermute x1, waiting for transfers between devices: 4.33 us -> 0.69 us  [padded(): lax.ppermute(lax.slice_in_dim(block, 0, width, axis=dim), axis, backward)]
    broadcast_in_dim x2 -> x0, local copies, waits for them, and re-layouts: 3.53 us -> none  [the longest x1 2.35 us: accumulate(): jnp.zeros((length, lanes - 3), jnp.bfloat16)]
    pallas_call x1, Pallas kernels: 19.4 us -> 21.8 us  [accumulate(): pl.pallas_call(pooled_sums_kernel, grid=(length // block,), in_specs=[pl....]
  transfers between devices with their start and end apart: 38 -> 38, of which waited for: 24 -> 25; matrix products, arithmetic and copies ran while one was open for 3% -> 4% of each run, Pallas kernels for 0% -> 0%
where the time goes in v3:
time: 174 us; the launch traced here: 173 us
  starting transfers between devices  83.3 us (48%)
  waiting for transfers between devices  40.3 us (23%)
  Pallas kernels  21.8 us (13%)
  other arithmetic  10.2 us (6%)
  local copies, waits for them, and re-layouts  7.85 us (5%)
  between operations  6.49 us (4%)
  matrix products  3.32 us (2%)
    ppermute x16, starting transfers between devices, all_sum(): got = lax.ppermute(buffers, axes, perm)  39.1 us
    ppermute x16, starting transfers between devices, all_sum(): got = lax.ppermute(tuple(sends), axes, perm)  25.3 us
    ppermute x16, waiting for transfers between devices, all_sum(): got = lax.ppermute(buffers, axes, perm)  22 us
    pallas_call x1, Pallas kernels, accumulate(): pl.pallas_call(pooled_sums_kernel, grid=(length // block,), in_specs=[pl....  21.8 us
    ppermute x16, waiting for transfers between devices, all_sum(): got = lax.ppermute(tuple(sends), axes, perm)  14.4 us
    ppermute x4, starting transfers between devices, passed_along(): lax.ppermute(value, axis, [(source, source + steps) for source in range(i...  12.6 us
    dynamic_slice x8, local copies, waits for them, and re-layouts, all_sum(): upper = jnp.asarray(bits, jnp.int32)[me] == 1  4.69 us
    ppermute x1, starting transfers between devices, padded(): lax.ppermute(lax.slice_in_dim(block, block.shape[dim] - width, None, axis...  4.39 us
  transfers between devices with their start and end apart: 38, of which 25 were waited for; matrix products, arithmetic and copies ran while one was open for 4% of the time, Pallas kernels for 0%

profile of v3, /device:TPU:1, one launch (start us, length us, event | category | flops | bytes accessed | tf_op | source)
XLA Modules:
  0.0 173.4 jit_solution(10066516329941025408)
XLA Ops:
  0.7 1.0 reduce-precision_subtract_fusion
  1.7 1.5 broadcast_subtract_fusion.ids_ref
  3.2 1.9 %stack.10.split_ref = f32[8,16384]{1,0:T(8,128)} concatenate(f32[1,16384]{1,0:T(1,128)S(1)} %get-tuple-element.23, f32[1,16384]{1,0:T(1,128)S(1)} %get-tuple-element.24, f32[1,16384]{1,0:T(1,128)S(1)} %get-tuple-element.22, f32[1,16384]{1,0:T(1,128)} %param.25, f32[4,16384]{1,0:T(4,128)S(1)} %stack.4), dimensions={0} | concatenate | bytes 1048576 | tf_op jit(solution)/shard_map/stack | solution.py:56
  5.1 21.8 %shard_map.255 = (f32[768,256]{1,0:T(8,128)}, f32[768,128]{1,0:T(8,128)}) custom-call(s32[1,16384]{1,0:T(1,128)} %broadcast_subtract_fusion.ids_ref, f32[8,16384]{1,0:T(8,128)} %stack.10.split_ref, bf16[16384,256]{1,0:T(8,128)(2,1)} %bitcast.72), custom_call_target="tpu_custom_call" | custom-call | flops 9663676416 | bytes 10158080 | tf_op jit(solution)/shard_map/pallas_call | solution.py:59
  26.9 1.8 %add_reduce_fusion = f32[768]{0:T(1024)S(1)} fusion(f32[768,128]{1,0:T(8,128)} %get-tuple-element.7), kind=kLoop, calls=%fused_computation.39 | loop fusion | flops 1536 | bytes 12288 | tf_op jit(solution)/shard_map/add | solution.py:81
  28.8 5.1 %collective-permute-start.2 = (f32[1,256]{1,0:T(1,128)S(1)}, f32[1,256]{1,0:T(1,128)S(1)}, u32[]{:S(2)}, u32[]{:S(2)}) collective-permute-start(f32[1,256]{1,0:T(1,128)S(1)} %get-tuple-element.47), channel_id=1, source_target_pairs={{32,0},{64,32},{96,64},{128,96},{160,128},{192,160},{224,192},{33,... | collective-permute-start | bytes 3080 | tf_op jit(solution)/shard_map/ppermute | solution.py:11
  33.9 1.9 %collective-permute-start.3 = (f32[1,256]{1,0:T(1,128)S(1)}, f32[1,256]{1,0:T(1,128)S(1)}, u32[]{:S(2)}, u32[]{:S(2)}) collective-permute-start(f32[1,256]{1,0:T(1,128)S(1)} %get-tuple-element.48), channel_id=1, source_target_pairs={{0,32},{32,64},{64,96},{96,128},{128,160},{160,192},{192,224},{1,3... | collective-permute-start | bytes 3080 | tf_op jit(solution)/shard_map/ppermute | solution.py:11
  35.8 1.1 fusion.29
  36.9 2.4 %collective-permute-start = (f32[1,256,256]{2,1,0:T(8,128)S(1)}, f32[1,256,256]{2,1,0:T(8,128)S(1)}, u32[]{:S(2)}, u32[]{:S(2)}) collective-permute-start(f32[1,256,256]{2,1,0:T(8,128)S(1)} %get-tuple-element.12), channel_id=1, source_target_pairs={{32,0},{64,32},{96,64},{128,96},{160,128},{192,160},{224,192},{33,... | collective-permute-start | bytes 786440 | tf_op jit(solution)/shard_map/ppermute | solution.py:11
  39.3 3.2 %collective-permute-start.1 = (f32[1,256,256]{2,1,0:T(8,128)S(1)}, f32[1,256,256]{2,1,0:T(8,128)S(1)}, u32[]{:S(2)}, u32[]{:S(2)}) collective-permute-start(f32[1,256,256]{2,1,0:T(8,128)S(1)} %get-tuple-element.13), channel_id=1, source_target_pairs={{0,32},{32,64},{64,96},{96,128},{128,160},{160,192},{192,224},{1,3... | collective-permute-start | bytes 786440 | tf_op jit(solution)/shard_map/ppermute | solution.py:11
  42.5 0.6 dynamic_slice.48
  43.8 0.8 collective-permute-done
  44.6 1.2 collective-permute-done.1
  45.8 1.1 fusion.19
  46.8 1.9 %collective-permute-start.5 = (bf16[1,256,256]{2,1,0:T(8,128)(2,1)S(1)}, bf16[1,256,256]{2,1,0:T(8,128)(2,1)S(1)}, u32[]{:S(2)}, u32[]{:S(2)}) collective-permute-start(bf16[1,256,256]{2,1,0:T(8,128)(2,1)S(1)} %fusion.19), channel_id=1, source_target_pairs={{32,0},{64,32},{96,64},{128,96},{160,128},{192,160},{224,192},{33,... | collective-permute-start | bytes 393224 | tf_op jit(solution)/shard_map/ppermute | solution.py:22
  48.8 4.4 %collective-permute-start.4 = (bf16[1,256,256]{2,1,0:T(8,128)(2,1)S(1)}, bf16[1,256,256]{2,1,0:T(8,128)(2,1)S(1)}, u32[]{:S(2)}, u32[]{:S(2)}) collective-permute-start(bf16[1,256,256]{2,1,0:T(8,128)(2,1)S(1)} %fusion.19), channel_id=1, source_target_pairs={{0,32},{32,64},{64,96},{96,128},{128,160},{160,192},{192,224},{1,3... | collective-permute-start | bytes 393224 | tf_op jit(solution)/shard_map/ppermute | solution.py:19
  53.2 0.7 collective-permute-done.5
  53.9 1.2 collective-permute-done.4
  55.1 1.0 fusion.2
  60.5 0.6 collective-permute-done.22
  61.2 0.8 collective-permute-start.23
  64.2 0.8 collective-permute-start.7
  65.0 1.6 collective-permute-start.24
  67.9 0.6 dynamic_slice.54
  72.9 2.3 %collective-permute-start.25 = (f32[512]{0:T(512)S(1)}, f32[512]{0:T(512)S(1)}, u32[]{:S(2)}, u32[]{:S(2)}) collective-permute-start(f32[512]{0:T(512)S(1)} %slice_select_fusion.8), channel_id=1, source_target_pairs={{0,1},{1,0},{2,3},{3,2},{4,5},{5,4},{6,7},{7,6},{8,9},{9,8},{10,11... | collective-permute-start | bytes 6152 | tf_op jit(solution)/shard_map/ppermute | solution.py:115
  75.4 0.7 collective-permute-done.25
  76.2 2.7 %collective-permute-start.26 = (f32[256]{0:T(256)S(1)}, f32[256]{0:T(256)S(1)}, u32[]{:S(2)}, u32[]{:S(2)}) collective-permute-start(f32[256]{0:T(256)S(1)} %broadcast_select_fusion.36), channel_id=1, source_target_pairs={{0,128},{1,129},{2,130},{3,131},{4,132},{5,133},{6,134},{7,135},{8... | collective-permute-start | bytes 3080 | tf_op jit(solution)/shard_map/ppermute | solution.py:115
  78.9 2.1 %collective-permute-done.8 = f32[64,1024]{1,0:T(8,128)S(1)} collective-permute-done((f32[64,1024]{1,0:T(8,128)S(1)}, f32[64,1024]{1,0:T(8,128)S(1)}, u32[]{:S(2)}, u32[]{:S(2)}) %collective-permute-start.8) | collective-permute-done | bytes 262176 | tf_op jit(solution)/shard_map/ppermute | solution.py:115
  81.2 3.8 %collective-permute-done.9 = f32[32,1024]{1,0:T(8,128)S(1)} collective-permute-done((f32[32,1024]{1,0:T(8,128)S(1)}, f32[32,1024]{1,0:T(8,128)S(1)}, u32[]{:S(2)}, u32[]{:S(2)}) %collective-permute-start.9) | collective-permute-done | bytes 131104 | tf_op jit(solution)/shard_map/ppermute | solution.py:115
  85.0 2.7 %collective-permute-start.10 = (f32[16,1024]{1,0:T(8,128)S(1)}, f32[16,1024]{1,0:T(8,128)S(1)}, u32[]{:S(2)}, u32[]{:S(2)}) collective-permute-start(f32[16,1024]{1,0:T(8,128)S(1)} %slice_select_fusion.3), channel_id=1, source_target_pairs={{0,128},{1,129},{2,130},{3,131},{4,132},{5,133},{6,134},{7,135},{8... | collective-permute-start | bytes 196616 | tf_op jit(solution)/shard_map/ppermute | solution.py:115
  87.7 3.0 %collective-permute-start.27 = (f32[128]{0:T(128)S(1)}, f32[128]{0:T(128)S(1)}, u32[]{:S(2)}, u32[]{:S(2)}) collective-permute-start(f32[128]{0:T(128)S(1)} %broadcast_select_fusion.32), channel_id=1, source_target_pairs={{0,16},{1,17},{2,18},{3,19},{4,20},{5,21},{6,22},{7,23},{8,24},{9,... | collective-permute-start | bytes 1544 | tf_op jit(solution)/shard_map/ppermute | solution.py:115
  90.7 2.1 %collective-permute-start.11 = (f32[8,1024]{1,0:T(8,128)S(1)}, f32[8,1024]{1,0:T(8,128)S(1)}, u32[]{:S(2)}, u32[]{:S(2)}) collective-permute-start(f32[8,1024]{1,0:T(8,128)S(1)} %slice_select_fusion.4), channel_id=1, source_target_pairs={{0,16},{1,17},{2,18},{3,19},{4,20},{5,21},{6,22},{7,23},{8,24},{9,... | collective-permute-start | bytes 98312 | tf_op jit(solution)/shard_map/ppermute | solution.py:115
  92.8 2.0 %collective-permute-done.11 = f32[8,1024]{1,0:T(8,128)S(1)} collective-permute-done((f32[8,1024]{1,0:T(8,128)S(1)}, f32[8,1024]{1,0:T(8,128)S(1)}, u32[]{:S(2)}, u32[]{:S(2)}) %collective-permute-start.11) | collective-permute-done | bytes 32800 | tf_op jit(solution)/shard_map/ppermute | solution.py:115
  94.8 2.8 %collective-permute-start.12 = (f32[4,1024]{1,0:T(4,128)S(1)}, f32[4,1024]{1,0:T(4,128)S(1)}, u32[]{:S(2)}, u32[]{:S(2)}) collective-permute-start(f32[4,1024]{1,0:T(4,128)S(1)} %slice_select_fusion.5), channel_id=1, source_target_pairs={{0,2},{1,3},{2,0},{3,1},{4,6},{5,7},{6,4},{7,5},{8,10},{9,11},{10,... | collective-permute-start | bytes 49160 | tf_op jit(solution)/shard_map/ppermute | solution.py:115
  98.0 1.1 collective-permute-done.12
  99.0 4.8 %collective-permute-start.13 = (f32[2,1024]{1,0:T(2,128)S(1)}, f32[2,1024]{1,0:T(2,128)S(1)}, u32[]{:S(2)}, u32[]{:S(2)}) collective-permute-start(f32[2,1024]{1,0:T(2,128)S(1)} %broadcast_select_fusion.15), channel_id=1, source_target_pairs={{0,4},{1,5},{2,6},{3,7},{4,0},{5,1},{6,2},{7,3},{8,12},{9,13},{10,... | collective-permute-start | bytes 24584 | tf_op jit(solution)/shard_map/ppermute | solution.py:115
  103.9 1.7 collective-permute-done.13
  105.6 4.8 %collective-permute-start.14 = (f32[2,1024]{1,0:T(2,128)S(1)}, f32[2,1024]{1,0:T(2,128)S(1)}, u32[]{:S(2)}, u32[]{:S(2)}) collective-permute-start(f32[2,1024]{1,0:T(2,128)S(1)} %select_add_fusion.8), channel_id=1, source_target_pairs={{0,4},{1,5},{2,6},{3,7},{4,0},{5,1},{6,2},{7,3},{8,12},{9,13},{10,... | collective-permute-start | bytes 24584 | tf_op jit(solution)/shard_map/ppermute | solution.py:119
  110.4 0.6 collective-permute-start.29
  111.1 1.0 collective-permute-done.14
  112.1 2.8 %collective-permute-start.15 = (f32[4,1024]{1,0:T(4,128)S(1)}, f32[4,1024]{1,0:T(4,128)S(1)}, u32[]{:S(2)}, u32[]{:S(2)}) collective-permute-start(f32[4,1024]{1,0:T(4,128)S(1)} %pad_maximum_fusion.6), channel_id=1, source_target_pairs={{0,2},{1,3},{2,0},{3,1},{4,6},{5,7},{6,4},{7,5},{8,10},{9,11},{10,... | collective-permute-start | bytes 49160 | tf_op jit(solution)/shard_map/ppermute | solution.py:119
  114.9 1.9 %collective-permute-done.29 = f32[32]{0:T(128)S(1)} collective-permute-done((f32[32]{0:T(128)S(1)}, f32[32]{0:T(128)S(1)}, u32[]{:S(2)}, u32[]{:S(2)}) %collective-permute-start.29) | collective-permute-done | bytes 160 | tf_op jit(solution)/shard_map/ppermute | solution.py:115
  116.8 2.9 %collective-permute-start.30 = (f32[32]{0:T(128)S(1)}, f32[32]{0:T(128)S(1)}, u32[]{:S(2)}, u32[]{:S(2)}) collective-permute-start(f32[32]{0:T(128)S(1)} %fusion.26), channel_id=1, source_target_pairs={{0,4},{1,5},{2,6},{3,7},{4,0},{5,1},{6,2},{7,3},{8,12},{9,13},{10,... | collective-permute-start | bytes 392 | tf_op jit(solution)/shard_map/ppermute | solution.py:119
  119.8 1.2 collective-permute-start.16
  121.0 2.2 %collective-permute-done.30 = f32[32]{0:T(128)S(1)} collective-permute-done((f32[32]{0:T(128)S(1)}, f32[32]{0:T(128)S(1)}, u32[]{:S(2)}, u32[]{:S(2)}) %collective-permute-start.30) | collective-permute-done | bytes 160 | tf_op jit(solution)/shard_map/ppermute | solution.py:119
  123.5 2.7 %collective-permute-start.17 = (f32[16,1024]{1,0:T(8,128)S(1)}, f32[16,1024]{1,0:T(8,128)S(1)}, u32[]{:S(2)}, u32[]{:S(2)}) collective-permute-start(f32[16,1024]{1,0:T(8,128)S(1)} %pad_maximum_fusion.4), channel_id=1, source_target_pairs={{0,128},{1,129},{2,130},{3,131},{4,132},{5,133},{6,134},{7,135},{8... | collective-permute-start | bytes 196616 | tf_op jit(solution)/shard_map/ppermute | solution.py:119
  126.3 2.4 %collective-permute-start.31 = (f32[64]{0:T(128)S(1)}, f32[64]{0:T(128)S(1)}, u32[]{:S(2)}, u32[]{:S(2)}) collective-permute-start(f32[64]{0:T(128)S(1)} %pad_maximum_fusion.12), channel_id=1, source_target_pairs={{0,2},{1,3},{2,0},{3,1},{4,6},{5,7},{6,4},{7,5},{8,10},{9,11},{10,... | collective-permute-start | bytes 776 | tf_op jit(solution)/shard_map/ppermute | solution.py:119
  128.9 1.4 collective-permute-done.31
  130.4 1.2 collective-permute-start.32
  131.6 1.4 collective-permute-done.18
  133.0 0.8 collective-permute-start.19
  134.1 1.9 %collective-permute-start.33 = (f32[256]{0:T(256)S(1)}, f32[256]{0:T(256)S(1)}, u32[]{:S(2)}, u32[]{:S(2)}) collective-permute-start(f32[256]{0:T(256)S(1)} %pad_maximum_fusion.11), channel_id=1, source_target_pairs={{0,128},{1,129},{2,130},{3,131},{4,132},{5,133},{6,134},{7,135},{8... | collective-permute-start | bytes 3080 | tf_op jit(solution)/shard_map/ppermute | solution.py:119
  136.0 2.3 %collective-permute-done.19 = f32[64,1024]{1,0:T(8,128)S(1)} collective-permute-done((f32[64,1024]{1,0:T(8,128)S(1)}, f32[64,1024]{1,0:T(8,128)S(1)}, u32[]{:S(2)}, u32[]{:S(2)}) %collective-permute-start.19) | collective-permute-done | bytes 262176 | tf_op jit(solution)/shard_map/ppermute | solution.py:119
  138.7 2.3 %collective-permute-done.34 = f32[512]{0:T(512)S(1)} collective-permute-done((f32[512]{0:T(512)S(1)}, f32[512]{0:T(512)S(1)}, u32[]{:S(2)}, u32[]{:S(2)}) %collective-permute-start.34) | collective-permute-done | bytes 2080 | tf_op jit(solution)/shard_map/ppermute | solution.py:119
  141.1 5.7 %collective-permute-done.20 = f32[128,1024]{1,0:T(8,128)S(1)} collective-permute-done((f32[128,1024]{1,0:T(8,128)S(1)}, f32[128,1024]{1,0:T(8,128)S(1)}, u32[]{:S(2)}, u32[]{:S(2)}) %collective-permute-start.20) | collective-permute-done | bytes 524320 | tf_op jit(solution)/shard_map/ppermute | solution.py:119
  146.9 1.0 pad_maximum_fusion
  148.0 14.9 %collective-permute-start.21 = (f32[256,1024]{1,0:T(8,128)}, f32[256,1024]{1,0:T(8,128)S(1)}, u32[]{:S(2)}, u32[]{:S(2)}) collective-permute-start(f32[256,1024]{1,0:T(8,128)} %pad_maximum_fusion), channel_id=1, source_target_pairs={{0,32},{1,33},{2,34},{3,35},{4,36},{5,37},{6,38},{7,39},{8,40},{9,... | collective-permute-start | bytes 3145736 | tf_op jit(solution)/shard_map/ppermute | solution.py:119
  162.8 0.7 collective-permute-start.35
  163.5 1.8 %collective-permute-done.35 = f32[1024]{0:T(1024)S(1)} collective-permute-done((f32[1024]{0:T(1024)S(1)}, f32[1024]{0:T(1024)S(1)}, u32[]{:S(2)}, u32[]{:S(2)}) %collective-permute-start.35) | collective-permute-done | bytes 4128 | tf_op jit(solution)/shard_map/ppermute | solution.py:119
  165.5 2.4 %collective-permute-done.36 = f32[2048]{0:T(1024)S(1)} collective-permute-done((f32[2048]{0:T(1024)S(1)}, f32[2048]{0:T(1024)S(1)}, u32[]{:S(2)}, u32[]{:S(2)}) %collective-permute-start.36) | collective-permute-done | bytes 8224 | tf_op jit(solution)/shard_map/ppermute | solution.py:119
  167.9 2.5 %collective-permute-start.37 = (f32[4096]{0:T(1024)S(1)}, f32[4096]{0:T(1024)S(1)}, u32[]{:S(2)}, u32[]{:S(2)}) collective-permute-start(f32[4096]{0:T(1024)S(1)} %pad_maximum_fusion.7), channel_id=1, source_target_pairs={{0,32},{1,33},{2,34},{3,35},{4,36},{5,37},{6,38},{7,39},{8,40},{9,... | collective-permute-start | bytes 49160 | tf_op jit(solution)/shard_map/ppermute | solution.py:119
  170.4 0.8 collective-permute-done.37
  171.2 0.6 maximum_bitcast_fusion.2
  171.9 1.5 broadcast_select_fusion.1
  (134 shorter events, 10.6 us)
Async XLA Ops:
  0.6 55.8 %copy-start = (bf16[256,1024]{1,0:T(8,128)(2,1)S(1)}, bf16[256,1024]{1,0:T(8,128)(2,1)}, u32[]{:S(2)}) copy-start(bf16[256,1024]{1,0:T(8,128)(2,1)} %param.29) | copy-start | bytes 1572868
  5.1 37.4 %copy-start.4 = (s32[1,256,8]{1,2,0:T(8,128)S(1)}, s32[1,256,8]{1,2,0:T(8,128)}, u32[]{:S(2)}) copy-start(s32[1,256,8]{1,2,0:T(8,128)} %param.27) | copy-start | bytes 24580
  5.1 37.4 %copy-start.13 = (s32[256]{0:T(256)S(1)}, s32[256]{0:T(256)}, u32[]{:S(2)}) copy-start(s32[256]{0:T(256)} %constant.62.clone) | copy-start | bytes 3076
  5.1 50.9 %copy-start.1 = (bf16[256,1024]{1,0:T(8,128)(2,1)S(1)}, bf16[256,1024]{1,0:T(8,128)(2,1)}, u32[]{:S(2)}) copy-start(bf16[256,1024]{1,0:T(8,128)(2,1)} %param.30) | copy-start | bytes 1572868
  26.9 29.9 %copy-start.3 = (bf16[1024,8]{0,1:T(8,128)(2,1)S(1)}, bf16[1024,8]{0,1:T(8,128)(2,1)}, u32[]{:S(2)}) copy-start(bf16[1024,8]{0,1:T(8,128)(2,1)} %param.31) | copy-start | bytes 49156
  26.9 30.2 %copy-start.5 = (s32[1,256]{1,0:T(1,128)S(1)}, s32[1,256]{1,0:T(1,128)}, u32[]{:S(2)}) copy-start(s32[1,256]{1,0:T(1,128)} %param.28) | copy-start | bytes 3076
  28.8 15.0 %collective-permute-start.2 = (f32[1,256]{1,0:T(1,128)S(1)}, f32[1,256]{1,0:T(1,128)S(1)}, u32[]{:S(2)}, u32[]{:S(2)}) collective-permute-start(f32[1,256]{1,0:T(1,128)S(1)} %get-tuple-element.47), channel_id=1, source_target_pairs={{32,0},{64,32},{96,64},{128,96},{160,128},{192,160},{224,192},{33,... | collective-permute-start | bytes 3080 | tf_op jit(solution)/shard_map/ppermute | solution.py:11
  33.9 9.9 %collective-permute-start.3 = (f32[1,256]{1,0:T(1,128)S(1)}, f32[1,256]{1,0:T(1,128)S(1)}, u32[]{:S(2)}, u32[]{:S(2)}) collective-permute-start(f32[1,256]{1,0:T(1,128)S(1)} %get-tuple-element.48), channel_id=1, source_target_pairs={{0,32},{32,64},{64,96},{96,128},{128,160},{160,192},{192,224},{1,3... | collective-permute-start | bytes 3080 | tf_op jit(solution)/shard_map/ppermute | solution.py:11
  36.9 7.7 %collective-permute-start = (f32[1,256,256]{2,1,0:T(8,128)S(1)}, f32[1,256,256]{2,1,0:T(8,128)S(1)}, u32[]{:S(2)}, u32[]{:S(2)}) collective-permute-start(f32[1,256,256]{2,1,0:T(8,128)S(1)} %get-tuple-element.12), channel_id=1, source_target_pairs={{32,0},{64,32},{96,64},{128,96},{160,128},{192,160},{224,192},{33,... | collective-permute-start | bytes 786440 | tf_op jit(solution)/shard_map/ppermute | solution.py:11
  39.3 6.5 %collective-permute-start.1 = (f32[1,256,256]{2,1,0:T(8,128)S(1)}, f32[1,256,256]{2,1,0:T(8,128)S(1)}, u32[]{:S(2)}, u32[]{:S(2)}) collective-permute-start(f32[1,256,256]{2,1,0:T(8,128)S(1)} %get-tuple-element.13), channel_id=1, source_target_pairs={{0,32},{32,64},{64,96},{96,128},{128,160},{160,192},{192,224},{1,3... | collective-permute-start | bytes 786440 | tf_op jit(solution)/shard_map/ppermute | solution.py:11
  46.8 7.0 %collective-permute-start.5 = (bf16[1,256,256]{2,1,0:T(8,128)(2,1)S(1)}, bf16[1,256,256]{2,1,0:T(8,128)(2,1)S(1)}, u32[]{:S(2)}, u32[]{:S(2)}) collective-permute-start(bf16[1,256,256]{2,1,0:T(8,128)(2,1)S(1)} %fusion.19), channel_id=1, source_target_pairs={{32,0},{64,32},{96,64},{128,96},{160,128},{192,160},{224,192},{33,... | collective-permute-start | bytes 393224 | tf_op jit(solution)/shard_map/ppermute | solution.py:22
  48.8 6.3 %collective-permute-start.4 = (bf16[1,256,256]{2,1,0:T(8,128)(2,1)S(1)}, bf16[1,256,256]{2,1,0:T(8,128)(2,1)S(1)}, u32[]{:S(2)}, u32[]{:S(2)}) collective-permute-start(bf16[1,256,256]{2,1,0:T(8,128)(2,1)S(1)} %fusion.19), channel_id=1, source_target_pairs={{0,32},{32,64},{64,96},{96,128},{128,160},{160,192},{192,224},{1,3... | collective-permute-start | bytes 393224 | tf_op jit(solution)/shard_map/ppermute | solution.py:19
  56.4 2.9 %copy-start.12 = (s32[256]{0:T(256)S(1)}, s32[256]{0:T(256)}, u32[]{:S(2)}) copy-start(s32[256]{0:T(256)} %constant.63.clone) | copy-start | bytes 3076
  56.4 5.6 %copy-start.11 = (s32[256]{0:T(256)S(1)}, s32[256]{0:T(256)}, u32[]{:S(2)}) copy-start(s32[256]{0:T(256)} %constant.64.clone) | copy-start | bytes 3076
  57.1 7.1 %copy-start.2 = (f32[256,8]{0,1:T(8,128)}, f32[256,8]{0,1:T(8,128)S(1)}, u32[]{:S(2)}) copy-start(f32[256,8]{0,1:T(8,128)S(1)} %fusion.33) | copy-start | bytes 24580
  57.1 9.5 %copy-start.10 = (s32[256]{0:T(256)S(1)}, s32[256]{0:T(256)}, u32[]{:S(2)}) copy-start(s32[256]{0:T(256)} %constant.69.clone) | copy-start | bytes 3076
  57.1 10.7 %copy-start.9 = (s32[256]{0:T(256)S(1)}, s32[256]{0:T(256)}, u32[]{:S(2)}) copy-start(s32[256]{0:T(256)} %constant.68.clone) | copy-start | bytes 3076
  57.2 11.9 %copy-start.8 = (s32[256]{0:T(256)S(1)}, s32[256]{0:T(256)}, u32[]{:S(2)}) copy-start(s32[256]{0:T(256)} %constant.67.clone) | copy-start | bytes 3076
  57.2 13.2 %copy-start.7 = (s32[256]{0:T(256)S(1)}, s32[256]{0:T(256)}, u32[]{:S(2)}) copy-start(s32[256]{0:T(256)} %constant.66.clone) | copy-start | bytes 3076
  57.2 14.4 %copy-start.6 = (s32[256]{0:T(256)S(1)}, s32[256]{0:T(256)}, u32[]{:S(2)}) copy-start(s32[256]{0:T(256)} %constant.65.clone) | copy-start | bytes 3076
  58.4 5.4 %collective-permute-start.6 = (f32[256,1024]{1,0:T(8,128)S(1)}, f32[256,1024]{1,0:T(8,128)S(1)}, u32[]{:S(2)}, u32[]{:S(2)}) collective-permute-start(f32[256,1024]{1,0:T(8,128)S(1)} %get-tuple-element.59), channel_id=1, source_target_pairs={{0,32},{1,33},{2,34},{3,35},{4,36},{5,37},{6,38},{7,39},{8,40},{9,... | collective-permute-start | bytes 3145736 | tf_op jit(solution)/shard_map/ppermute | solution.py:115
  58.7 2.5 %collective-permute-start.22 = (f32[4096]{0:T(1024)S(1)}, f32[4096]{0:T(1024)S(1)}, u32[]{:S(2)}, u32[]{:S(2)}) collective-permute-start(f32[4096]{0:T(1024)S(1)} %bitcast.60), channel_id=1, source_target_pairs={{0,32},{1,33},{2,34},{3,35},{4,36},{5,37},{6,38},{7,39},{8,40},{9,... | collective-permute-start | bytes 49160 | tf_op jit(solution)/shard_map/ppermute | solution.py:115
  61.2 2.6 %collective-permute-start.23 = (f32[2048]{0:T(1024)S(1)}, f32[2048]{0:T(1024)S(1)}, u32[]{:S(2)}, u32[]{:S(2)}) collective-permute-start(f32[2048]{0:T(1024)S(1)} %slice_select_fusion.6), channel_id=1, source_target_pairs={{0,64},{1,65},{2,66},{3,67},{4,68},{5,69},{6,70},{7,71},{8,72},{9,... | collective-permute-start | bytes 24584 | tf_op jit(solution)/shard_map/ppermute | solution.py:115
  64.2 11.0 %collective-permute-start.7 = (f32[128,1024]{1,0:T(8,128)S(1)}, f32[128,1024]{1,0:T(8,128)S(1)}, u32[]{:S(2)}, u32[]{:S(2)}) collective-permute-start(f32[128,1024]{1,0:T(8,128)S(1)} %slice_select_fusion), channel_id=1, source_target_pairs={{0,64},{1,65},{2,66},{3,67},{4,68},{5,69},{6,70},{7,71},{8,72},{9,... | collective-permute-start | bytes 1572872 | tf_op jit(solution)/shard_map/ppermute | solution.py:115
  65.0 7.9 %collective-permute-start.24 = (f32[1024]{0:T(1024)S(1)}, f32[1024]{0:T(1024)S(1)}, u32[]{:S(2)}, u32[]{:S(2)}) collective-permute-start(f32[1024]{0:T(1024)S(1)} %slice_select_fusion.7), channel_id=1, source_target_pairs={{0,8},{1,9},{2,10},{3,11},{4,12},{5,13},{6,14},{7,15},{8,0},{9,1},... | collective-permute-start | bytes 12296 | tf_op jit(solution)/shard_map/ppermute | solution.py:115
  72.9 3.3 %collective-permute-start.25 = (f32[512]{0:T(512)S(1)}, f32[512]{0:T(512)S(1)}, u32[]{:S(2)}, u32[]{:S(2)}) collective-permute-start(f32[512]{0:T(512)S(1)} %slice_select_fusion.8), channel_id=1, source_target_pairs={{0,1},{1,0},{2,3},{3,2},{4,5},{5,4},{6,7},{7,6},{8,9},{9,8},{10,11... | collective-permute-start | bytes 6152 | tf_op jit(solution)/shard_map/ppermute | solution.py:115
  75.3 5.6 %collective-permute-start.8 = (f32[64,1024]{1,0:T(8,128)S(1)}, f32[64,1024]{1,0:T(8,128)S(1)}, u32[]{:S(2)}, u32[]{:S(2)}) collective-permute-start(f32[64,1024]{1,0:T(8,128)S(1)} %slice_select_fusion.1), channel_id=1, source_target_pairs={{0,8},{1,9},{2,10},{3,11},{4,12},{5,13},{6,14},{7,15},{8,0},{9,1},... | collective-permute-start | bytes 786440 | tf_op jit(solution)/shard_map/ppermute | solution.py:115
  76.2 5.0 %collective-permute-start.26 = (f32[256]{0:T(256)S(1)}, f32[256]{0:T(256)S(1)}, u32[]{:S(2)}, u32[]{:S(2)}) collective-permute-start(f32[256]{0:T(256)S(1)} %broadcast_select_fusion.36), channel_id=1, source_target_pairs={{0,128},{1,129},{2,130},{3,131},{4,132},{5,133},{6,134},{7,135},{8... | collective-permute-start | bytes 3080 | tf_op jit(solution)/shard_map/ppermute | solution.py:115
  81.0 3.9 %collective-permute-start.9 = (f32[32,1024]{1,0:T(8,128)S(1)}, f32[32,1024]{1,0:T(8,128)S(1)}, u32[]{:S(2)}, u32[]{:S(2)}) collective-permute-start(f32[32,1024]{1,0:T(8,128)S(1)} %slice_select_fusion.2), channel_id=1, source_target_pairs={{0,1},{1,0},{2,3},{3,2},{4,5},{5,4},{6,7},{7,6},{8,9},{9,8},{10,11... | collective-permute-start | bytes 393224 | tf_op jit(solution)/shard_map/ppermute | solution.py:115
  85.0 5.7 %collective-permute-start.10 = (f32[16,1024]{1,0:T(8,128)S(1)}, f32[16,1024]{1,0:T(8,128)S(1)}, u32[]{:S(2)}, u32[]{:S(2)}) collective-permute-start(f32[16,1024]{1,0:T(8,128)S(1)} %slice_select_fusion.3), channel_id=1, source_target_pairs={{0,128},{1,129},{2,130},{3,131},{4,132},{5,133},{6,134},{7,135},{8... | collective-permute-start | bytes 196616 | tf_op jit(solution)/shard_map/ppermute | solution.py:115
  87.7 5.1 %collective-permute-start.27 = (f32[128]{0:T(128)S(1)}, f32[128]{0:T(128)S(1)}, u32[]{:S(2)}, u32[]{:S(2)}) collective-permute-start(f32[128]{0:T(128)S(1)} %broadcast_select_fusion.32), channel_id=1, source_target_pairs={{0,16},{1,17},{2,18},{3,19},{4,20},{5,21},{6,22},{7,23},{8,24},{9,... | collective-permute-start | bytes 1544 | tf_op jit(solution)/shard_map/ppermute | solution.py:115
  90.7 4.1 %collective-permute-start.11 = (f32[8,1024]{1,0:T(8,128)S(1)}, f32[8,1024]{1,0:T(8,128)S(1)}, u32[]{:S(2)}, u32[]{:S(2)}) collective-permute-start(f32[8,1024]{1,0:T(8,128)S(1)} %slice_select_fusion.4), channel_id=1, source_target_pairs={{0,16},{1,17},{2,18},{3,19},{4,20},{5,21},{6,22},{7,23},{8,24},{9,... | collective-permute-start | bytes 98312 | tf_op jit(solution)/shard_map/ppermute | solution.py:115
  94.8 4.2 %collective-permute-start.12 = (f32[4,1024]{1,0:T(4,128)S(1)}, f32[4,1024]{1,0:T(4,128)S(1)}, u32[]{:S(2)}, u32[]{:S(2)}) collective-permute-start(f32[4,1024]{1,0:T(4,128)S(1)} %slice_select_fusion.5), channel_id=1, source_target_pairs={{0,2},{1,3},{2,0},{3,1},{4,6},{5,7},{6,4},{7,5},{8,10},{9,11},{10,... | collective-permute-start | bytes 49160 | tf_op jit(solution)/shard_map/ppermute | solution.py:115
  97.7 6.1 %collective-permute-start.28 = (f32[64]{0:T(128)S(1)}, f32[64]{0:T(128)S(1)}, u32[]{:S(2)}, u32[]{:S(2)}) collective-permute-start(f32[64]{0:T(128)S(1)} %broadcast_select_fusion.28), channel_id=1, source_target_pairs={{0,2},{1,3},{2,0},{3,1},{4,6},{5,7},{6,4},{7,5},{8,10},{9,11},{10,... | collective-permute-start | bytes 776 | tf_op jit(solution)/shard_map/ppermute | solution.py:115
  99.0 6.5 %collective-permute-start.13 = (f32[2,1024]{1,0:T(2,128)S(1)}, f32[2,1024]{1,0:T(2,128)S(1)}, u32[]{:S(2)}, u32[]{:S(2)}) collective-permute-start(f32[2,1024]{1,0:T(2,128)S(1)} %broadcast_select_fusion.15), channel_id=1, source_target_pairs={{0,4},{1,5},{2,6},{3,7},{4,0},{5,1},{6,2},{7,3},{8,12},{9,13},{10,... | collective-permute-start | bytes 24584 | tf_op jit(solution)/shard_map/ppermute | solution.py:115
  105.6 6.5 %collective-permute-start.14 = (f32[2,1024]{1,0:T(2,128)S(1)}, f32[2,1024]{1,0:T(2,128)S(1)}, u32[]{:S(2)}, u32[]{:S(2)}) collective-permute-start(f32[2,1024]{1,0:T(2,128)S(1)} %select_add_fusion.8), channel_id=1, source_target_pairs={{0,4},{1,5},{2,6},{3,7},{4,0},{5,1},{6,2},{7,3},{8,12},{9,13},{10,... | collective-permute-start | bytes 24584 | tf_op jit(solution)/shard_map/ppermute | solution.py:119
  110.4 6.3 %collective-permute-start.29 = (f32[32]{0:T(128)S(1)}, f32[32]{0:T(128)S(1)}, u32[]{:S(2)}, u32[]{:S(2)}) collective-permute-start(f32[32]{0:T(128)S(1)} %broadcast_select_fusion.24), channel_id=1, source_target_pairs={{0,4},{1,5},{2,6},{3,7},{4,0},{5,1},{6,2},{7,3},{8,12},{9,13},{10,... | collective-permute-start | bytes 392 | tf_op jit(solution)/shard_map/ppermute | solution.py:115
  112.1 7.6 %collective-permute-start.15 = (f32[4,1024]{1,0:T(4,128)S(1)}, f32[4,1024]{1,0:T(4,128)S(1)}, u32[]{:S(2)}, u32[]{:S(2)}) collective-permute-start(f32[4,1024]{1,0:T(4,128)S(1)} %pad_maximum_fusion.6), channel_id=1, source_target_pairs={{0,2},{1,3},{2,0},{3,1},{4,6},{5,7},{6,4},{7,5},{8,10},{9,11},{10,... | collective-permute-start | bytes 49160 | tf_op jit(solution)/shard_map/ppermute | solution.py:119
  116.8 6.3 %collective-permute-start.30 = (f32[32]{0:T(128)S(1)}, f32[32]{0:T(128)S(1)}, u32[]{:S(2)}, u32[]{:S(2)}) collective-permute-start(f32[32]{0:T(128)S(1)} %fusion.26), channel_id=1, source_target_pairs={{0,4},{1,5},{2,6},{3,7},{4,0},{5,1},{6,2},{7,3},{8,12},{9,13},{10,... | collective-permute-start | bytes 392 | tf_op jit(solution)/shard_map/ppermute | solution.py:119
  119.8 3.8 %collective-permute-start.16 = (f32[8,1024]{1,0:T(8,128)S(1)}, f32[8,1024]{1,0:T(8,128)S(1)}, u32[]{:S(2)}, u32[]{:S(2)}) collective-permute-start(f32[8,1024]{1,0:T(8,128)S(1)} %pad_maximum_fusion.5), channel_id=1, source_target_pairs={{0,16},{1,17},{2,18},{3,19},{4,20},{5,21},{6,22},{7,23},{8,24},{9,... | collective-permute-start | bytes 98312 | tf_op jit(solution)/shard_map/ppermute | solution.py:119
  123.5 5.2 %collective-permute-start.17 = (f32[16,1024]{1,0:T(8,128)S(1)}, f32[16,1024]{1,0:T(8,128)S(1)}, u32[]{:S(2)}, u32[]{:S(2)}) collective-permute-start(f32[16,1024]{1,0:T(8,128)S(1)} %pad_maximum_fusion.4), channel_id=1, source_target_pairs={{0,128},{1,129},{2,130},{3,131},{4,132},{5,133},{6,134},{7,135},{8... | collective-permute-start | bytes 196616 | tf_op jit(solution)/shard_map/ppermute | solution.py:119
  126.3 3.9 %collective-permute-start.31 = (f32[64]{0:T(128)S(1)}, f32[64]{0:T(128)S(1)}, u32[]{:S(2)}, u32[]{:S(2)}) collective-permute-start(f32[64]{0:T(128)S(1)} %pad_maximum_fusion.12), channel_id=1, source_target_pairs={{0,2},{1,3},{2,0},{3,1},{4,6},{5,7},{6,4},{7,5},{8,10},{9,11},{10,... | collective-permute-start | bytes 776 | tf_op jit(solution)/shard_map/ppermute | solution.py:119
  128.8 4.2 %collective-permute-start.18 = (f32[32,1024]{1,0:T(8,128)S(1)}, f32[32,1024]{1,0:T(8,128)S(1)}, u32[]{:S(2)}, u32[]{:S(2)}) collective-permute-start(f32[32,1024]{1,0:T(8,128)S(1)} %pad_maximum_fusion.3), channel_id=1, source_target_pairs={{0,1},{1,0},{2,3},{3,2},{4,5},{5,4},{6,7},{7,6},{8,9},{9,8},{10,11... | collective-permute-start | bytes 393224 | tf_op jit(solution)/shard_map/ppermute | solution.py:119
  130.4 3.6 %collective-permute-start.32 = (f32[128]{0:T(128)S(1)}, f32[128]{0:T(128)S(1)}, u32[]{:S(2)}, u32[]{:S(2)}) collective-permute-start(f32[128]{0:T(128)S(1)} %pad_maximum_fusion.13), channel_id=1, source_target_pairs={{0,16},{1,17},{2,18},{3,19},{4,20},{5,21},{6,22},{7,23},{8,24},{9,... | collective-permute-start | bytes 1544 | tf_op jit(solution)/shard_map/ppermute | solution.py:119
  133.0 5.3 %collective-permute-start.19 = (f32[64,1024]{1,0:T(8,128)S(1)}, f32[64,1024]{1,0:T(8,128)S(1)}, u32[]{:S(2)}, u32[]{:S(2)}) collective-permute-start(f32[64,1024]{1,0:T(8,128)S(1)} %pad_maximum_fusion.2), channel_id=1, source_target_pairs={{0,8},{1,9},{2,10},{3,11},{4,12},{5,13},{6,14},{7,15},{8,0},{9,1},... | collective-permute-start | bytes 786440 | tf_op jit(solution)/shard_map/ppermute | solution.py:119
  134.1 4.4 %collective-permute-start.33 = (f32[256]{0:T(256)S(1)}, f32[256]{0:T(256)S(1)}, u32[]{:S(2)}, u32[]{:S(2)}) collective-permute-start(f32[256]{0:T(256)S(1)} %pad_maximum_fusion.11), channel_id=1, source_target_pairs={{0,128},{1,129},{2,130},{3,131},{4,132},{5,133},{6,134},{7,135},{8... | collective-permute-start | bytes 3080 | tf_op jit(solution)/shard_map/ppermute | solution.py:119
  138.4 8.4 %collective-permute-start.20 = (f32[128,1024]{1,0:T(8,128)S(1)}, f32[128,1024]{1,0:T(8,128)S(1)}, u32[]{:S(2)}, u32[]{:S(2)}) collective-permute-start(f32[128,1024]{1,0:T(8,128)S(1)} %pad_maximum_fusion.1), channel_id=1, source_target_pairs={{0,64},{1,65},{2,66},{3,67},{4,68},{5,69},{6,70},{7,71},{8,72},{9,... | collective-permute-start | bytes 1572872 | tf_op jit(solution)/shard_map/ppermute | solution.py:119
  138.6 2.5 %collective-permute-start.34 = (f32[512]{0:T(512)S(1)}, f32[512]{0:T(512)S(1)}, u32[]{:S(2)}, u32[]{:S(2)}) collective-permute-start(f32[512]{0:T(512)S(1)} %pad_maximum_fusion.10), channel_id=1, source_target_pairs={{0,1},{1,0},{2,3},{3,2},{4,5},{5,4},{6,7},{7,6},{8,9},{9,8},{10,11... | collective-permute-start | bytes 6152 | tf_op jit(solution)/shard_map/ppermute | solution.py:119
  148.0 23.9 %collective-permute-start.21 = (f32[256,1024]{1,0:T(8,128)}, f32[256,1024]{1,0:T(8,128)S(1)}, u32[]{:S(2)}, u32[]{:S(2)}) collective-permute-start(f32[256,1024]{1,0:T(8,128)} %pad_maximum_fusion), channel_id=1, source_target_pairs={{0,32},{1,33},{2,34},{3,35},{4,36},{5,37},{6,38},{7,39},{8,40},{9,... | collective-permute-start | bytes 3145736 | tf_op jit(solution)/shard_map/ppermute | solution.py:119
  162.8 2.5 %collective-permute-start.35 = (f32[1024]{0:T(1024)S(1)}, f32[1024]{0:T(1024)S(1)}, u32[]{:S(2)}, u32[]{:S(2)}) collective-permute-start(f32[1024]{0:T(1024)S(1)} %pad_maximum_fusion.9), channel_id=1, source_target_pairs={{0,8},{1,9},{2,10},{3,11},{4,12},{5,13},{6,14},{7,15},{8,0},{9,1},... | collective-permute-start | bytes 12296 | tf_op jit(solution)/shard_map/ppermute | solution.py:119
  165.3 2.6 %collective-permute-start.36 = (f32[2048]{0:T(1024)S(1)}, f32[2048]{0:T(1024)S(1)}, u32[]{:S(2)}, u32[]{:S(2)}) collective-permute-start(f32[2048]{0:T(1024)S(1)} %pad_maximum_fusion.8), channel_id=1, source_target_pairs={{0,64},{1,65},{2,66},{3,67},{4,68},{5,69},{6,70},{7,71},{8,72},{9,... | collective-permute-start | bytes 24584 | tf_op jit(solution)/shard_map/ppermute | solution.py:119
  167.9 3.3 %collective-permute-start.37 = (f32[4096]{0:T(1024)S(1)}, f32[4096]{0:T(1024)S(1)}, u32[]{:S(2)}, u32[]{:S(2)}) collective-permute-start(f32[4096]{0:T(1024)S(1)} %pad_maximum_fusion.7), channel_id=1, source_target_pairs={{0,32},{1,33},{2,34},{3,35},{4,36},{5,37},{6,38},{7,39},{8,40},{9,... | collective-permute-start | bytes 49160 | tf_op jit(solution)/shard_map/ppermute | solution.py:119

commit v4 on v3

--- a/solution.py
+++ b/solution.py
@@ -89,39 +89,41 @@
     width = sizes["dp"]
     steps = []
     for flip0, flip1 in zip(core + first, core + second):
-        perm, bits = [], []
+        perm = []
         for device in range(sizes["region"] * width):
             at = {"region": device // width, "dp": device % width}
             axis, bit = flip1 if at["region"] & 1 else flip0
-            bits.append(1 if at[axis] & bit else 0)
             at[axis] ^= bit
             perm.append((device, at["region"] * width + at["dp"]))
-        steps.append((perm, bits))
+        steps.append((perm, flip0, flip1))
     return steps
 
 
-def all_sum(buffers, sizes):
+def upper_half(flip0, flip1):
+    core = lax.axis_index("region") % 2
+    bit0 = (lax.axis_index(flip0[0]) // flip0[1]) % 2
+    bit1 = (lax.axis_index(flip1[0]) // flip1[1]) % 2
+    return jnp.where(core == 1, bit1, bit0) == 1
+
+
+def all_sum(value, sizes, halvings):
     axes = ("region", "dp")
-    me = lax.axis_index("region") * sizes["dp"] + lax.axis_index("dp")
     steps = halving_plan(sizes)
-    for perm, bits in steps:
-        upper = jnp.asarray(bits, jnp.int32)[me] == 1
-        keeps, sends = [], []
-        for value in buffers:
-            half = value.shape[0] // 2
-            low, high = value[:half], value[half:]
-            keeps.append(jnp.where(upper, high, low))
-            sends.append(jnp.where(upper, low, high))
-        got = lax.ppermute(tuple(sends), axes, perm)
-        buffers = tuple(k + g for k, g in zip(keeps, got))
-    for perm, bits in reversed(steps):
-        upper = jnp.asarray(bits, jnp.int32)[me] == 1
-        got = lax.ppermute(buffers, axes, perm)
-        buffers = tuple(
-            jnp.concatenate([jnp.where(upper, g, v), jnp.where(upper, v, g)], axis=0)
-            for v, g in zip(buffers, got)
+    for perm, flip0, flip1 in steps[:halvings]:
+        upper = upper_half(flip0, flip1)
+        half = value.shape[0] // 2
+        low, high = value[:half], value[half:]
+        got = lax.ppermute(jnp.where(upper, low, high), axes, perm)
+        value = jnp.where(upper, high, low) + got
+    for perm, _, _ in steps[halvings:]:
+        value = value + lax.ppermute(value, axes, perm)
+    for perm, flip0, flip1 in reversed(steps[:halvings]):
+        upper = upper_half(flip0, flip1)
+        got = lax.ppermute(value, axes, perm)
+        value = jnp.concatenate(
+            [jnp.where(upper, got, value), jnp.where(upper, value, got)], axis=0
         )
-    return buffers
+    return value
 
 
 def local(cells, cell_weight, cell_cluster, cluster_edges, labels, w_self, w_nbr, w_out):
@@ -161,18 +163,20 @@
     classes = jnp.arange(w_out.shape[1], dtype=jnp.int32)
     target = (labels[..., None] == classes[None, None, :]).astype(jnp.float32)
     d_logits = ((jax.nn.sigmoid(scores) - target) / events).astype(jnp.bfloat16)
-    grad_head = jnp.einsum("ekh,ekc->ch", units, d_logits, preferred_element_type=jnp.float32)
+    grad_head = jnp.einsum("ekh,ekc->hc", units, d_logits, preferred_element_type=jnp.float32)
     d_units = jnp.einsum("ekc,hc->ekh", d_logits, w_out, preferred_element_type=jnp.float32)
     d_z = (d_units * sig * (1.0 + zval * (1.0 - sig))).astype(jnp.bfloat16)
     grad_own = jnp.einsum("ekf,ekh->fh", pooled, d_z, preferred_element_type=jnp.float32)
     grad_side = jnp.einsum("ekf,ekh->fh", agg, d_z, preferred_element_type=jnp.float32)
     sizes = {"region": lax.axis_size("region"), "dp": lax.axis_size("dp")}
-    hid = grad_own.shape[1]
-    grads, head = all_sum(
-        (jnp.concatenate([grad_own, grad_side], axis=0), grad_head.reshape(-1)), sizes
+    feats, hid = grad_own.shape
+    rows = 2 * feats
+    packed = jnp.concatenate(
+        [jnp.concatenate([grad_own, grad_side], axis=0), grad_head.reshape(rows, -1)], axis=1
     )
-    grad_own, grad_side = grads[: pooled.shape[2]], grads[pooled.shape[2] :]
-    grad_head = head.reshape(-1, hid).T
+    packed = all_sum(packed, sizes, 4)
+    grad_own, grad_side = packed[:feats, :hid], packed[feats:, :hid]
+    grad_head = packed[:, hid:].reshape(hid, -1)
     return (scores, grad_own, grad_side, grad_head)
 
 

time: 174 us -> 167 us (0.960)
  starting transfers between devices: 83.3 us -> 49.8 us
  waiting for transfers between devices: 40.3 us -> 62.8 us
  local copies, waits for them, and re-layouts: 7.85 us -> 15.6 us
  between operations: 6.49 us -> 1.08 us
  matrix products: 3.32 us -> 5.46 us
    ppermute x32 -> x12, starting transfers between devices: 64.4 us -> 30.9 us  [the longest x4 14.2 us: all_sum(): value = value + lax.ppermute(value, axes, perm)]
    ppermute x32 -> x12, waiting for transfers between devices: 36.4 us -> 55.2 us  [the longest x4 22.6 us: all_sum(): got = lax.ppermute(value, axes, perm)]
    dynamic_slice x8 -> x0, local copies, waits for them, and re-layouts: 4.69 us -> none  [all_sum(): upper = jnp.asarray(bits, jnp.int32)[me] == 1]
    ppermute x0 -> x4, local copies, waits for them, and re-layouts: none -> 4.68 us  [the longest x2 2.86 us: all_sum(): got = lax.ppermute(jnp.where(upper, low, high), axes, perm)]
    ppermute x1, waiting for transfers between devices: 0.69 us -> 4.33 us  [padded(): lax.ppermute(lax.slice_in_dim(block, 0, width, axis=dim), axis, backward)]
    select_n x0 -> x2, local copies, waits for them, and re-layouts: none -> 2.78 us  [all_sum(): got = lax.ppermute(jnp.where(upper, low, high), axes, perm)]
    slice x0 -> x2, local copies, waits for them, and re-layouts: none -> 2.19 us  [local(): grad_own, grad_side = (packed[:feats, :hid], packed[feats:, :hid])]
    unnamed x29 -> x19, local copies, waits for them, and re-layouts: 0.1 us -> 2.14 us
  transfers between devices with their start and end apart: 38 -> 18, of which waited for: 25 -> 15; matrix products, arithmetic and copies ran while one was open for 4% -> 0% of each run, Pallas kernels for 0% -> 0%
where the time goes in v4:
time: 167 us; the launch traced here: 166 us
  waiting for transfers between devices  62.8 us (38%)
  starting transfers between devices  49.8 us (30%)
  Pallas kernels  21.7 us (13%)
  local copies, waits for them, and re-layouts  15.6 us (9%)
  other arithmetic  9.46 us (6%)
  matrix products  5.46 us (3%)
    ppermute x4, waiting for transfers between devices, all_sum(): got = lax.ppermute(value, axes, perm)  22.6 us
    pallas_call x1, Pallas kernels, accumulate(): pl.pallas_call(pooled_sums_kernel, grid=(length // block,), in_specs=[pl....  21.7 us
    ppermute x4, waiting for transfers between devices, all_sum(): got = lax.ppermute(jnp.where(upper, low, high), axes, perm)  18.8 us
    ppermute x4, starting transfers between devices, all_sum(): value = value + lax.ppermute(value, axes, perm)  14.2 us
    ppermute x4, starting transfers between devices, all_sum(): got = lax.ppermute(value, axes, perm)  14 us
    ppermute x4, waiting for transfers between devices, all_sum(): value = value + lax.ppermute(value, axes, perm)  13.8 us
    ppermute x4, starting transfers between devices, passed_along(): lax.ppermute(value, axis, [(source, source + steps) for source in range(i...  12.6 us
    ppermute x1, starting transfers between devices, padded(): lax.ppermute(lax.slice_in_dim(block, block.shape[dim] - width, None, axis...  4.39 us
  transfers between devices with their start and end apart: 18, of which 15 were waited for; matrix products, arithmetic and copies ran while one was open for 0% of the time, Pallas kernels for 0%

profile of v4, /device:TPU:1, one launch (start us, length us, event | category | flops | bytes accessed | tf_op | source)
XLA Modules:
  0.0 165.9 jit_solution(7598858238528478584)
XLA Ops:
  0.6 1.0 reduce-precision_subtract_fusion
  1.7 1.5 broadcast_subtract_fusion.ids_ref
  3.2 1.9 %stack.10.split_ref = f32[8,16384]{1,0:T(8,128)} concatenate(f32[1,16384]{1,0:T(1,128)S(1)} %get-tuple-element.31, f32[1,16384]{1,0:T(1,128)S(1)} %get-tuple-element.32, f32[1,16384]{1,0:T(1,128)S(1)} %get-tuple-element.30, f32[1,16384]{1,0:T(1,128)} %param.9, f32[4,16384]{1,0:T(4,128)S(1)} %stack.4), dimensions={0} | concatenate | bytes 1048576 | tf_op jit(solution)/shard_map/stack | solution.py:56
  5.1 21.7 %shard_map.111 = (f32[768,256]{1,0:T(8,128)}, f32[768,128]{1,0:T(8,128)}) custom-call(s32[1,16384]{1,0:T(1,128)} %broadcast_subtract_fusion.ids_ref, f32[8,16384]{1,0:T(8,128)} %stack.10.split_ref, bf16[16384,256]{1,0:T(8,128)(2,1)} %bitcast.50), custom_call_target="tpu_custom_call" | custom-call | flops 9663676416 | bytes 10158080 | tf_op jit(solution)/shard_map/pallas_call | solution.py:59
  26.9 1.7 %add_reduce_fusion = f32[768]{0:T(1024)S(1)} fusion(f32[768,128]{1,0:T(8,128)} %get-tuple-element.7), kind=kLoop, calls=%fused_computation.40 | loop fusion | flops 1536 | bytes 12288 | tf_op jit(solution)/shard_map/add | solution.py:81
  28.6 5.1 %collective-permute-start.2 = (f32[1,256]{1,0:T(1,128)S(1)}, f32[1,256]{1,0:T(1,128)S(1)}, u32[]{:S(2)}, u32[]{:S(2)}) collective-permute-start(f32[1,256]{1,0:T(1,128)S(1)} %get-tuple-element.41), channel_id=1, source_target_pairs={{32,0},{64,32},{96,64},{128,96},{160,128},{192,160},{224,192},{33,... | collective-permute-start | bytes 3080 | tf_op jit(solution)/shard_map/ppermute | solution.py:11
  33.7 1.9 %collective-permute-start.3 = (f32[1,256]{1,0:T(1,128)S(1)}, f32[1,256]{1,0:T(1,128)S(1)}, u32[]{:S(2)}, u32[]{:S(2)}) collective-permute-start(f32[1,256]{1,0:T(1,128)S(1)} %get-tuple-element.42), channel_id=1, source_target_pairs={{0,32},{32,64},{64,96},{96,128},{128,160},{160,192},{192,224},{1,3... | collective-permute-start | bytes 3080 | tf_op jit(solution)/shard_map/ppermute | solution.py:11
  35.7 2.4 %collective-permute-start = (f32[1,256,256]{2,1,0:T(8,128)S(1)}, f32[1,256,256]{2,1,0:T(8,128)S(1)}, u32[]{:S(2)}, u32[]{:S(2)}) collective-permute-start(f32[1,256,256]{2,1,0:T(8,128)S(1)} %get-tuple-element.24), channel_id=1, source_target_pairs={{32,0},{64,32},{96,64},{128,96},{160,128},{192,160},{224,192},{33,... | collective-permute-start | bytes 786440 | tf_op jit(solution)/shard_map/ppermute | solution.py:11
  38.1 3.2 %collective-permute-start.1 = (f32[1,256,256]{2,1,0:T(8,128)S(1)}, f32[1,256,256]{2,1,0:T(8,128)S(1)}, u32[]{:S(2)}, u32[]{:S(2)}) collective-permute-start(f32[1,256,256]{2,1,0:T(8,128)S(1)} %get-tuple-element.25), channel_id=1, source_target_pairs={{0,32},{32,64},{64,96},{96,128},{128,160},{160,192},{192,224},{1,3... | collective-permute-start | bytes 786440 | tf_op jit(solution)/shard_map/ppermute | solution.py:11
  41.4 2.0 %collective-permute-done = f32[1,256,256]{2,1,0:T(8,128)S(1)} collective-permute-done((f32[1,256,256]{2,1,0:T(8,128)S(1)}, f32[1,256,256]{2,1,0:T(8,128)S(1)}, u32[]{:S(2)}, u32[]{:S(2)}) %collective-permute-start) | collective-permute-done | bytes 262176 | tf_op jit(solution)/shard_map/ppermute | solution.py:11
  43.4 1.2 collective-permute-done.1
  44.6 0.1 fusion.19
  44.7 4.4 %collective-permute-start.4 = (bf16[1,256,256]{2,1,0:T(8,128)(2,1)S(1)}, bf16[1,256,256]{2,1,0:T(8,128)(2,1)S(1)}, u32[]{:S(2)}, u32[]{:S(2)}) collective-permute-start(bf16[1,256,256]{2,1,0:T(8,128)(2,1)S(1)} %fusion.19), channel_id=1, source_target_pairs={{0,32},{32,64},{64,96},{96,128},{128,160},{160,192},{192,224},{1,3... | collective-permute-start | bytes 393224 | tf_op jit(solution)/shard_map/ppermute | solution.py:19
  49.1 1.9 %collective-permute-start.5 = (bf16[1,256,256]{2,1,0:T(8,128)(2,1)S(1)}, bf16[1,256,256]{2,1,0:T(8,128)(2,1)S(1)}, u32[]{:S(2)}, u32[]{:S(2)}) collective-permute-start(bf16[1,256,256]{2,1,0:T(8,128)(2,1)S(1)} %fusion.19), channel_id=1, source_target_pairs={{32,0},{64,32},{96,64},{128,96},{160,128},{192,160},{224,192},{33,... | collective-permute-start | bytes 393224 | tf_op jit(solution)/shard_map/ppermute | solution.py:22
  51.1 4.3 %collective-permute-done.5 = bf16[1,256,256]{2,1,0:T(8,128)(2,1)S(1)} collective-permute-done((bf16[1,256,256]{2,1,0:T(8,128)(2,1)S(1)}, bf16[1,256,256]{2,1,0:T(8,128)(2,1)S(1)}, u32[]{:S(2)}, u32[]{:S(2)}) %collective-permute-start.5) | collective-permute-done | bytes 131104 | tf_op jit(solution)/shard_map/ppermute | solution.py:22
  55.4 1.0 fusion.2
  56.4 0.3 fusion.29
  56.8 0.5 multiply_convert_fusion
  57.2 0.2 copy-done.6
  57.5 0.2 fusion.30
  57.7 0.6 fusion.1
  58.3 1.3 fusion.20
  59.6 1.3 fusion.31
  60.9 0.3 fusion.25
  61.2 0.1 reshape.567
  61.4 1.7 %pad_maximum_fusion = f32[512,1040]{1,0:T(8,128)S(1)} fusion(f32[512,16]{1,0:T(8,128)S(1)} %reshape.567, f32[256,1024]{1,0:T(8,128)} %fusion.31, f32[256,1024]{1,0:T(8,128)} %fusion.20), kind=kLoop, calls=%fused_computation | loop fusion | flops 1064960 | bytes 4259840 | tf_op jit(solution)/shard_map/concatenate | solution.py:174
  63.1 1.2 slice_select_fusion
  64.2 2.6 %copy.17 = f32[256,1040]{0,1:T(8,128)} copy(f32[256,1040]{1,0:T(8,128)} %slice_select_fusion) | data formatting | bytes 2129920 | tf_op jit(solution)/shard_map/jit(_where)/select_n | solution.py:116
  66.8 3.0 %collective-permute-done.6 = f32[256,1040]{0,1:T(8,128)} collective-permute-done((f32[256,1040]{0,1:T(8,128)}, f32[256,1040]{0,1:T(8,128)}, u32[]{:S(2)}, u32[]{:S(2)}) %collective-permute-start.6) | collective-permute-done | bytes 1064992 | tf_op jit(solution)/shard_map/ppermute | solution.py:116
  69.9 2.6 %copy.18 = f32[256,1040]{1,0:T(8,128)} copy(f32[256,1040]{0,1:T(8,128)} %collective-permute-done.6) | data formatting | bytes 2129920 | tf_op jit(solution)/shard_map/ppermute | solution.py:116
  72.5 1.4 select_add_fusion
  73.9 1.0 copy-done.1
  75.0 0.2 copy.19
  75.2 0.8 collective-permute-start.7
  76.0 7.7 %collective-permute-done.7 = f32[128,1040]{0,1:T(8,128)S(1)} collective-permute-done((f32[128,1040]{0,1:T(8,128)S(1)}, f32[128,1040]{0,1:T(8,128)S(1)}, u32[]{:S(2)}, u32[]{:S(2)}) %collective-permute-start.7) | collective-permute-done | bytes 532512 | tf_op jit(solution)/shard_map/ppermute | solution.py:116
  83.8 0.2 copy.20
  84.1 1.1 collective-permute-start.8
  85.2 4.8 %collective-permute-done.8 = f32[64,1040]{1,0:T(8,128)S(1)} collective-permute-done((f32[64,1040]{1,0:T(8,128)S(1)}, f32[64,1040]{1,0:T(8,128)S(1)}, u32[]{:S(2)}, u32[]{:S(2)}) %collective-permute-start.8) | collective-permute-done | bytes 266272 | tf_op jit(solution)/shard_map/ppermute | solution.py:116
  90.2 0.9 collective-permute-start.9
  91.0 3.2 %collective-permute-done.9 = f32[32,1040]{1,0:T(8,128)S(1)} collective-permute-done((f32[32,1040]{1,0:T(8,128)S(1)}, f32[32,1040]{1,0:T(8,128)S(1)}, u32[]{:S(2)}, u32[]{:S(2)}) %collective-permute-start.9) | collective-permute-done | bytes 133152 | tf_op jit(solution)/shard_map/ppermute | solution.py:116
  94.3 2.6 %collective-permute-start.10 = (f32[32,1040]{1,0:T(8,128)S(1)}, f32[32,1040]{1,0:T(8,128)S(1)}, u32[]{:S(2)}, u32[]{:S(2)}) collective-permute-start(f32[32,1040]{1,0:T(8,128)S(1)} %select_add_fusion.3), channel_id=1, source_target_pairs={{0,128},{1,129},{2,130},{3,131},{4,132},{5,133},{6,134},{7,135},{8... | collective-permute-start | bytes 399368 | tf_op jit(solution)/shard_map/ppermute | solution.py:119
  96.8 3.0 %collective-permute-done.10 = f32[32,1040]{1,0:T(8,128)S(1)} collective-permute-done((f32[32,1040]{1,0:T(8,128)S(1)}, f32[32,1040]{1,0:T(8,128)S(1)}, u32[]{:S(2)}, u32[]{:S(2)}) %collective-permute-start.10) | collective-permute-done | bytes 133152 | tf_op jit(solution)/shard_map/ppermute | solution.py:119
  99.9 2.7 %collective-permute-start.11 = (f32[32,1040]{1,0:T(8,128)S(1)}, f32[32,1040]{1,0:T(8,128)S(1)}, u32[]{:S(2)}, u32[]{:S(2)}) collective-permute-start(f32[32,1040]{1,0:T(8,128)S(1)} %add.273), channel_id=1, source_target_pairs={{0,16},{1,17},{2,18},{3,19},{4,20},{5,21},{6,22},{7,23},{8,24},{9,... | collective-permute-start | bytes 399368 | tf_op jit(solution)/shard_map/ppermute | solution.py:119
  102.5 4.1 %collective-permute-done.11 = f32[32,1040]{1,0:T(8,128)S(1)} collective-permute-done((f32[32,1040]{1,0:T(8,128)S(1)}, f32[32,1040]{1,0:T(8,128)S(1)}, u32[]{:S(2)}, u32[]{:S(2)}) %collective-permute-start.11) | collective-permute-done | bytes 133152 | tf_op jit(solution)/shard_map/ppermute | solution.py:119
  106.7 2.8 %collective-permute-start.12 = (f32[32,1040]{1,0:T(8,128)S(1)}, f32[32,1040]{1,0:T(8,128)S(1)}, u32[]{:S(2)}, u32[]{:S(2)}) collective-permute-start(f32[32,1040]{1,0:T(8,128)S(1)} %add.274), channel_id=1, source_target_pairs={{0,2},{1,3},{2,0},{3,1},{4,6},{5,7},{6,4},{7,5},{8,10},{9,11},{10,... | collective-permute-start | bytes 399368 | tf_op jit(solution)/shard_map/ppermute | solution.py:119
  109.5 2.8 %collective-permute-done.12 = f32[32,1040]{1,0:T(8,128)S(1)} collective-permute-done((f32[32,1040]{1,0:T(8,128)S(1)}, f32[32,1040]{1,0:T(8,128)S(1)}, u32[]{:S(2)}, u32[]{:S(2)}) %collective-permute-start.12) | collective-permute-done | bytes 133152 | tf_op jit(solution)/shard_map/ppermute | solution.py:119
  112.3 6.2 %collective-permute-start.13 = (f32[32,1040]{1,0:T(8,128)S(1)}, f32[32,1040]{1,0:T(8,128)S(1)}, u32[]{:S(2)}, u32[]{:S(2)}) collective-permute-start(f32[32,1040]{1,0:T(8,128)S(1)} %add.275), channel_id=1, source_target_pairs={{0,4},{1,5},{2,6},{3,7},{4,0},{5,1},{6,2},{7,3},{8,12},{9,13},{10,... | collective-permute-start | bytes 399368 | tf_op jit(solution)/shard_map/ppermute | solution.py:119
  118.4 3.9 %collective-permute-done.13 = f32[32,1040]{1,0:T(8,128)S(1)} collective-permute-done((f32[32,1040]{1,0:T(8,128)S(1)}, f32[32,1040]{1,0:T(8,128)S(1)}, u32[]{:S(2)}, u32[]{:S(2)}) %collective-permute-start.13) | collective-permute-done | bytes 133152 | tf_op jit(solution)/shard_map/ppermute | solution.py:119
  122.3 1.5 collective-permute-start.14
  123.8 2.8 %collective-permute-done.14 = f32[32,1040]{1,0:T(8,128)S(1)} collective-permute-done((f32[32,1040]{1,0:T(8,128)S(1)}, f32[32,1040]{1,0:T(8,128)S(1)}, u32[]{:S(2)}, u32[]{:S(2)}) %collective-permute-start.14) | collective-permute-done | bytes 133152 | tf_op jit(solution)/shard_map/ppermute | solution.py:122
  126.7 7.9 %collective-permute-done.15 = f32[64,1040]{1,0:T(8,128)S(1)} collective-permute-done((f32[64,1040]{1,0:T(8,128)S(1)}, f32[64,1040]{1,0:T(8,128)S(1)}, u32[]{:S(2)}, u32[]{:S(2)}) %collective-permute-start.15) | collective-permute-done | bytes 266272 | tf_op jit(solution)/shard_map/ppermute | solution.py:122
  134.7 0.2 copy.21
  134.9 1.4 collective-permute-start.16
  136.3 9.3 %collective-permute-done.16 = f32[128,1040]{0,1:T(8,128)S(1)} collective-permute-done((f32[128,1040]{0,1:T(8,128)S(1)}, f32[128,1040]{0,1:T(8,128)S(1)}, u32[]{:S(2)}, u32[]{:S(2)}) %collective-permute-start.16) | collective-permute-done | bytes 532512 | tf_op jit(solution)/shard_map/ppermute | solution.py:122
  145.6 0.2 copy.22
  146.0 1.3 copy.24
  147.3 11.0 %collective-permute-start.17 = (f32[256,1040]{0,1:T(8,128)}, f32[256,1040]{0,1:T(8,128)}, u32[]{:S(2)}, u32[]{:S(2)}) collective-permute-start(f32[256,1040]{0,1:T(8,128)} %copy.24), channel_id=1, source_target_pairs={{0,32},{1,33},{2,34},{3,35},{4,36},{5,37},{6,38},{7,39},{8,40},{9,... | collective-permute-start | bytes 3194888 | tf_op jit(solution)/shard_map/ppermute | solution.py:122
  158.3 2.7 %collective-permute-done.17 = f32[256,1040]{0,1:T(8,128)} collective-permute-done((f32[256,1040]{0,1:T(8,128)}, f32[256,1040]{0,1:T(8,128)}, u32[]{:S(2)}, u32[]{:S(2)}) %collective-permute-start.17) | collective-permute-done | bytes 1064992 | tf_op jit(solution)/shard_map/ppermute | solution.py:122
  161.0 1.6 copy.25
  162.6 0.2 broadcast_select_fusion
  162.8 1.1 slice.158
  163.9 1.1 slice.159
  165.0 0.1 reshape.568
  165.1 0.8 copy.27
  (45 shorter events, 0.9 us)
Async XLA Ops:
  0.6 56.1 %copy-start = (bf16[256,1024]{1,0:T(8,128)(2,1)S(1)}, bf16[256,1024]{1,0:T(8,128)(2,1)}, u32[]{:S(2)}) copy-start(bf16[256,1024]{1,0:T(8,128)(2,1)} %param.13) | copy-start | bytes 1572868
  26.9 8.8 %copy-start.3 = (f32[768,256]{1,0:T(8,128)S(1)}, f32[768,256]{1,0:T(8,128)}, u32[]{:S(2)}) copy-start(f32[768,256]{1,0:T(8,128)} %get-tuple-element.6) | copy-start | bytes 2359300
  26.9 14.4 %copy-start.7 = (s32[1,256,8]{1,2,0:T(8,128)S(1)}, s32[1,256,8]{1,2,0:T(8,128)}, u32[]{:S(2)}) copy-start(s32[1,256,8]{1,2,0:T(8,128)} %param.11) | copy-start | bytes 24580
  28.6 12.7 %collective-permute-start.2 = (f32[1,256]{1,0:T(1,128)S(1)}, f32[1,256]{1,0:T(1,128)S(1)}, u32[]{:S(2)}, u32[]{:S(2)}) collective-permute-start(f32[1,256]{1,0:T(1,128)S(1)} %get-tuple-element.41), channel_id=1, source_target_pairs={{32,0},{64,32},{96,64},{128,96},{160,128},{192,160},{224,192},{33,... | collective-permute-start | bytes 3080 | tf_op jit(solution)/shard_map/ppermute | solution.py:11
  33.7 7.6 %collective-permute-start.3 = (f32[1,256]{1,0:T(1,128)S(1)}, f32[1,256]{1,0:T(1,128)S(1)}, u32[]{:S(2)}, u32[]{:S(2)}) collective-permute-start(f32[1,256]{1,0:T(1,128)S(1)} %get-tuple-element.42), channel_id=1, source_target_pairs={{0,32},{32,64},{64,96},{96,128},{128,160},{160,192},{192,224},{1,3... | collective-permute-start | bytes 3080 | tf_op jit(solution)/shard_map/ppermute | solution.py:11
  35.7 7.7 %collective-permute-start = (f32[1,256,256]{2,1,0:T(8,128)S(1)}, f32[1,256,256]{2,1,0:T(8,128)S(1)}, u32[]{:S(2)}, u32[]{:S(2)}) collective-permute-start(f32[1,256,256]{2,1,0:T(8,128)S(1)} %get-tuple-element.24), channel_id=1, source_target_pairs={{32,0},{64,32},{96,64},{128,96},{160,128},{192,160},{224,192},{33,... | collective-permute-start | bytes 786440 | tf_op jit(solution)/shard_map/ppermute | solution.py:11
  38.1 6.5 %collective-permute-start.1 = (f32[1,256,256]{2,1,0:T(8,128)S(1)}, f32[1,256,256]{2,1,0:T(8,128)S(1)}, u32[]{:S(2)}, u32[]{:S(2)}) collective-permute-start(f32[1,256,256]{2,1,0:T(8,128)S(1)} %get-tuple-element.25), channel_id=1, source_target_pairs={{0,32},{32,64},{64,96},{96,128},{128,160},{160,192},{192,224},{1,3... | collective-permute-start | bytes 786440 | tf_op jit(solution)/shard_map/ppermute | solution.py:11
  44.7 6.3 %collective-permute-start.4 = (bf16[1,256,256]{2,1,0:T(8,128)(2,1)S(1)}, bf16[1,256,256]{2,1,0:T(8,128)(2,1)S(1)}, u32[]{:S(2)}, u32[]{:S(2)}) collective-permute-start(bf16[1,256,256]{2,1,0:T(8,128)(2,1)S(1)} %fusion.19), channel_id=1, source_target_pairs={{0,32},{32,64},{64,96},{96,128},{128,160},{160,192},{192,224},{1,3... | collective-permute-start | bytes 393224 | tf_op jit(solution)/shard_map/ppermute | solution.py:19
  49.1 6.3 %collective-permute-start.5 = (bf16[1,256,256]{2,1,0:T(8,128)(2,1)S(1)}, bf16[1,256,256]{2,1,0:T(8,128)(2,1)S(1)}, u32[]{:S(2)}, u32[]{:S(2)}) collective-permute-start(bf16[1,256,256]{2,1,0:T(8,128)(2,1)S(1)} %fusion.19), channel_id=1, source_target_pairs={{32,0},{64,32},{96,64},{128,96},{160,128},{192,160},{224,192},{33,... | collective-permute-start | bytes 393224 | tf_op jit(solution)/shard_map/ppermute | solution.py:22
  55.4 1.0 copy-start.4
  56.7 0.7 copy-start.6
  56.8 0.9 copy-start.8
  57.7 3.2 %copy-start.5 = (f32[256,8]{0,1:T(8,128)}, f32[256,8]{0,1:T(8,128)S(1)}, u32[]{:S(2)}) copy-start(f32[256,8]{0,1:T(8,128)S(1)} %fusion.30) | copy-start | bytes 24580
  66.8 3.0 %collective-permute-start.6 = (f32[256,1040]{0,1:T(8,128)}, f32[256,1040]{0,1:T(8,128)}, u32[]{:S(2)}, u32[]{:S(2)}) collective-permute-start(f32[256,1040]{0,1:T(8,128)} %copy.17), channel_id=1, source_target_pairs={{0,32},{1,33},{2,34},{3,35},{4,36},{5,37},{6,38},{7,39},{8,40},{9,... | collective-permute-start | bytes 3194888 | tf_op jit(solution)/shard_map/ppermute | solution.py:116
  73.9 1.0 copy-start.1
  75.0 8.9 %copy-start.2 = (f32[256,1040]{1,0:T(8,128)S(1)}, f32[256,1040]{1,0:T(8,128)}, u32[]{:S(2)}) copy-start(f32[256,1040]{1,0:T(8,128)} %copy-done.1) | copy-start | bytes 3194884
  75.2 8.5 %collective-permute-start.7 = (f32[128,1040]{0,1:T(8,128)S(1)}, f32[128,1040]{0,1:T(8,128)S(1)}, u32[]{:S(2)}, u32[]{:S(2)}) collective-permute-start(f32[128,1040]{0,1:T(8,128)S(1)} %copy.19), channel_id=1, source_target_pairs={{0,64},{1,65},{2,66},{3,67},{4,68},{5,69},{6,70},{7,71},{8,72},{9,... | collective-permute-start | bytes 1597448 | tf_op jit(solution)/shard_map/ppermute | solution.py:116
  84.1 6.0 %collective-permute-start.8 = (f32[64,1040]{1,0:T(8,128)S(1)}, f32[64,1040]{1,0:T(8,128)S(1)}, u32[]{:S(2)}, u32[]{:S(2)}) collective-permute-start(f32[64,1040]{1,0:T(8,128)S(1)} %slice_select_fusion.2), channel_id=1, source_target_pairs={{0,8},{1,9},{2,10},{3,11},{4,12},{5,13},{6,14},{7,15},{8,0},{9,1},... | collective-permute-start | bytes 798728 | tf_op jit(solution)/shard_map/ppermute | solution.py:116
  90.2 4.1 %collective-permute-start.9 = (f32[32,1040]{1,0:T(8,128)S(1)}, f32[32,1040]{1,0:T(8,128)S(1)}, u32[]{:S(2)}, u32[]{:S(2)}) collective-permute-start(f32[32,1040]{1,0:T(8,128)S(1)} %slice_select_fusion.3), channel_id=1, source_target_pairs={{0,1},{1,0},{2,3},{3,2},{4,5},{5,4},{6,7},{7,6},{8,9},{9,8},{10,11... | collective-permute-start | bytes 399368 | tf_op jit(solution)/shard_map/ppermute | solution.py:116
  94.3 5.6 %collective-permute-start.10 = (f32[32,1040]{1,0:T(8,128)S(1)}, f32[32,1040]{1,0:T(8,128)S(1)}, u32[]{:S(2)}, u32[]{:S(2)}) collective-permute-start(f32[32,1040]{1,0:T(8,128)S(1)} %select_add_fusion.3), channel_id=1, source_target_pairs={{0,128},{1,129},{2,130},{3,131},{4,132},{5,133},{6,134},{7,135},{8... | collective-permute-start | bytes 399368 | tf_op jit(solution)/shard_map/ppermute | solution.py:119
  99.9 6.8 %collective-permute-start.11 = (f32[32,1040]{1,0:T(8,128)S(1)}, f32[32,1040]{1,0:T(8,128)S(1)}, u32[]{:S(2)}, u32[]{:S(2)}) collective-permute-start(f32[32,1040]{1,0:T(8,128)S(1)} %add.273), channel_id=1, source_target_pairs={{0,16},{1,17},{2,18},{3,19},{4,20},{5,21},{6,22},{7,23},{8,24},{9,... | collective-permute-start | bytes 399368 | tf_op jit(solution)/shard_map/ppermute | solution.py:119
  106.7 5.6 %collective-permute-start.12 = (f32[32,1040]{1,0:T(8,128)S(1)}, f32[32,1040]{1,0:T(8,128)S(1)}, u32[]{:S(2)}, u32[]{:S(2)}) collective-permute-start(f32[32,1040]{1,0:T(8,128)S(1)} %add.274), channel_id=1, source_target_pairs={{0,2},{1,3},{2,0},{3,1},{4,6},{5,7},{6,4},{7,5},{8,10},{9,11},{10,... | collective-permute-start | bytes 399368 | tf_op jit(solution)/shard_map/ppermute | solution.py:119
  112.3 10.0 %collective-permute-start.13 = (f32[32,1040]{1,0:T(8,128)S(1)}, f32[32,1040]{1,0:T(8,128)S(1)}, u32[]{:S(2)}, u32[]{:S(2)}) collective-permute-start(f32[32,1040]{1,0:T(8,128)S(1)} %add.275), channel_id=1, source_target_pairs={{0,4},{1,5},{2,6},{3,7},{4,0},{5,1},{6,2},{7,3},{8,12},{9,13},{10,... | collective-permute-start | bytes 399368 | tf_op jit(solution)/shard_map/ppermute | solution.py:119
  122.3 4.3 %collective-permute-start.14 = (f32[32,1040]{1,0:T(8,128)S(1)}, f32[32,1040]{1,0:T(8,128)S(1)}, u32[]{:S(2)}, u32[]{:S(2)}) collective-permute-start(f32[32,1040]{1,0:T(8,128)S(1)} %add.276), channel_id=1, source_target_pairs={{0,1},{1,0},{2,3},{3,2},{4,5},{5,4},{6,7},{7,6},{8,9},{9,8},{10,11... | collective-permute-start | bytes 399368 | tf_op jit(solution)/shard_map/ppermute | solution.py:122
  126.6 8.0 %collective-permute-start.15 = (f32[64,1040]{1,0:T(8,128)S(1)}, f32[64,1040]{1,0:T(8,128)S(1)}, u32[]{:S(2)}, u32[]{:S(2)}) collective-permute-start(f32[64,1040]{1,0:T(8,128)S(1)} %pad_maximum_fusion.3), channel_id=1, source_target_pairs={{0,8},{1,9},{2,10},{3,11},{4,12},{5,13},{6,14},{7,15},{8,0},{9,1},... | collective-permute-start | bytes 798728 | tf_op jit(solution)/shard_map/ppermute | solution.py:122
  134.9 10.7 %collective-permute-start.16 = (f32[128,1040]{0,1:T(8,128)S(1)}, f32[128,1040]{0,1:T(8,128)S(1)}, u32[]{:S(2)}, u32[]{:S(2)}) collective-permute-start(f32[128,1040]{0,1:T(8,128)S(1)} %copy.21), channel_id=1, source_target_pairs={{0,64},{1,65},{2,66},{3,67},{4,68},{5,69},{6,70},{7,71},{8,72},{9,... | collective-permute-start | bytes 1597448 | tf_op jit(solution)/shard_map/ppermute | solution.py:122
  147.3 13.7 %collective-permute-start.17 = (f32[256,1040]{0,1:T(8,128)}, f32[256,1040]{0,1:T(8,128)}, u32[]{:S(2)}, u32[]{:S(2)}) collective-permute-start(f32[256,1040]{0,1:T(8,128)} %copy.24), channel_id=1, source_target_pairs={{0,32},{1,33},{2,34},{3,35},{4,36},{5,37},{6,38},{7,39},{8,40},{9,... | collective-permute-start | bytes 3194888 | tf_op jit(solution)/shard_map/ppermute | solution.py:122

commit v5 on v4

--- a/solution.py
+++ b/solution.py
@@ -106,24 +106,22 @@
     return jnp.where(core == 1, bit1, bit0) == 1
 
 
-def all_sum(value, sizes, halvings):
+def all_sum(value, sizes):
     axes = ("region", "dp")
     steps = halving_plan(sizes)
-    for perm, flip0, flip1 in steps[:halvings]:
+    for perm, flip0, flip1 in steps:
         upper = upper_half(flip0, flip1)
         half = value.shape[0] // 2
         low, high = value[:half], value[half:]
         got = lax.ppermute(jnp.where(upper, low, high), axes, perm)
         value = jnp.where(upper, high, low) + got
-    for perm, _, _ in steps[halvings:]:
-        value = value + lax.ppermute(value, axes, perm)
-    for perm, flip0, flip1 in reversed(steps[:halvings]):
+    for index, (perm, flip0, flip1) in enumerate(reversed(steps)):
         upper = upper_half(flip0, flip1)
         got = lax.ppermute(value, axes, perm)
-        value = jnp.concatenate(
-            [jnp.where(upper, got, value), jnp.where(upper, value, got)], axis=0
-        )
-    return value
+        pair = (jnp.where(upper, got, value), jnp.where(upper, value, got))
+        if index == len(steps) - 1:
+            return pair
+        value = jnp.concatenate(pair, axis=0)
 
 
 def local(cells, cell_weight, cell_cluster, cluster_edges, labels, w_self, w_nbr, w_out):
@@ -174,9 +172,9 @@
     packed = jnp.concatenate(
         [jnp.concatenate([grad_own, grad_side], axis=0), grad_head.reshape(rows, -1)], axis=1
     )
-    packed = all_sum(packed, sizes, 4)
-    grad_own, grad_side = packed[:feats, :hid], packed[feats:, :hid]
-    grad_head = packed[:, hid:].reshape(hid, -1)
+    first, second = all_sum(packed, sizes)
+    grad_own, grad_side = first[:, :hid], second[:, :hid]
+    grad_head = jnp.concatenate([first[:, hid:], second[:, hid:]], axis=0).reshape(hid, -1)
     return (scores, grad_own, grad_side, grad_head)
 
 

time: 167 us -> 178 us (1.066)
  starting transfers between devices: 49.8 us -> 68.6 us
  waiting for transfers between devices: 62.8 us -> 55.1 us
    ppermute x4 -> x8, starting transfers between devices: 14 us -> 32.5 us  [all_sum(): got = lax.ppermute(value, axes, perm)]
    ppermute x4 -> x8, starting transfers between devices: 2.75 us -> 17.1 us  [all_sum(): got = lax.ppermute(jnp.where(upper, low, high), axes, perm)]
    ppermute x4 -> x0, starting transfers between devices: 14.2 us -> none  [all_sum(): value = value + lax.ppermute(value, axes, perm)]
    ppermute x4 -> x0, waiting for transfers between devices: 13.8 us -> none  [all_sum(): value = value + lax.ppermute(value, axes, perm)]
    ppermute x4 -> x8, waiting for transfers between devices: 18.8 us -> 24.8 us  [all_sum(): got = lax.ppermute(jnp.where(upper, low, high), axes, perm)]
    ppermute x4 -> x8, waiting for transfers between devices: 22.6 us -> 22.7 us  [all_sum(): got = lax.ppermute(value, axes, perm)]
  transfers between devices with their start and end apart: 18 -> 22, of which waited for: 15 -> 19; matrix products, arithmetic and copies ran while one was open for 0% -> 0% of each run, Pallas kernels for 0% -> 0%
where the time goes in v5:
time: 178 us; the launch traced here: 177 us
  starting transfers between devices  68.6 us (39%)
  waiting for transfers between devices  55.1 us (31%)
  Pallas kernels  21.7 us (12%)
  local copies, waits for them, and re-layouts  15.7 us (9%)
  other arithmetic  9.77 us (5%)
  matrix products  5.45 us (3%)
    ppermute x8, starting transfers between devices, all_sum(): got = lax.ppermute(value, axes, perm)  32.5 us
    ppermute x8, waiting for transfers between devices, all_sum(): got = lax.ppermute(jnp.where(upper, low, high), axes, perm)  24.8 us
    ppermute x8, waiting for transfers between devices, all_sum(): got = lax.ppermute(value, axes, perm)  22.7 us
    pallas_call x1, Pallas kernels, accumulate(): pl.pallas_call(pooled_sums_kernel, grid=(length // block,), in_specs=[pl....  21.7 us
    ppermute x8, starting transfers between devices, all_sum(): got = lax.ppermute(jnp.where(upper, low, high), axes, perm)  17.1 us
    ppermute x4, starting transfers between devices, passed_along(): lax.ppermute(value, axis, [(source, source + steps) for source in range(i...  12.6 us
    ppermute x1, starting transfers between devices, padded(): lax.ppermute(lax.slice_in_dim(block, block.shape[dim] - width, None, axis...  4.39 us
    ppermute x1, waiting for transfers between devices, padded(): lax.ppermute(lax.slice_in_dim(block, 0, width, axis=dim), axis, backward)  4.33 us
  transfers between devices with their start and end apart: 22, of which 19 were waited for; matrix products, arithmetic and copies ran while one was open for 0% of the time, Pallas kernels for 0%

profile of v5, /device:TPU:1, one launch (start us, length us, event | category | flops | bytes accessed | tf_op | source)
XLA Modules:
  0.0 177.5 jit_solution(79420654193442999)
XLA Ops:
  0.6 1.0 reduce-precision_subtract_fusion
  1.7 1.5 broadcast_subtract_fusion.ids_ref
  3.2 1.9 %stack.10.split_ref = f32[8,16384]{1,0:T(8,128)} concatenate(f32[1,16384]{1,0:T(1,128)S(1)} %get-tuple-element.39, f32[1,16384]{1,0:T(1,128)S(1)} %get-tuple-element.40, f32[1,16384]{1,0:T(1,128)S(1)} %get-tuple-element.38, f32[1,16384]{1,0:T(1,128)} %param.9, f32[4,16384]{1,0:T(4,128)S(1)} %stack.4), dimensions={0} | concatenate | bytes 1048576 | tf_op jit(solution)/shard_map/stack | solution.py:56
  5.1 21.7 %shard_map.111 = (f32[768,256]{1,0:T(8,128)}, f32[768,128]{1,0:T(8,128)}) custom-call(s32[1,16384]{1,0:T(1,128)} %broadcast_subtract_fusion.ids_ref, f32[8,16384]{1,0:T(8,128)} %stack.10.split_ref, bf16[16384,256]{1,0:T(8,128)(2,1)} %bitcast.50), custom_call_target="tpu_custom_call" | custom-call | flops 9663676416 | bytes 10158080 | tf_op jit(solution)/shard_map/pallas_call | solution.py:59
  26.9 1.9 %add_reduce_fusion = f32[768]{0:T(1024)S(1)} fusion(f32[768,128]{1,0:T(8,128)} %get-tuple-element.7), kind=kLoop, calls=%fused_computation.40 | loop fusion | flops 1536 | bytes 12288 | tf_op jit(solution)/shard_map/add | solution.py:81
  28.8 5.1 %collective-permute-start.2 = (f32[1,256]{1,0:T(1,128)S(1)}, f32[1,256]{1,0:T(1,128)S(1)}, u32[]{:S(2)}, u32[]{:S(2)}) collective-permute-start(f32[1,256]{1,0:T(1,128)S(1)} %get-tuple-element.53), channel_id=1, source_target_pairs={{32,0},{64,32},{96,64},{128,96},{160,128},{192,160},{224,192},{33,... | collective-permute-start | bytes 3080 | tf_op jit(solution)/shard_map/ppermute | solution.py:11
  33.9 1.9 %collective-permute-start.3 = (f32[1,256]{1,0:T(1,128)S(1)}, f32[1,256]{1,0:T(1,128)S(1)}, u32[]{:S(2)}, u32[]{:S(2)}) collective-permute-start(f32[1,256]{1,0:T(1,128)S(1)} %get-tuple-element.54), channel_id=1, source_target_pairs={{0,32},{32,64},{64,96},{96,128},{128,160},{160,192},{192,224},{1,3... | collective-permute-start | bytes 3080 | tf_op jit(solution)/shard_map/ppermute | solution.py:11
  35.9 2.4 %collective-permute-start = (f32[1,256,256]{2,1,0:T(8,128)S(1)}, f32[1,256,256]{2,1,0:T(8,128)S(1)}, u32[]{:S(2)}, u32[]{:S(2)}) collective-permute-start(f32[1,256,256]{2,1,0:T(8,128)S(1)} %get-tuple-element.28), channel_id=1, source_target_pairs={{32,0},{64,32},{96,64},{128,96},{160,128},{192,160},{224,192},{33,... | collective-permute-start | bytes 786440 | tf_op jit(solution)/shard_map/ppermute | solution.py:11
  38.3 3.2 %collective-permute-start.1 = (f32[1,256,256]{2,1,0:T(8,128)S(1)}, f32[1,256,256]{2,1,0:T(8,128)S(1)}, u32[]{:S(2)}, u32[]{:S(2)}) collective-permute-start(f32[1,256,256]{2,1,0:T(8,128)S(1)} %get-tuple-element.29), channel_id=1, source_target_pairs={{0,32},{32,64},{64,96},{96,128},{128,160},{160,192},{192,224},{1,3... | collective-permute-start | bytes 786440 | tf_op jit(solution)/shard_map/ppermute | solution.py:11
  41.5 2.0 %collective-permute-done = f32[1,256,256]{2,1,0:T(8,128)S(1)} collective-permute-done((f32[1,256,256]{2,1,0:T(8,128)S(1)}, f32[1,256,256]{2,1,0:T(8,128)S(1)}, u32[]{:S(2)}, u32[]{:S(2)}) %collective-permute-start) | collective-permute-done | bytes 262176 | tf_op jit(solution)/shard_map/ppermute | solution.py:11
  43.6 1.2 collective-permute-done.1
  44.9 4.4 %collective-permute-start.4 = (bf16[1,256,256]{2,1,0:T(8,128)(2,1)S(1)}, bf16[1,256,256]{2,1,0:T(8,128)(2,1)S(1)}, u32[]{:S(2)}, u32[]{:S(2)}) collective-permute-start(bf16[1,256,256]{2,1,0:T(8,128)(2,1)S(1)} %fusion.19), channel_id=1, source_target_pairs={{0,32},{32,64},{64,96},{96,128},{128,160},{160,192},{192,224},{1,3... | collective-permute-start | bytes 393224 | tf_op jit(solution)/shard_map/ppermute | solution.py:19
  49.3 1.9 %collective-permute-start.5 = (bf16[1,256,256]{2,1,0:T(8,128)(2,1)S(1)}, bf16[1,256,256]{2,1,0:T(8,128)(2,1)S(1)}, u32[]{:S(2)}, u32[]{:S(2)}) collective-permute-start(bf16[1,256,256]{2,1,0:T(8,128)(2,1)S(1)} %fusion.19), channel_id=1, source_target_pairs={{32,0},{64,32},{96,64},{128,96},{160,128},{192,160},{224,192},{33,... | collective-permute-start | bytes 393224 | tf_op jit(solution)/shard_map/ppermute | solution.py:22
  51.2 4.3 %collective-permute-done.5 = bf16[1,256,256]{2,1,0:T(8,128)(2,1)S(1)} collective-permute-done((bf16[1,256,256]{2,1,0:T(8,128)(2,1)S(1)}, bf16[1,256,256]{2,1,0:T(8,128)(2,1)S(1)}, u32[]{:S(2)}, u32[]{:S(2)}) %collective-permute-start.5) | collective-permute-done | bytes 131104 | tf_op jit(solution)/shard_map/ppermute | solution.py:22
  55.6 1.0 fusion.2
  56.6 0.3 fusion.29
  56.9 0.5 multiply_convert_fusion
  57.6 0.2 fusion.30
  57.9 0.6 fusion.1
  58.4 1.3 fusion.20
  59.7 1.3 fusion.31
  61.0 0.3 fusion.25
  61.5 1.7 pad_maximum_fusion
  63.3 1.2 slice_select_fusion
  64.4 2.6 %copy.32 = f32[256,1040]{0,1:T(8,128)} copy(f32[256,1040]{1,0:T(8,128)} %slice_select_fusion) | data formatting | bytes 2129920 | tf_op jit(solution)/shard_map/jit(_where)/select_n | solution.py:116
  67.0 3.0 %collective-permute-done.6 = f32[256,1040]{0,1:T(8,128)} collective-permute-done((f32[256,1040]{0,1:T(8,128)}, f32[256,1040]{0,1:T(8,128)}, u32[]{:S(2)}, u32[]{:S(2)}) %collective-permute-start.6) | collective-permute-done | bytes 1064992 | tf_op jit(solution)/shard_map/ppermute | solution.py:116
  70.1 2.6 %copy.33 = f32[256,1040]{1,0:T(8,128)} copy(f32[256,1040]{0,1:T(8,128)} %collective-permute-done.6) | data formatting | bytes 2129920 | tf_op jit(solution)/shard_map/ppermute | solution.py:116
  72.7 1.4 select_add_fusion
  74.1 1.0 copy-done.1
  75.5 0.8 collective-permute-start.7
  76.2 7.7 %collective-permute-done.7 = f32[128,1040]{0,1:T(8,128)S(1)} collective-permute-done((f32[128,1040]{0,1:T(8,128)S(1)}, f32[128,1040]{0,1:T(8,128)S(1)}, u32[]{:S(2)}, u32[]{:S(2)}) %collective-permute-start.7) | collective-permute-done | bytes 532512 | tf_op jit(solution)/shard_map/ppermute | solution.py:116
  84.3 1.1 collective-permute-start.8
  85.5 4.8 %collective-permute-done.8 = f32[64,1040]{1,0:T(8,128)S(1)} collective-permute-done((f32[64,1040]{1,0:T(8,128)S(1)}, f32[64,1040]{1,0:T(8,128)S(1)}, u32[]{:S(2)}, u32[]{:S(2)}) %collective-permute-start.8) | collective-permute-done | bytes 266272 | tf_op jit(solution)/shard_map/ppermute | solution.py:116
  90.4 0.9 collective-permute-start.9
  91.2 3.2 %collective-permute-done.9 = f32[32,1040]{1,0:T(8,128)S(1)} collective-permute-done((f32[32,1040]{1,0:T(8,128)S(1)}, f32[32,1040]{1,0:T(8,128)S(1)}, u32[]{:S(2)}, u32[]{:S(2)}) %collective-permute-start.9) | collective-permute-done | bytes 133152 | tf_op jit(solution)/shard_map/ppermute | solution.py:116
  94.5 2.6 %collective-permute-start.10 = (f32[16,1040]{1,0:T(8,128)S(1)}, f32[16,1040]{1,0:T(8,128)S(1)}, u32[]{:S(2)}, u32[]{:S(2)}) collective-permute-start(f32[16,1040]{1,0:T(8,128)S(1)} %slice_select_fusion.4), channel_id=1, source_target_pairs={{0,128},{1,129},{2,130},{3,131},{4,132},{5,133},{6,134},{7,135},{8... | collective-permute-start | bytes 199688 | tf_op jit(solution)/shard_map/ppermute | solution.py:116
  97.1 2.2 %collective-permute-done.10 = f32[16,1040]{1,0:T(8,128)S(1)} collective-permute-done((f32[16,1040]{1,0:T(8,128)S(1)}, f32[16,1040]{1,0:T(8,128)S(1)}, u32[]{:S(2)}, u32[]{:S(2)}) %collective-permute-start.10) | collective-permute-done | bytes 66592 | tf_op jit(solution)/shard_map/ppermute | solution.py:116
  99.3 2.6 %collective-permute-start.11 = (f32[8,1040]{1,0:T(8,128)S(1)}, f32[8,1040]{1,0:T(8,128)S(1)}, u32[]{:S(2)}, u32[]{:S(2)}) collective-permute-start(f32[8,1040]{1,0:T(8,128)S(1)} %slice_select_fusion.5), channel_id=1, source_target_pairs={{0,16},{1,17},{2,18},{3,19},{4,20},{5,21},{6,22},{7,23},{8,24},{9,... | collective-permute-start | bytes 99848 | tf_op jit(solution)/shard_map/ppermute | solution.py:116
  102.0 1.3 collective-permute-done.11
  103.3 2.8 %collective-permute-start.12 = (f32[4,1040]{1,0:T(4,128)S(1)}, f32[4,1040]{1,0:T(4,128)S(1)}, u32[]{:S(2)}, u32[]{:S(2)}) collective-permute-start(f32[4,1040]{1,0:T(4,128)S(1)} %slice_select_fusion.6), channel_id=1, source_target_pairs={{0,2},{1,3},{2,0},{3,1},{4,6},{5,7},{6,4},{7,5},{8,10},{9,11},{10,... | collective-permute-start | bytes 49928 | tf_op jit(solution)/shard_map/ppermute | solution.py:116
  106.1 1.4 collective-permute-done.12
  107.6 6.4 %collective-permute-start.13 = (f32[2,1040]{1,0:T(2,128)S(1)}, f32[2,1040]{1,0:T(2,128)S(1)}, u32[]{:S(2)}, u32[]{:S(2)}) collective-permute-start(f32[2,1040]{1,0:T(2,128)S(1)} %broadcast_select_fusion.14), channel_id=1, source_target_pairs={{0,4},{1,5},{2,6},{3,7},{4,0},{5,1},{6,2},{7,3},{8,12},{9,13},{10,... | collective-permute-start | bytes 24968 | tf_op jit(solution)/shard_map/ppermute | solution.py:116
  113.9 1.1 collective-permute-done.13
  115.0 5.5 %collective-permute-start.14 = (f32[2,1040]{1,0:T(2,128)S(1)}, f32[2,1040]{1,0:T(2,128)S(1)}, u32[]{:S(2)}, u32[]{:S(2)}) collective-permute-start(f32[2,1040]{1,0:T(2,128)S(1)} %select_add_fusion.7), channel_id=1, source_target_pairs={{0,4},{1,5},{2,6},{3,7},{4,0},{5,1},{6,2},{7,3},{8,12},{9,13},{10,... | collective-permute-start | bytes 24968 | tf_op jit(solution)/shard_map/ppermute | solution.py:120
  120.5 1.1 collective-permute-done.14
  121.5 2.8 %collective-permute-start.15 = (f32[4,1040]{1,0:T(4,128)S(1)}, f32[4,1040]{1,0:T(4,128)S(1)}, u32[]{:S(2)}, u32[]{:S(2)}) collective-permute-start(f32[4,1040]{1,0:T(4,128)S(1)} %pad_maximum_fusion.8), channel_id=1, source_target_pairs={{0,2},{1,3},{2,0},{3,1},{4,6},{5,7},{6,4},{7,5},{8,10},{9,11},{10,... | collective-permute-start | bytes 49928 | tf_op jit(solution)/shard_map/ppermute | solution.py:120
  124.3 1.4 collective-permute-done.15
  125.8 1.7 collective-permute-start.16
  127.5 2.1 %collective-permute-done.16 = f32[8,1040]{1,0:T(8,128)S(1)} collective-permute-done((f32[8,1040]{1,0:T(8,128)S(1)}, f32[8,1040]{1,0:T(8,128)S(1)}, u32[]{:S(2)}, u32[]{:S(2)}) %collective-permute-start.16) | collective-permute-done | bytes 33312 | tf_op jit(solution)/shard_map/ppermute | solution.py:120
  129.6 3.0 %collective-permute-start.17 = (f32[16,1040]{1,0:T(8,128)S(1)}, f32[16,1040]{1,0:T(8,128)S(1)}, u32[]{:S(2)}, u32[]{:S(2)}) collective-permute-start(f32[16,1040]{1,0:T(8,128)S(1)} %pad_maximum_fusion.6), channel_id=1, source_target_pairs={{0,128},{1,129},{2,130},{3,131},{4,132},{5,133},{6,134},{7,135},{8... | collective-permute-start | bytes 199688 | tf_op jit(solution)/shard_map/ppermute | solution.py:120
  132.6 1.8 %collective-permute-done.17 = f32[16,1040]{1,0:T(8,128)S(1)} collective-permute-done((f32[16,1040]{1,0:T(8,128)S(1)}, f32[16,1040]{1,0:T(8,128)S(1)}, u32[]{:S(2)}, u32[]{:S(2)}) %collective-permute-start.17) | collective-permute-done | bytes 66592 | tf_op jit(solution)/shard_map/ppermute | solution.py:120
  134.5 1.3 collective-permute-start.18
  135.8 2.8 %collective-permute-done.18 = f32[32,1040]{1,0:T(8,128)S(1)} collective-permute-done((f32[32,1040]{1,0:T(8,128)S(1)}, f32[32,1040]{1,0:T(8,128)S(1)}, u32[]{:S(2)}, u32[]{:S(2)}) %collective-permute-start.18) | collective-permute-done | bytes 133152 | tf_op jit(solution)/shard_map/ppermute | solution.py:120
  138.6 1.5 collective-permute-start.19
  140.1 4.1 %collective-permute-done.19 = f32[64,1040]{1,0:T(8,128)S(1)} collective-permute-done((f32[64,1040]{1,0:T(8,128)S(1)}, f32[64,1040]{1,0:T(8,128)S(1)}, u32[]{:S(2)}, u32[]{:S(2)}) %collective-permute-start.19) | collective-permute-done | bytes 266272 | tf_op jit(solution)/shard_map/ppermute | solution.py:120
  144.6 1.4 collective-permute-start.20
  145.9 6.8 %collective-permute-done.20 = f32[128,1040]{0,1:T(8,128)S(1)} collective-permute-done((f32[128,1040]{0,1:T(8,128)S(1)}, f32[128,1040]{0,1:T(8,128)S(1)}, u32[]{:S(2)}, u32[]{:S(2)}) %collective-permute-start.20) | collective-permute-done | bytes 532512 | tf_op jit(solution)/shard_map/ppermute | solution.py:120
  153.2 1.3 copy.39
  154.5 15.4 %collective-permute-start.21 = (f32[256,1040]{0,1:T(8,128)}, f32[256,1040]{0,1:T(8,128)}, u32[]{:S(2)}, u32[]{:S(2)}) collective-permute-start(f32[256,1040]{0,1:T(8,128)} %copy.39), channel_id=1, source_target_pairs={{0,32},{1,33},{2,34},{3,35},{4,36},{5,37},{6,38},{7,39},{8,40},{9,... | collective-permute-start | bytes 3194888 | tf_op jit(solution)/shard_map/ppermute | solution.py:120
  169.9 2.7 %collective-permute-done.21 = f32[256,1040]{0,1:T(8,128)} collective-permute-done((f32[256,1040]{0,1:T(8,128)}, f32[256,1040]{0,1:T(8,128)}, u32[]{:S(2)}, u32[]{:S(2)}) %collective-permute-start.21) | collective-permute-done | bytes 1064992 | tf_op jit(solution)/shard_map/ppermute | solution.py:120
  172.5 1.6 copy.40
  174.3 1.1 slice.202
  175.4 1.1 slice.203
  176.7 0.8 copy.42
  (67 shorter events, 2.6 us)
Async XLA Ops:
  0.6 56.3 %copy-start = (bf16[256,1024]{1,0:T(8,128)(2,1)S(1)}, bf16[256,1024]{1,0:T(8,128)(2,1)}, u32[]{:S(2)}) copy-start(bf16[256,1024]{1,0:T(8,128)(2,1)} %param.13) | copy-start | bytes 1572868
  26.9 9.0 %copy-start.3 = (f32[768,256]{1,0:T(8,128)S(1)}, f32[768,256]{1,0:T(8,128)}, u32[]{:S(2)}) copy-start(f32[768,256]{1,0:T(8,128)} %get-tuple-element.6) | copy-start | bytes 2359300
  26.9 14.6 %copy-start.7 = (s32[1,256,8]{1,2,0:T(8,128)S(1)}, s32[1,256,8]{1,2,0:T(8,128)}, u32[]{:S(2)}) copy-start(s32[1,256,8]{1,2,0:T(8,128)} %param.11) | copy-start | bytes 24580
  28.8 12.7 %collective-permute-start.2 = (f32[1,256]{1,0:T(1,128)S(1)}, f32[1,256]{1,0:T(1,128)S(1)}, u32[]{:S(2)}, u32[]{:S(2)}) collective-permute-start(f32[1,256]{1,0:T(1,128)S(1)} %get-tuple-element.53), channel_id=1, source_target_pairs={{32,0},{64,32},{96,64},{128,96},{160,128},{192,160},{224,192},{33,... | collective-permute-start | bytes 3080 | tf_op jit(solution)/shard_map/ppermute | solution.py:11
  33.9 7.6 %collective-permute-start.3 = (f32[1,256]{1,0:T(1,128)S(1)}, f32[1,256]{1,0:T(1,128)S(1)}, u32[]{:S(2)}, u32[]{:S(2)}) collective-permute-start(f32[1,256]{1,0:T(1,128)S(1)} %get-tuple-element.54), channel_id=1, source_target_pairs={{0,32},{32,64},{64,96},{96,128},{128,160},{160,192},{192,224},{1,3... | collective-permute-start | bytes 3080 | tf_op jit(solution)/shard_map/ppermute | solution.py:11
  35.9 7.7 %collective-permute-start = (f32[1,256,256]{2,1,0:T(8,128)S(1)}, f32[1,256,256]{2,1,0:T(8,128)S(1)}, u32[]{:S(2)}, u32[]{:S(2)}) collective-permute-start(f32[1,256,256]{2,1,0:T(8,128)S(1)} %get-tuple-element.28), channel_id=1, source_target_pairs={{32,0},{64,32},{96,64},{128,96},{160,128},{192,160},{224,192},{33,... | collective-permute-start | bytes 786440 | tf_op jit(solution)/shard_map/ppermute | solution.py:11
  38.3 6.5 %collective-permute-start.1 = (f32[1,256,256]{2,1,0:T(8,128)S(1)}, f32[1,256,256]{2,1,0:T(8,128)S(1)}, u32[]{:S(2)}, u32[]{:S(2)}) collective-permute-start(f32[1,256,256]{2,1,0:T(8,128)S(1)} %get-tuple-element.29), channel_id=1, source_target_pairs={{0,32},{32,64},{64,96},{96,128},{128,160},{160,192},{192,224},{1,3... | collective-permute-start | bytes 786440 | tf_op jit(solution)/shard_map/ppermute | solution.py:11
  44.9 6.3 %collective-permute-start.4 = (bf16[1,256,256]{2,1,0:T(8,128)(2,1)S(1)}, bf16[1,256,256]{2,1,0:T(8,128)(2,1)S(1)}, u32[]{:S(2)}, u32[]{:S(2)}) collective-permute-start(bf16[1,256,256]{2,1,0:T(8,128)(2,1)S(1)} %fusion.19), channel_id=1, source_target_pairs={{0,32},{32,64},{64,96},{96,128},{128,160},{160,192},{192,224},{1,3... | collective-permute-start | bytes 393224 | tf_op jit(solution)/shard_map/ppermute | solution.py:19
  49.3 6.3 %collective-permute-start.5 = (bf16[1,256,256]{2,1,0:T(8,128)(2,1)S(1)}, bf16[1,256,256]{2,1,0:T(8,128)(2,1)S(1)}, u32[]{:S(2)}, u32[]{:S(2)}) collective-permute-start(bf16[1,256,256]{2,1,0:T(8,128)(2,1)S(1)} %fusion.19), channel_id=1, source_target_pairs={{32,0},{64,32},{96,64},{128,96},{160,128},{192,160},{224,192},{33,... | collective-permute-start | bytes 393224 | tf_op jit(solution)/shard_map/ppermute | solution.py:22
  55.6 1.0 copy-start.4
  56.9 0.7 copy-start.6
  56.9 0.9 copy-start.8
  57.9 3.2 %copy-start.5 = (f32[256,8]{0,1:T(8,128)}, f32[256,8]{0,1:T(8,128)S(1)}, u32[]{:S(2)}) copy-start(f32[256,8]{0,1:T(8,128)S(1)} %fusion.30) | copy-start | bytes 24580
  67.0 3.0 %collective-permute-start.6 = (f32[256,1040]{0,1:T(8,128)}, f32[256,1040]{0,1:T(8,128)}, u32[]{:S(2)}, u32[]{:S(2)}) collective-permute-start(f32[256,1040]{0,1:T(8,128)} %copy.32), channel_id=1, source_target_pairs={{0,32},{1,33},{2,34},{3,35},{4,36},{5,37},{6,38},{7,39},{8,40},{9,... | collective-permute-start | bytes 3194888 | tf_op jit(solution)/shard_map/ppermute | solution.py:116
  74.1 1.0 copy-start.1
  75.2 8.9 %copy-start.2 = (f32[256,1040]{1,0:T(8,128)S(1)}, f32[256,1040]{1,0:T(8,128)}, u32[]{:S(2)}) copy-start(f32[256,1040]{1,0:T(8,128)} %copy-done.1) | copy-start | bytes 3194884
  75.5 8.5 %collective-permute-start.7 = (f32[128,1040]{0,1:T(8,128)S(1)}, f32[128,1040]{0,1:T(8,128)S(1)}, u32[]{:S(2)}, u32[]{:S(2)}) collective-permute-start(f32[128,1040]{0,1:T(8,128)S(1)} %copy.34), channel_id=1, source_target_pairs={{0,64},{1,65},{2,66},{3,67},{4,68},{5,69},{6,70},{7,71},{8,72},{9,... | collective-permute-start | bytes 1597448 | tf_op jit(solution)/shard_map/ppermute | solution.py:116
  84.3 6.0 %collective-permute-start.8 = (f32[64,1040]{1,0:T(8,128)S(1)}, f32[64,1040]{1,0:T(8,128)S(1)}, u32[]{:S(2)}, u32[]{:S(2)}) collective-permute-start(f32[64,1040]{1,0:T(8,128)S(1)} %slice_select_fusion.2), channel_id=1, source_target_pairs={{0,8},{1,9},{2,10},{3,11},{4,12},{5,13},{6,14},{7,15},{8,0},{9,1},... | collective-permute-start | bytes 798728 | tf_op jit(solution)/shard_map/ppermute | solution.py:116
  90.4 4.1 %collective-permute-start.9 = (f32[32,1040]{1,0:T(8,128)S(1)}, f32[32,1040]{1,0:T(8,128)S(1)}, u32[]{:S(2)}, u32[]{:S(2)}) collective-permute-start(f32[32,1040]{1,0:T(8,128)S(1)} %slice_select_fusion.3), channel_id=1, source_target_pairs={{0,1},{1,0},{2,3},{3,2},{4,5},{5,4},{6,7},{7,6},{8,9},{9,8},{10,11... | collective-permute-start | bytes 399368 | tf_op jit(solution)/shard_map/ppermute | solution.py:116
  94.5 4.8 %collective-permute-start.10 = (f32[16,1040]{1,0:T(8,128)S(1)}, f32[16,1040]{1,0:T(8,128)S(1)}, u32[]{:S(2)}, u32[]{:S(2)}) collective-permute-start(f32[16,1040]{1,0:T(8,128)S(1)} %slice_select_fusion.4), channel_id=1, source_target_pairs={{0,128},{1,129},{2,130},{3,131},{4,132},{5,133},{6,134},{7,135},{8... | collective-permute-start | bytes 199688 | tf_op jit(solution)/shard_map/ppermute | solution.py:116
  99.3 4.0 %collective-permute-start.11 = (f32[8,1040]{1,0:T(8,128)S(1)}, f32[8,1040]{1,0:T(8,128)S(1)}, u32[]{:S(2)}, u32[]{:S(2)}) collective-permute-start(f32[8,1040]{1,0:T(8,128)S(1)} %slice_select_fusion.5), channel_id=1, source_target_pairs={{0,16},{1,17},{2,18},{3,19},{4,20},{5,21},{6,22},{7,23},{8,24},{9,... | collective-permute-start | bytes 99848 | tf_op jit(solution)/shard_map/ppermute | solution.py:116
  103.3 4.2 %collective-permute-start.12 = (f32[4,1040]{1,0:T(4,128)S(1)}, f32[4,1040]{1,0:T(4,128)S(1)}, u32[]{:S(2)}, u32[]{:S(2)}) collective-permute-start(f32[4,1040]{1,0:T(4,128)S(1)} %slice_select_fusion.6), channel_id=1, source_target_pairs={{0,2},{1,3},{2,0},{3,1},{4,6},{5,7},{6,4},{7,5},{8,10},{9,11},{10,... | collective-permute-start | bytes 49928 | tf_op jit(solution)/shard_map/ppermute | solution.py:116
  107.6 7.4 %collective-permute-start.13 = (f32[2,1040]{1,0:T(2,128)S(1)}, f32[2,1040]{1,0:T(2,128)S(1)}, u32[]{:S(2)}, u32[]{:S(2)}) collective-permute-start(f32[2,1040]{1,0:T(2,128)S(1)} %broadcast_select_fusion.14), channel_id=1, source_target_pairs={{0,4},{1,5},{2,6},{3,7},{4,0},{5,1},{6,2},{7,3},{8,12},{9,13},{10,... | collective-permute-start | bytes 24968 | tf_op jit(solution)/shard_map/ppermute | solution.py:116
  115.0 6.5 %collective-permute-start.14 = (f32[2,1040]{1,0:T(2,128)S(1)}, f32[2,1040]{1,0:T(2,128)S(1)}, u32[]{:S(2)}, u32[]{:S(2)}) collective-permute-start(f32[2,1040]{1,0:T(2,128)S(1)} %select_add_fusion.7), channel_id=1, source_target_pairs={{0,4},{1,5},{2,6},{3,7},{4,0},{5,1},{6,2},{7,3},{8,12},{9,13},{10,... | collective-permute-start | bytes 24968 | tf_op jit(solution)/shard_map/ppermute | solution.py:120
  121.5 4.2 %collective-permute-start.15 = (f32[4,1040]{1,0:T(4,128)S(1)}, f32[4,1040]{1,0:T(4,128)S(1)}, u32[]{:S(2)}, u32[]{:S(2)}) collective-permute-start(f32[4,1040]{1,0:T(4,128)S(1)} %pad_maximum_fusion.8), channel_id=1, source_target_pairs={{0,2},{1,3},{2,0},{3,1},{4,6},{5,7},{6,4},{7,5},{8,10},{9,11},{10,... | collective-permute-start | bytes 49928 | tf_op jit(solution)/shard_map/ppermute | solution.py:120
  125.8 3.8 %collective-permute-start.16 = (f32[8,1040]{1,0:T(8,128)S(1)}, f32[8,1040]{1,0:T(8,128)S(1)}, u32[]{:S(2)}, u32[]{:S(2)}) collective-permute-start(f32[8,1040]{1,0:T(8,128)S(1)} %pad_maximum_fusion.7), channel_id=1, source_target_pairs={{0,16},{1,17},{2,18},{3,19},{4,20},{5,21},{6,22},{7,23},{8,24},{9,... | collective-permute-start | bytes 99848 | tf_op jit(solution)/shard_map/ppermute | solution.py:120
  129.6 4.8 %collective-permute-start.17 = (f32[16,1040]{1,0:T(8,128)S(1)}, f32[16,1040]{1,0:T(8,128)S(1)}, u32[]{:S(2)}, u32[]{:S(2)}) collective-permute-start(f32[16,1040]{1,0:T(8,128)S(1)} %pad_maximum_fusion.6), channel_id=1, source_target_pairs={{0,128},{1,129},{2,130},{3,131},{4,132},{5,133},{6,134},{7,135},{8... | collective-permute-start | bytes 199688 | tf_op jit(solution)/shard_map/ppermute | solution.py:120
  134.5 4.1 %collective-permute-start.18 = (f32[32,1040]{1,0:T(8,128)S(1)}, f32[32,1040]{1,0:T(8,128)S(1)}, u32[]{:S(2)}, u32[]{:S(2)}) collective-permute-start(f32[32,1040]{1,0:T(8,128)S(1)} %pad_maximum_fusion.5), channel_id=1, source_target_pairs={{0,1},{1,0},{2,3},{3,2},{4,5},{5,4},{6,7},{7,6},{8,9},{9,8},{10,11... | collective-permute-start | bytes 399368 | tf_op jit(solution)/shard_map/ppermute | solution.py:120
  138.6 5.7 %collective-permute-start.19 = (f32[64,1040]{1,0:T(8,128)S(1)}, f32[64,1040]{1,0:T(8,128)S(1)}, u32[]{:S(2)}, u32[]{:S(2)}) collective-permute-start(f32[64,1040]{1,0:T(8,128)S(1)} %pad_maximum_fusion.3), channel_id=1, source_target_pairs={{0,8},{1,9},{2,10},{3,11},{4,12},{5,13},{6,14},{7,15},{8,0},{9,1},... | collective-permute-start | bytes 798728 | tf_op jit(solution)/shard_map/ppermute | solution.py:120
  144.6 8.2 %collective-permute-start.20 = (f32[128,1040]{0,1:T(8,128)S(1)}, f32[128,1040]{0,1:T(8,128)S(1)}, u32[]{:S(2)}, u32[]{:S(2)}) collective-permute-start(f32[128,1040]{0,1:T(8,128)S(1)} %copy.36), channel_id=1, source_target_pairs={{0,64},{1,65},{2,66},{3,67},{4,68},{5,69},{6,70},{7,71},{8,72},{9,... | collective-permute-start | bytes 1597448 | tf_op jit(solution)/shard_map/ppermute | solution.py:120
  154.5 18.0 %collective-permute-start.21 = (f32[256,1040]{0,1:T(8,128)}, f32[256,1040]{0,1:T(8,128)}, u32[]{:S(2)}, u32[]{:S(2)}) collective-permute-start(f32[256,1040]{0,1:T(8,128)} %copy.39), channel_id=1, source_target_pairs={{0,32},{1,33},{2,34},{3,35},{4,36},{5,37},{6,38},{7,39},{8,40},{9,... | collective-permute-start | bytes 3194888 | tf_op jit(solution)/shard_map/ppermute | solution.py:120

commit v6 on v5

--- a/solution.py
+++ b/solution.py
@@ -83,40 +83,36 @@
 
 
 def halving_plan(sizes):
-    core = [("region", 1)]
-    first = [("region", 2), ("dp", 8), ("dp", 1), ("region", 4), ("dp", 16), ("dp", 2), ("dp", 4)]
-    second = [("dp", 8), ("dp", 1), ("region", 2), ("dp", 16), ("dp", 2), ("region", 4), ("dp", 4)]
     width = sizes["dp"]
     steps = []
-    for flip0, flip1 in zip(core + first, core + second):
+    bit = 1
+    while bit < sizes["region"]:
         perm = []
         for device in range(sizes["region"] * width):
-            at = {"region": device // width, "dp": device % width}
-            axis, bit = flip1 if at["region"] & 1 else flip0
-            at[axis] ^= bit
-            perm.append((device, at["region"] * width + at["dp"]))
-        steps.append((perm, flip0, flip1))
+            region, dp = divmod(device, width)
+            perm.append((device, (region ^ bit) * width + dp))
+        steps.append((perm, bit))
+        bit *= 2
     return steps
-
-
-def upper_half(flip0, flip1):
-    core = lax.axis_index("region") % 2
-    bit0 = (lax.axis_index(flip0[0]) // flip0[1]) % 2
-    bit1 = (lax.axis_index(flip1[0]) // flip1[1]) % 2
-    return jnp.where(core == 1, bit1, bit0) == 1
 
 
 def all_sum(value, sizes):
     axes = ("region", "dp")
     steps = halving_plan(sizes)
-    for perm, flip0, flip1 in steps:
-        upper = upper_half(flip0, flip1)
+    for perm, bit in steps:
+        upper = (lax.axis_index("region") // bit) % 2 == 1
         half = value.shape[0] // 2
         low, high = value[:half], value[half:]
         got = lax.ppermute(jnp.where(upper, low, high), axes, perm)
         value = jnp.where(upper, high, low) + got
-    for index, (perm, flip0, flip1) in enumerate(reversed(steps)):
-        upper = upper_half(flip0, flip1)
+    count = sizes["dp"]
+    pieces = value.reshape((count, value.shape[0] // count) + value.shape[1:])
+    value = lax.all_to_all(pieces, "dp", 0, 0, tiled=False).sum(axis=0)
+    copies = jnp.broadcast_to(value[None], (count,) + value.shape)
+    value = lax.all_to_all(copies, "dp", 0, 0, tiled=False)
+    value = value.reshape((count * value.shape[1],) + value.shape[2:])
+    for index, (perm, bit) in enumerate(reversed(steps)):
+        upper = (lax.axis_index("region") // bit) % 2 == 1
         got = lax.ppermute(value, axes, perm)
         pair = (jnp.where(upper, got, value), jnp.where(upper, value, got))
         if index == len(steps) - 1:

time: 178 us -> 170 us (0.955)
  blocking collectives: 0 us -> 35.7 us
  starting transfers between devices: 68.6 us -> 33.1 us
  waiting for transfers between devices: 55.1 us -> 46.6 us
    all_to_all x0 -> x2, blocking collectives: none -> 35.7 us  [the longest x1 20.2 us: all_sum(): value = lax.all_to_all(pieces, 'dp', 0, 0, tiled=False).sum(axis=0)]
    ppermute x8 -> x3, starting transfers between devices: 32.5 us -> 11.3 us  [all_sum(): got = lax.ppermute(value, axes, perm)]
    ppermute x8 -> x3, starting transfers between devices: 17.1 us -> 2.87 us  [all_sum(): got = lax.ppermute(jnp.where(upper, low, high), axes, perm)]
    ppermute x8 -> x3, waiting for transfers between devices: 22.7 us -> 16.1 us  [all_sum(): got = lax.ppermute(value, axes, perm)]
    ppermute x8 -> x3, waiting for transfers between devices: 24.8 us -> 22.9 us  [all_sum(): got = lax.ppermute(jnp.where(upper, low, high), axes, perm)]
  transfers between devices with their start and end apart: 22 -> 12, of which waited for: 19 -> 9; matrix products, arithmetic and copies ran while one was open for 0% -> 0% of each run, Pallas kernels for 0% -> 0%
where the time goes in v6:
time: 170 us; the launch traced here: 169 us
  waiting for transfers between devices  46.6 us (27%)
  blocking collectives  35.7 us (21%)
  starting transfers between devices  33.1 us (19%)
  Pallas kernels  21.7 us (13%)
  local copies, waits for them, and re-layouts  16.1 us (9%)
  other arithmetic  9.44 us (6%)
  matrix products  5.47 us (3%)
    ppermute x3, waiting for transfers between devices, all_sum(): got = lax.ppermute(jnp.where(upper, low, high), axes, perm)  22.9 us
    pallas_call x1, Pallas kernels, accumulate(): pl.pallas_call(pooled_sums_kernel, grid=(length // block,), in_specs=[pl....  21.7 us
    all_to_all x1, blocking collectives, all_sum(): value = lax.all_to_all(pieces, 'dp', 0, 0, tiled=False).sum(axis=0)  20.2 us
    ppermute x3, waiting for transfers between devices, all_sum(): got = lax.ppermute(value, axes, perm)  16.1 us
    all_to_all x1, blocking collectives, all_sum(): value = lax.all_to_all(copies, 'dp', 0, 0, tiled=False)  15.4 us
    ppermute x4, starting transfers between devices, passed_along(): lax.ppermute(value, axis, [(source, source + steps) for source in range(i...  12.6 us
    ppermute x3, starting transfers between devices, all_sum(): got = lax.ppermute(value, axes, perm)  11.3 us
    ppermute x1, starting transfers between devices, padded(): lax.ppermute(lax.slice_in_dim(block, block.shape[dim] - width, None, axis...  4.39 us
  transfers between devices with their start and end apart: 12, of which 9 were waited for; matrix products, arithmetic and copies ran while one was open for 0% of the time, Pallas kernels for 0%

profile of v6, /device:TPU:1, one launch (start us, length us, event | category | flops | bytes accessed | tf_op | source)
XLA Modules:
  0.0 169.2 jit_solution(15388030915199557842)
XLA Ops:
  0.6 1.0 reduce-precision_subtract_fusion
  1.7 1.5 broadcast_subtract_fusion.ids_ref
  3.2 1.9 %stack.10.split_ref = f32[8,16384]{1,0:T(8,128)} concatenate(f32[1,16384]{1,0:T(1,128)S(1)} %get-tuple-element.33, f32[1,16384]{1,0:T(1,128)S(1)} %get-tuple-element.34, f32[1,16384]{1,0:T(1,128)S(1)} %get-tuple-element.32, f32[1,16384]{1,0:T(1,128)} %param.9, f32[4,16384]{1,0:T(4,128)S(1)} %stack.4), dimensions={0} | concatenate | bytes 1048576 | tf_op jit(solution)/shard_map/stack | solution.py:56
  5.1 21.7 %shard_map.111 = (f32[768,256]{1,0:T(8,128)}, f32[768,128]{1,0:T(8,128)}) custom-call(s32[1,16384]{1,0:T(1,128)} %broadcast_subtract_fusion.ids_ref, f32[8,16384]{1,0:T(8,128)} %stack.10.split_ref, bf16[16384,256]{1,0:T(8,128)(2,1)} %bitcast.50), custom_call_target="tpu_custom_call" | custom-call | flops 9663676416 | bytes 10158080 | tf_op jit(solution)/shard_map/pallas_call | solution.py:59
  26.9 1.7 %add_reduce_fusion = f32[768]{0:T(1024)S(1)} fusion(f32[768,128]{1,0:T(8,128)} %get-tuple-element.7), kind=kLoop, calls=%fused_computation.40 | loop fusion | flops 1536 | bytes 12288 | tf_op jit(solution)/shard_map/add | solution.py:81
  28.6 5.1 %collective-permute-start.2 = (f32[1,256]{1,0:T(1,128)S(1)}, f32[1,256]{1,0:T(1,128)S(1)}, u32[]{:S(2)}, u32[]{:S(2)}) collective-permute-start(f32[1,256]{1,0:T(1,128)S(1)} %get-tuple-element.43), channel_id=1, source_target_pairs={{32,0},{64,32},{96,64},{128,96},{160,128},{192,160},{224,192},{33,... | collective-permute-start | bytes 3080 | tf_op jit(solution)/shard_map/ppermute | solution.py:11
  33.8 1.9 %collective-permute-start.3 = (f32[1,256]{1,0:T(1,128)S(1)}, f32[1,256]{1,0:T(1,128)S(1)}, u32[]{:S(2)}, u32[]{:S(2)}) collective-permute-start(f32[1,256]{1,0:T(1,128)S(1)} %get-tuple-element.44), channel_id=1, source_target_pairs={{0,32},{32,64},{64,96},{96,128},{128,160},{160,192},{192,224},{1,3... | collective-permute-start | bytes 3080 | tf_op jit(solution)/shard_map/ppermute | solution.py:11
  35.7 2.4 %collective-permute-start = (f32[1,256,256]{2,1,0:T(8,128)S(1)}, f32[1,256,256]{2,1,0:T(8,128)S(1)}, u32[]{:S(2)}, u32[]{:S(2)}) collective-permute-start(f32[1,256,256]{2,1,0:T(8,128)S(1)} %get-tuple-element.28), channel_id=1, source_target_pairs={{32,0},{64,32},{96,64},{128,96},{160,128},{192,160},{224,192},{33,... | collective-permute-start | bytes 786440 | tf_op jit(solution)/shard_map/ppermute | solution.py:11
  38.1 3.2 %collective-permute-start.1 = (f32[1,256,256]{2,1,0:T(8,128)S(1)}, f32[1,256,256]{2,1,0:T(8,128)S(1)}, u32[]{:S(2)}, u32[]{:S(2)}) collective-permute-start(f32[1,256,256]{2,1,0:T(8,128)S(1)} %get-tuple-element.29), channel_id=1, source_target_pairs={{0,32},{32,64},{64,96},{96,128},{128,160},{160,192},{192,224},{1,3... | collective-permute-start | bytes 786440 | tf_op jit(solution)/shard_map/ppermute | solution.py:11
  41.4 2.0 %collective-permute-done = f32[1,256,256]{2,1,0:T(8,128)S(1)} collective-permute-done((f32[1,256,256]{2,1,0:T(8,128)S(1)}, f32[1,256,256]{2,1,0:T(8,128)S(1)}, u32[]{:S(2)}, u32[]{:S(2)}) %collective-permute-start) | collective-permute-done | bytes 262176 | tf_op jit(solution)/shard_map/ppermute | solution.py:11
  43.4 1.2 collective-permute-done.1
  44.6 0.1 fusion.19
  44.7 4.4 %collective-permute-start.4 = (bf16[1,256,256]{2,1,0:T(8,128)(2,1)S(1)}, bf16[1,256,256]{2,1,0:T(8,128)(2,1)S(1)}, u32[]{:S(2)}, u32[]{:S(2)}) collective-permute-start(bf16[1,256,256]{2,1,0:T(8,128)(2,1)S(1)} %fusion.19), channel_id=1, source_target_pairs={{0,32},{32,64},{64,96},{96,128},{128,160},{160,192},{192,224},{1,3... | collective-permute-start | bytes 393224 | tf_op jit(solution)/shard_map/ppermute | solution.py:19
  49.1 1.9 %collective-permute-start.5 = (bf16[1,256,256]{2,1,0:T(8,128)(2,1)S(1)}, bf16[1,256,256]{2,1,0:T(8,128)(2,1)S(1)}, u32[]{:S(2)}, u32[]{:S(2)}) collective-permute-start(bf16[1,256,256]{2,1,0:T(8,128)(2,1)S(1)} %fusion.19), channel_id=1, source_target_pairs={{32,0},{64,32},{96,64},{128,96},{160,128},{192,160},{224,192},{33,... | collective-permute-start | bytes 393224 | tf_op jit(solution)/shard_map/ppermute | solution.py:22
  51.1 4.3 %collective-permute-done.5 = bf16[1,256,256]{2,1,0:T(8,128)(2,1)S(1)} collective-permute-done((bf16[1,256,256]{2,1,0:T(8,128)(2,1)S(1)}, bf16[1,256,256]{2,1,0:T(8,128)(2,1)S(1)}, u32[]{:S(2)}, u32[]{:S(2)}) %collective-permute-start.5) | collective-permute-done | bytes 131104 | tf_op jit(solution)/shard_map/ppermute | solution.py:22
  55.4 1.0 fusion.2
  56.4 0.1 copy-done.4
  56.5 0.3 fusion.29
  56.8 0.5 multiply_convert_fusion
  57.3 0.2 copy-done.6
  57.5 0.2 fusion.30
  57.7 0.6 fusion.1
  58.3 1.3 fusion.20
  59.6 1.3 fusion.31
  60.9 0.3 fusion.25
  61.2 0.1 reshape.574
  61.4 1.7 %pad_maximum_fusion = f32[512,1040]{1,0:T(8,128)S(1)} fusion(f32[512,16]{1,0:T(8,128)S(1)} %reshape.574, f32[256,1024]{1,0:T(8,128)} %fusion.31, f32[256,1024]{1,0:T(8,128)} %fusion.20), kind=kLoop, calls=%fused_computation | loop fusion | flops 1064960 | bytes 4259840 | tf_op jit(solution)/shard_map/concatenate | solution.py:168
  63.1 1.2 slice_select_fusion
  64.3 2.6 %copy.32 = f32[256,1040]{0,1:T(8,128)} copy(f32[256,1040]{1,0:T(8,128)} %slice_select_fusion) | data formatting | bytes 2129920 | tf_op jit(solution)/shard_map/jit(_where)/select_n | solution.py:106
  66.9 3.0 %collective-permute-done.6 = f32[256,1040]{0,1:T(8,128)} collective-permute-done((f32[256,1040]{0,1:T(8,128)}, f32[256,1040]{0,1:T(8,128)}, u32[]{:S(2)}, u32[]{:S(2)}) %collective-permute-start.6) | collective-permute-done | bytes 1064992 | tf_op jit(solution)/shard_map/ppermute | solution.py:106
  69.9 2.6 %copy.33 = f32[256,1040]{1,0:T(8,128)} copy(f32[256,1040]{0,1:T(8,128)} %collective-permute-done.6) | data formatting | bytes 2129920 | tf_op jit(solution)/shard_map/ppermute | solution.py:106
  72.5 1.4 select_add_fusion
  74.0 1.0 copy-done.1
  75.0 0.1 slice_select_fusion.1
  75.1 0.2 copy.34
  75.3 0.7 collective-permute-start.7
  75.9 12.9 %collective-permute-done.7 = f32[128,1040]{0,1:T(8,128)S(1)} collective-permute-done((f32[128,1040]{0,1:T(8,128)S(1)}, f32[128,1040]{0,1:T(8,128)S(1)}, u32[]{:S(2)}, u32[]{:S(2)}) %collective-permute-start.7) | collective-permute-done | bytes 532512 | tf_op jit(solution)/shard_map/ppermute | solution.py:106
  88.9 0.2 copy.35
  89.1 0.1 select_add_fusion.1
  89.2 2.2 %collective-permute-start.8 = (f32[64,1040]{1,0:T(8,128)S(1)}, f32[64,1040]{1,0:T(8,128)S(1)}, u32[]{:S(2)}, u32[]{:S(2)}) collective-permute-start(f32[64,1040]{1,0:T(8,128)S(1)} %slice_select_fusion.2), channel_id=1, source_target_pairs={{0,128},{1,129},{2,130},{3,131},{4,132},{5,133},{6,134},{7,135},{8... | collective-permute-start | bytes 798728 | tf_op jit(solution)/shard_map/ppermute | solution.py:106
  91.4 7.0 %collective-permute-done.8 = f32[64,1040]{1,0:T(8,128)S(1)} collective-permute-done((f32[64,1040]{1,0:T(8,128)S(1)}, f32[64,1040]{1,0:T(8,128)S(1)}, u32[]{:S(2)}, u32[]{:S(2)}) %collective-permute-start.8) | collective-permute-done | bytes 266272 | tf_op jit(solution)/shard_map/ppermute | solution.py:106
  98.5 0.2 reshape.575
  98.6 20.2 %all_to_all.10 = f32[32,2,1040]{2,1,0:T(2,128)S(1)} all-to-all(f32[32,2,1040]{2,1,0:T(2,128)S(1)} %reshape.575), channel_id=1, replica_groups=mesh['region'=8,'dp'=32] {'dp'}, dimensions={0} | all-to-all | bytes 532480 | tf_op jit(solution)/shard_map/all_to_all | solution.py:110
  118.9 0.1 reduce_sum.9
  119.0 0.1 broadcast_in_dim.5
  119.1 15.4 %all_to_all.11 = f32[32,2,1040]{2,1,0:T(2,128)S(1)} all-to-all(f32[32,2,1040]{2,1,0:T(2,128)S(1)} %broadcast_in_dim.5), channel_id=1, replica_groups=mesh['region'=8,'dp'=32] {'dp'}, dimensions={0} | all-to-all | bytes 532480 | tf_op jit(solution)/shard_map/all_to_all | solution.py:112
  134.5 0.2 reshape.576
  134.7 2.8 %collective-permute-start.9 = (f32[64,1040]{1,0:T(8,128)S(1)}, f32[64,1040]{1,0:T(8,128)S(1)}, u32[]{:S(2)}, u32[]{:S(2)}) collective-permute-start(f32[64,1040]{1,0:T(8,128)S(1)} %reshape.576), channel_id=1, source_target_pairs={{0,128},{1,129},{2,130},{3,131},{4,132},{5,133},{6,134},{7,135},{8... | collective-permute-start | bytes 798728 | tf_op jit(solution)/shard_map/ppermute | solution.py:116
  137.5 4.4 %collective-permute-done.9 = f32[64,1040]{1,0:T(8,128)S(1)} collective-permute-done((f32[64,1040]{1,0:T(8,128)S(1)}, f32[64,1040]{1,0:T(8,128)S(1)}, u32[]{:S(2)}, u32[]{:S(2)}) %collective-permute-start.9) | collective-permute-done | bytes 266272 | tf_op jit(solution)/shard_map/ppermute | solution.py:116
  142.0 0.2 copy.36
  142.2 1.3 collective-permute-start.10
  143.5 9.1 %collective-permute-done.10 = f32[128,1040]{0,1:T(8,128)S(1)} collective-permute-done((f32[128,1040]{0,1:T(8,128)S(1)}, f32[128,1040]{0,1:T(8,128)S(1)}, u32[]{:S(2)}, u32[]{:S(2)}) %collective-permute-start.10) | collective-permute-done | bytes 532512 | tf_op jit(solution)/shard_map/ppermute | solution.py:116
  152.6 0.2 copy.37
  152.8 0.1 broadcast_select_fusion.3
  152.9 0.1 pad_maximum_fusion.1
  153.0 1.4 copy.39
  154.3 7.2 %collective-permute-start.11 = (f32[256,1040]{0,1:T(8,128)}, f32[256,1040]{0,1:T(8,128)}, u32[]{:S(2)}, u32[]{:S(2)}) collective-permute-start(f32[256,1040]{0,1:T(8,128)} %copy.39), channel_id=1, source_target_pairs={{0,32},{1,33},{2,34},{3,35},{4,36},{5,37},{6,38},{7,39},{8,40},{9,... | collective-permute-start | bytes 3194888 | tf_op jit(solution)/shard_map/ppermute | solution.py:116
  161.6 2.7 %collective-permute-done.11 = f32[256,1040]{0,1:T(8,128)} collective-permute-done((f32[256,1040]{0,1:T(8,128)}, f32[256,1040]{0,1:T(8,128)}, u32[]{:S(2)}, u32[]{:S(2)}) %collective-permute-start.11) | collective-permute-done | bytes 1064992 | tf_op jit(solution)/shard_map/ppermute | solution.py:116
  164.2 1.6 copy.40
  165.8 0.2 broadcast_select_fusion
  166.0 1.1 slice.152
  167.1 1.1 slice.153
  168.2 0.1 reshape.577
  168.4 0.8 copy.42
  (33 shorter events, 0.4 us)
Async XLA Ops:
  0.6 56.1 %copy-start = (bf16[256,1024]{1,0:T(8,128)(2,1)S(1)}, bf16[256,1024]{1,0:T(8,128)(2,1)}, u32[]{:S(2)}) copy-start(bf16[256,1024]{1,0:T(8,128)(2,1)} %param.13) | copy-start | bytes 1572868
  26.9 8.8 %copy-start.3 = (f32[768,256]{1,0:T(8,128)S(1)}, f32[768,256]{1,0:T(8,128)}, u32[]{:S(2)}) copy-start(f32[768,256]{1,0:T(8,128)} %get-tuple-element.6) | copy-start | bytes 2359300
  26.9 14.4 %copy-start.7 = (s32[1,256,8]{1,2,0:T(8,128)S(1)}, s32[1,256,8]{1,2,0:T(8,128)}, u32[]{:S(2)}) copy-start(s32[1,256,8]{1,2,0:T(8,128)} %param.11) | copy-start | bytes 24580
  28.6 12.7 %collective-permute-start.2 = (f32[1,256]{1,0:T(1,128)S(1)}, f32[1,256]{1,0:T(1,128)S(1)}, u32[]{:S(2)}, u32[]{:S(2)}) collective-permute-start(f32[1,256]{1,0:T(1,128)S(1)} %get-tuple-element.43), channel_id=1, source_target_pairs={{32,0},{64,32},{96,64},{128,96},{160,128},{192,160},{224,192},{33,... | collective-permute-start | bytes 3080 | tf_op jit(solution)/shard_map/ppermute | solution.py:11
  33.8 7.6 %collective-permute-start.3 = (f32[1,256]{1,0:T(1,128)S(1)}, f32[1,256]{1,0:T(1,128)S(1)}, u32[]{:S(2)}, u32[]{:S(2)}) collective-permute-start(f32[1,256]{1,0:T(1,128)S(1)} %get-tuple-element.44), channel_id=1, source_target_pairs={{0,32},{32,64},{64,96},{96,128},{128,160},{160,192},{192,224},{1,3... | collective-permute-start | bytes 3080 | tf_op jit(solution)/shard_map/ppermute | solution.py:11
  35.7 7.7 %collective-permute-start = (f32[1,256,256]{2,1,0:T(8,128)S(1)}, f32[1,256,256]{2,1,0:T(8,128)S(1)}, u32[]{:S(2)}, u32[]{:S(2)}) collective-permute-start(f32[1,256,256]{2,1,0:T(8,128)S(1)} %get-tuple-element.28), channel_id=1, source_target_pairs={{32,0},{64,32},{96,64},{128,96},{160,128},{192,160},{224,192},{33,... | collective-permute-start | bytes 786440 | tf_op jit(solution)/shard_map/ppermute | solution.py:11
  38.1 6.5 %collective-permute-start.1 = (f32[1,256,256]{2,1,0:T(8,128)S(1)}, f32[1,256,256]{2,1,0:T(8,128)S(1)}, u32[]{:S(2)}, u32[]{:S(2)}) collective-permute-start(f32[1,256,256]{2,1,0:T(8,128)S(1)} %get-tuple-element.29), channel_id=1, source_target_pairs={{0,32},{32,64},{64,96},{96,128},{128,160},{160,192},{192,224},{1,3... | collective-permute-start | bytes 786440 | tf_op jit(solution)/shard_map/ppermute | solution.py:11
  44.7 6.3 %collective-permute-start.4 = (bf16[1,256,256]{2,1,0:T(8,128)(2,1)S(1)}, bf16[1,256,256]{2,1,0:T(8,128)(2,1)S(1)}, u32[]{:S(2)}, u32[]{:S(2)}) collective-permute-start(bf16[1,256,256]{2,1,0:T(8,128)(2,1)S(1)} %fusion.19), channel_id=1, source_target_pairs={{0,32},{32,64},{64,96},{96,128},{128,160},{160,192},{192,224},{1,3... | collective-permute-start | bytes 393224 | tf_op jit(solution)/shard_map/ppermute | solution.py:19
  49.1 6.3 %collective-permute-start.5 = (bf16[1,256,256]{2,1,0:T(8,128)(2,1)S(1)}, bf16[1,256,256]{2,1,0:T(8,128)(2,1)S(1)}, u32[]{:S(2)}, u32[]{:S(2)}) collective-permute-start(bf16[1,256,256]{2,1,0:T(8,128)(2,1)S(1)} %fusion.19), channel_id=1, source_target_pairs={{32,0},{64,32},{96,64},{128,96},{160,128},{192,160},{224,192},{33,... | collective-permute-start | bytes 393224 | tf_op jit(solution)/shard_map/ppermute | solution.py:22
  55.4 1.0 copy-start.4
  56.8 0.7 copy-start.6
  56.8 0.9 copy-start.8
  57.7 3.2 %copy-start.5 = (f32[256,8]{0,1:T(8,128)}, f32[256,8]{0,1:T(8,128)S(1)}, u32[]{:S(2)}) copy-start(f32[256,8]{0,1:T(8,128)S(1)} %fusion.30) | copy-start | bytes 24580
  66.9 3.0 %collective-permute-start.6 = (f32[256,1040]{0,1:T(8,128)}, f32[256,1040]{0,1:T(8,128)}, u32[]{:S(2)}, u32[]{:S(2)}) collective-permute-start(f32[256,1040]{0,1:T(8,128)} %copy.32), channel_id=1, source_target_pairs={{0,32},{1,33},{2,34},{3,35},{4,36},{5,37},{6,38},{7,39},{8,40},{9,... | collective-permute-start | bytes 3194888 | tf_op jit(solution)/shard_map/ppermute | solution.py:106
  74.0 1.0 copy-start.1
  75.0 14.1 %copy-start.2 = (f32[256,1040]{1,0:T(8,128)S(1)}, f32[256,1040]{1,0:T(8,128)}, u32[]{:S(2)}) copy-start(f32[256,1040]{1,0:T(8,128)} %copy-done.1) | copy-start | bytes 3194884
  75.3 13.6 %collective-permute-start.7 = (f32[128,1040]{0,1:T(8,128)S(1)}, f32[128,1040]{0,1:T(8,128)S(1)}, u32[]{:S(2)}, u32[]{:S(2)}) collective-permute-start(f32[128,1040]{0,1:T(8,128)S(1)} %copy.34), channel_id=1, source_target_pairs={{0,64},{1,65},{2,66},{3,67},{4,68},{5,69},{6,70},{7,71},{8,72},{9,... | collective-permute-start | bytes 1597448 | tf_op jit(solution)/shard_map/ppermute | solution.py:106
  89.2 9.2 %collective-permute-start.8 = (f32[64,1040]{1,0:T(8,128)S(1)}, f32[64,1040]{1,0:T(8,128)S(1)}, u32[]{:S(2)}, u32[]{:S(2)}) collective-permute-start(f32[64,1040]{1,0:T(8,128)S(1)} %slice_select_fusion.2), channel_id=1, source_target_pairs={{0,128},{1,129},{2,130},{3,131},{4,132},{5,133},{6,134},{7,135},{8... | collective-permute-start | bytes 798728 | tf_op jit(solution)/shard_map/ppermute | solution.py:106
  134.7 7.2 %collective-permute-start.9 = (f32[64,1040]{1,0:T(8,128)S(1)}, f32[64,1040]{1,0:T(8,128)S(1)}, u32[]{:S(2)}, u32[]{:S(2)}) collective-permute-start(f32[64,1040]{1,0:T(8,128)S(1)} %reshape.576), channel_id=1, source_target_pairs={{0,128},{1,129},{2,130},{3,131},{4,132},{5,133},{6,134},{7,135},{8... | collective-permute-start | bytes 798728 | tf_op jit(solution)/shard_map/ppermute | solution.py:116
  142.2 10.4 %collective-permute-start.10 = (f32[128,1040]{0,1:T(8,128)S(1)}, f32[128,1040]{0,1:T(8,128)S(1)}, u32[]{:S(2)}, u32[]{:S(2)}) collective-permute-start(f32[128,1040]{0,1:T(8,128)S(1)} %copy.36), channel_id=1, source_target_pairs={{0,64},{1,65},{2,66},{3,67},{4,68},{5,69},{6,70},{7,71},{8,72},{9,... | collective-permute-start | bytes 1597448 | tf_op jit(solution)/shard_map/ppermute | solution.py:116
  154.3 9.9 %collective-permute-start.11 = (f32[256,1040]{0,1:T(8,128)}, f32[256,1040]{0,1:T(8,128)}, u32[]{:S(2)}, u32[]{:S(2)}) collective-permute-start(f32[256,1040]{0,1:T(8,128)} %copy.39), channel_id=1, source_target_pairs={{0,32},{1,33},{2,34},{3,35},{4,36},{5,37},{6,38},{7,39},{8,40},{9,... | collective-permute-start | bytes 3194888 | tf_op jit(solution)/shard_map/ppermute | solution.py:116

commit v7 on v4

--- a/solution.py
+++ b/solution.py
@@ -24,15 +24,15 @@
     return block
 
 
-def pooled_sums_kernel(ids_ref, split_ref, cells_ref, numer_ref, denom_ref):
+def pooled_sums_kernel(ids_ref, split_ref, cells_ref, sums_ref):
     @pl.when(pl.program_id(0) == 0)
     def _():
-        numer_ref[...] = jnp.zeros_like(numer_ref)
-        denom_ref[...] = jnp.zeros_like(denom_ref)
+        sums_ref[...] = jnp.zeros_like(sums_ref)
 
-    width = numer_ref.shape[0]
+    width = sums_ref.shape[0]
     block = ids_ref.shape[1]
-    lanes = denom_ref.shape[1]
+    feats = cells_ref.shape[1]
+    lanes = sums_ref.shape[1] - feats
     slots = lax.broadcasted_iota(jnp.int32, (width, block), 0)
     member = (ids_ref[...] == slots).astype(jnp.bfloat16)
     split = split_ref[...]
@@ -42,8 +42,8 @@
     parts = jnp.where(lane < 3, columns, 0.0).astype(jnp.bfloat16)
     weight = columns[:, 3:4]
     weighted = (weight * cells_ref[...].astype(jnp.float32)).astype(jnp.bfloat16)
-    numer_ref[...] += jnp.dot(member, weighted, preferred_element_type=jnp.float32)
-    denom_ref[...] += jnp.dot(member, parts, preferred_element_type=jnp.float32)
+    sums_ref[:, :feats] += jnp.dot(member, weighted, preferred_element_type=jnp.float32)
+    sums_ref[:, feats:] += jnp.dot(member, parts, preferred_element_type=jnp.float32)
 
 
 def accumulate(cluster_ids, cells, weights, width):
@@ -56,7 +56,7 @@
     split = jnp.stack([high, middle, low, weights, zero, zero, zero, zero], axis=0)
     block = min(1024, length)
     lanes = 128
-    numer, denom = pl.pallas_call(
+    sums = pl.pallas_call(
         pooled_sums_kernel,
         grid=(length // block,),
         in_specs=[
@@ -64,22 +64,15 @@
             pl.BlockSpec((8, block), lambda i: (0, i)),
             pl.BlockSpec((block, feats), lambda i: (i, 0)),
         ],
-        out_specs=[
-            pl.BlockSpec((width, feats), lambda i: (0, 0)),
-            pl.BlockSpec((width, lanes), lambda i: (0, 0)),
-        ],
-        out_shape=[
-            jax.ShapeDtypeStruct((width, feats), jnp.float32),
-            jax.ShapeDtypeStruct((width, lanes), jnp.float32),
-        ],
+        out_specs=pl.BlockSpec((width, feats + lanes), lambda i: (0, 0)),
+        out_shape=jax.ShapeDtypeStruct((width, feats + lanes), jnp.float32),
         cost_estimate=pl.CostEstimate(
             flops=2 * width * length * (feats + lanes),
             bytes_accessed=length * (feats * 2 + 36) + width * (feats + lanes) * 4,
             transcendentals=0,
         ),
     )(cluster_ids.reshape(1, length), split, cells)
-    total = denom[:, 0] + denom[:, 1] + denom[:, 2]
-    return numer[None], total[None]
+    return sums
 
 
 def halving_plan(sizes):
@@ -131,15 +124,13 @@
     owned = cluster_edges.shape[1]
     degree = cluster_edges.shape[2]
     relative = cell_cluster - (region - 1) * owned
-    numer_three, denom_three = accumulate(relative[0], cells[0], cell_weight[0], 3 * owned)
-    above_numer, above_denom = passed_along(
-        (numer_three[:, :owned], denom_three[:, :owned]), "region", -1
-    )
-    below_numer, below_denom = passed_along(
-        (numer_three[:, 2 * owned :], denom_three[:, 2 * owned :]), "region", 1
-    )
-    numer = numer_three[:, owned : 2 * owned] + above_numer + below_numer
-    denom = denom_three[:, owned : 2 * owned] + above_denom + below_denom
+    sums = accumulate(relative[0], cells[0], cell_weight[0], 3 * owned)
+    above = passed_along(sums[:owned], "region", -1)
+    below = passed_along(sums[2 * owned :], "region", 1)
+    total = (sums[owned : 2 * owned] + above + below)[None]
+    feats = cells.shape[2]
+    numer = total[..., :feats]
+    denom = total[..., feats] + total[..., feats + 1] + total[..., feats + 2]
     pooled = (numer / denom[..., None]).astype(jnp.bfloat16)
     table = padded(pooled, (("region", 1),), owned)
     targets = cluster_edges - (region - 1) * owned

time: 167 us -> 163 us (0.976)
  starting transfers between devices: 49.8 us -> 44.3 us
    ppermute x4 -> x2, starting transfers between devices: 12.6 us -> 7.03 us  [passed_along(): lax.ppermute(value, axis, [(source, source + steps) for source in range(i...]
    ppermute x4 -> x2, waiting for transfers between devices: 3.23 us -> 4.64 us  [passed_along(): lax.ppermute(value, axis, [(source, source + steps) for source in range(i...]
  transfers between devices with their start and end apart: 18 -> 16, of which waited for: 15 -> 15; matrix products, arithmetic and copies ran while one was open for 0% -> 0% of each run, Pallas kernels for 0% -> 0%
where the time goes in v7:
time: 163 us; the launch traced here: 162 us
  waiting for transfers between devices  63.8 us (39%)
  starting transfers between devices  44.3 us (27%)
  Pallas kernels  21.9 us (13%)
  local copies, waits for them, and re-layouts  16.7 us (10%)
  other arithmetic  9.02 us (6%)
  matrix products  5.46 us (3%)
    ppermute x4, waiting for transfers between devices, all_sum(): got = lax.ppermute(value, axes, perm)  22.6 us
    pallas_call x1, Pallas kernels, accumulate(): pl.pallas_call(pooled_sums_kernel, grid=(length // block,), in_specs=[pl....  21.9 us
    ppermute x4, waiting for transfers between devices, all_sum(): got = lax.ppermute(jnp.where(upper, low, high), axes, perm)  18.8 us
    ppermute x4, starting transfers between devices, all_sum(): value = value + lax.ppermute(value, axes, perm)  14.2 us
    ppermute x4, starting transfers between devices, all_sum(): got = lax.ppermute(value, axes, perm)  14 us
    ppermute x4, waiting for transfers between devices, all_sum(): value = value + lax.ppermute(value, axes, perm)  13.8 us
    ppermute x2, starting transfers between devices, passed_along(): lax.ppermute(value, axis, [(source, source + steps) for source in range(i...  7.03 us
    ppermute x2, waiting for transfers between devices, passed_along(): lax.ppermute(value, axis, [(source, source + steps) for source in range(i...  4.64 us
  transfers between devices with their start and end apart: 16, of which 15 were waited for; matrix products, arithmetic and copies ran while one was open for 0% of the time, Pallas kernels for 0%

profile of v7, /device:TPU:1, one launch (start us, length us, event | category | flops | bytes accessed | tf_op | source)
XLA Modules:
  0.0 162.2 jit_solution(16631323334326752282)
XLA Ops:
  0.6 1.0 reduce-precision_subtract_fusion
  1.7 1.5 broadcast_subtract_fusion.ids_ref
  3.2 1.9 %stack.10.split_ref = f32[8,16384]{1,0:T(8,128)} concatenate(f32[1,16384]{1,0:T(1,128)S(1)} %get-tuple-element.27, f32[1,16384]{1,0:T(1,128)S(1)} %get-tuple-element.28, f32[1,16384]{1,0:T(1,128)S(1)} %get-tuple-element.26, f32[1,16384]{1,0:T(1,128)} %param.9, f32[4,16384]{1,0:T(4,128)S(1)} %stack.4), dimensions={0} | concatenate | bytes 1048576 | tf_op jit(solution)/shard_map/stack | solution.py:56
  5.1 21.9 %shard_map.111 = f32[768,384]{1,0:T(8,128)} custom-call(s32[1,16384]{1,0:T(1,128)} %broadcast_subtract_fusion.ids_ref, f32[8,16384]{1,0:T(8,128)} %stack.10.split_ref, bf16[16384,256]{1,0:T(8,128)(2,1)} %bitcast.45), custom_call_target="tpu_custom_call" | custom-call | flops 9663676416 | bytes 10158080 | tf_op jit(solution)/shard_map/pallas_call | solution.py:59
  27.0 1.2 fusion.27
  28.2 5.1 %collective-permute-start = (f32[256,384]{1,0:T(8,128)S(1)}, f32[256,384]{1,0:T(8,128)S(1)}, u32[]{:S(2)}, u32[]{:S(2)}) collective-permute-start(f32[256,384]{1,0:T(8,128)S(1)} %get-tuple-element.20), channel_id=1, source_target_pairs={{32,0},{64,32},{96,64},{128,96},{160,128},{192,160},{224,192},{33,... | collective-permute-start | bytes 1179656 | tf_op jit(solution)/shard_map/ppermute | solution.py:11
  33.3 1.9 %collective-permute-start.1 = (f32[256,384]{1,0:T(8,128)S(1)}, f32[256,384]{1,0:T(8,128)S(1)}, u32[]{:S(2)}, u32[]{:S(2)}) collective-permute-start(f32[256,384]{1,0:T(8,128)S(1)} %get-tuple-element.21), channel_id=1, source_target_pairs={{0,32},{32,64},{64,96},{96,128},{128,160},{160,192},{192,224},{1,3... | collective-permute-start | bytes 1179656 | tf_op jit(solution)/shard_map/ppermute | solution.py:11
  35.3 2.8 %collective-permute-done = f32[256,384]{1,0:T(8,128)S(1)} collective-permute-done((f32[256,384]{1,0:T(8,128)S(1)}, f32[256,384]{1,0:T(8,128)S(1)}, u32[]{:S(2)}, u32[]{:S(2)}) %collective-permute-start) | collective-permute-done | bytes 393248 | tf_op jit(solution)/shard_map/ppermute | solution.py:11
  38.1 1.8 %collective-permute-done.1 = f32[256,384]{1,0:T(8,128)S(1)} collective-permute-done((f32[256,384]{1,0:T(8,128)S(1)}, f32[256,384]{1,0:T(8,128)S(1)}, u32[]{:S(2)}, u32[]{:S(2)}) %collective-permute-start.1) | collective-permute-done | bytes 393248 | tf_op jit(solution)/shard_map/ppermute | solution.py:11
  39.9 1.1 fusion.6
  41.0 0.2 fusion.20
  41.2 0.1 fusion.19
  41.3 4.4 %collective-permute-start.2 = (bf16[1,256,256]{2,1,0:T(8,128)(2,1)S(1)}, bf16[1,256,256]{2,1,0:T(8,128)(2,1)S(1)}, u32[]{:S(2)}, u32[]{:S(2)}) collective-permute-start(bf16[1,256,256]{2,1,0:T(8,128)(2,1)S(1)} %fusion.19), channel_id=1, source_target_pairs={{0,32},{32,64},{64,96},{96,128},{128,160},{160,192},{192,224},{1,3... | collective-permute-start | bytes 393224 | tf_op jit(solution)/shard_map/ppermute | solution.py:19
  45.7 1.9 %collective-permute-start.3 = (bf16[1,256,256]{2,1,0:T(8,128)(2,1)S(1)}, bf16[1,256,256]{2,1,0:T(8,128)(2,1)S(1)}, u32[]{:S(2)}, u32[]{:S(2)}) collective-permute-start(bf16[1,256,256]{2,1,0:T(8,128)(2,1)S(1)} %fusion.19), channel_id=1, source_target_pairs={{32,0},{64,32},{96,64},{128,96},{160,128},{192,160},{224,192},{33,... | collective-permute-start | bytes 393224 | tf_op jit(solution)/shard_map/ppermute | solution.py:22
  47.7 0.3 fusion.23
  48.0 4.0 %collective-permute-done.3 = bf16[1,256,256]{2,1,0:T(8,128)(2,1)S(1)} collective-permute-done((bf16[1,256,256]{2,1,0:T(8,128)(2,1)S(1)}, bf16[1,256,256]{2,1,0:T(8,128)(2,1)S(1)}, u32[]{:S(2)}, u32[]{:S(2)}) %collective-permute-start.3) | collective-permute-done | bytes 131104 | tf_op jit(solution)/shard_map/ppermute | solution.py:22
  52.0 1.0 fusion.2
  53.0 0.5 multiply_convert_fusion
  53.5 0.2 copy-done.5
  53.7 0.2 fusion.29
  53.9 0.6 fusion.1
  54.5 1.3 fusion.21
  55.8 1.3 fusion.30
  57.1 0.3 fusion.26
  57.5 0.1 reshape.545
  57.6 1.7 %pad_maximum_fusion = f32[512,1040]{1,0:T(8,128)S(1)} fusion(f32[512,16]{1,0:T(8,128)S(1)} %reshape.545, f32[256,1024]{1,0:T(8,128)} %fusion.30, f32[256,1024]{1,0:T(8,128)} %fusion.21), kind=kLoop, calls=%fused_computation | loop fusion | flops 1064960 | bytes 4259840 | tf_op jit(solution)/shard_map/concatenate | solution.py:165
  59.3 1.2 slice_select_fusion
  60.5 2.6 %copy.17 = f32[256,1040]{0,1:T(8,128)} copy(f32[256,1040]{1,0:T(8,128)} %slice_select_fusion) | data formatting | bytes 2129920 | tf_op jit(solution)/shard_map/jit(_where)/select_n | solution.py:109
  63.1 3.0 %collective-permute-done.4 = f32[256,1040]{0,1:T(8,128)} collective-permute-done((f32[256,1040]{0,1:T(8,128)}, f32[256,1040]{0,1:T(8,128)}, u32[]{:S(2)}, u32[]{:S(2)}) %collective-permute-start.4) | collective-permute-done | bytes 1064992 | tf_op jit(solution)/shard_map/ppermute | solution.py:109
  66.1 2.6 %copy.18 = f32[256,1040]{1,0:T(8,128)} copy(f32[256,1040]{0,1:T(8,128)} %collective-permute-done.4) | data formatting | bytes 2129920 | tf_op jit(solution)/shard_map/ppermute | solution.py:109
  68.7 1.4 select_add_fusion
  70.2 1.0 copy-done.1
  71.3 0.2 copy.19
  71.5 0.8 collective-permute-start.5
  72.3 7.7 %collective-permute-done.5 = f32[128,1040]{0,1:T(8,128)S(1)} collective-permute-done((f32[128,1040]{0,1:T(8,128)S(1)}, f32[128,1040]{0,1:T(8,128)S(1)}, u32[]{:S(2)}, u32[]{:S(2)}) %collective-permute-start.5) | collective-permute-done | bytes 532512 | tf_op jit(solution)/shard_map/ppermute | solution.py:109
  80.0 0.2 copy.20
  80.4 1.1 collective-permute-start.6
  81.5 4.8 %collective-permute-done.6 = f32[64,1040]{1,0:T(8,128)S(1)} collective-permute-done((f32[64,1040]{1,0:T(8,128)S(1)}, f32[64,1040]{1,0:T(8,128)S(1)}, u32[]{:S(2)}, u32[]{:S(2)}) %collective-permute-start.6) | collective-permute-done | bytes 266272 | tf_op jit(solution)/shard_map/ppermute | solution.py:109
  86.4 0.9 collective-permute-start.7
  87.3 3.2 %collective-permute-done.7 = f32[32,1040]{1,0:T(8,128)S(1)} collective-permute-done((f32[32,1040]{1,0:T(8,128)S(1)}, f32[32,1040]{1,0:T(8,128)S(1)}, u32[]{:S(2)}, u32[]{:S(2)}) %collective-permute-start.7) | collective-permute-done | bytes 133152 | tf_op jit(solution)/shard_map/ppermute | solution.py:109
  90.5 2.6 %collective-permute-start.8 = (f32[32,1040]{1,0:T(8,128)S(1)}, f32[32,1040]{1,0:T(8,128)S(1)}, u32[]{:S(2)}, u32[]{:S(2)}) collective-permute-start(f32[32,1040]{1,0:T(8,128)S(1)} %select_add_fusion.3), channel_id=1, source_target_pairs={{0,128},{1,129},{2,130},{3,131},{4,132},{5,133},{6,134},{7,135},{8... | collective-permute-start | bytes 399368 | tf_op jit(solution)/shard_map/ppermute | solution.py:112
  93.1 3.0 %collective-permute-done.8 = f32[32,1040]{1,0:T(8,128)S(1)} collective-permute-done((f32[32,1040]{1,0:T(8,128)S(1)}, f32[32,1040]{1,0:T(8,128)S(1)}, u32[]{:S(2)}, u32[]{:S(2)}) %collective-permute-start.8) | collective-permute-done | bytes 133152 | tf_op jit(solution)/shard_map/ppermute | solution.py:112
  96.1 2.6 %collective-permute-start.9 = (f32[32,1040]{1,0:T(8,128)S(1)}, f32[32,1040]{1,0:T(8,128)S(1)}, u32[]{:S(2)}, u32[]{:S(2)}) collective-permute-start(f32[32,1040]{1,0:T(8,128)S(1)} %add.252), channel_id=1, source_target_pairs={{0,16},{1,17},{2,18},{3,19},{4,20},{5,21},{6,22},{7,23},{8,24},{9,... | collective-permute-start | bytes 399368 | tf_op jit(solution)/shard_map/ppermute | solution.py:112
  98.7 4.1 %collective-permute-done.9 = f32[32,1040]{1,0:T(8,128)S(1)} collective-permute-done((f32[32,1040]{1,0:T(8,128)S(1)}, f32[32,1040]{1,0:T(8,128)S(1)}, u32[]{:S(2)}, u32[]{:S(2)}) %collective-permute-start.9) | collective-permute-done | bytes 133152 | tf_op jit(solution)/shard_map/ppermute | solution.py:112
  102.9 2.8 %collective-permute-start.10 = (f32[32,1040]{1,0:T(8,128)S(1)}, f32[32,1040]{1,0:T(8,128)S(1)}, u32[]{:S(2)}, u32[]{:S(2)}) collective-permute-start(f32[32,1040]{1,0:T(8,128)S(1)} %add.253), channel_id=1, source_target_pairs={{0,2},{1,3},{2,0},{3,1},{4,6},{5,7},{6,4},{7,5},{8,10},{9,11},{10,... | collective-permute-start | bytes 399368 | tf_op jit(solution)/shard_map/ppermute | solution.py:112
  105.7 2.8 %collective-permute-done.10 = f32[32,1040]{1,0:T(8,128)S(1)} collective-permute-done((f32[32,1040]{1,0:T(8,128)S(1)}, f32[32,1040]{1,0:T(8,128)S(1)}, u32[]{:S(2)}, u32[]{:S(2)}) %collective-permute-start.10) | collective-permute-done | bytes 133152 | tf_op jit(solution)/shard_map/ppermute | solution.py:112
  108.5 6.2 %collective-permute-start.11 = (f32[32,1040]{1,0:T(8,128)S(1)}, f32[32,1040]{1,0:T(8,128)S(1)}, u32[]{:S(2)}, u32[]{:S(2)}) collective-permute-start(f32[32,1040]{1,0:T(8,128)S(1)} %add.254), channel_id=1, source_target_pairs={{0,4},{1,5},{2,6},{3,7},{4,0},{5,1},{6,2},{7,3},{8,12},{9,13},{10,... | collective-permute-start | bytes 399368 | tf_op jit(solution)/shard_map/ppermute | solution.py:112
  114.7 3.8 %collective-permute-done.11 = f32[32,1040]{1,0:T(8,128)S(1)} collective-permute-done((f32[32,1040]{1,0:T(8,128)S(1)}, f32[32,1040]{1,0:T(8,128)S(1)}, u32[]{:S(2)}, u32[]{:S(2)}) %collective-permute-start.11) | collective-permute-done | bytes 133152 | tf_op jit(solution)/shard_map/ppermute | solution.py:112
  118.5 1.5 collective-permute-start.12
  120.1 2.8 %collective-permute-done.12 = f32[32,1040]{1,0:T(8,128)S(1)} collective-permute-done((f32[32,1040]{1,0:T(8,128)S(1)}, f32[32,1040]{1,0:T(8,128)S(1)}, u32[]{:S(2)}, u32[]{:S(2)}) %collective-permute-start.12) | collective-permute-done | bytes 133152 | tf_op jit(solution)/shard_map/ppermute | solution.py:115
  123.0 7.9 %collective-permute-done.13 = f32[64,1040]{1,0:T(8,128)S(1)} collective-permute-done((f32[64,1040]{1,0:T(8,128)S(1)}, f32[64,1040]{1,0:T(8,128)S(1)}, u32[]{:S(2)}, u32[]{:S(2)}) %collective-permute-start.13) | collective-permute-done | bytes 266272 | tf_op jit(solution)/shard_map/ppermute | solution.py:115
  130.9 0.2 copy.21
  131.1 1.4 collective-permute-start.14
  132.5 9.3 %collective-permute-done.14 = f32[128,1040]{0,1:T(8,128)S(1)} collective-permute-done((f32[128,1040]{0,1:T(8,128)S(1)}, f32[128,1040]{0,1:T(8,128)S(1)}, u32[]{:S(2)}, u32[]{:S(2)}) %collective-permute-start.14) | collective-permute-done | bytes 532512 | tf_op jit(solution)/shard_map/ppermute | solution.py:115
  141.8 0.2 copy.22
  142.2 1.3 copy.24
  143.6 11.0 %collective-permute-start.15 = (f32[256,1040]{0,1:T(8,128)}, f32[256,1040]{0,1:T(8,128)}, u32[]{:S(2)}, u32[]{:S(2)}) collective-permute-start(f32[256,1040]{0,1:T(8,128)} %copy.24), channel_id=1, source_target_pairs={{0,32},{1,33},{2,34},{3,35},{4,36},{5,37},{6,38},{7,39},{8,40},{9,... | collective-permute-start | bytes 3194888 | tf_op jit(solution)/shard_map/ppermute | solution.py:115
  154.6 2.7 %collective-permute-done.15 = f32[256,1040]{0,1:T(8,128)} collective-permute-done((f32[256,1040]{0,1:T(8,128)}, f32[256,1040]{0,1:T(8,128)}, u32[]{:S(2)}, u32[]{:S(2)}) %collective-permute-start.15) | collective-permute-done | bytes 1064992 | tf_op jit(solution)/shard_map/ppermute | solution.py:115
  157.2 1.6 copy.25
  158.8 0.2 broadcast_select_fusion
  159.0 1.1 slice.151
  160.1 1.1 slice.152
  161.2 0.1 reshape.546
  161.4 0.8 copy.27
  (37 shorter events, 0.8 us)
Async XLA Ops:
  0.6 52.4 %copy-start = (bf16[256,1024]{1,0:T(8,128)(2,1)S(1)}, bf16[256,1024]{1,0:T(8,128)(2,1)}, u32[]{:S(2)}) copy-start(bf16[256,1024]{1,0:T(8,128)(2,1)} %param.14) | copy-start | bytes 1572868
  27.0 8.2 %copy-start.6 = (s32[1,256,8]{1,2,0:T(8,128)S(1)}, s32[1,256,8]{1,2,0:T(8,128)}, u32[]{:S(2)}) copy-start(s32[1,256,8]{1,2,0:T(8,128)} %param.11) | copy-start | bytes 24580
  28.2 10.0 %collective-permute-start = (f32[256,384]{1,0:T(8,128)S(1)}, f32[256,384]{1,0:T(8,128)S(1)}, u32[]{:S(2)}, u32[]{:S(2)}) collective-permute-start(f32[256,384]{1,0:T(8,128)S(1)} %get-tuple-element.20), channel_id=1, source_target_pairs={{32,0},{64,32},{96,64},{128,96},{160,128},{192,160},{224,192},{33,... | collective-permute-start | bytes 1179656 | tf_op jit(solution)/shard_map/ppermute | solution.py:11
  33.3 6.6 %collective-permute-start.1 = (f32[256,384]{1,0:T(8,128)S(1)}, f32[256,384]{1,0:T(8,128)S(1)}, u32[]{:S(2)}, u32[]{:S(2)}) collective-permute-start(f32[256,384]{1,0:T(8,128)S(1)} %get-tuple-element.21), channel_id=1, source_target_pairs={{0,32},{32,64},{64,96},{96,128},{128,160},{160,192},{192,224},{1,3... | collective-permute-start | bytes 1179656 | tf_op jit(solution)/shard_map/ppermute | solution.py:11
  35.3 12.4 %copy-start.3 = (bf16[256,1024]{1,0:T(8,128)(2,1)S(1)}, bf16[256,1024]{1,0:T(8,128)(2,1)}, u32[]{:S(2)}) copy-start(bf16[256,1024]{1,0:T(8,128)(2,1)} %param.13) | copy-start | bytes 1572868
  41.3 6.6 %collective-permute-start.2 = (bf16[1,256,256]{2,1,0:T(8,128)(2,1)S(1)}, bf16[1,256,256]{2,1,0:T(8,128)(2,1)S(1)}, u32[]{:S(2)}, u32[]{:S(2)}) collective-permute-start(bf16[1,256,256]{2,1,0:T(8,128)(2,1)S(1)} %fusion.19), channel_id=1, source_target_pairs={{0,32},{32,64},{64,96},{96,128},{128,160},{160,192},{192,224},{1,3... | collective-permute-start | bytes 393224 | tf_op jit(solution)/shard_map/ppermute | solution.py:19
  45.7 6.3 %collective-permute-start.3 = (bf16[1,256,256]{2,1,0:T(8,128)(2,1)S(1)}, bf16[1,256,256]{2,1,0:T(8,128)(2,1)S(1)}, u32[]{:S(2)}, u32[]{:S(2)}) collective-permute-start(bf16[1,256,256]{2,1,0:T(8,128)(2,1)S(1)} %fusion.19), channel_id=1, source_target_pairs={{32,0},{64,32},{96,64},{128,96},{160,128},{192,160},{224,192},{33,... | collective-permute-start | bytes 393224 | tf_op jit(solution)/shard_map/ppermute | solution.py:22
  53.0 0.7 copy-start.5
  53.0 0.9 copy-start.7
  53.9 3.2 %copy-start.4 = (f32[256,8]{0,1:T(8,128)}, f32[256,8]{0,1:T(8,128)S(1)}, u32[]{:S(2)}) copy-start(f32[256,8]{0,1:T(8,128)S(1)} %fusion.29) | copy-start | bytes 24580
  63.1 3.0 %collective-permute-start.4 = (f32[256,1040]{0,1:T(8,128)}, f32[256,1040]{0,1:T(8,128)}, u32[]{:S(2)}, u32[]{:S(2)}) collective-permute-start(f32[256,1040]{0,1:T(8,128)} %copy.17), channel_id=1, source_target_pairs={{0,32},{1,33},{2,34},{3,35},{4,36},{5,37},{6,38},{7,39},{8,40},{9,... | collective-permute-start | bytes 3194888 | tf_op jit(solution)/shard_map/ppermute | solution.py:109
  70.2 1.0 copy-start.1
  71.3 8.9 %copy-start.2 = (f32[256,1040]{1,0:T(8,128)S(1)}, f32[256,1040]{1,0:T(8,128)}, u32[]{:S(2)}) copy-start(f32[256,1040]{1,0:T(8,128)} %copy-done.1) | copy-start | bytes 3194884
  71.5 8.5 %collective-permute-start.5 = (f32[128,1040]{0,1:T(8,128)S(1)}, f32[128,1040]{0,1:T(8,128)S(1)}, u32[]{:S(2)}, u32[]{:S(2)}) collective-permute-start(f32[128,1040]{0,1:T(8,128)S(1)} %copy.19), channel_id=1, source_target_pairs={{0,64},{1,65},{2,66},{3,67},{4,68},{5,69},{6,70},{7,71},{8,72},{9,... | collective-permute-start | bytes 1597448 | tf_op jit(solution)/shard_map/ppermute | solution.py:109
  80.4 6.0 %collective-permute-start.6 = (f32[64,1040]{1,0:T(8,128)S(1)}, f32[64,1040]{1,0:T(8,128)S(1)}, u32[]{:S(2)}, u32[]{:S(2)}) collective-permute-start(f32[64,1040]{1,0:T(8,128)S(1)} %slice_select_fusion.2), channel_id=1, source_target_pairs={{0,8},{1,9},{2,10},{3,11},{4,12},{5,13},{6,14},{7,15},{8,0},{9,1},... | collective-permute-start | bytes 798728 | tf_op jit(solution)/shard_map/ppermute | solution.py:109
  86.4 4.1 %collective-permute-start.7 = (f32[32,1040]{1,0:T(8,128)S(1)}, f32[32,1040]{1,0:T(8,128)S(1)}, u32[]{:S(2)}, u32[]{:S(2)}) collective-permute-start(f32[32,1040]{1,0:T(8,128)S(1)} %slice_select_fusion.3), channel_id=1, source_target_pairs={{0,1},{1,0},{2,3},{3,2},{4,5},{5,4},{6,7},{7,6},{8,9},{9,8},{10,11... | collective-permute-start | bytes 399368 | tf_op jit(solution)/shard_map/ppermute | solution.py:109
  90.5 5.6 %collective-permute-start.8 = (f32[32,1040]{1,0:T(8,128)S(1)}, f32[32,1040]{1,0:T(8,128)S(1)}, u32[]{:S(2)}, u32[]{:S(2)}) collective-permute-start(f32[32,1040]{1,0:T(8,128)S(1)} %select_add_fusion.3), channel_id=1, source_target_pairs={{0,128},{1,129},{2,130},{3,131},{4,132},{5,133},{6,134},{7,135},{8... | collective-permute-start | bytes 399368 | tf_op jit(solution)/shard_map/ppermute | solution.py:112
  96.1 6.8 %collective-permute-start.9 = (f32[32,1040]{1,0:T(8,128)S(1)}, f32[32,1040]{1,0:T(8,128)S(1)}, u32[]{:S(2)}, u32[]{:S(2)}) collective-permute-start(f32[32,1040]{1,0:T(8,128)S(1)} %add.252), channel_id=1, source_target_pairs={{0,16},{1,17},{2,18},{3,19},{4,20},{5,21},{6,22},{7,23},{8,24},{9,... | collective-permute-start | bytes 399368 | tf_op jit(solution)/shard_map/ppermute | solution.py:112
  102.9 5.6 %collective-permute-start.10 = (f32[32,1040]{1,0:T(8,128)S(1)}, f32[32,1040]{1,0:T(8,128)S(1)}, u32[]{:S(2)}, u32[]{:S(2)}) collective-permute-start(f32[32,1040]{1,0:T(8,128)S(1)} %add.253), channel_id=1, source_target_pairs={{0,2},{1,3},{2,0},{3,1},{4,6},{5,7},{6,4},{7,5},{8,10},{9,11},{10,... | collective-permute-start | bytes 399368 | tf_op jit(solution)/shard_map/ppermute | solution.py:112
  108.5 10.0 %collective-permute-start.11 = (f32[32,1040]{1,0:T(8,128)S(1)}, f32[32,1040]{1,0:T(8,128)S(1)}, u32[]{:S(2)}, u32[]{:S(2)}) collective-permute-start(f32[32,1040]{1,0:T(8,128)S(1)} %add.254), channel_id=1, source_target_pairs={{0,4},{1,5},{2,6},{3,7},{4,0},{5,1},{6,2},{7,3},{8,12},{9,13},{10,... | collective-permute-start | bytes 399368 | tf_op jit(solution)/shard_map/ppermute | solution.py:112
  118.5 4.3 %collective-permute-start.12 = (f32[32,1040]{1,0:T(8,128)S(1)}, f32[32,1040]{1,0:T(8,128)S(1)}, u32[]{:S(2)}, u32[]{:S(2)}) collective-permute-start(f32[32,1040]{1,0:T(8,128)S(1)} %add.255), channel_id=1, source_target_pairs={{0,1},{1,0},{2,3},{3,2},{4,5},{5,4},{6,7},{7,6},{8,9},{9,8},{10,11... | collective-permute-start | bytes 399368 | tf_op jit(solution)/shard_map/ppermute | solution.py:115
  122.9 8.0 %collective-permute-start.13 = (f32[64,1040]{1,0:T(8,128)S(1)}, f32[64,1040]{1,0:T(8,128)S(1)}, u32[]{:S(2)}, u32[]{:S(2)}) collective-permute-start(f32[64,1040]{1,0:T(8,128)S(1)} %pad_maximum_fusion.3), channel_id=1, source_target_pairs={{0,8},{1,9},{2,10},{3,11},{4,12},{5,13},{6,14},{7,15},{8,0},{9,1},... | collective-permute-start | bytes 798728 | tf_op jit(solution)/shard_map/ppermute | solution.py:115
  131.1 10.7 %collective-permute-start.14 = (f32[128,1040]{0,1:T(8,128)S(1)}, f32[128,1040]{0,1:T(8,128)S(1)}, u32[]{:S(2)}, u32[]{:S(2)}) collective-permute-start(f32[128,1040]{0,1:T(8,128)S(1)} %copy.21), channel_id=1, source_target_pairs={{0,64},{1,65},{2,66},{3,67},{4,68},{5,69},{6,70},{7,71},{8,72},{9,... | collective-permute-start | bytes 1597448 | tf_op jit(solution)/shard_map/ppermute | solution.py:115
  143.6 13.7 %collective-permute-start.15 = (f32[256,1040]{0,1:T(8,128)}, f32[256,1040]{0,1:T(8,128)}, u32[]{:S(2)}, u32[]{:S(2)}) collective-permute-start(f32[256,1040]{0,1:T(8,128)} %copy.24), channel_id=1, source_target_pairs={{0,32},{1,33},{2,34},{3,35},{4,36},{5,37},{6,38},{7,39},{8,40},{9,... | collective-permute-start | bytes 3194888 | tf_op jit(solution)/shard_map/ppermute | solution.py:115

commit v8 on v7

--- a/solution.py
+++ b/solution.py
@@ -54,7 +54,7 @@
     low = rest - middle
     zero = jnp.zeros_like(weights)
     split = jnp.stack([high, middle, low, weights, zero, zero, zero, zero], axis=0)
-    block = min(1024, length)
+    block = min(2048, length)
     lanes = 128
     sums = pl.pallas_call(
         pooled_sums_kernel,
@@ -110,6 +110,7 @@
         value = jnp.where(upper, high, low) + got
     for perm, _, _ in steps[halvings:]:
         value = value + lax.ppermute(value, axes, perm)
+    value = value.astype(jnp.bfloat16)
     for perm, flip0, flip1 in reversed(steps[:halvings]):
         upper = upper_half(flip0, flip1)
         got = lax.ppermute(value, axes, perm)
@@ -166,6 +167,7 @@
         [jnp.concatenate([grad_own, grad_side], axis=0), grad_head.reshape(rows, -1)], axis=1
     )
     packed = all_sum(packed, sizes, 4)
+    packed = packed.astype(jnp.float32)
     grad_own, grad_side = packed[:feats, :hid], packed[feats:, :hid]
     grad_head = packed[:, hid:].reshape(hid, -1)
     return (scores, grad_own, grad_side, grad_head)

time: 163 us -> 149 us (0.914)
  waiting for transfers between devices: 63.8 us -> 55.1 us
  Pallas kernels: 21.9 us -> 18.9 us
  local copies, waits for them, and re-layouts: 16.7 us -> 14.2 us
    ppermute x4, waiting for transfers between devices: 22.6 us -> 13.6 us  [all_sum(): got = lax.ppermute(value, axes, perm)]
    pallas_call x1, Pallas kernels: 21.9 us -> 18.9 us  [accumulate(): pl.pallas_call(pooled_sums_kernel, grid=(length // block,), in_specs=[pl....]
where the time goes in v8:
time: 149 us; the launch traced here: 148 us
  waiting for transfers between devices  55.1 us (37%)
  starting transfers between devices  43.9 us (29%)
  Pallas kernels  18.9 us (13%)
  local copies, waits for them, and re-layouts  14.2 us (10%)
  other arithmetic  9.92 us (7%)
  matrix products  5.47 us (4%)
    pallas_call x1, Pallas kernels, accumulate(): pl.pallas_call(pooled_sums_kernel, grid=(length // block,), in_specs=[pl....  18.9 us
    ppermute x4, waiting for transfers between devices, all_sum(): got = lax.ppermute(jnp.where(upper, low, high), axes, perm)  18.8 us
    ppermute x4, starting transfers between devices, all_sum(): value = value + lax.ppermute(value, axes, perm)  14.4 us
    ppermute x4, waiting for transfers between devices, all_sum(): value = value + lax.ppermute(value, axes, perm)  14 us
    ppermute x4, waiting for transfers between devices, all_sum(): got = lax.ppermute(value, axes, perm)  13.6 us
    ppermute x4, starting transfers between devices, all_sum(): got = lax.ppermute(value, axes, perm)  13.4 us
    ppermute x2, starting transfers between devices, passed_along(): lax.ppermute(value, axis, [(source, source + steps) for source in range(i...  7.03 us
    ppermute x2, waiting for transfers between devices, passed_along(): lax.ppermute(value, axis, [(source, source + steps) for source in range(i...  4.64 us
  transfers between devices with their start and end apart: 16, of which 15 were waited for; matrix products, arithmetic and copies ran while one was open for 0% of the time, Pallas kernels for 0%

profile of v8, /device:TPU:1, one launch (start us, length us, event | category | flops | bytes accessed | tf_op | source)
XLA Modules:
  0.0 148.5 jit_solution(13701454710261565232)
XLA Ops:
  0.6 1.0 reduce-precision_subtract_fusion
  1.7 1.5 %broadcast_subtract_fusion.ids_ref = s32[1,16384]{1,0:T(1,128)} fusion(s32[1,16384]{1,0:T(1,128)} %param.10, s32[]{:T(128)S(6)} %mul.20), kind=kLoop, calls=%fused_computation.66 | loop fusion | flops 16384 | bytes 131076 | tf_op jit(solution)/shard_map/sub | solution.py:127
  3.2 1.9 %stack.10.split_ref = f32[8,16384]{1,0:T(8,128)} concatenate(f32[1,16384]{1,0:T(1,128)S(1)} %get-tuple-element.29, f32[1,16384]{1,0:T(1,128)S(1)} %get-tuple-element.30, f32[1,16384]{1,0:T(1,128)S(1)} %get-tuple-element.28, f32[1,16384]{1,0:T(1,128)} %param.9, f32[4,16384]{1,0:T(4,128)S(1)} %stack.4), dimensions={0} | concatenate | bytes 1048576 | tf_op jit(solution)/shard_map/stack | solution.py:56
  5.1 18.9 %shard_map.111 = f32[768,384]{1,0:T(8,128)} custom-call(s32[1,16384]{1,0:T(1,128)} %broadcast_subtract_fusion.ids_ref, f32[8,16384]{1,0:T(8,128)} %stack.10.split_ref, bf16[16384,256]{1,0:T(8,128)(2,1)} %bitcast.45), custom_call_target="tpu_custom_call" | custom-call | flops 9663676416 | bytes 10158080 | tf_op jit(solution)/shard_map/pallas_call | solution.py:59
  24.0 1.2 fusion.28
  25.2 5.1 %collective-permute-start = (f32[256,384]{1,0:T(8,128)S(1)}, f32[256,384]{1,0:T(8,128)S(1)}, u32[]{:S(2)}, u32[]{:S(2)}) collective-permute-start(f32[256,384]{1,0:T(8,128)S(1)} %get-tuple-element.20), channel_id=1, source_target_pairs={{32,0},{64,32},{96,64},{128,96},{160,128},{192,160},{224,192},{33,... | collective-permute-start | bytes 1179656 | tf_op jit(solution)/shard_map/ppermute | solution.py:11
  30.3 1.9 %collective-permute-start.1 = (f32[256,384]{1,0:T(8,128)S(1)}, f32[256,384]{1,0:T(8,128)S(1)}, u32[]{:S(2)}, u32[]{:S(2)}) collective-permute-start(f32[256,384]{1,0:T(8,128)S(1)} %get-tuple-element.21), channel_id=1, source_target_pairs={{0,32},{32,64},{64,96},{96,128},{128,160},{160,192},{192,224},{1,3... | collective-permute-start | bytes 1179656 | tf_op jit(solution)/shard_map/ppermute | solution.py:11
  32.3 2.8 %collective-permute-done = f32[256,384]{1,0:T(8,128)S(1)} collective-permute-done((f32[256,384]{1,0:T(8,128)S(1)}, f32[256,384]{1,0:T(8,128)S(1)}, u32[]{:S(2)}, u32[]{:S(2)}) %collective-permute-start) | collective-permute-done | bytes 393248 | tf_op jit(solution)/shard_map/ppermute | solution.py:11
  35.2 1.8 %collective-permute-done.1 = f32[256,384]{1,0:T(8,128)S(1)} collective-permute-done((f32[256,384]{1,0:T(8,128)S(1)}, f32[256,384]{1,0:T(8,128)S(1)}, u32[]{:S(2)}, u32[]{:S(2)}) %collective-permute-start.1) | collective-permute-done | bytes 393248 | tf_op jit(solution)/shard_map/ppermute | solution.py:11
  37.0 1.1 fusion.6
  38.0 0.2 fusion.20
  38.2 0.1 fusion.19
  38.4 4.4 %collective-permute-start.2 = (bf16[1,256,256]{2,1,0:T(8,128)(2,1)S(1)}, bf16[1,256,256]{2,1,0:T(8,128)(2,1)S(1)}, u32[]{:S(2)}, u32[]{:S(2)}) collective-permute-start(bf16[1,256,256]{2,1,0:T(8,128)(2,1)S(1)} %fusion.19), channel_id=1, source_target_pairs={{0,32},{32,64},{64,96},{96,128},{128,160},{160,192},{192,224},{1,3... | collective-permute-start | bytes 393224 | tf_op jit(solution)/shard_map/ppermute | solution.py:19
  42.7 1.9 %collective-permute-start.3 = (bf16[1,256,256]{2,1,0:T(8,128)(2,1)S(1)}, bf16[1,256,256]{2,1,0:T(8,128)(2,1)S(1)}, u32[]{:S(2)}, u32[]{:S(2)}) collective-permute-start(bf16[1,256,256]{2,1,0:T(8,128)(2,1)S(1)} %fusion.19), channel_id=1, source_target_pairs={{32,0},{64,32},{96,64},{128,96},{160,128},{192,160},{224,192},{33,... | collective-permute-start | bytes 393224 | tf_op jit(solution)/shard_map/ppermute | solution.py:22
  44.7 0.3 fusion.23
  45.0 4.0 %collective-permute-done.3 = bf16[1,256,256]{2,1,0:T(8,128)(2,1)S(1)} collective-permute-done((bf16[1,256,256]{2,1,0:T(8,128)(2,1)S(1)}, bf16[1,256,256]{2,1,0:T(8,128)(2,1)S(1)}, u32[]{:S(2)}, u32[]{:S(2)}) %collective-permute-start.3) | collective-permute-done | bytes 131104 | tf_op jit(solution)/shard_map/ppermute | solution.py:22
  49.0 1.0 fusion.2
  50.0 0.5 multiply_convert_fusion
  50.5 0.2 copy-done.5
  50.7 0.2 fusion.30
  51.0 0.6 fusion.1
  51.6 1.3 fusion.21
  52.9 1.3 fusion.31
  54.1 0.3 fusion.26
  54.5 0.1 reshape.545
  54.6 1.7 %pad_maximum_fusion = f32[512,1040]{1,0:T(8,128)S(1)} fusion(f32[512,16]{1,0:T(8,128)S(1)} %reshape.545, f32[256,1024]{1,0:T(8,128)} %fusion.31, f32[256,1024]{1,0:T(8,128)} %fusion.21), kind=kLoop, calls=%fused_computation | loop fusion | flops 1064960 | bytes 4259840 | tf_op jit(solution)/shard_map/concatenate | solution.py:166
  56.4 1.1 slice_select_fusion
  57.5 2.6 %copy.17 = f32[256,1040]{0,1:T(8,128)} copy(f32[256,1040]{1,0:T(8,128)} %slice_select_fusion) | data formatting | bytes 2129920 | tf_op jit(solution)/shard_map/jit(_where)/select_n | solution.py:109
  60.1 3.0 %collective-permute-done.4 = f32[256,1040]{0,1:T(8,128)} collective-permute-done((f32[256,1040]{0,1:T(8,128)}, f32[256,1040]{0,1:T(8,128)}, u32[]{:S(2)}, u32[]{:S(2)}) %collective-permute-start.4) | collective-permute-done | bytes 1064992 | tf_op jit(solution)/shard_map/ppermute | solution.py:109
  63.1 2.6 %copy.18 = f32[256,1040]{1,0:T(8,128)} copy(f32[256,1040]{0,1:T(8,128)} %collective-permute-done.4) | data formatting | bytes 2129920 | tf_op jit(solution)/shard_map/ppermute | solution.py:109
  65.8 1.4 select_add_fusion
  67.2 1.0 copy-done.1
  68.3 0.2 copy.19
  68.5 0.8 collective-permute-start.5
  69.3 7.7 %collective-permute-done.5 = f32[128,1040]{0,1:T(8,128)S(1)} collective-permute-done((f32[128,1040]{0,1:T(8,128)S(1)}, f32[128,1040]{0,1:T(8,128)S(1)}, u32[]{:S(2)}, u32[]{:S(2)}) %collective-permute-start.5) | collective-permute-done | bytes 532512 | tf_op jit(solution)/shard_map/ppermute | solution.py:109
  77.0 0.2 copy.20
  77.4 1.1 collective-permute-start.6
  78.5 4.8 %collective-permute-done.6 = f32[64,1040]{1,0:T(8,128)S(1)} collective-permute-done((f32[64,1040]{1,0:T(8,128)S(1)}, f32[64,1040]{1,0:T(8,128)S(1)}, u32[]{:S(2)}, u32[]{:S(2)}) %collective-permute-start.6) | collective-permute-done | bytes 266272 | tf_op jit(solution)/shard_map/ppermute | solution.py:109
  83.4 0.9 collective-permute-start.7
  84.3 3.2 %collective-permute-done.7 = f32[32,1040]{1,0:T(8,128)S(1)} collective-permute-done((f32[32,1040]{1,0:T(8,128)S(1)}, f32[32,1040]{1,0:T(8,128)S(1)}, u32[]{:S(2)}, u32[]{:S(2)}) %collective-permute-start.7) | collective-permute-done | bytes 133152 | tf_op jit(solution)/shard_map/ppermute | solution.py:109
  87.5 2.6 %collective-permute-start.8 = (f32[32,1040]{1,0:T(8,128)S(1)}, f32[32,1040]{1,0:T(8,128)S(1)}, u32[]{:S(2)}, u32[]{:S(2)}) collective-permute-start(f32[32,1040]{1,0:T(8,128)S(1)} %select_add_fusion.3), channel_id=1, source_target_pairs={{0,128},{1,129},{2,130},{3,131},{4,132},{5,133},{6,134},{7,135},{8... | collective-permute-start | bytes 399368 | tf_op jit(solution)/shard_map/ppermute | solution.py:112
  90.1 3.0 %collective-permute-done.8 = f32[32,1040]{1,0:T(8,128)S(1)} collective-permute-done((f32[32,1040]{1,0:T(8,128)S(1)}, f32[32,1040]{1,0:T(8,128)S(1)}, u32[]{:S(2)}, u32[]{:S(2)}) %collective-permute-start.8) | collective-permute-done | bytes 133152 | tf_op jit(solution)/shard_map/ppermute | solution.py:112
  93.1 2.6 %collective-permute-start.9 = (f32[32,1040]{1,0:T(8,128)S(1)}, f32[32,1040]{1,0:T(8,128)S(1)}, u32[]{:S(2)}, u32[]{:S(2)}) collective-permute-start(f32[32,1040]{1,0:T(8,128)S(1)} %add.252), channel_id=1, source_target_pairs={{0,16},{1,17},{2,18},{3,19},{4,20},{5,21},{6,22},{7,23},{8,24},{9,... | collective-permute-start | bytes 399368 | tf_op jit(solution)/shard_map/ppermute | solution.py:112
  95.8 4.1 %collective-permute-done.9 = f32[32,1040]{1,0:T(8,128)S(1)} collective-permute-done((f32[32,1040]{1,0:T(8,128)S(1)}, f32[32,1040]{1,0:T(8,128)S(1)}, u32[]{:S(2)}, u32[]{:S(2)}) %collective-permute-start.9) | collective-permute-done | bytes 133152 | tf_op jit(solution)/shard_map/ppermute | solution.py:112
  99.9 2.8 %collective-permute-start.10 = (f32[32,1040]{1,0:T(8,128)S(1)}, f32[32,1040]{1,0:T(8,128)S(1)}, u32[]{:S(2)}, u32[]{:S(2)}) collective-permute-start(f32[32,1040]{1,0:T(8,128)S(1)} %add.253), channel_id=1, source_target_pairs={{0,2},{1,3},{2,0},{3,1},{4,6},{5,7},{6,4},{7,5},{8,10},{9,11},{10,... | collective-permute-start | bytes 399368 | tf_op jit(solution)/shard_map/ppermute | solution.py:112
  102.7 2.8 %collective-permute-done.10 = f32[32,1040]{1,0:T(8,128)S(1)} collective-permute-done((f32[32,1040]{1,0:T(8,128)S(1)}, f32[32,1040]{1,0:T(8,128)S(1)}, u32[]{:S(2)}, u32[]{:S(2)}) %collective-permute-start.10) | collective-permute-done | bytes 133152 | tf_op jit(solution)/shard_map/ppermute | solution.py:112
  105.5 6.4 %collective-permute-start.11 = (f32[32,1040]{1,0:T(8,128)S(1)}, f32[32,1040]{1,0:T(8,128)S(1)}, u32[]{:S(2)}, u32[]{:S(2)}) collective-permute-start(f32[32,1040]{1,0:T(8,128)S(1)} %add.254), channel_id=1, source_target_pairs={{0,4},{1,5},{2,6},{3,7},{4,0},{5,1},{6,2},{7,3},{8,12},{9,13},{10,... | collective-permute-start | bytes 399368 | tf_op jit(solution)/shard_map/ppermute | solution.py:112
  111.9 4.1 %collective-permute-done.11 = f32[32,1040]{1,0:T(8,128)S(1)} collective-permute-done((f32[32,1040]{1,0:T(8,128)S(1)}, f32[32,1040]{1,0:T(8,128)S(1)}, u32[]{:S(2)}, u32[]{:S(2)}) %collective-permute-start.11) | collective-permute-done | bytes 133152 | tf_op jit(solution)/shard_map/ppermute | solution.py:112
  116.0 1.3 collective-permute-start.12
  117.3 2.0 %collective-permute-done.12 = bf16[32,1040]{1,0:T(8,128)(2,1)S(1)} collective-permute-done((bf16[32,1040]{1,0:T(8,128)(2,1)S(1)}, bf16[32,1040]{1,0:T(8,128)(2,1)S(1)}, u32[]{:S(2)}, u32[]{:S(2)}) %collective-permute-start.12) | collective-permute-done | bytes 66592 | tf_op jit(solution)/shard_map/ppermute | solution.py:116
  119.4 5.8 %collective-permute-done.13 = bf16[64,1040]{1,0:T(8,128)(2,1)S(1)} collective-permute-done((bf16[64,1040]{1,0:T(8,128)(2,1)S(1)}, bf16[64,1040]{1,0:T(8,128)(2,1)S(1)}, u32[]{:S(2)}, u32[]{:S(2)}) %collective-permute-start.13) | collective-permute-done | bytes 133152 | tf_op jit(solution)/shard_map/ppermute | solution.py:116
  125.3 1.4 collective-permute-start.14
  126.7 4.3 %collective-permute-done.14 = bf16[128,1040]{1,0:T(8,128)(2,1)S(1)} collective-permute-done((bf16[128,1040]{1,0:T(8,128)(2,1)S(1)}, bf16[128,1040]{1,0:T(8,128)(2,1)S(1)}, u32[]{:S(2)}, u32[]{:S(2)}) %collective-permute-start.14) | collective-permute-done | bytes 266272 | tf_op jit(solution)/shard_map/ppermute | solution.py:116
  131.0 0.1 broadcast_select_fusion.3
  131.1 0.2 copy.21
  131.4 10.7 %collective-permute-start.15 = (bf16[256,1040]{0,1:T(8,128)(2,1)S(1)}, bf16[256,1040]{0,1:T(8,128)(2,1)S(1)}, u32[]{:S(2)}, u32[]{:S(2)}) collective-permute-start(bf16[256,1040]{0,1:T(8,128)(2,1)S(1)} %copy.21), channel_id=1, source_target_pairs={{0,32},{1,33},{2,34},{3,35},{4,36},{5,37},{6,38},{7,39},{8,40},{9,... | collective-permute-start | bytes 1597448 | tf_op jit(solution)/shard_map/ppermute | solution.py:116
  142.0 1.5 %collective-permute-done.15 = bf16[256,1040]{0,1:T(8,128)(2,1)S(1)} collective-permute-done((bf16[256,1040]{0,1:T(8,128)(2,1)S(1)}, bf16[256,1040]{0,1:T(8,128)(2,1)S(1)}, u32[]{:S(2)}, u32[]{:S(2)}) %collective-permute-start.15) | collective-permute-done | bytes 532512 | tf_op jit(solution)/shard_map/ppermute | solution.py:116
  143.6 0.3 copy.22
  143.9 0.2 broadcast_select_fusion.1
  144.1 0.7 maximum_convert_fusion.1
  144.8 0.2 maximum_convert_fusion
  145.0 1.1 reshape.546
  146.1 0.8 copy.24
  146.9 1.6 %fusion.27 = (f32[256,1024]{1,0:T(8,128)}, f32[256,1024]{1,0:T(8,128)}) fusion(f32[512,1040]{1,0:T(8,128)S(1)} %maximum_convert_fusion), kind=kLoop, calls=%fused_computation.74 | loop fusion | bytes 4194304 | tf_op jit(solution)/shard_map/slice | solution.py:171
  (35 shorter events, 0.7 us)
Async XLA Ops:
  0.6 49.4 %copy-start = (bf16[256,1024]{1,0:T(8,128)(2,1)S(1)}, bf16[256,1024]{1,0:T(8,128)(2,1)}, u32[]{:S(2)}) copy-start(bf16[256,1024]{1,0:T(8,128)(2,1)} %param.14) | copy-start | bytes 1572868
  24.0 8.2 %copy-start.6 = (s32[1,256,8]{1,2,0:T(8,128)S(1)}, s32[1,256,8]{1,2,0:T(8,128)}, u32[]{:S(2)}) copy-start(s32[1,256,8]{1,2,0:T(8,128)} %param.11) | copy-start | bytes 24580
  25.2 10.0 %collective-permute-start = (f32[256,384]{1,0:T(8,128)S(1)}, f32[256,384]{1,0:T(8,128)S(1)}, u32[]{:S(2)}, u32[]{:S(2)}) collective-permute-start(f32[256,384]{1,0:T(8,128)S(1)} %get-tuple-element.20), channel_id=1, source_target_pairs={{32,0},{64,32},{96,64},{128,96},{160,128},{192,160},{224,192},{33,... | collective-permute-start | bytes 1179656 | tf_op jit(solution)/shard_map/ppermute | solution.py:11
  30.3 6.6 %collective-permute-start.1 = (f32[256,384]{1,0:T(8,128)S(1)}, f32[256,384]{1,0:T(8,128)S(1)}, u32[]{:S(2)}, u32[]{:S(2)}) collective-permute-start(f32[256,384]{1,0:T(8,128)S(1)} %get-tuple-element.21), channel_id=1, source_target_pairs={{0,32},{32,64},{64,96},{96,128},{128,160},{160,192},{192,224},{1,3... | collective-permute-start | bytes 1179656 | tf_op jit(solution)/shard_map/ppermute | solution.py:11
  32.3 12.4 %copy-start.3 = (bf16[256,1024]{1,0:T(8,128)(2,1)S(1)}, bf16[256,1024]{1,0:T(8,128)(2,1)}, u32[]{:S(2)}) copy-start(bf16[256,1024]{1,0:T(8,128)(2,1)} %param.13) | copy-start | bytes 1572868
  38.4 6.6 %collective-permute-start.2 = (bf16[1,256,256]{2,1,0:T(8,128)(2,1)S(1)}, bf16[1,256,256]{2,1,0:T(8,128)(2,1)S(1)}, u32[]{:S(2)}, u32[]{:S(2)}) collective-permute-start(bf16[1,256,256]{2,1,0:T(8,128)(2,1)S(1)} %fusion.19), channel_id=1, source_target_pairs={{0,32},{32,64},{64,96},{96,128},{128,160},{160,192},{192,224},{1,3... | collective-permute-start | bytes 393224 | tf_op jit(solution)/shard_map/ppermute | solution.py:19
  42.7 6.3 %collective-permute-start.3 = (bf16[1,256,256]{2,1,0:T(8,128)(2,1)S(1)}, bf16[1,256,256]{2,1,0:T(8,128)(2,1)S(1)}, u32[]{:S(2)}, u32[]{:S(2)}) collective-permute-start(bf16[1,256,256]{2,1,0:T(8,128)(2,1)S(1)} %fusion.19), channel_id=1, source_target_pairs={{32,0},{64,32},{96,64},{128,96},{160,128},{192,160},{224,192},{33,... | collective-permute-start | bytes 393224 | tf_op jit(solution)/shard_map/ppermute | solution.py:22
  50.0 0.7 copy-start.5
  50.0 0.9 copy-start.7
  51.0 3.2 %copy-start.4 = (f32[256,8]{0,1:T(8,128)}, f32[256,8]{0,1:T(8,128)S(1)}, u32[]{:S(2)}) copy-start(f32[256,8]{0,1:T(8,128)S(1)} %fusion.30) | copy-start | bytes 24580
  60.1 3.0 %collective-permute-start.4 = (f32[256,1040]{0,1:T(8,128)}, f32[256,1040]{0,1:T(8,128)}, u32[]{:S(2)}, u32[]{:S(2)}) collective-permute-start(f32[256,1040]{0,1:T(8,128)} %copy.17), channel_id=1, source_target_pairs={{0,32},{1,33},{2,34},{3,35},{4,36},{5,37},{6,38},{7,39},{8,40},{9,... | collective-permute-start | bytes 3194888 | tf_op jit(solution)/shard_map/ppermute | solution.py:109
  67.2 1.0 copy-start.1
  68.3 8.9 %copy-start.2 = (f32[256,1040]{1,0:T(8,128)S(1)}, f32[256,1040]{1,0:T(8,128)}, u32[]{:S(2)}) copy-start(f32[256,1040]{1,0:T(8,128)} %copy-done.1) | copy-start | bytes 3194884
  68.5 8.5 %collective-permute-start.5 = (f32[128,1040]{0,1:T(8,128)S(1)}, f32[128,1040]{0,1:T(8,128)S(1)}, u32[]{:S(2)}, u32[]{:S(2)}) collective-permute-start(f32[128,1040]{0,1:T(8,128)S(1)} %copy.19), channel_id=1, source_target_pairs={{0,64},{1,65},{2,66},{3,67},{4,68},{5,69},{6,70},{7,71},{8,72},{9,... | collective-permute-start | bytes 1597448 | tf_op jit(solution)/shard_map/ppermute | solution.py:109
  77.4 6.0 %collective-permute-start.6 = (f32[64,1040]{1,0:T(8,128)S(1)}, f32[64,1040]{1,0:T(8,128)S(1)}, u32[]{:S(2)}, u32[]{:S(2)}) collective-permute-start(f32[64,1040]{1,0:T(8,128)S(1)} %slice_select_fusion.2), channel_id=1, source_target_pairs={{0,8},{1,9},{2,10},{3,11},{4,12},{5,13},{6,14},{7,15},{8,0},{9,1},... | collective-permute-start | bytes 798728 | tf_op jit(solution)/shard_map/ppermute | solution.py:109
  83.4 4.1 %collective-permute-start.7 = (f32[32,1040]{1,0:T(8,128)S(1)}, f32[32,1040]{1,0:T(8,128)S(1)}, u32[]{:S(2)}, u32[]{:S(2)}) collective-permute-start(f32[32,1040]{1,0:T(8,128)S(1)} %slice_select_fusion.3), channel_id=1, source_target_pairs={{0,1},{1,0},{2,3},{3,2},{4,5},{5,4},{6,7},{7,6},{8,9},{9,8},{10,11... | collective-permute-start | bytes 399368 | tf_op jit(solution)/shard_map/ppermute | solution.py:109
  87.5 5.6 %collective-permute-start.8 = (f32[32,1040]{1,0:T(8,128)S(1)}, f32[32,1040]{1,0:T(8,128)S(1)}, u32[]{:S(2)}, u32[]{:S(2)}) collective-permute-start(f32[32,1040]{1,0:T(8,128)S(1)} %select_add_fusion.3), channel_id=1, source_target_pairs={{0,128},{1,129},{2,130},{3,131},{4,132},{5,133},{6,134},{7,135},{8... | collective-permute-start | bytes 399368 | tf_op jit(solution)/shard_map/ppermute | solution.py:112
  93.1 6.7 %collective-permute-start.9 = (f32[32,1040]{1,0:T(8,128)S(1)}, f32[32,1040]{1,0:T(8,128)S(1)}, u32[]{:S(2)}, u32[]{:S(2)}) collective-permute-start(f32[32,1040]{1,0:T(8,128)S(1)} %add.252), channel_id=1, source_target_pairs={{0,16},{1,17},{2,18},{3,19},{4,20},{5,21},{6,22},{7,23},{8,24},{9,... | collective-permute-start | bytes 399368 | tf_op jit(solution)/shard_map/ppermute | solution.py:112
  99.9 5.6 %collective-permute-start.10 = (f32[32,1040]{1,0:T(8,128)S(1)}, f32[32,1040]{1,0:T(8,128)S(1)}, u32[]{:S(2)}, u32[]{:S(2)}) collective-permute-start(f32[32,1040]{1,0:T(8,128)S(1)} %add.253), channel_id=1, source_target_pairs={{0,2},{1,3},{2,0},{3,1},{4,6},{5,7},{6,4},{7,5},{8,10},{9,11},{10,... | collective-permute-start | bytes 399368 | tf_op jit(solution)/shard_map/ppermute | solution.py:112
  105.5 10.5 %collective-permute-start.11 = (f32[32,1040]{1,0:T(8,128)S(1)}, f32[32,1040]{1,0:T(8,128)S(1)}, u32[]{:S(2)}, u32[]{:S(2)}) collective-permute-start(f32[32,1040]{1,0:T(8,128)S(1)} %add.254), channel_id=1, source_target_pairs={{0,4},{1,5},{2,6},{3,7},{4,0},{5,1},{6,2},{7,3},{8,12},{9,13},{10,... | collective-permute-start | bytes 399368 | tf_op jit(solution)/shard_map/ppermute | solution.py:112
  116.0 3.3 %collective-permute-start.12 = (bf16[32,1040]{1,0:T(8,128)(2,1)S(1)}, bf16[32,1040]{1,0:T(8,128)(2,1)S(1)}, u32[]{:S(2)}, u32[]{:S(2)}) collective-permute-start(bf16[32,1040]{1,0:T(8,128)(2,1)S(1)} %add_convert_fusion.1), channel_id=1, source_target_pairs={{0,1},{1,0},{2,3},{3,2},{4,5},{5,4},{6,7},{7,6},{8,9},{9,8},{10,11... | collective-permute-start | bytes 199688 | tf_op jit(solution)/shard_map/ppermute | solution.py:116
  119.3 5.9 %collective-permute-start.13 = (bf16[64,1040]{1,0:T(8,128)(2,1)S(1)}, bf16[64,1040]{1,0:T(8,128)(2,1)S(1)}, u32[]{:S(2)}, u32[]{:S(2)}) collective-permute-start(bf16[64,1040]{1,0:T(8,128)(2,1)S(1)} %pad_maximum_fusion.3), channel_id=1, source_target_pairs={{0,8},{1,9},{2,10},{3,11},{4,12},{5,13},{6,14},{7,15},{8,0},{9,1},... | collective-permute-start | bytes 399368 | tf_op jit(solution)/shard_map/ppermute | solution.py:116
  125.3 5.7 %collective-permute-start.14 = (bf16[128,1040]{1,0:T(8,128)(2,1)S(1)}, bf16[128,1040]{1,0:T(8,128)(2,1)S(1)}, u32[]{:S(2)}, u32[]{:S(2)}) collective-permute-start(bf16[128,1040]{1,0:T(8,128)(2,1)S(1)} %pad_maximum_fusion.2), channel_id=1, source_target_pairs={{0,64},{1,65},{2,66},{3,67},{4,68},{5,69},{6,70},{7,71},{8,72},{9,... | collective-permute-start | bytes 798728 | tf_op jit(solution)/shard_map/ppermute | solution.py:116
  131.4 12.2 %collective-permute-start.15 = (bf16[256,1040]{0,1:T(8,128)(2,1)S(1)}, bf16[256,1040]{0,1:T(8,128)(2,1)S(1)}, u32[]{:S(2)}, u32[]{:S(2)}) collective-permute-start(bf16[256,1040]{0,1:T(8,128)(2,1)S(1)} %copy.21), channel_id=1, source_target_pairs={{0,32},{1,33},{2,34},{3,35},{4,36},{5,37},{6,38},{7,39},{8,40},{9,... | collective-permute-start | bytes 1597448 | tf_op jit(solution)/shard_map/ppermute | solution.py:116

commit v9 on v8

--- a/solution.py
+++ b/solution.py
@@ -163,13 +163,16 @@
     sizes = {"region": lax.axis_size("region"), "dp": lax.axis_size("dp")}
     feats, hid = grad_own.shape
     rows = 2 * feats
+    head = grad_head.reshape(rows, -1)
+    lanes = 128
+    spare = jnp.zeros((rows, lanes - head.shape[1]), jnp.float32)
     packed = jnp.concatenate(
-        [jnp.concatenate([grad_own, grad_side], axis=0), grad_head.reshape(rows, -1)], axis=1
+        [jnp.concatenate([grad_own, grad_side], axis=0), head, spare], axis=1
     )
     packed = all_sum(packed, sizes, 4)
     packed = packed.astype(jnp.float32)
     grad_own, grad_side = packed[:feats, :hid], packed[feats:, :hid]
-    grad_head = packed[:, hid:].reshape(hid, -1)
+    grad_head = packed[:, hid : hid + head.shape[1]].reshape(hid, -1)
     return (scores, grad_own, grad_side, grad_head)
 
 

time: 149 us -> 145 us (0.973)
  local copies, waits for them, and re-layouts: 14.2 us -> 10.6 us
  matrix products: 5.47 us -> 3.52 us
    ppermute x3 -> x0, local copies, waits for them, and re-layouts: 3.15 us -> none  [the longest x2 2.85 us: all_sum(): got = lax.ppermute(jnp.where(upper, low, high), axes, perm)]
    select_n x2 -> x0, local copies, waits for them, and re-layouts: 2.79 us -> none  [all_sum(): got = lax.ppermute(jnp.where(upper, low, high), axes, perm)]
    concatenate x1, local copies, waits for them, and re-layouts: 0.22 us -> 2.57 us  [local(): jnp.concatenate([jnp.concatenate([grad_own, grad_side], axis=0), head, sp...]
where the time goes in v9:
time: 145 us
  waiting for transfers between devices  55.7 us (38%)
  starting transfers between devices  44.2 us (30%)
  Pallas kernels  18.9 us (13%)
  other arithmetic  10.9 us (8%)
  local copies, waits for them, and re-layouts  10.6 us (7%)
  matrix products  3.52 us (2%)
    ppermute x4, waiting for transfers between devices, all_sum(): got = lax.ppermute(jnp.where(upper, low, high), axes, perm)  19.6 us
    pallas_call x1, Pallas kernels, accumulate(): pl.pallas_call(pooled_sums_kernel, grid=(length // block,), in_specs=[pl....  18.9 us
    ppermute x4, starting transfers between devices, all_sum(): value = value + lax.ppermute(value, axes, perm)  14.2 us
    ppermute x4, starting transfers between devices, all_sum(): got = lax.ppermute(value, axes, perm)  13.8 us
    ppermute x4, waiting for transfers between devices, all_sum(): value = value + lax.ppermute(value, axes, perm)  13.8 us
    ppermute x4, waiting for transfers between devices, all_sum(): got = lax.ppermute(value, axes, perm)  13.7 us
    ppermute x2, starting transfers between devices, passed_along(): lax.ppermute(value, axis, [(source, source + steps) for source in range(i...  7.03 us
    ppermute x2, waiting for transfers between devices, passed_along(): lax.ppermute(value, axis, [(source, source + steps) for source in range(i...  4.64 us
  transfers between devices with their start and end apart: 16, of which 15 were waited for; matrix products, arithmetic and copies ran while one was open for 0% of the time, Pallas kernels for 0%

profile of v9, /device:TPU:1, one launch (start us, length us, event | category | flops | bytes accessed | tf_op | source)
XLA Modules:
  0.0 144.8 jit_solution(10823469168555067245)
XLA Ops:
  0.6 0.0 copy-start
  0.6 1.0 reduce-precision_subtract_fusion
  1.7 1.5 %broadcast_subtract_fusion.ids_ref = s32[1,16384]{1,0:T(1,128)} fusion(s32[1,16384]{1,0:T(1,128)} %param.10, s32[]{:T(128)S(6)} %mul.20), kind=kLoop, calls=%fused_computation.66 | loop fusion | flops 16384 | bytes 131076 | tf_op jit(solution)/shard_map/sub | solution.py:127
  3.2 1.9 %stack.10.split_ref = f32[8,16384]{1,0:T(8,128)} concatenate(f32[1,16384]{1,0:T(1,128)S(1)} %get-tuple-element.25, f32[1,16384]{1,0:T(1,128)S(1)} %get-tuple-element.26, f32[1,16384]{1,0:T(1,128)S(1)} %get-tuple-element.24, f32[1,16384]{1,0:T(1,128)} %param.9, f32[4,16384]{1,0:T(4,128)S(1)} %stack.4), dimensions={0} | concatenate | bytes 1048576 | tf_op jit(solution)/shard_map/stack | solution.py:56
  5.1 18.9 %shard_map.111 = f32[768,384]{1,0:T(8,128)} custom-call(s32[1,16384]{1,0:T(1,128)} %broadcast_subtract_fusion.ids_ref, f32[8,16384]{1,0:T(8,128)} %stack.10.split_ref, bf16[16384,256]{1,0:T(8,128)(2,1)} %bitcast.45), custom_call_target="tpu_custom_call" | custom-call | flops 9663676416 | bytes 10158080 | tf_op jit(solution)/shard_map/pallas_call | solution.py:59
  24.0 1.2 fusion.28
  25.2 5.1 %collective-permute-start = (f32[256,384]{1,0:T(8,128)S(1)}, f32[256,384]{1,0:T(8,128)S(1)}, u32[]{:S(2)}, u32[]{:S(2)}) collective-permute-start(f32[256,384]{1,0:T(8,128)S(1)} %get-tuple-element.16), channel_id=1, source_target_pairs={{32,0},{64,32},{96,64},{128,96},{160,128},{192,160},{224,192},{33,... | collective-permute-start | bytes 1179656 | tf_op jit(solution)/shard_map/ppermute | solution.py:11
  30.3 1.9 %collective-permute-start.1 = (f32[256,384]{1,0:T(8,128)S(1)}, f32[256,384]{1,0:T(8,128)S(1)}, u32[]{:S(2)}, u32[]{:S(2)}) collective-permute-start(f32[256,384]{1,0:T(8,128)S(1)} %get-tuple-element.17), channel_id=1, source_target_pairs={{0,32},{32,64},{64,96},{96,128},{128,160},{160,192},{192,224},{1,3... | collective-permute-start | bytes 1179656 | tf_op jit(solution)/shard_map/ppermute | solution.py:11
  32.3 2.8 %collective-permute-done = f32[256,384]{1,0:T(8,128)S(1)} collective-permute-done((f32[256,384]{1,0:T(8,128)S(1)}, f32[256,384]{1,0:T(8,128)S(1)}, u32[]{:S(2)}, u32[]{:S(2)}) %collective-permute-start) | collective-permute-done | bytes 393248 | tf_op jit(solution)/shard_map/ppermute | solution.py:11
  35.2 1.8 %collective-permute-done.1 = f32[256,384]{1,0:T(8,128)S(1)} collective-permute-done((f32[256,384]{1,0:T(8,128)S(1)}, f32[256,384]{1,0:T(8,128)S(1)}, u32[]{:S(2)}, u32[]{:S(2)}) %collective-permute-start.1) | collective-permute-done | bytes 393248 | tf_op jit(solution)/shard_map/ppermute | solution.py:11
  37.0 1.1 fusion.6
  38.0 0.2 fusion.20
  38.2 0.1 fusion.19
  38.4 4.4 %collective-permute-start.2 = (bf16[1,256,256]{2,1,0:T(8,128)(2,1)S(1)}, bf16[1,256,256]{2,1,0:T(8,128)(2,1)S(1)}, u32[]{:S(2)}, u32[]{:S(2)}) collective-permute-start(bf16[1,256,256]{2,1,0:T(8,128)(2,1)S(1)} %fusion.19), channel_id=1, source_target_pairs={{0,32},{32,64},{64,96},{96,128},{128,160},{160,192},{192,224},{1,3... | collective-permute-start | bytes 393224 | tf_op jit(solution)/shard_map/ppermute | solution.py:19
  42.8 1.9 %collective-permute-start.3 = (bf16[1,256,256]{2,1,0:T(8,128)(2,1)S(1)}, bf16[1,256,256]{2,1,0:T(8,128)(2,1)S(1)}, u32[]{:S(2)}, u32[]{:S(2)}) collective-permute-start(bf16[1,256,256]{2,1,0:T(8,128)(2,1)S(1)} %fusion.19), channel_id=1, source_target_pairs={{32,0},{64,32},{96,64},{128,96},{160,128},{192,160},{224,192},{33,... | collective-permute-start | bytes 393224 | tf_op jit(solution)/shard_map/ppermute | solution.py:22
  44.7 0.3 fusion.23
  45.0 4.0 %collective-permute-done.3 = bf16[1,256,256]{2,1,0:T(8,128)(2,1)S(1)} collective-permute-done((bf16[1,256,256]{2,1,0:T(8,128)(2,1)S(1)}, bf16[1,256,256]{2,1,0:T(8,128)(2,1)S(1)}, u32[]{:S(2)}, u32[]{:S(2)}) %collective-permute-start.3) | collective-permute-done | bytes 131104 | tf_op jit(solution)/shard_map/ppermute | solution.py:22
  49.0 1.0 fusion.2
  50.0 0.5 multiply_convert_fusion
  50.5 0.2 copy-done.4
  50.7 0.2 fusion.30
  51.0 0.4 fusion.26
  51.4 0.5 fusion.1
  51.9 0.3 fusion.21
  52.2 0.3 fusion.31
  52.6 0.1 reshape.545
  52.7 1.5 %pad_maximum_fusion = f32[512,1024]{1,0:T(8,128)} fusion(f32[256,1024]{1,0:T(8,128)S(1)} %fusion.31, f32[256,1024]{1,0:T(8,128)S(1)} %fusion.21), kind=kLoop, calls=%fused_computation | loop fusion | flops 524288 | bytes 4194304 | tf_op jit(solution)/shard_map/concatenate | solution.py:170
  54.2 2.6 %concatenate.23 = f32[512,1152]{1,0:T(8,128)S(1)} concatenate(f32[512,1024]{1,0:T(8,128)} %pad_maximum_fusion, f32[512,16]{1,0:T(8,128)S(1)} %reshape.545, f32[512,112]{1,0:T(8,128)S(1)} %broadcast_in_dim.5), dimensions={1} | concatenate | bytes 4718592 | tf_op jit(solution)/shard_map/concatenate | solution.py:169
  56.8 1.2 slice_select_fusion
  57.9 3.2 %collective-permute-done.4 = f32[256,1152]{1,0:T(8,128)} collective-permute-done((f32[256,1152]{1,0:T(8,128)}, f32[256,1152]{1,0:T(8,128)}, u32[]{:S(2)}, u32[]{:S(2)}) %collective-permute-start.4) | collective-permute-done | bytes 1179680 | tf_op jit(solution)/shard_map/ppermute | solution.py:109
  61.1 1.4 select_add_fusion
  62.6 1.0 copy-done.1
  63.6 0.1 slice_select_fusion.1
  63.7 0.8 collective-permute-start.5
  64.4 8.3 %collective-permute-done.5 = f32[128,1152]{1,0:T(8,128)S(1)} collective-permute-done((f32[128,1152]{1,0:T(8,128)S(1)}, f32[128,1152]{1,0:T(8,128)S(1)}, u32[]{:S(2)}, u32[]{:S(2)}) %collective-permute-start.5) | collective-permute-done | bytes 589856 | tf_op jit(solution)/shard_map/ppermute | solution.py:109
  72.8 1.3 select_add_fusion.1
  74.1 1.1 collective-permute-start.6
  75.3 4.8 %collective-permute-done.6 = f32[64,1152]{1,0:T(8,128)S(1)} collective-permute-done((f32[64,1152]{1,0:T(8,128)S(1)}, f32[64,1152]{1,0:T(8,128)S(1)}, u32[]{:S(2)}, u32[]{:S(2)}) %collective-permute-start.6) | collective-permute-done | bytes 294944 | tf_op jit(solution)/shard_map/ppermute | solution.py:109
  80.2 0.9 collective-permute-start.7
  81.0 3.2 %collective-permute-done.7 = f32[32,1152]{1,0:T(8,128)S(1)} collective-permute-done((f32[32,1152]{1,0:T(8,128)S(1)}, f32[32,1152]{1,0:T(8,128)S(1)}, u32[]{:S(2)}, u32[]{:S(2)}) %collective-permute-start.7) | collective-permute-done | bytes 147488 | tf_op jit(solution)/shard_map/ppermute | solution.py:109
  84.3 2.6 %collective-permute-start.8 = (f32[32,1152]{1,0:T(8,128)S(1)}, f32[32,1152]{1,0:T(8,128)S(1)}, u32[]{:S(2)}, u32[]{:S(2)}) collective-permute-start(f32[32,1152]{1,0:T(8,128)S(1)} %select_add_fusion.3), channel_id=1, source_target_pairs={{0,128},{1,129},{2,130},{3,131},{4,132},{5,133},{6,134},{7,135},{8... | collective-permute-start | bytes 442376 | tf_op jit(solution)/shard_map/ppermute | solution.py:112
  86.9 3.0 %collective-permute-done.8 = f32[32,1152]{1,0:T(8,128)S(1)} collective-permute-done((f32[32,1152]{1,0:T(8,128)S(1)}, f32[32,1152]{1,0:T(8,128)S(1)}, u32[]{:S(2)}, u32[]{:S(2)}) %collective-permute-start.8) | collective-permute-done | bytes 147488 | tf_op jit(solution)/shard_map/ppermute | solution.py:112
  89.9 2.7 %collective-permute-start.9 = (f32[32,1152]{1,0:T(8,128)S(1)}, f32[32,1152]{1,0:T(8,128)S(1)}, u32[]{:S(2)}, u32[]{:S(2)}) collective-permute-start(f32[32,1152]{1,0:T(8,128)S(1)} %add.252), channel_id=1, source_target_pairs={{0,16},{1,17},{2,18},{3,19},{4,20},{5,21},{6,22},{7,23},{8,24},{9,... | collective-permute-start | bytes 442376 | tf_op jit(solution)/shard_map/ppermute | solution.py:112
  92.5 4.1 %collective-permute-done.9 = f32[32,1152]{1,0:T(8,128)S(1)} collective-permute-done((f32[32,1152]{1,0:T(8,128)S(1)}, f32[32,1152]{1,0:T(8,128)S(1)}, u32[]{:S(2)}, u32[]{:S(2)}) %collective-permute-start.9) | collective-permute-done | bytes 147488 | tf_op jit(solution)/shard_map/ppermute | solution.py:112
  96.7 2.8 %collective-permute-start.10 = (f32[32,1152]{1,0:T(8,128)S(1)}, f32[32,1152]{1,0:T(8,128)S(1)}, u32[]{:S(2)}, u32[]{:S(2)}) collective-permute-start(f32[32,1152]{1,0:T(8,128)S(1)} %add.253), channel_id=1, source_target_pairs={{0,2},{1,3},{2,0},{3,1},{4,6},{5,7},{6,4},{7,5},{8,10},{9,11},{10,... | collective-permute-start | bytes 442376 | tf_op jit(solution)/shard_map/ppermute | solution.py:112
  99.5 2.8 %collective-permute-done.10 = f32[32,1152]{1,0:T(8,128)S(1)} collective-permute-done((f32[32,1152]{1,0:T(8,128)S(1)}, f32[32,1152]{1,0:T(8,128)S(1)}, u32[]{:S(2)}, u32[]{:S(2)}) %collective-permute-start.10) | collective-permute-done | bytes 147488 | tf_op jit(solution)/shard_map/ppermute | solution.py:112
  102.3 6.2 %collective-permute-start.11 = (f32[32,1152]{1,0:T(8,128)S(1)}, f32[32,1152]{1,0:T(8,128)S(1)}, u32[]{:S(2)}, u32[]{:S(2)}) collective-permute-start(f32[32,1152]{1,0:T(8,128)S(1)} %add.254), channel_id=1, source_target_pairs={{0,4},{1,5},{2,6},{3,7},{4,0},{5,1},{6,2},{7,3},{8,12},{9,13},{10,... | collective-permute-start | bytes 442376 | tf_op jit(solution)/shard_map/ppermute | solution.py:112
  108.5 3.9 %collective-permute-done.11 = f32[32,1152]{1,0:T(8,128)S(1)} collective-permute-done((f32[32,1152]{1,0:T(8,128)S(1)}, f32[32,1152]{1,0:T(8,128)S(1)}, u32[]{:S(2)}, u32[]{:S(2)}) %collective-permute-start.11) | collective-permute-done | bytes 147488 | tf_op jit(solution)/shard_map/ppermute | solution.py:112
  112.3 1.5 %collective-permute-start.12 = (bf16[32,1152]{1,0:T(8,128)(2,1)S(1)}, bf16[32,1152]{1,0:T(8,128)(2,1)S(1)}, u32[]{:S(2)}, u32[]{:S(2)}) collective-permute-start(bf16[32,1152]{1,0:T(8,128)(2,1)S(1)} %add_convert_fusion.1), channel_id=1, source_target_pairs={{0,1},{1,0},{2,3},{3,2},{4,5},{5,4},{6,7},{7,6},{8,9},{9,8},{10,11... | collective-permute-start | bytes 221192 | tf_op jit(solution)/shard_map/ppermute | solution.py:116
  113.9 2.0 %collective-permute-done.12 = bf16[32,1152]{1,0:T(8,128)(2,1)S(1)} collective-permute-done((bf16[32,1152]{1,0:T(8,128)(2,1)S(1)}, bf16[32,1152]{1,0:T(8,128)(2,1)S(1)}, u32[]{:S(2)}, u32[]{:S(2)}) %collective-permute-start.12) | collective-permute-done | bytes 73760 | tf_op jit(solution)/shard_map/ppermute | solution.py:116
  115.9 0.1 collective-permute-start.13
  116.0 5.8 %collective-permute-done.13 = bf16[64,1152]{1,0:T(8,128)(2,1)S(1)} collective-permute-done((bf16[64,1152]{1,0:T(8,128)(2,1)S(1)}, bf16[64,1152]{1,0:T(8,128)(2,1)S(1)}, u32[]{:S(2)}, u32[]{:S(2)}) %collective-permute-start.13) | collective-permute-done | bytes 147488 | tf_op jit(solution)/shard_map/ppermute | solution.py:116
  121.8 0.1 broadcast_select_fusion.5
  121.9 1.4 collective-permute-start.14
  123.3 4.3 %collective-permute-done.14 = bf16[128,1152]{1,0:T(8,128)(2,1)S(1)} collective-permute-done((bf16[128,1152]{1,0:T(8,128)(2,1)S(1)}, bf16[128,1152]{1,0:T(8,128)(2,1)S(1)}, u32[]{:S(2)}, u32[]{:S(2)}) %collective-permute-start.14) | collective-permute-done | bytes 294944 | tf_op jit(solution)/shard_map/ppermute | solution.py:116
  127.5 0.1 broadcast_select_fusion.3
  127.7 10.8 %collective-permute-start.15 = (bf16[256,1152]{1,0:T(8,128)(2,1)S(1)}, bf16[256,1152]{1,0:T(8,128)(2,1)S(1)}, u32[]{:S(2)}, u32[]{:S(2)}) collective-permute-start(bf16[256,1152]{1,0:T(8,128)(2,1)S(1)} %pad_maximum_fusion.1), channel_id=1, source_target_pairs={{0,32},{1,33},{2,34},{3,35},{4,36},{5,37},{6,38},{7,39},{8,40},{9,... | collective-permute-start | bytes 1769480 | tf_op jit(solution)/shard_map/ppermute | solution.py:116
  138.5 1.6 %collective-permute-done.15 = bf16[256,1152]{1,0:T(8,128)(2,1)S(1)} collective-permute-done((bf16[256,1152]{1,0:T(8,128)(2,1)S(1)}, bf16[256,1152]{1,0:T(8,128)(2,1)S(1)}, u32[]{:S(2)}, u32[]{:S(2)}) %collective-permute-start.15) | collective-permute-done | bytes 589856 | tf_op jit(solution)/shard_map/ppermute | solution.py:116
  140.2 0.2 broadcast_select_fusion.1
  140.4 0.7 maximum_convert_fusion.1
  141.1 0.2 maximum_convert_fusion
  141.3 1.1 reshape.546
  142.4 0.8 copy.15
  143.2 1.6 %fusion.27 = (f32[256,1024]{1,0:T(8,128)}, f32[256,1024]{1,0:T(8,128)}) fusion(f32[512,1152]{1,0:T(8,128)S(1)} %maximum_convert_fusion), kind=kLoop, calls=%fused_computation.74 | loop fusion | bytes 4194304 | tf_op jit(solution)/shard_map/slice | solution.py:174
  (29 shorter events, 0.4 us)
Async XLA Ops:
  0.6 49.4 %copy-start = (bf16[256,1024]{1,0:T(8,128)(2,1)S(1)}, bf16[256,1024]{1,0:T(8,128)(2,1)}, u32[]{:S(2)}) copy-start(bf16[256,1024]{1,0:T(8,128)(2,1)} %param.14) | copy-start | bytes 1572868
  24.0 8.2 %copy-start.5 = (s32[1,256,8]{1,2,0:T(8,128)S(1)}, s32[1,256,8]{1,2,0:T(8,128)}, u32[]{:S(2)}) copy-start(s32[1,256,8]{1,2,0:T(8,128)} %param.11) | copy-start | bytes 24580
  25.2 10.0 %collective-permute-start = (f32[256,384]{1,0:T(8,128)S(1)}, f32[256,384]{1,0:T(8,128)S(1)}, u32[]{:S(2)}, u32[]{:S(2)}) collective-permute-start(f32[256,384]{1,0:T(8,128)S(1)} %get-tuple-element.16), channel_id=1, source_target_pairs={{32,0},{64,32},{96,64},{128,96},{160,128},{192,160},{224,192},{33,... | collective-permute-start | bytes 1179656 | tf_op jit(solution)/shard_map/ppermute | solution.py:11
  30.3 6.6 %collective-permute-start.1 = (f32[256,384]{1,0:T(8,128)S(1)}, f32[256,384]{1,0:T(8,128)S(1)}, u32[]{:S(2)}, u32[]{:S(2)}) collective-permute-start(f32[256,384]{1,0:T(8,128)S(1)} %get-tuple-element.17), channel_id=1, source_target_pairs={{0,32},{32,64},{64,96},{96,128},{128,160},{160,192},{192,224},{1,3... | collective-permute-start | bytes 1179656 | tf_op jit(solution)/shard_map/ppermute | solution.py:11
  32.3 12.4 %copy-start.2 = (bf16[256,1024]{1,0:T(8,128)(2,1)S(1)}, bf16[256,1024]{1,0:T(8,128)(2,1)}, u32[]{:S(2)}) copy-start(bf16[256,1024]{1,0:T(8,128)(2,1)} %param.13) | copy-start | bytes 1572868
  38.4 6.6 %collective-permute-start.2 = (bf16[1,256,256]{2,1,0:T(8,128)(2,1)S(1)}, bf16[1,256,256]{2,1,0:T(8,128)(2,1)S(1)}, u32[]{:S(2)}, u32[]{:S(2)}) collective-permute-start(bf16[1,256,256]{2,1,0:T(8,128)(2,1)S(1)} %fusion.19), channel_id=1, source_target_pairs={{0,32},{32,64},{64,96},{96,128},{128,160},{160,192},{192,224},{1,3... | collective-permute-start | bytes 393224 | tf_op jit(solution)/shard_map/ppermute | solution.py:19
  42.8 6.3 %collective-permute-start.3 = (bf16[1,256,256]{2,1,0:T(8,128)(2,1)S(1)}, bf16[1,256,256]{2,1,0:T(8,128)(2,1)S(1)}, u32[]{:S(2)}, u32[]{:S(2)}) collective-permute-start(bf16[1,256,256]{2,1,0:T(8,128)(2,1)S(1)} %fusion.19), channel_id=1, source_target_pairs={{32,0},{64,32},{96,64},{128,96},{160,128},{192,160},{224,192},{33,... | collective-permute-start | bytes 393224 | tf_op jit(solution)/shard_map/ppermute | solution.py:22
  50.0 0.7 copy-start.4
  50.0 0.9 copy-start.6
  51.0 0.9 copy-start.3
  57.9 3.2 %collective-permute-start.4 = (f32[256,1152]{1,0:T(8,128)}, f32[256,1152]{1,0:T(8,128)}, u32[]{:S(2)}, u32[]{:S(2)}) collective-permute-start(f32[256,1152]{1,0:T(8,128)} %slice_select_fusion), channel_id=1, source_target_pairs={{0,32},{1,33},{2,34},{3,35},{4,36},{5,37},{6,38},{7,39},{8,40},{9,... | collective-permute-start | bytes 3538952 | tf_op jit(solution)/shard_map/ppermute | solution.py:109
  62.6 1.0 copy-start.1
  63.7 9.1 %collective-permute-start.5 = (f32[128,1152]{1,0:T(8,128)S(1)}, f32[128,1152]{1,0:T(8,128)S(1)}, u32[]{:S(2)}, u32[]{:S(2)}) collective-permute-start(f32[128,1152]{1,0:T(8,128)S(1)} %slice_select_fusion.1), channel_id=1, source_target_pairs={{0,64},{1,65},{2,66},{3,67},{4,68},{5,69},{6,70},{7,71},{8,72},{9,... | collective-permute-start | bytes 1769480 | tf_op jit(solution)/shard_map/ppermute | solution.py:109
  74.1 6.0 %collective-permute-start.6 = (f32[64,1152]{1,0:T(8,128)S(1)}, f32[64,1152]{1,0:T(8,128)S(1)}, u32[]{:S(2)}, u32[]{:S(2)}) collective-permute-start(f32[64,1152]{1,0:T(8,128)S(1)} %slice_select_fusion.2), channel_id=1, source_target_pairs={{0,8},{1,9},{2,10},{3,11},{4,12},{5,13},{6,14},{7,15},{8,0},{9,1},... | collective-permute-start | bytes 884744 | tf_op jit(solution)/shard_map/ppermute | solution.py:109
  80.2 4.1 %collective-permute-start.7 = (f32[32,1152]{1,0:T(8,128)S(1)}, f32[32,1152]{1,0:T(8,128)S(1)}, u32[]{:S(2)}, u32[]{:S(2)}) collective-permute-start(f32[32,1152]{1,0:T(8,128)S(1)} %slice_select_fusion.3), channel_id=1, source_target_pairs={{0,1},{1,0},{2,3},{3,2},{4,5},{5,4},{6,7},{7,6},{8,9},{9,8},{10,11... | collective-permute-start | bytes 442376 | tf_op jit(solution)/shard_map/ppermute | solution.py:109
  84.3 5.6 %collective-permute-start.8 = (f32[32,1152]{1,0:T(8,128)S(1)}, f32[32,1152]{1,0:T(8,128)S(1)}, u32[]{:S(2)}, u32[]{:S(2)}) collective-permute-start(f32[32,1152]{1,0:T(8,128)S(1)} %select_add_fusion.3), channel_id=1, source_target_pairs={{0,128},{1,129},{2,130},{3,131},{4,132},{5,133},{6,134},{7,135},{8... | collective-permute-start | bytes 442376 | tf_op jit(solution)/shard_map/ppermute | solution.py:112
  89.9 6.8 %collective-permute-start.9 = (f32[32,1152]{1,0:T(8,128)S(1)}, f32[32,1152]{1,0:T(8,128)S(1)}, u32[]{:S(2)}, u32[]{:S(2)}) collective-permute-start(f32[32,1152]{1,0:T(8,128)S(1)} %add.252), channel_id=1, source_target_pairs={{0,16},{1,17},{2,18},{3,19},{4,20},{5,21},{6,22},{7,23},{8,24},{9,... | collective-permute-start | bytes 442376 | tf_op jit(solution)/shard_map/ppermute | solution.py:112
  96.7 5.6 %collective-permute-start.10 = (f32[32,1152]{1,0:T(8,128)S(1)}, f32[32,1152]{1,0:T(8,128)S(1)}, u32[]{:S(2)}, u32[]{:S(2)}) collective-permute-start(f32[32,1152]{1,0:T(8,128)S(1)} %add.253), channel_id=1, source_target_pairs={{0,2},{1,3},{2,0},{3,1},{4,6},{5,7},{6,4},{7,5},{8,10},{9,11},{10,... | collective-permute-start | bytes 442376 | tf_op jit(solution)/shard_map/ppermute | solution.py:112
  102.3 10.0 %collective-permute-start.11 = (f32[32,1152]{1,0:T(8,128)S(1)}, f32[32,1152]{1,0:T(8,128)S(1)}, u32[]{:S(2)}, u32[]{:S(2)}) collective-permute-start(f32[32,1152]{1,0:T(8,128)S(1)} %add.254), channel_id=1, source_target_pairs={{0,4},{1,5},{2,6},{3,7},{4,0},{5,1},{6,2},{7,3},{8,12},{9,13},{10,... | collective-permute-start | bytes 442376 | tf_op jit(solution)/shard_map/ppermute | solution.py:112
  112.3 3.5 %collective-permute-start.12 = (bf16[32,1152]{1,0:T(8,128)(2,1)S(1)}, bf16[32,1152]{1,0:T(8,128)(2,1)S(1)}, u32[]{:S(2)}, u32[]{:S(2)}) collective-permute-start(bf16[32,1152]{1,0:T(8,128)(2,1)S(1)} %add_convert_fusion.1), channel_id=1, source_target_pairs={{0,1},{1,0},{2,3},{3,2},{4,5},{5,4},{6,7},{7,6},{8,9},{9,8},{10,11... | collective-permute-start | bytes 221192 | tf_op jit(solution)/shard_map/ppermute | solution.py:116
  115.9 5.9 %collective-permute-start.13 = (bf16[64,1152]{1,0:T(8,128)(2,1)S(1)}, bf16[64,1152]{1,0:T(8,128)(2,1)S(1)}, u32[]{:S(2)}, u32[]{:S(2)}) collective-permute-start(bf16[64,1152]{1,0:T(8,128)(2,1)S(1)} %pad_maximum_fusion.3), channel_id=1, source_target_pairs={{0,8},{1,9},{2,10},{3,11},{4,12},{5,13},{6,14},{7,15},{8,0},{9,1},... | collective-permute-start | bytes 442376 | tf_op jit(solution)/shard_map/ppermute | solution.py:116
  121.9 5.7 %collective-permute-start.14 = (bf16[128,1152]{1,0:T(8,128)(2,1)S(1)}, bf16[128,1152]{1,0:T(8,128)(2,1)S(1)}, u32[]{:S(2)}, u32[]{:S(2)}) collective-permute-start(bf16[128,1152]{1,0:T(8,128)(2,1)S(1)} %pad_maximum_fusion.2), channel_id=1, source_target_pairs={{0,64},{1,65},{2,66},{3,67},{4,68},{5,69},{6,70},{7,71},{8,72},{9,... | collective-permute-start | bytes 884744 | tf_op jit(solution)/shard_map/ppermute | solution.py:116
  127.7 12.5 %collective-permute-start.15 = (bf16[256,1152]{1,0:T(8,128)(2,1)S(1)}, bf16[256,1152]{1,0:T(8,128)(2,1)S(1)}, u32[]{:S(2)}, u32[]{:S(2)}) collective-permute-start(bf16[256,1152]{1,0:T(8,128)(2,1)S(1)} %pad_maximum_fusion.1), channel_id=1, source_target_pairs={{0,32},{1,33},{2,34},{3,35},{4,36},{5,37},{6,38},{7,39},{8,40},{9,... | collective-permute-start | bytes 1769480 | tf_op jit(solution)/shard_map/ppermute | solution.py:116

commit v10 on v9

--- a/solution.py
+++ b/solution.py
@@ -24,7 +24,7 @@
     return block
 
 
-def pooled_sums_kernel(ids_ref, split_ref, cells_ref, sums_ref):
+def pooled_sums_kernel(offset_ref, ids_ref, weight_ref, cells_ref, sums_ref):
     @pl.when(pl.program_id(0) == 0)
     def _():
         sums_ref[...] = jnp.zeros_like(sums_ref)
@@ -33,45 +33,45 @@
     block = ids_ref.shape[1]
     feats = cells_ref.shape[1]
     lanes = sums_ref.shape[1] - feats
+    ids = ids_ref[...] - offset_ref[0:1, 0:1]
     slots = lax.broadcasted_iota(jnp.int32, (width, block), 0)
-    member = (ids_ref[...] == slots).astype(jnp.bfloat16)
-    split = split_ref[...]
-    pad = jnp.zeros((lanes - split.shape[0], block), jnp.float32)
-    columns = jnp.concatenate([split, pad], axis=0).T
+    member = (ids == slots).astype(jnp.bfloat16)
+    weight = weight_ref[...]
+    high = weight.astype(jnp.bfloat16).astype(jnp.float32)
+    rest = weight - high
+    middle = rest.astype(jnp.bfloat16).astype(jnp.float32)
+    low = rest - middle
+    pad = jnp.zeros((lanes - 4, block), jnp.float32)
+    columns = jnp.concatenate([high, middle, low, weight, pad], axis=0).T
     lane = lax.broadcasted_iota(jnp.int32, (block, lanes), 1)
     parts = jnp.where(lane < 3, columns, 0.0).astype(jnp.bfloat16)
-    weight = columns[:, 3:4]
-    weighted = (weight * cells_ref[...].astype(jnp.float32)).astype(jnp.bfloat16)
+    weighted = (columns[:, 3:4] * cells_ref[...].astype(jnp.float32)).astype(jnp.bfloat16)
     sums_ref[:, :feats] += jnp.dot(member, weighted, preferred_element_type=jnp.float32)
     sums_ref[:, feats:] += jnp.dot(member, parts, preferred_element_type=jnp.float32)
 
 
-def accumulate(cluster_ids, cells, weights, width):
+def accumulate(offset, cluster_ids, cells, weights, width):
     length, feats = cells.shape
-    high = lax.reduce_precision(weights, exponent_bits=8, mantissa_bits=7)
-    rest = weights - high
-    middle = lax.reduce_precision(rest, exponent_bits=8, mantissa_bits=7)
-    low = rest - middle
-    zero = jnp.zeros_like(weights)
-    split = jnp.stack([high, middle, low, weights, zero, zero, zero, zero], axis=0)
     block = min(2048, length)
     lanes = 128
+    offsets = jnp.full((8, lanes), offset, jnp.int32)
     sums = pl.pallas_call(
         pooled_sums_kernel,
         grid=(length // block,),
         in_specs=[
+            pl.BlockSpec((8, lanes), lambda i: (0, 0)),
             pl.BlockSpec((1, block), lambda i: (0, i)),
-            pl.BlockSpec((8, block), lambda i: (0, i)),
+            pl.BlockSpec((1, block), lambda i: (0, i)),
             pl.BlockSpec((block, feats), lambda i: (i, 0)),
         ],
         out_specs=pl.BlockSpec((width, feats + lanes), lambda i: (0, 0)),
         out_shape=jax.ShapeDtypeStruct((width, feats + lanes), jnp.float32),
         cost_estimate=pl.CostEstimate(
             flops=2 * width * length * (feats + lanes),
-            bytes_accessed=length * (feats * 2 + 36) + width * (feats + lanes) * 4,
+            bytes_accessed=length * (feats * 2 + 8) + width * (feats + lanes) * 4,
             transcendentals=0,
         ),
-    )(cluster_ids.reshape(1, length), split, cells)
+    )(offsets, cluster_ids.reshape(1, length), weights.reshape(1, length), cells)
     return sums
 
 
@@ -124,8 +124,7 @@
     region = lax.axis_index("region")
     owned = cluster_edges.shape[1]
     degree = cluster_edges.shape[2]
-    relative = cell_cluster - (region - 1) * owned
-    sums = accumulate(relative[0], cells[0], cell_weight[0], 3 * owned)
+    sums = accumulate((region - 1) * owned, cell_cluster[0], cells[0], cell_weight[0], 3 * owned)
     above = passed_along(sums[:owned], "region", -1)
     below = passed_along(sums[2 * owned :], "region", 1)
     total = (sums[owned : 2 * owned] + above + below)[None]

time: 145 us -> 141 us (0.972)
  other arithmetic: 10.9 us -> 8.42 us
    sub x2 -> x0, other arithmetic: 2.52 us -> none  [the longest x1 1.52 us: local(): relative = cell_cluster - (region - 1) * owned]
    another operation x2 -> x0, local copies, waits for them, and re-layouts: 1.95 us -> none  [accumulate(): jnp.stack([high, middle, low, weights, zero, zero, zero, zero], axis=0)]
where the time goes in v10:
time: 141 us
  waiting for transfers between devices  55.7 us (40%)
  starting transfers between devices  44 us (31%)
  Pallas kernels  19 us (13%)
  local copies, waits for them, and re-layouts  9.28 us (7%)
  other arithmetic  8.42 us (6%)
  matrix products  3.52 us (2%)
    ppermute x4, waiting for transfers between devices, all_sum(): got = lax.ppermute(jnp.where(upper, low, high), axes, perm)  19.6 us
    pallas_call x1, Pallas kernels, accumulate(): pl.pallas_call(pooled_sums_kernel, grid=(length // block,), in_specs=[pl....  19 us
    ppermute x4, starting transfers between devices, all_sum(): value = value + lax.ppermute(value, axes, perm)  14.2 us
    ppermute x4, waiting for transfers between devices, all_sum(): value = value + lax.ppermute(value, axes, perm)  13.8 us
    ppermute x4, starting transfers between devices, all_sum(): got = lax.ppermute(value, axes, perm)  13.7 us
    ppermute x4, waiting for transfers between devices, all_sum(): got = lax.ppermute(value, axes, perm)  13.6 us
    ppermute x2, starting transfers between devices, passed_along(): lax.ppermute(value, axis, [(source, source + steps) for source in range(i...  7.03 us
    ppermute x2, waiting for transfers between devices, passed_along(): lax.ppermute(value, axis, [(source, source + steps) for source in range(i...  4.64 us
  transfers between devices with their start and end apart: 16, of which 15 were waited for; matrix products, arithmetic and copies ran while one was open for 0% of the time, Pallas kernels for 0%

profile of v10, /device:TPU:1, one launch (start us, length us, event | category | flops | bytes accessed | tf_op | source)
XLA Modules:
  0.0 140.8 jit_solution(1969824288277232283)
XLA Ops:
  0.6 0.0 copy-start
  0.7 0.6 broadcast_in_dim.6.offset_ref
  1.2 19.0 %shard_map.111 = f32[768,384]{1,0:T(8,128)} custom-call(s32[8,128]{1,0:T(8,128)} %broadcast_in_dim.6.offset_ref, s32[1,16384]{1,0:T(1,128)} %ids_ref.1, f32[1,16384]{1,0:T(1,128)} %weight_ref.1, bf16[16384,256]{1,0:T(8,128)(2,1)} %bitcast.45), custom_call_target="tpu_custom_call" | custom-call | flops 9663676416 | bytes 9699328 | tf_op jit(solution)/shard_map/pallas_call | solution.py:58
  20.2 1.2 fusion.28
  21.4 5.1 %collective-permute-start = (f32[256,384]{1,0:T(8,128)S(1)}, f32[256,384]{1,0:T(8,128)S(1)}, u32[]{:S(2)}, u32[]{:S(2)}) collective-permute-start(f32[256,384]{1,0:T(8,128)S(1)} %get-tuple-element.16), channel_id=1, source_target_pairs={{32,0},{64,32},{96,64},{128,96},{160,128},{192,160},{224,192},{33,... | collective-permute-start | bytes 1179656 | tf_op jit(solution)/shard_map/ppermute | solution.py:11
  26.5 1.9 %collective-permute-start.1 = (f32[256,384]{1,0:T(8,128)S(1)}, f32[256,384]{1,0:T(8,128)S(1)}, u32[]{:S(2)}, u32[]{:S(2)}) collective-permute-start(f32[256,384]{1,0:T(8,128)S(1)} %get-tuple-element.17), channel_id=1, source_target_pairs={{0,32},{32,64},{64,96},{96,128},{128,160},{160,192},{192,224},{1,3... | collective-permute-start | bytes 1179656 | tf_op jit(solution)/shard_map/ppermute | solution.py:11
  28.5 0.0 copy-start.2
  28.5 2.8 %collective-permute-done = f32[256,384]{1,0:T(8,128)S(1)} collective-permute-done((f32[256,384]{1,0:T(8,128)S(1)}, f32[256,384]{1,0:T(8,128)S(1)}, u32[]{:S(2)}, u32[]{:S(2)}) %collective-permute-start) | collective-permute-done | bytes 393248 | tf_op jit(solution)/shard_map/ppermute | solution.py:11
  31.4 1.8 %collective-permute-done.1 = f32[256,384]{1,0:T(8,128)S(1)} collective-permute-done((f32[256,384]{1,0:T(8,128)S(1)}, f32[256,384]{1,0:T(8,128)S(1)}, u32[]{:S(2)}, u32[]{:S(2)}) %collective-permute-start.1) | collective-permute-done | bytes 393248 | tf_op jit(solution)/shard_map/ppermute | solution.py:11
  33.2 1.1 fusion.6
  34.2 0.2 fusion.20
  34.4 0.1 fusion.19
  34.6 4.4 %collective-permute-start.2 = (bf16[1,256,256]{2,1,0:T(8,128)(2,1)S(1)}, bf16[1,256,256]{2,1,0:T(8,128)(2,1)S(1)}, u32[]{:S(2)}, u32[]{:S(2)}) collective-permute-start(bf16[1,256,256]{2,1,0:T(8,128)(2,1)S(1)} %fusion.19), channel_id=1, source_target_pairs={{0,32},{32,64},{64,96},{96,128},{128,160},{160,192},{192,224},{1,3... | collective-permute-start | bytes 393224 | tf_op jit(solution)/shard_map/ppermute | solution.py:19
  39.0 1.9 %collective-permute-start.3 = (bf16[1,256,256]{2,1,0:T(8,128)(2,1)S(1)}, bf16[1,256,256]{2,1,0:T(8,128)(2,1)S(1)}, u32[]{:S(2)}, u32[]{:S(2)}) collective-permute-start(bf16[1,256,256]{2,1,0:T(8,128)(2,1)S(1)} %fusion.19), channel_id=1, source_target_pairs={{32,0},{64,32},{96,64},{128,96},{160,128},{192,160},{224,192},{33,... | collective-permute-start | bytes 393224 | tf_op jit(solution)/shard_map/ppermute | solution.py:22
  40.9 0.3 fusion.23
  41.2 4.0 %collective-permute-done.3 = bf16[1,256,256]{2,1,0:T(8,128)(2,1)S(1)} collective-permute-done((bf16[1,256,256]{2,1,0:T(8,128)(2,1)S(1)}, bf16[1,256,256]{2,1,0:T(8,128)(2,1)S(1)}, u32[]{:S(2)}, u32[]{:S(2)}) %collective-permute-start.3) | collective-permute-done | bytes 131104 | tf_op jit(solution)/shard_map/ppermute | solution.py:22
  45.2 1.0 fusion.2
  46.2 0.0 copy-start.4
  46.3 0.5 multiply_convert_fusion
  46.7 0.2 copy-done.4
  46.9 0.2 fusion.30
  47.2 0.4 fusion.26
  47.6 0.5 fusion.1
  48.1 0.3 fusion.21
  48.4 0.3 fusion.31
  48.8 0.1 reshape.545
  48.9 1.5 %pad_maximum_fusion = f32[512,1024]{1,0:T(8,128)} fusion(f32[256,1024]{1,0:T(8,128)S(1)} %fusion.31, f32[256,1024]{1,0:T(8,128)S(1)} %fusion.21), kind=kLoop, calls=%fused_computation | loop fusion | flops 524288 | bytes 4194304 | tf_op jit(solution)/shard_map/concatenate | solution.py:169
  50.4 2.6 %concatenate.23 = f32[512,1152]{1,0:T(8,128)S(1)} concatenate(f32[512,1024]{1,0:T(8,128)} %pad_maximum_fusion, f32[512,16]{1,0:T(8,128)S(1)} %reshape.545, f32[512,112]{1,0:T(8,128)S(1)} %broadcast_in_dim.8), dimensions={1} | concatenate | bytes 4718592 | tf_op jit(solution)/shard_map/concatenate | solution.py:168
  53.0 1.2 slice_select_fusion
  54.2 3.2 %collective-permute-done.4 = f32[256,1152]{1,0:T(8,128)} collective-permute-done((f32[256,1152]{1,0:T(8,128)}, f32[256,1152]{1,0:T(8,128)}, u32[]{:S(2)}, u32[]{:S(2)}) %collective-permute-start.4) | collective-permute-done | bytes 1179680 | tf_op jit(solution)/shard_map/ppermute | solution.py:109
  57.3 1.4 %select_add_fusion = f32[256,1152]{1,0:T(8,128)S(1)} fusion(f32[256,1152]{1,0:T(8,128)} %collective-permute-done.4, f32[512,1152]{1,0:T(8,128)S(1)} %concatenate.23, pred[]{:T(512)S(6)} %eq.321), kind=kLoop, calls=%fused_computation.6 | loop fusion | flops 589824 | bytes 4718593 | tf_op jit(solution)/shard_map/add | solution.py:110
  58.8 1.0 copy-done.1
  59.8 0.1 slice_select_fusion.1
  59.9 0.8 collective-permute-start.5
  60.7 8.3 %collective-permute-done.5 = f32[128,1152]{1,0:T(8,128)S(1)} collective-permute-done((f32[128,1152]{1,0:T(8,128)S(1)}, f32[128,1152]{1,0:T(8,128)S(1)}, u32[]{:S(2)}, u32[]{:S(2)}) %collective-permute-start.5) | collective-permute-done | bytes 589856 | tf_op jit(solution)/shard_map/ppermute | solution.py:109
  69.0 1.3 select_add_fusion.1
  70.4 1.1 collective-permute-start.6
  71.5 4.8 %collective-permute-done.6 = f32[64,1152]{1,0:T(8,128)S(1)} collective-permute-done((f32[64,1152]{1,0:T(8,128)S(1)}, f32[64,1152]{1,0:T(8,128)S(1)}, u32[]{:S(2)}, u32[]{:S(2)}) %collective-permute-start.6) | collective-permute-done | bytes 294944 | tf_op jit(solution)/shard_map/ppermute | solution.py:109
  76.4 0.9 collective-permute-start.7
  77.3 3.2 %collective-permute-done.7 = f32[32,1152]{1,0:T(8,128)S(1)} collective-permute-done((f32[32,1152]{1,0:T(8,128)S(1)}, f32[32,1152]{1,0:T(8,128)S(1)}, u32[]{:S(2)}, u32[]{:S(2)}) %collective-permute-start.7) | collective-permute-done | bytes 147488 | tf_op jit(solution)/shard_map/ppermute | solution.py:109
  80.5 2.6 %collective-permute-start.8 = (f32[32,1152]{1,0:T(8,128)S(1)}, f32[32,1152]{1,0:T(8,128)S(1)}, u32[]{:S(2)}, u32[]{:S(2)}) collective-permute-start(f32[32,1152]{1,0:T(8,128)S(1)} %select_add_fusion.3), channel_id=1, source_target_pairs={{0,128},{1,129},{2,130},{3,131},{4,132},{5,133},{6,134},{7,135},{8... | collective-permute-start | bytes 442376 | tf_op jit(solution)/shard_map/ppermute | solution.py:112
  83.1 3.0 %collective-permute-done.8 = f32[32,1152]{1,0:T(8,128)S(1)} collective-permute-done((f32[32,1152]{1,0:T(8,128)S(1)}, f32[32,1152]{1,0:T(8,128)S(1)}, u32[]{:S(2)}, u32[]{:S(2)}) %collective-permute-start.8) | collective-permute-done | bytes 147488 | tf_op jit(solution)/shard_map/ppermute | solution.py:112
  86.1 2.7 %collective-permute-start.9 = (f32[32,1152]{1,0:T(8,128)S(1)}, f32[32,1152]{1,0:T(8,128)S(1)}, u32[]{:S(2)}, u32[]{:S(2)}) collective-permute-start(f32[32,1152]{1,0:T(8,128)S(1)} %add.252), channel_id=1, source_target_pairs={{0,16},{1,17},{2,18},{3,19},{4,20},{5,21},{6,22},{7,23},{8,24},{9,... | collective-permute-start | bytes 442376 | tf_op jit(solution)/shard_map/ppermute | solution.py:112
  88.8 4.1 %collective-permute-done.9 = f32[32,1152]{1,0:T(8,128)S(1)} collective-permute-done((f32[32,1152]{1,0:T(8,128)S(1)}, f32[32,1152]{1,0:T(8,128)S(1)}, u32[]{:S(2)}, u32[]{:S(2)}) %collective-permute-start.9) | collective-permute-done | bytes 147488 | tf_op jit(solution)/shard_map/ppermute | solution.py:112
  92.9 2.8 %collective-permute-start.10 = (f32[32,1152]{1,0:T(8,128)S(1)}, f32[32,1152]{1,0:T(8,128)S(1)}, u32[]{:S(2)}, u32[]{:S(2)}) collective-permute-start(f32[32,1152]{1,0:T(8,128)S(1)} %add.253), channel_id=1, source_target_pairs={{0,2},{1,3},{2,0},{3,1},{4,6},{5,7},{6,4},{7,5},{8,10},{9,11},{10,... | collective-permute-start | bytes 442376 | tf_op jit(solution)/shard_map/ppermute | solution.py:112
  95.7 2.8 %collective-permute-done.10 = f32[32,1152]{1,0:T(8,128)S(1)} collective-permute-done((f32[32,1152]{1,0:T(8,128)S(1)}, f32[32,1152]{1,0:T(8,128)S(1)}, u32[]{:S(2)}, u32[]{:S(2)}) %collective-permute-start.10) | collective-permute-done | bytes 147488 | tf_op jit(solution)/shard_map/ppermute | solution.py:112
  98.5 6.2 %collective-permute-start.11 = (f32[32,1152]{1,0:T(8,128)S(1)}, f32[32,1152]{1,0:T(8,128)S(1)}, u32[]{:S(2)}, u32[]{:S(2)}) collective-permute-start(f32[32,1152]{1,0:T(8,128)S(1)} %add.254), channel_id=1, source_target_pairs={{0,4},{1,5},{2,6},{3,7},{4,0},{5,1},{6,2},{7,3},{8,12},{9,13},{10,... | collective-permute-start | bytes 442376 | tf_op jit(solution)/shard_map/ppermute | solution.py:112
  104.7 3.9 %collective-permute-done.11 = f32[32,1152]{1,0:T(8,128)S(1)} collective-permute-done((f32[32,1152]{1,0:T(8,128)S(1)}, f32[32,1152]{1,0:T(8,128)S(1)}, u32[]{:S(2)}, u32[]{:S(2)}) %collective-permute-start.11) | collective-permute-done | bytes 147488 | tf_op jit(solution)/shard_map/ppermute | solution.py:112
  108.6 1.3 collective-permute-start.12
  109.9 2.0 %collective-permute-done.12 = bf16[32,1152]{1,0:T(8,128)(2,1)S(1)} collective-permute-done((bf16[32,1152]{1,0:T(8,128)(2,1)S(1)}, bf16[32,1152]{1,0:T(8,128)(2,1)S(1)}, u32[]{:S(2)}, u32[]{:S(2)}) %collective-permute-start.12) | collective-permute-done | bytes 73760 | tf_op jit(solution)/shard_map/ppermute | solution.py:116
  111.9 0.1 collective-permute-start.13
  112.0 5.6 %collective-permute-done.13 = bf16[64,1152]{1,0:T(8,128)(2,1)S(1)} collective-permute-done((bf16[64,1152]{1,0:T(8,128)(2,1)S(1)}, bf16[64,1152]{1,0:T(8,128)(2,1)S(1)}, u32[]{:S(2)}, u32[]{:S(2)}) %collective-permute-start.13) | collective-permute-done | bytes 147488 | tf_op jit(solution)/shard_map/ppermute | solution.py:116
  117.6 0.1 broadcast_select_fusion.5
  117.7 1.2 collective-permute-start.14
  119.0 4.4 %collective-permute-done.14 = bf16[128,1152]{1,0:T(8,128)(2,1)S(1)} collective-permute-done((bf16[128,1152]{1,0:T(8,128)(2,1)S(1)}, bf16[128,1152]{1,0:T(8,128)(2,1)S(1)}, u32[]{:S(2)}, u32[]{:S(2)}) %collective-permute-start.14) | collective-permute-done | bytes 294944 | tf_op jit(solution)/shard_map/ppermute | solution.py:116
  123.4 0.1 broadcast_select_fusion.3
  123.5 11.1 %collective-permute-start.15 = (bf16[256,1152]{1,0:T(8,128)(2,1)S(1)}, bf16[256,1152]{1,0:T(8,128)(2,1)S(1)}, u32[]{:S(2)}, u32[]{:S(2)}) collective-permute-start(bf16[256,1152]{1,0:T(8,128)(2,1)S(1)} %pad_maximum_fusion.1), channel_id=1, source_target_pairs={{0,32},{1,33},{2,34},{3,35},{4,36},{5,37},{6,38},{7,39},{8,40},{9,... | collective-permute-start | bytes 1769480 | tf_op jit(solution)/shard_map/ppermute | solution.py:116
  134.6 1.6 %collective-permute-done.15 = bf16[256,1152]{1,0:T(8,128)(2,1)S(1)} collective-permute-done((bf16[256,1152]{1,0:T(8,128)(2,1)S(1)}, bf16[256,1152]{1,0:T(8,128)(2,1)S(1)}, u32[]{:S(2)}, u32[]{:S(2)}) %collective-permute-start.15) | collective-permute-done | bytes 589856 | tf_op jit(solution)/shard_map/ppermute | solution.py:116
  136.3 0.2 broadcast_select_fusion.1
  136.5 0.7 maximum_convert_fusion.1
  137.2 0.2 maximum_convert_fusion
  137.4 1.1 reshape.546
  138.5 0.8 copy.15
  139.2 1.6 %fusion.27 = (f32[256,1024]{1,0:T(8,128)}, f32[256,1024]{1,0:T(8,128)}) fusion(f32[512,1152]{1,0:T(8,128)S(1)} %maximum_convert_fusion), kind=kLoop, calls=%fused_computation.71 | loop fusion | bytes 4194304 | tf_op jit(solution)/shard_map/slice | solution.py:173
  (26 shorter events, 0.4 us)
Async XLA Ops:
  0.6 45.6 %copy-start = (bf16[256,1024]{1,0:T(8,128)(2,1)S(1)}, bf16[256,1024]{1,0:T(8,128)(2,1)}, u32[]{:S(2)}) copy-start(bf16[256,1024]{1,0:T(8,128)(2,1)} %param.14) | copy-start | bytes 1572868
  20.2 8.2 %copy-start.5 = (s32[1,256,8]{1,2,0:T(8,128)S(1)}, s32[1,256,8]{1,2,0:T(8,128)}, u32[]{:S(2)}) copy-start(s32[1,256,8]{1,2,0:T(8,128)} %param.11) | copy-start | bytes 24580
  21.4 10.0 %collective-permute-start = (f32[256,384]{1,0:T(8,128)S(1)}, f32[256,384]{1,0:T(8,128)S(1)}, u32[]{:S(2)}, u32[]{:S(2)}) collective-permute-start(f32[256,384]{1,0:T(8,128)S(1)} %get-tuple-element.16), channel_id=1, source_target_pairs={{32,0},{64,32},{96,64},{128,96},{160,128},{192,160},{224,192},{33,... | collective-permute-start | bytes 1179656 | tf_op jit(solution)/shard_map/ppermute | solution.py:11
  26.5 6.6 %collective-permute-start.1 = (f32[256,384]{1,0:T(8,128)S(1)}, f32[256,384]{1,0:T(8,128)S(1)}, u32[]{:S(2)}, u32[]{:S(2)}) collective-permute-start(f32[256,384]{1,0:T(8,128)S(1)} %get-tuple-element.17), channel_id=1, source_target_pairs={{0,32},{32,64},{64,96},{96,128},{128,160},{160,192},{192,224},{1,3... | collective-permute-start | bytes 1179656 | tf_op jit(solution)/shard_map/ppermute | solution.py:11
  28.5 12.4 %copy-start.2 = (bf16[256,1024]{1,0:T(8,128)(2,1)S(1)}, bf16[256,1024]{1,0:T(8,128)(2,1)}, u32[]{:S(2)}) copy-start(bf16[256,1024]{1,0:T(8,128)(2,1)} %param.13) | copy-start | bytes 1572868
  34.6 6.6 %collective-permute-start.2 = (bf16[1,256,256]{2,1,0:T(8,128)(2,1)S(1)}, bf16[1,256,256]{2,1,0:T(8,128)(2,1)S(1)}, u32[]{:S(2)}, u32[]{:S(2)}) collective-permute-start(bf16[1,256,256]{2,1,0:T(8,128)(2,1)S(1)} %fusion.19), channel_id=1, source_target_pairs={{0,32},{32,64},{64,96},{96,128},{128,160},{160,192},{192,224},{1,3... | collective-permute-start | bytes 393224 | tf_op jit(solution)/shard_map/ppermute | solution.py:19
  39.0 6.3 %collective-permute-start.3 = (bf16[1,256,256]{2,1,0:T(8,128)(2,1)S(1)}, bf16[1,256,256]{2,1,0:T(8,128)(2,1)S(1)}, u32[]{:S(2)}, u32[]{:S(2)}) collective-permute-start(bf16[1,256,256]{2,1,0:T(8,128)(2,1)S(1)} %fusion.19), channel_id=1, source_target_pairs={{32,0},{64,32},{96,64},{128,96},{160,128},{192,160},{224,192},{33,... | collective-permute-start | bytes 393224 | tf_op jit(solution)/shard_map/ppermute | solution.py:22
  46.2 0.7 copy-start.4
  46.2 0.9 copy-start.6
  47.2 0.9 copy-start.3
  54.2 3.2 %collective-permute-start.4 = (f32[256,1152]{1,0:T(8,128)}, f32[256,1152]{1,0:T(8,128)}, u32[]{:S(2)}, u32[]{:S(2)}) collective-permute-start(f32[256,1152]{1,0:T(8,128)} %slice_select_fusion), channel_id=1, source_target_pairs={{0,32},{1,33},{2,34},{3,35},{4,36},{5,37},{6,38},{7,39},{8,40},{9,... | collective-permute-start | bytes 3538952 | tf_op jit(solution)/shard_map/ppermute | solution.py:109
  58.8 1.0 copy-start.1
  59.9 9.1 %collective-permute-start.5 = (f32[128,1152]{1,0:T(8,128)S(1)}, f32[128,1152]{1,0:T(8,128)S(1)}, u32[]{:S(2)}, u32[]{:S(2)}) collective-permute-start(f32[128,1152]{1,0:T(8,128)S(1)} %slice_select_fusion.1), channel_id=1, source_target_pairs={{0,64},{1,65},{2,66},{3,67},{4,68},{5,69},{6,70},{7,71},{8,72},{9,... | collective-permute-start | bytes 1769480 | tf_op jit(solution)/shard_map/ppermute | solution.py:109
  70.4 6.0 %collective-permute-start.6 = (f32[64,1152]{1,0:T(8,128)S(1)}, f32[64,1152]{1,0:T(8,128)S(1)}, u32[]{:S(2)}, u32[]{:S(2)}) collective-permute-start(f32[64,1152]{1,0:T(8,128)S(1)} %slice_select_fusion.2), channel_id=1, source_target_pairs={{0,8},{1,9},{2,10},{3,11},{4,12},{5,13},{6,14},{7,15},{8,0},{9,1},... | collective-permute-start | bytes 884744 | tf_op jit(solution)/shard_map/ppermute | solution.py:109
  76.4 4.1 %collective-permute-start.7 = (f32[32,1152]{1,0:T(8,128)S(1)}, f32[32,1152]{1,0:T(8,128)S(1)}, u32[]{:S(2)}, u32[]{:S(2)}) collective-permute-start(f32[32,1152]{1,0:T(8,128)S(1)} %slice_select_fusion.3), channel_id=1, source_target_pairs={{0,1},{1,0},{2,3},{3,2},{4,5},{5,4},{6,7},{7,6},{8,9},{9,8},{10,11... | collective-permute-start | bytes 442376 | tf_op jit(solution)/shard_map/ppermute | solution.py:109
  80.5 5.6 %collective-permute-start.8 = (f32[32,1152]{1,0:T(8,128)S(1)}, f32[32,1152]{1,0:T(8,128)S(1)}, u32[]{:S(2)}, u32[]{:S(2)}) collective-permute-start(f32[32,1152]{1,0:T(8,128)S(1)} %select_add_fusion.3), channel_id=1, source_target_pairs={{0,128},{1,129},{2,130},{3,131},{4,132},{5,133},{6,134},{7,135},{8... | collective-permute-start | bytes 442376 | tf_op jit(solution)/shard_map/ppermute | solution.py:112
  86.1 6.8 %collective-permute-start.9 = (f32[32,1152]{1,0:T(8,128)S(1)}, f32[32,1152]{1,0:T(8,128)S(1)}, u32[]{:S(2)}, u32[]{:S(2)}) collective-permute-start(f32[32,1152]{1,0:T(8,128)S(1)} %add.252), channel_id=1, source_target_pairs={{0,16},{1,17},{2,18},{3,19},{4,20},{5,21},{6,22},{7,23},{8,24},{9,... | collective-permute-start | bytes 442376 | tf_op jit(solution)/shard_map/ppermute | solution.py:112
  92.9 5.6 %collective-permute-start.10 = (f32[32,1152]{1,0:T(8,128)S(1)}, f32[32,1152]{1,0:T(8,128)S(1)}, u32[]{:S(2)}, u32[]{:S(2)}) collective-permute-start(f32[32,1152]{1,0:T(8,128)S(1)} %add.253), channel_id=1, source_target_pairs={{0,2},{1,3},{2,0},{3,1},{4,6},{5,7},{6,4},{7,5},{8,10},{9,11},{10,... | collective-permute-start | bytes 442376 | tf_op jit(solution)/shard_map/ppermute | solution.py:112
  98.5 10.1 %collective-permute-start.11 = (f32[32,1152]{1,0:T(8,128)S(1)}, f32[32,1152]{1,0:T(8,128)S(1)}, u32[]{:S(2)}, u32[]{:S(2)}) collective-permute-start(f32[32,1152]{1,0:T(8,128)S(1)} %add.254), channel_id=1, source_target_pairs={{0,4},{1,5},{2,6},{3,7},{4,0},{5,1},{6,2},{7,3},{8,12},{9,13},{10,... | collective-permute-start | bytes 442376 | tf_op jit(solution)/shard_map/ppermute | solution.py:112
  108.6 3.3 %collective-permute-start.12 = (bf16[32,1152]{1,0:T(8,128)(2,1)S(1)}, bf16[32,1152]{1,0:T(8,128)(2,1)S(1)}, u32[]{:S(2)}, u32[]{:S(2)}) collective-permute-start(bf16[32,1152]{1,0:T(8,128)(2,1)S(1)} %add_convert_fusion.1), channel_id=1, source_target_pairs={{0,1},{1,0},{2,3},{3,2},{4,5},{5,4},{6,7},{7,6},{8,9},{9,8},{10,11... | collective-permute-start | bytes 221192 | tf_op jit(solution)/shard_map/ppermute | solution.py:116
  111.9 5.7 %collective-permute-start.13 = (bf16[64,1152]{1,0:T(8,128)(2,1)S(1)}, bf16[64,1152]{1,0:T(8,128)(2,1)S(1)}, u32[]{:S(2)}, u32[]{:S(2)}) collective-permute-start(bf16[64,1152]{1,0:T(8,128)(2,1)S(1)} %pad_maximum_fusion.3), channel_id=1, source_target_pairs={{0,8},{1,9},{2,10},{3,11},{4,12},{5,13},{6,14},{7,15},{8,0},{9,1},... | collective-permute-start | bytes 442376 | tf_op jit(solution)/shard_map/ppermute | solution.py:116
  117.7 5.7 %collective-permute-start.14 = (bf16[128,1152]{1,0:T(8,128)(2,1)S(1)}, bf16[128,1152]{1,0:T(8,128)(2,1)S(1)}, u32[]{:S(2)}, u32[]{:S(2)}) collective-permute-start(bf16[128,1152]{1,0:T(8,128)(2,1)S(1)} %pad_maximum_fusion.2), channel_id=1, source_target_pairs={{0,64},{1,65},{2,66},{3,67},{4,68},{5,69},{6,70},{7,71},{8,72},{9,... | collective-permute-start | bytes 884744 | tf_op jit(solution)/shard_map/ppermute | solution.py:116
  123.5 12.7 %collective-permute-start.15 = (bf16[256,1152]{1,0:T(8,128)(2,1)S(1)}, bf16[256,1152]{1,0:T(8,128)(2,1)S(1)}, u32[]{:S(2)}, u32[]{:S(2)}) collective-permute-start(bf16[256,1152]{1,0:T(8,128)(2,1)S(1)} %pad_maximum_fusion.1), channel_id=1, source_target_pairs={{0,32},{1,33},{2,34},{3,35},{4,36},{5,37},{6,38},{7,39},{8,40},{9,... | collective-permute-start | bytes 1769480 | tf_op jit(solution)/shard_map/ppermute | solution.py:116

commit v11 on v10

--- a/solution.py
+++ b/solution.py
@@ -77,8 +77,8 @@
 
 def halving_plan(sizes):
     core = [("region", 1)]
-    first = [("region", 2), ("dp", 8), ("dp", 1), ("region", 4), ("dp", 16), ("dp", 2), ("dp", 4)]
-    second = [("dp", 8), ("dp", 1), ("region", 2), ("dp", 16), ("dp", 2), ("region", 4), ("dp", 4)]
+    first = [("region", 2), ("dp", 8), ("dp", 1), ("dp", 4), ("region", 4), ("dp", 16), ("dp", 2)]
+    second = [("dp", 8), ("dp", 1), ("region", 2), ("dp", 4), ("dp", 16), ("dp", 2), ("region", 4)]
     width = sizes["dp"]
     steps = []
     for flip0, flip1 in zip(core + first, core + second):
@@ -168,7 +168,7 @@
     packed = jnp.concatenate(
         [jnp.concatenate([grad_own, grad_side], axis=0), head, spare], axis=1
     )
-    packed = all_sum(packed, sizes, 4)
+    packed = all_sum(packed, sizes, 5)
     packed = packed.astype(jnp.float32)
     grad_own, grad_side = packed[:feats, :hid], packed[feats:, :hid]
     grad_head = packed[:, hid : hid + head.shape[1]].reshape(hid, -1)

time: 141 us -> 144 us (1.021)
  starting transfers between devices: 44 us -> 50.9 us
  waiting for transfers between devices: 55.7 us -> 51.9 us
    ppermute x4 -> x5, starting transfers between devices: 13.7 us -> 20.9 us  [all_sum(): got = lax.ppermute(value, axes, perm)]
    ppermute x4 -> x3, starting transfers between devices: 14.2 us -> 7.46 us  [all_sum(): value = value + lax.ppermute(value, axes, perm)]
    ppermute x4 -> x5, starting transfers between devices: 2.77 us -> 9.2 us  [all_sum(): got = lax.ppermute(jnp.where(upper, low, high), axes, perm)]
    ppermute x4 -> x3, waiting for transfers between devices: 13.8 us -> 7.4 us  [all_sum(): value = value + lax.ppermute(value, axes, perm)]
    ppermute x4 -> x5, waiting for transfers between devices: 19.6 us -> 21.8 us  [all_sum(): got = lax.ppermute(jnp.where(upper, low, high), axes, perm)]
    ppermute x4 -> x5, waiting for transfers between devices: 13.6 us -> 14.1 us  [all_sum(): got = lax.ppermute(value, axes, perm)]
  transfers between devices with their start and end apart: 16 -> 17, of which waited for: 15 -> 16; matrix products, arithmetic and copies ran while one was open for 0% -> 0% of each run, Pallas kernels for 0% -> 0%
where the time goes in v11:
time: 144 us
  waiting for transfers between devices  51.9 us (36%)
  starting transfers between devices  50.9 us (35%)
  Pallas kernels  19 us (13%)
  local copies, waits for them, and re-layouts  9.25 us (6%)
  other arithmetic  8.42 us (6%)
  matrix products  3.52 us (2%)
    ppermute x5, waiting for transfers between devices, all_sum(): got = lax.ppermute(jnp.where(upper, low, high), axes, perm)  21.8 us
    ppermute x5, starting transfers between devices, all_sum(): got = lax.ppermute(value, axes, perm)  20.9 us
    pallas_call x1, Pallas kernels, accumulate(): pl.pallas_call(pooled_sums_kernel, grid=(length // block,), in_specs=[pl....  19 us
    ppermute x5, waiting for transfers between devices, all_sum(): got = lax.ppermute(value, axes, perm)  14.1 us
    ppermute x5, starting transfers between devices, all_sum(): got = lax.ppermute(jnp.where(upper, low, high), axes, perm)  9.2 us
    ppermute x3, starting transfers between devices, all_sum(): value = value + lax.ppermute(value, axes, perm)  7.46 us
    ppermute x3, waiting for transfers between devices, all_sum(): value = value + lax.ppermute(value, axes, perm)  7.4 us
    ppermute x2, starting transfers between devices, passed_along(): lax.ppermute(value, axis, [(source, source + steps) for source in range(i...  7.02 us
  transfers between devices with their start and end apart: 17, of which 16 were waited for; matrix products, arithmetic and copies ran while one was open for 0% of the time, Pallas kernels for 0%

profile of v11, /device:TPU:1, one launch (start us, length us, event | category | flops | bytes accessed | tf_op | source)
XLA Modules:
  0.0 143.9 jit_solution(1056487681349317797)
XLA Ops:
  0.6 0.0 copy-start
  0.7 0.6 broadcast_in_dim.6.offset_ref
  1.2 19.0 %shard_map.111 = f32[768,384]{1,0:T(8,128)} custom-call(s32[8,128]{1,0:T(8,128)} %broadcast_in_dim.6.offset_ref, s32[1,16384]{1,0:T(1,128)} %ids_ref.1, f32[1,16384]{1,0:T(1,128)} %weight_ref.1, bf16[16384,256]{1,0:T(8,128)(2,1)} %bitcast.45), custom_call_target="tpu_custom_call" | custom-call | flops 9663676416 | bytes 9699328 | tf_op jit(solution)/shard_map/pallas_call | solution.py:58
  20.2 1.2 fusion.28
  21.4 5.1 %collective-permute-start = (f32[256,384]{1,0:T(8,128)S(1)}, f32[256,384]{1,0:T(8,128)S(1)}, u32[]{:S(2)}, u32[]{:S(2)}) collective-permute-start(f32[256,384]{1,0:T(8,128)S(1)} %get-tuple-element.16), channel_id=1, source_target_pairs={{32,0},{64,32},{96,64},{128,96},{160,128},{192,160},{224,192},{33,... | collective-permute-start | bytes 1179656 | tf_op jit(solution)/shard_map/ppermute | solution.py:11
  26.5 1.9 %collective-permute-start.1 = (f32[256,384]{1,0:T(8,128)S(1)}, f32[256,384]{1,0:T(8,128)S(1)}, u32[]{:S(2)}, u32[]{:S(2)}) collective-permute-start(f32[256,384]{1,0:T(8,128)S(1)} %get-tuple-element.17), channel_id=1, source_target_pairs={{0,32},{32,64},{64,96},{96,128},{128,160},{160,192},{192,224},{1,3... | collective-permute-start | bytes 1179656 | tf_op jit(solution)/shard_map/ppermute | solution.py:11
  28.5 2.8 %collective-permute-done = f32[256,384]{1,0:T(8,128)S(1)} collective-permute-done((f32[256,384]{1,0:T(8,128)S(1)}, f32[256,384]{1,0:T(8,128)S(1)}, u32[]{:S(2)}, u32[]{:S(2)}) %collective-permute-start) | collective-permute-done | bytes 393248 | tf_op jit(solution)/shard_map/ppermute | solution.py:11
  31.3 1.8 %collective-permute-done.1 = f32[256,384]{1,0:T(8,128)S(1)} collective-permute-done((f32[256,384]{1,0:T(8,128)S(1)}, f32[256,384]{1,0:T(8,128)S(1)}, u32[]{:S(2)}, u32[]{:S(2)}) %collective-permute-start.1) | collective-permute-done | bytes 393248 | tf_op jit(solution)/shard_map/ppermute | solution.py:11
  33.1 1.1 fusion.6
  34.2 0.2 fusion.20
  34.4 0.1 fusion.19
  34.5 4.4 %collective-permute-start.2 = (bf16[1,256,256]{2,1,0:T(8,128)(2,1)S(1)}, bf16[1,256,256]{2,1,0:T(8,128)(2,1)S(1)}, u32[]{:S(2)}, u32[]{:S(2)}) collective-permute-start(bf16[1,256,256]{2,1,0:T(8,128)(2,1)S(1)} %fusion.19), channel_id=1, source_target_pairs={{0,32},{32,64},{64,96},{96,128},{128,160},{160,192},{192,224},{1,3... | collective-permute-start | bytes 393224 | tf_op jit(solution)/shard_map/ppermute | solution.py:19
  38.9 1.9 %collective-permute-start.3 = (bf16[1,256,256]{2,1,0:T(8,128)(2,1)S(1)}, bf16[1,256,256]{2,1,0:T(8,128)(2,1)S(1)}, u32[]{:S(2)}, u32[]{:S(2)}) collective-permute-start(bf16[1,256,256]{2,1,0:T(8,128)(2,1)S(1)} %fusion.19), channel_id=1, source_target_pairs={{32,0},{64,32},{96,64},{128,96},{160,128},{192,160},{224,192},{33,... | collective-permute-start | bytes 393224 | tf_op jit(solution)/shard_map/ppermute | solution.py:22
  40.9 0.3 fusion.23
  41.2 4.0 %collective-permute-done.3 = bf16[1,256,256]{2,1,0:T(8,128)(2,1)S(1)} collective-permute-done((bf16[1,256,256]{2,1,0:T(8,128)(2,1)S(1)}, bf16[1,256,256]{2,1,0:T(8,128)(2,1)S(1)}, u32[]{:S(2)}, u32[]{:S(2)}) %collective-permute-start.3) | collective-permute-done | bytes 131104 | tf_op jit(solution)/shard_map/ppermute | solution.py:22
  45.2 1.0 fusion.2
  46.2 0.5 multiply_convert_fusion
  46.7 0.2 copy-done.4
  46.9 0.2 fusion.30
  47.2 0.4 fusion.26
  47.5 0.5 fusion.1
  48.1 0.3 fusion.21
  48.4 0.3 fusion.31
  48.7 0.1 reshape.545
  48.9 1.5 %pad_maximum_fusion = f32[512,1024]{1,0:T(8,128)} fusion(f32[256,1024]{1,0:T(8,128)S(1)} %fusion.31, f32[256,1024]{1,0:T(8,128)S(1)} %fusion.21), kind=kLoop, calls=%fused_computation | loop fusion | flops 524288 | bytes 4194304 | tf_op jit(solution)/shard_map/concatenate | solution.py:169
  50.4 2.6 %concatenate.26 = f32[512,1152]{1,0:T(8,128)S(1)} concatenate(f32[512,1024]{1,0:T(8,128)} %pad_maximum_fusion, f32[512,16]{1,0:T(8,128)S(1)} %reshape.545, f32[512,112]{1,0:T(8,128)S(1)} %broadcast_in_dim.8), dimensions={1} | concatenate | bytes 4718592 | tf_op jit(solution)/shard_map/concatenate | solution.py:168
  53.0 1.1 slice_select_fusion
  54.1 3.2 %collective-permute-done.4 = f32[256,1152]{1,0:T(8,128)} collective-permute-done((f32[256,1152]{1,0:T(8,128)}, f32[256,1152]{1,0:T(8,128)}, u32[]{:S(2)}, u32[]{:S(2)}) %collective-permute-start.4) | collective-permute-done | bytes 1179680 | tf_op jit(solution)/shard_map/ppermute | solution.py:109
  57.3 1.4 %select_add_fusion = f32[256,1152]{1,0:T(8,128)S(1)} fusion(f32[256,1152]{1,0:T(8,128)} %collective-permute-done.4, f32[512,1152]{1,0:T(8,128)S(1)} %concatenate.26, pred[]{:T(512)S(6)} %eq.333), kind=kLoop, calls=%fused_computation.6 | loop fusion | flops 589824 | bytes 4718593 | tf_op jit(solution)/shard_map/add | solution.py:110
  58.8 1.0 copy-done.1
  59.8 0.1 slice_select_fusion.1
  59.8 0.8 collective-permute-start.5
  60.6 8.3 %collective-permute-done.5 = f32[128,1152]{1,0:T(8,128)S(1)} collective-permute-done((f32[128,1152]{1,0:T(8,128)S(1)}, f32[128,1152]{1,0:T(8,128)S(1)}, u32[]{:S(2)}, u32[]{:S(2)}) %collective-permute-start.5) | collective-permute-done | bytes 589856 | tf_op jit(solution)/shard_map/ppermute | solution.py:109
  69.0 1.3 select_add_fusion.1
  70.3 1.1 collective-permute-start.6
  71.5 4.8 %collective-permute-done.6 = f32[64,1152]{1,0:T(8,128)S(1)} collective-permute-done((f32[64,1152]{1,0:T(8,128)S(1)}, f32[64,1152]{1,0:T(8,128)S(1)}, u32[]{:S(2)}, u32[]{:S(2)}) %collective-permute-start.6) | collective-permute-done | bytes 294944 | tf_op jit(solution)/shard_map/ppermute | solution.py:109
  76.4 0.9 collective-permute-start.7
  77.2 3.2 %collective-permute-done.7 = f32[32,1152]{1,0:T(8,128)S(1)} collective-permute-done((f32[32,1152]{1,0:T(8,128)S(1)}, f32[32,1152]{1,0:T(8,128)S(1)}, u32[]{:S(2)}, u32[]{:S(2)}) %collective-permute-start.7) | collective-permute-done | bytes 147488 | tf_op jit(solution)/shard_map/ppermute | solution.py:109
  80.5 6.4 %collective-permute-start.8 = (f32[16,1152]{1,0:T(8,128)S(1)}, f32[16,1152]{1,0:T(8,128)S(1)}, u32[]{:S(2)}, u32[]{:S(2)}) collective-permute-start(f32[16,1152]{1,0:T(8,128)S(1)} %slice_select_fusion.4), channel_id=1, source_target_pairs={{0,4},{1,5},{2,6},{3,7},{4,0},{5,1},{6,2},{7,3},{8,12},{9,13},{10,... | collective-permute-start | bytes 221192 | tf_op jit(solution)/shard_map/ppermute | solution.py:109
  86.9 2.2 %collective-permute-done.8 = f32[16,1152]{1,0:T(8,128)S(1)} collective-permute-done((f32[16,1152]{1,0:T(8,128)S(1)}, f32[16,1152]{1,0:T(8,128)S(1)}, u32[]{:S(2)}, u32[]{:S(2)}) %collective-permute-start.8) | collective-permute-done | bytes 73760 | tf_op jit(solution)/shard_map/ppermute | solution.py:109
  89.1 3.0 %collective-permute-start.9 = (f32[16,1152]{1,0:T(8,128)S(1)}, f32[16,1152]{1,0:T(8,128)S(1)}, u32[]{:S(2)}, u32[]{:S(2)}) collective-permute-start(f32[16,1152]{1,0:T(8,128)S(1)} %select_add_fusion.4), channel_id=1, source_target_pairs={{0,128},{1,129},{2,130},{3,131},{4,132},{5,133},{6,134},{7,135},{8... | collective-permute-start | bytes 221192 | tf_op jit(solution)/shard_map/ppermute | solution.py:112
  92.1 1.8 %collective-permute-done.9 = f32[16,1152]{1,0:T(8,128)S(1)} collective-permute-done((f32[16,1152]{1,0:T(8,128)S(1)}, f32[16,1152]{1,0:T(8,128)S(1)}, u32[]{:S(2)}, u32[]{:S(2)}) %collective-permute-start.9) | collective-permute-done | bytes 73760 | tf_op jit(solution)/shard_map/ppermute | solution.py:112
  93.9 1.7 %collective-permute-start.10 = (f32[16,1152]{1,0:T(8,128)S(1)}, f32[16,1152]{1,0:T(8,128)S(1)}, u32[]{:S(2)}, u32[]{:S(2)}) collective-permute-start(f32[16,1152]{1,0:T(8,128)S(1)} %add.263), channel_id=1, source_target_pairs={{0,16},{1,17},{2,18},{3,19},{4,20},{5,21},{6,22},{7,23},{8,24},{9,... | collective-permute-start | bytes 221192 | tf_op jit(solution)/shard_map/ppermute | solution.py:112
  95.6 3.6 %collective-permute-done.10 = f32[16,1152]{1,0:T(8,128)S(1)} collective-permute-done((f32[16,1152]{1,0:T(8,128)S(1)}, f32[16,1152]{1,0:T(8,128)S(1)}, u32[]{:S(2)}, u32[]{:S(2)}) %collective-permute-start.10) | collective-permute-done | bytes 73760 | tf_op jit(solution)/shard_map/ppermute | solution.py:112
  99.2 2.8 %collective-permute-start.11 = (f32[16,1152]{1,0:T(8,128)S(1)}, f32[16,1152]{1,0:T(8,128)S(1)}, u32[]{:S(2)}, u32[]{:S(2)}) collective-permute-start(f32[16,1152]{1,0:T(8,128)S(1)} %add.264), channel_id=1, source_target_pairs={{0,2},{1,3},{2,0},{3,1},{4,6},{5,7},{6,4},{7,5},{8,10},{9,11},{10,... | collective-permute-start | bytes 221192 | tf_op jit(solution)/shard_map/ppermute | solution.py:112
  102.0 2.0 %collective-permute-done.11 = f32[16,1152]{1,0:T(8,128)S(1)} collective-permute-done((f32[16,1152]{1,0:T(8,128)S(1)}, f32[16,1152]{1,0:T(8,128)S(1)}, u32[]{:S(2)}, u32[]{:S(2)}) %collective-permute-start.11) | collective-permute-done | bytes 73760 | tf_op jit(solution)/shard_map/ppermute | solution.py:112
  104.0 5.1 %collective-permute-start.12 = (bf16[16,1152]{1,0:T(8,128)(2,1)S(1)}, bf16[16,1152]{1,0:T(8,128)(2,1)S(1)}, u32[]{:S(2)}, u32[]{:S(2)}) collective-permute-start(bf16[16,1152]{1,0:T(8,128)(2,1)S(1)} %add_convert_fusion.1), channel_id=1, source_target_pairs={{0,4},{1,5},{2,6},{3,7},{4,0},{5,1},{6,2},{7,3},{8,12},{9,13},{10,... | collective-permute-start | bytes 110600 | tf_op jit(solution)/shard_map/ppermute | solution.py:116
  109.1 1.7 %collective-permute-done.12 = bf16[16,1152]{1,0:T(8,128)(2,1)S(1)} collective-permute-done((bf16[16,1152]{1,0:T(8,128)(2,1)S(1)}, bf16[16,1152]{1,0:T(8,128)(2,1)S(1)}, u32[]{:S(2)}, u32[]{:S(2)}) %collective-permute-start.12) | collective-permute-done | bytes 36896 | tf_op jit(solution)/shard_map/ppermute | solution.py:116
  110.9 1.5 %collective-permute-start.13 = (bf16[32,1152]{1,0:T(8,128)(2,1)S(1)}, bf16[32,1152]{1,0:T(8,128)(2,1)S(1)}, u32[]{:S(2)}, u32[]{:S(2)}) collective-permute-start(bf16[32,1152]{1,0:T(8,128)(2,1)S(1)} %pad_maximum_fusion.4), channel_id=1, source_target_pairs={{0,1},{1,0},{2,3},{3,2},{4,5},{5,4},{6,7},{7,6},{8,9},{9,8},{10,11... | collective-permute-start | bytes 221192 | tf_op jit(solution)/shard_map/ppermute | solution.py:116
  112.4 2.0 %collective-permute-done.13 = bf16[32,1152]{1,0:T(8,128)(2,1)S(1)} collective-permute-done((bf16[32,1152]{1,0:T(8,128)(2,1)S(1)}, bf16[32,1152]{1,0:T(8,128)(2,1)S(1)}, u32[]{:S(2)}, u32[]{:S(2)}) %collective-permute-start.13) | collective-permute-done | bytes 73760 | tf_op jit(solution)/shard_map/ppermute | solution.py:116
  114.4 0.2 collective-permute-start.14
  114.6 4.1 %collective-permute-done.14 = bf16[64,1152]{1,0:T(8,128)(2,1)S(1)} collective-permute-done((bf16[64,1152]{1,0:T(8,128)(2,1)S(1)}, bf16[64,1152]{1,0:T(8,128)(2,1)S(1)}, u32[]{:S(2)}, u32[]{:S(2)}) %collective-permute-start.14) | collective-permute-done | bytes 147488 | tf_op jit(solution)/shard_map/ppermute | solution.py:116
  118.8 0.1 broadcast_select_fusion.5
  118.9 1.4 collective-permute-start.15
  120.3 4.6 %collective-permute-done.15 = bf16[128,1152]{1,0:T(8,128)(2,1)S(1)} collective-permute-done((bf16[128,1152]{1,0:T(8,128)(2,1)S(1)}, bf16[128,1152]{1,0:T(8,128)(2,1)S(1)}, u32[]{:S(2)}, u32[]{:S(2)}) %collective-permute-start.15) | collective-permute-done | bytes 294944 | tf_op jit(solution)/shard_map/ppermute | solution.py:116
  124.8 0.1 broadcast_select_fusion.3
  125.0 12.7 %collective-permute-start.16 = (bf16[256,1152]{1,0:T(8,128)(2,1)S(1)}, bf16[256,1152]{1,0:T(8,128)(2,1)S(1)}, u32[]{:S(2)}, u32[]{:S(2)}) collective-permute-start(bf16[256,1152]{1,0:T(8,128)(2,1)S(1)} %pad_maximum_fusion.1), channel_id=1, source_target_pairs={{0,32},{1,33},{2,34},{3,35},{4,36},{5,37},{6,38},{7,39},{8,40},{9,... | collective-permute-start | bytes 1769480 | tf_op jit(solution)/shard_map/ppermute | solution.py:116
  137.7 1.6 %collective-permute-done.16 = bf16[256,1152]{1,0:T(8,128)(2,1)S(1)} collective-permute-done((bf16[256,1152]{1,0:T(8,128)(2,1)S(1)}, bf16[256,1152]{1,0:T(8,128)(2,1)S(1)}, u32[]{:S(2)}, u32[]{:S(2)}) %collective-permute-start.16) | collective-permute-done | bytes 589856 | tf_op jit(solution)/shard_map/ppermute | solution.py:116
  139.3 0.2 broadcast_select_fusion.1
  139.5 0.7 maximum_convert_fusion.1
  140.2 0.2 maximum_convert_fusion
  140.4 1.1 reshape.546
  141.5 0.8 copy.15
  142.3 1.6 %fusion.27 = (f32[256,1024]{1,0:T(8,128)}, f32[256,1024]{1,0:T(8,128)}) fusion(f32[512,1152]{1,0:T(8,128)S(1)} %maximum_convert_fusion), kind=kLoop, calls=%fused_computation.76 | loop fusion | bytes 4194304 | tf_op jit(solution)/shard_map/slice | solution.py:173
  (31 shorter events, 0.4 us)
Async XLA Ops:
  0.6 45.6 %copy-start = (bf16[256,1024]{1,0:T(8,128)(2,1)S(1)}, bf16[256,1024]{1,0:T(8,128)(2,1)}, u32[]{:S(2)}) copy-start(bf16[256,1024]{1,0:T(8,128)(2,1)} %param.14) | copy-start | bytes 1572868
  20.2 8.2 %copy-start.5 = (s32[1,256,8]{1,2,0:T(8,128)S(1)}, s32[1,256,8]{1,2,0:T(8,128)}, u32[]{:S(2)}) copy-start(s32[1,256,8]{1,2,0:T(8,128)} %param.11) | copy-start | bytes 24580
  21.4 9.9 %collective-permute-start = (f32[256,384]{1,0:T(8,128)S(1)}, f32[256,384]{1,0:T(8,128)S(1)}, u32[]{:S(2)}, u32[]{:S(2)}) collective-permute-start(f32[256,384]{1,0:T(8,128)S(1)} %get-tuple-element.16), channel_id=1, source_target_pairs={{32,0},{64,32},{96,64},{128,96},{160,128},{192,160},{224,192},{33,... | collective-permute-start | bytes 1179656 | tf_op jit(solution)/shard_map/ppermute | solution.py:11
  26.5 6.6 %collective-permute-start.1 = (f32[256,384]{1,0:T(8,128)S(1)}, f32[256,384]{1,0:T(8,128)S(1)}, u32[]{:S(2)}, u32[]{:S(2)}) collective-permute-start(f32[256,384]{1,0:T(8,128)S(1)} %get-tuple-element.17), channel_id=1, source_target_pairs={{0,32},{32,64},{64,96},{96,128},{128,160},{160,192},{192,224},{1,3... | collective-permute-start | bytes 1179656 | tf_op jit(solution)/shard_map/ppermute | solution.py:11
  28.5 12.4 %copy-start.2 = (bf16[256,1024]{1,0:T(8,128)(2,1)S(1)}, bf16[256,1024]{1,0:T(8,128)(2,1)}, u32[]{:S(2)}) copy-start(bf16[256,1024]{1,0:T(8,128)(2,1)} %param.13) | copy-start | bytes 1572868
  34.5 6.6 %collective-permute-start.2 = (bf16[1,256,256]{2,1,0:T(8,128)(2,1)S(1)}, bf16[1,256,256]{2,1,0:T(8,128)(2,1)S(1)}, u32[]{:S(2)}, u32[]{:S(2)}) collective-permute-start(bf16[1,256,256]{2,1,0:T(8,128)(2,1)S(1)} %fusion.19), channel_id=1, source_target_pairs={{0,32},{32,64},{64,96},{96,128},{128,160},{160,192},{192,224},{1,3... | collective-permute-start | bytes 393224 | tf_op jit(solution)/shard_map/ppermute | solution.py:19
  38.9 6.3 %collective-permute-start.3 = (bf16[1,256,256]{2,1,0:T(8,128)(2,1)S(1)}, bf16[1,256,256]{2,1,0:T(8,128)(2,1)S(1)}, u32[]{:S(2)}, u32[]{:S(2)}) collective-permute-start(bf16[1,256,256]{2,1,0:T(8,128)(2,1)S(1)} %fusion.19), channel_id=1, source_target_pairs={{32,0},{64,32},{96,64},{128,96},{160,128},{192,160},{224,192},{33,... | collective-permute-start | bytes 393224 | tf_op jit(solution)/shard_map/ppermute | solution.py:22
  46.2 0.7 copy-start.4
  46.2 0.9 copy-start.6
  47.2 0.9 copy-start.3
  54.1 3.2 %collective-permute-start.4 = (f32[256,1152]{1,0:T(8,128)}, f32[256,1152]{1,0:T(8,128)}, u32[]{:S(2)}, u32[]{:S(2)}) collective-permute-start(f32[256,1152]{1,0:T(8,128)} %slice_select_fusion), channel_id=1, source_target_pairs={{0,32},{1,33},{2,34},{3,35},{4,36},{5,37},{6,38},{7,39},{8,40},{9,... | collective-permute-start | bytes 3538952 | tf_op jit(solution)/shard_map/ppermute | solution.py:109
  58.7 1.0 copy-start.1
  59.8 9.1 %collective-permute-start.5 = (f32[128,1152]{1,0:T(8,128)S(1)}, f32[128,1152]{1,0:T(8,128)S(1)}, u32[]{:S(2)}, u32[]{:S(2)}) collective-permute-start(f32[128,1152]{1,0:T(8,128)S(1)} %slice_select_fusion.1), channel_id=1, source_target_pairs={{0,64},{1,65},{2,66},{3,67},{4,68},{5,69},{6,70},{7,71},{8,72},{9,... | collective-permute-start | bytes 1769480 | tf_op jit(solution)/shard_map/ppermute | solution.py:109
  70.3 6.0 %collective-permute-start.6 = (f32[64,1152]{1,0:T(8,128)S(1)}, f32[64,1152]{1,0:T(8,128)S(1)}, u32[]{:S(2)}, u32[]{:S(2)}) collective-permute-start(f32[64,1152]{1,0:T(8,128)S(1)} %slice_select_fusion.2), channel_id=1, source_target_pairs={{0,8},{1,9},{2,10},{3,11},{4,12},{5,13},{6,14},{7,15},{8,0},{9,1},... | collective-permute-start | bytes 884744 | tf_op jit(solution)/shard_map/ppermute | solution.py:109
  76.4 4.1 %collective-permute-start.7 = (f32[32,1152]{1,0:T(8,128)S(1)}, f32[32,1152]{1,0:T(8,128)S(1)}, u32[]{:S(2)}, u32[]{:S(2)}) collective-permute-start(f32[32,1152]{1,0:T(8,128)S(1)} %slice_select_fusion.3), channel_id=1, source_target_pairs={{0,1},{1,0},{2,3},{3,2},{4,5},{5,4},{6,7},{7,6},{8,9},{9,8},{10,11... | collective-permute-start | bytes 442376 | tf_op jit(solution)/shard_map/ppermute | solution.py:109
  80.5 8.6 %collective-permute-start.8 = (f32[16,1152]{1,0:T(8,128)S(1)}, f32[16,1152]{1,0:T(8,128)S(1)}, u32[]{:S(2)}, u32[]{:S(2)}) collective-permute-start(f32[16,1152]{1,0:T(8,128)S(1)} %slice_select_fusion.4), channel_id=1, source_target_pairs={{0,4},{1,5},{2,6},{3,7},{4,0},{5,1},{6,2},{7,3},{8,12},{9,13},{10,... | collective-permute-start | bytes 221192 | tf_op jit(solution)/shard_map/ppermute | solution.py:109
  89.1 4.8 %collective-permute-start.9 = (f32[16,1152]{1,0:T(8,128)S(1)}, f32[16,1152]{1,0:T(8,128)S(1)}, u32[]{:S(2)}, u32[]{:S(2)}) collective-permute-start(f32[16,1152]{1,0:T(8,128)S(1)} %select_add_fusion.4), channel_id=1, source_target_pairs={{0,128},{1,129},{2,130},{3,131},{4,132},{5,133},{6,134},{7,135},{8... | collective-permute-start | bytes 221192 | tf_op jit(solution)/shard_map/ppermute | solution.py:112
  93.9 5.3 %collective-permute-start.10 = (f32[16,1152]{1,0:T(8,128)S(1)}, f32[16,1152]{1,0:T(8,128)S(1)}, u32[]{:S(2)}, u32[]{:S(2)}) collective-permute-start(f32[16,1152]{1,0:T(8,128)S(1)} %add.263), channel_id=1, source_target_pairs={{0,16},{1,17},{2,18},{3,19},{4,20},{5,21},{6,22},{7,23},{8,24},{9,... | collective-permute-start | bytes 221192 | tf_op jit(solution)/shard_map/ppermute | solution.py:112
  99.2 4.8 %collective-permute-start.11 = (f32[16,1152]{1,0:T(8,128)S(1)}, f32[16,1152]{1,0:T(8,128)S(1)}, u32[]{:S(2)}, u32[]{:S(2)}) collective-permute-start(f32[16,1152]{1,0:T(8,128)S(1)} %add.264), channel_id=1, source_target_pairs={{0,2},{1,3},{2,0},{3,1},{4,6},{5,7},{6,4},{7,5},{8,10},{9,11},{10,... | collective-permute-start | bytes 221192 | tf_op jit(solution)/shard_map/ppermute | solution.py:112
  104.0 6.8 %collective-permute-start.12 = (bf16[16,1152]{1,0:T(8,128)(2,1)S(1)}, bf16[16,1152]{1,0:T(8,128)(2,1)S(1)}, u32[]{:S(2)}, u32[]{:S(2)}) collective-permute-start(bf16[16,1152]{1,0:T(8,128)(2,1)S(1)} %add_convert_fusion.1), channel_id=1, source_target_pairs={{0,4},{1,5},{2,6},{3,7},{4,0},{5,1},{6,2},{7,3},{8,12},{9,13},{10,... | collective-permute-start | bytes 110600 | tf_op jit(solution)/shard_map/ppermute | solution.py:116
  110.9 3.5 %collective-permute-start.13 = (bf16[32,1152]{1,0:T(8,128)(2,1)S(1)}, bf16[32,1152]{1,0:T(8,128)(2,1)S(1)}, u32[]{:S(2)}, u32[]{:S(2)}) collective-permute-start(bf16[32,1152]{1,0:T(8,128)(2,1)S(1)} %pad_maximum_fusion.4), channel_id=1, source_target_pairs={{0,1},{1,0},{2,3},{3,2},{4,5},{5,4},{6,7},{7,6},{8,9},{9,8},{10,11... | collective-permute-start | bytes 221192 | tf_op jit(solution)/shard_map/ppermute | solution.py:116
  114.4 4.4 %collective-permute-start.14 = (bf16[64,1152]{1,0:T(8,128)(2,1)S(1)}, bf16[64,1152]{1,0:T(8,128)(2,1)S(1)}, u32[]{:S(2)}, u32[]{:S(2)}) collective-permute-start(bf16[64,1152]{1,0:T(8,128)(2,1)S(1)} %pad_maximum_fusion.3), channel_id=1, source_target_pairs={{0,8},{1,9},{2,10},{3,11},{4,12},{5,13},{6,14},{7,15},{8,0},{9,1},... | collective-permute-start | bytes 442376 | tf_op jit(solution)/shard_map/ppermute | solution.py:116
  118.9 6.0 %collective-permute-start.15 = (bf16[128,1152]{1,0:T(8,128)(2,1)S(1)}, bf16[128,1152]{1,0:T(8,128)(2,1)S(1)}, u32[]{:S(2)}, u32[]{:S(2)}) collective-permute-start(bf16[128,1152]{1,0:T(8,128)(2,1)S(1)} %pad_maximum_fusion.2), channel_id=1, source_target_pairs={{0,64},{1,65},{2,66},{3,67},{4,68},{5,69},{6,70},{7,71},{8,72},{9,... | collective-permute-start | bytes 884744 | tf_op jit(solution)/shard_map/ppermute | solution.py:116
  125.0 14.3 %collective-permute-start.16 = (bf16[256,1152]{1,0:T(8,128)(2,1)S(1)}, bf16[256,1152]{1,0:T(8,128)(2,1)S(1)}, u32[]{:S(2)}, u32[]{:S(2)}) collective-permute-start(bf16[256,1152]{1,0:T(8,128)(2,1)S(1)} %pad_maximum_fusion.1), channel_id=1, source_target_pairs={{0,32},{1,33},{2,34},{3,35},{4,36},{5,37},{6,38},{7,39},{8,40},{9,... | collective-permute-start | bytes 1769480 | tf_op jit(solution)/shard_map/ppermute | solution.py:116

commit v12 on v10

--- a/solution.py
+++ b/solution.py
@@ -52,7 +52,7 @@
 
 def accumulate(offset, cluster_ids, cells, weights, width):
     length, feats = cells.shape
-    block = min(2048, length)
+    block = min(4096, length)
     lanes = 128
     offsets = jnp.full((8, lanes), offset, jnp.int32)
     sums = pl.pallas_call(

time: 141 us -> 140 us (level)
  no operation moved by 1% of the time
where the time goes in v12:
time: 140 us
  waiting for transfers between devices  55.6 us (40%)
  starting transfers between devices  44.3 us (32%)
  Pallas kernels  17.6 us (13%)
  local copies, waits for them, and re-layouts  9.28 us (7%)
  other arithmetic  8.42 us (6%)
  matrix products  3.53 us (3%)
    ppermute x4, waiting for transfers between devices, all_sum(): got = lax.ppermute(jnp.where(upper, low, high), axes, perm)  19.6 us
    pallas_call x1, Pallas kernels, accumulate(): pl.pallas_call(pooled_sums_kernel, grid=(length // block,), in_specs=[pl....  17.6 us
    ppermute x4, starting transfers between devices, all_sum(): value = value + lax.ppermute(value, axes, perm)  14.4 us
    ppermute x4, starting transfers between devices, all_sum(): got = lax.ppermute(value, axes, perm)  13.8 us
    ppermute x4, waiting for transfers between devices, all_sum(): value = value + lax.ppermute(value, axes, perm)  13.8 us
    ppermute x4, waiting for transfers between devices, all_sum(): got = lax.ppermute(value, axes, perm)  13.5 us
    ppermute x2, starting transfers between devices, passed_along(): lax.ppermute(value, axis, [(source, source + steps) for source in range(i...  7.02 us
    ppermute x2, waiting for transfers between devices, passed_along(): lax.ppermute(value, axis, [(source, source + steps) for source in range(i...  4.64 us
  transfers between devices with their start and end apart: 16, of which 15 were waited for; matrix products, arithmetic and copies ran while one was open for 0% of the time, Pallas kernels for 0%

profile of v12, /device:TPU:1, one launch (start us, length us, event | category | flops | bytes accessed | tf_op | source)
XLA Modules:
  0.0 139.7 jit_solution(10433135897961221539)
XLA Ops:
  0.6 0.0 copy-start
  0.7 0.6 broadcast_in_dim.6.offset_ref
  1.2 17.6 %shard_map.111 = f32[768,384]{1,0:T(8,128)} custom-call(s32[8,128]{1,0:T(8,128)} %broadcast_in_dim.6.offset_ref, s32[1,16384]{1,0:T(1,128)} %ids_ref.1, f32[1,16384]{1,0:T(1,128)} %weight_ref.1, bf16[16384,256]{1,0:T(8,128)(2,1)} %bitcast.45), custom_call_target="tpu_custom_call" | custom-call | flops 9663676416 | bytes 9699328 | tf_op jit(solution)/shard_map/pallas_call | solution.py:58
  18.9 1.2 fusion.28
  20.1 5.1 %collective-permute-start = (f32[256,384]{1,0:T(8,128)S(1)}, f32[256,384]{1,0:T(8,128)S(1)}, u32[]{:S(2)}, u32[]{:S(2)}) collective-permute-start(f32[256,384]{1,0:T(8,128)S(1)} %get-tuple-element.16), channel_id=1, source_target_pairs={{32,0},{64,32},{96,64},{128,96},{160,128},{192,160},{224,192},{33,... | collective-permute-start | bytes 1179656 | tf_op jit(solution)/shard_map/ppermute | solution.py:11
  25.2 1.9 %collective-permute-start.1 = (f32[256,384]{1,0:T(8,128)S(1)}, f32[256,384]{1,0:T(8,128)S(1)}, u32[]{:S(2)}, u32[]{:S(2)}) collective-permute-start(f32[256,384]{1,0:T(8,128)S(1)} %get-tuple-element.17), channel_id=1, source_target_pairs={{0,32},{32,64},{64,96},{96,128},{128,160},{160,192},{192,224},{1,3... | collective-permute-start | bytes 1179656 | tf_op jit(solution)/shard_map/ppermute | solution.py:11
  27.1 0.0 copy-start.2
  27.2 2.8 %collective-permute-done = f32[256,384]{1,0:T(8,128)S(1)} collective-permute-done((f32[256,384]{1,0:T(8,128)S(1)}, f32[256,384]{1,0:T(8,128)S(1)}, u32[]{:S(2)}, u32[]{:S(2)}) %collective-permute-start) | collective-permute-done | bytes 393248 | tf_op jit(solution)/shard_map/ppermute | solution.py:11
  30.0 1.8 %collective-permute-done.1 = f32[256,384]{1,0:T(8,128)S(1)} collective-permute-done((f32[256,384]{1,0:T(8,128)S(1)}, f32[256,384]{1,0:T(8,128)S(1)}, u32[]{:S(2)}, u32[]{:S(2)}) %collective-permute-start.1) | collective-permute-done | bytes 393248 | tf_op jit(solution)/shard_map/ppermute | solution.py:11
  31.8 1.1 fusion.6
  32.9 0.2 fusion.20
  33.1 0.1 fusion.19
  33.2 4.4 %collective-permute-start.2 = (bf16[1,256,256]{2,1,0:T(8,128)(2,1)S(1)}, bf16[1,256,256]{2,1,0:T(8,128)(2,1)S(1)}, u32[]{:S(2)}, u32[]{:S(2)}) collective-permute-start(bf16[1,256,256]{2,1,0:T(8,128)(2,1)S(1)} %fusion.19), channel_id=1, source_target_pairs={{0,32},{32,64},{64,96},{96,128},{128,160},{160,192},{192,224},{1,3... | collective-permute-start | bytes 393224 | tf_op jit(solution)/shard_map/ppermute | solution.py:19
  37.6 1.9 %collective-permute-start.3 = (bf16[1,256,256]{2,1,0:T(8,128)(2,1)S(1)}, bf16[1,256,256]{2,1,0:T(8,128)(2,1)S(1)}, u32[]{:S(2)}, u32[]{:S(2)}) collective-permute-start(bf16[1,256,256]{2,1,0:T(8,128)(2,1)S(1)} %fusion.19), channel_id=1, source_target_pairs={{32,0},{64,32},{96,64},{128,96},{160,128},{192,160},{224,192},{33,... | collective-permute-start | bytes 393224 | tf_op jit(solution)/shard_map/ppermute | solution.py:22
  39.5 0.3 fusion.23
  39.8 4.0 %collective-permute-done.3 = bf16[1,256,256]{2,1,0:T(8,128)(2,1)S(1)} collective-permute-done((bf16[1,256,256]{2,1,0:T(8,128)(2,1)S(1)}, bf16[1,256,256]{2,1,0:T(8,128)(2,1)S(1)}, u32[]{:S(2)}, u32[]{:S(2)}) %collective-permute-start.3) | collective-permute-done | bytes 131104 | tf_op jit(solution)/shard_map/ppermute | solution.py:22
  43.9 1.0 fusion.2
  44.9 0.0 copy-start.6
  44.9 0.5 multiply_convert_fusion
  45.4 0.2 copy-done.4
  45.6 0.2 fusion.30
  45.8 0.4 fusion.26
  46.2 0.6 fusion.1
  46.8 0.3 fusion.21
  47.1 0.3 fusion.31
  47.4 0.1 reshape.545
  47.5 1.5 %pad_maximum_fusion = f32[512,1024]{1,0:T(8,128)} fusion(f32[256,1024]{1,0:T(8,128)S(1)} %fusion.31, f32[256,1024]{1,0:T(8,128)S(1)} %fusion.21), kind=kLoop, calls=%fused_computation | loop fusion | flops 524288 | bytes 4194304 | tf_op jit(solution)/shard_map/concatenate | solution.py:169
  49.0 2.6 %concatenate.23 = f32[512,1152]{1,0:T(8,128)S(1)} concatenate(f32[512,1024]{1,0:T(8,128)} %pad_maximum_fusion, f32[512,16]{1,0:T(8,128)S(1)} %reshape.545, f32[512,112]{1,0:T(8,128)S(1)} %broadcast_in_dim.8), dimensions={1} | concatenate | bytes 4718592 | tf_op jit(solution)/shard_map/concatenate | solution.py:168
  51.6 1.2 slice_select_fusion
  52.8 3.2 %collective-permute-done.4 = f32[256,1152]{1,0:T(8,128)} collective-permute-done((f32[256,1152]{1,0:T(8,128)}, f32[256,1152]{1,0:T(8,128)}, u32[]{:S(2)}, u32[]{:S(2)}) %collective-permute-start.4) | collective-permute-done | bytes 1179680 | tf_op jit(solution)/shard_map/ppermute | solution.py:109
  56.0 1.4 %select_add_fusion = f32[256,1152]{1,0:T(8,128)S(1)} fusion(f32[256,1152]{1,0:T(8,128)} %collective-permute-done.4, f32[512,1152]{1,0:T(8,128)S(1)} %concatenate.23, pred[]{:T(512)S(6)} %eq.321), kind=kLoop, calls=%fused_computation.6 | loop fusion | flops 589824 | bytes 4718593 | tf_op jit(solution)/shard_map/add | solution.py:110
  57.4 1.0 copy-done.1
  58.5 0.1 slice_select_fusion.1
  58.5 0.8 collective-permute-start.5
  59.3 8.3 %collective-permute-done.5 = f32[128,1152]{1,0:T(8,128)S(1)} collective-permute-done((f32[128,1152]{1,0:T(8,128)S(1)}, f32[128,1152]{1,0:T(8,128)S(1)}, u32[]{:S(2)}, u32[]{:S(2)}) %collective-permute-start.5) | collective-permute-done | bytes 589856 | tf_op jit(solution)/shard_map/ppermute | solution.py:109
  67.7 1.3 select_add_fusion.1
  69.0 1.1 collective-permute-start.6
  70.1 4.8 %collective-permute-done.6 = f32[64,1152]{1,0:T(8,128)S(1)} collective-permute-done((f32[64,1152]{1,0:T(8,128)S(1)}, f32[64,1152]{1,0:T(8,128)S(1)}, u32[]{:S(2)}, u32[]{:S(2)}) %collective-permute-start.6) | collective-permute-done | bytes 294944 | tf_op jit(solution)/shard_map/ppermute | solution.py:109
  75.1 0.9 collective-permute-start.7
  75.9 3.2 %collective-permute-done.7 = f32[32,1152]{1,0:T(8,128)S(1)} collective-permute-done((f32[32,1152]{1,0:T(8,128)S(1)}, f32[32,1152]{1,0:T(8,128)S(1)}, u32[]{:S(2)}, u32[]{:S(2)}) %collective-permute-start.7) | collective-permute-done | bytes 147488 | tf_op jit(solution)/shard_map/ppermute | solution.py:109
  79.2 2.6 %collective-permute-start.8 = (f32[32,1152]{1,0:T(8,128)S(1)}, f32[32,1152]{1,0:T(8,128)S(1)}, u32[]{:S(2)}, u32[]{:S(2)}) collective-permute-start(f32[32,1152]{1,0:T(8,128)S(1)} %select_add_fusion.3), channel_id=1, source_target_pairs={{0,128},{1,129},{2,130},{3,131},{4,132},{5,133},{6,134},{7,135},{8... | collective-permute-start | bytes 442376 | tf_op jit(solution)/shard_map/ppermute | solution.py:112
  81.7 3.0 %collective-permute-done.8 = f32[32,1152]{1,0:T(8,128)S(1)} collective-permute-done((f32[32,1152]{1,0:T(8,128)S(1)}, f32[32,1152]{1,0:T(8,128)S(1)}, u32[]{:S(2)}, u32[]{:S(2)}) %collective-permute-start.8) | collective-permute-done | bytes 147488 | tf_op jit(solution)/shard_map/ppermute | solution.py:112
  84.8 2.6 %collective-permute-start.9 = (f32[32,1152]{1,0:T(8,128)S(1)}, f32[32,1152]{1,0:T(8,128)S(1)}, u32[]{:S(2)}, u32[]{:S(2)}) collective-permute-start(f32[32,1152]{1,0:T(8,128)S(1)} %add.252), channel_id=1, source_target_pairs={{0,16},{1,17},{2,18},{3,19},{4,20},{5,21},{6,22},{7,23},{8,24},{9,... | collective-permute-start | bytes 442376 | tf_op jit(solution)/shard_map/ppermute | solution.py:112
  87.4 4.1 %collective-permute-done.9 = f32[32,1152]{1,0:T(8,128)S(1)} collective-permute-done((f32[32,1152]{1,0:T(8,128)S(1)}, f32[32,1152]{1,0:T(8,128)S(1)}, u32[]{:S(2)}, u32[]{:S(2)}) %collective-permute-start.9) | collective-permute-done | bytes 147488 | tf_op jit(solution)/shard_map/ppermute | solution.py:112
  91.5 3.0 %collective-permute-start.10 = (f32[32,1152]{1,0:T(8,128)S(1)}, f32[32,1152]{1,0:T(8,128)S(1)}, u32[]{:S(2)}, u32[]{:S(2)}) collective-permute-start(f32[32,1152]{1,0:T(8,128)S(1)} %add.253), channel_id=1, source_target_pairs={{0,2},{1,3},{2,0},{3,1},{4,6},{5,7},{6,4},{7,5},{8,10},{9,11},{10,... | collective-permute-start | bytes 442376 | tf_op jit(solution)/shard_map/ppermute | solution.py:112
  94.5 2.8 %collective-permute-done.10 = f32[32,1152]{1,0:T(8,128)S(1)} collective-permute-done((f32[32,1152]{1,0:T(8,128)S(1)}, f32[32,1152]{1,0:T(8,128)S(1)}, u32[]{:S(2)}, u32[]{:S(2)}) %collective-permute-start.10) | collective-permute-done | bytes 147488 | tf_op jit(solution)/shard_map/ppermute | solution.py:112
  97.3 6.2 %collective-permute-start.11 = (f32[32,1152]{1,0:T(8,128)S(1)}, f32[32,1152]{1,0:T(8,128)S(1)}, u32[]{:S(2)}, u32[]{:S(2)}) collective-permute-start(f32[32,1152]{1,0:T(8,128)S(1)} %add.254), channel_id=1, source_target_pairs={{0,4},{1,5},{2,6},{3,7},{4,0},{5,1},{6,2},{7,3},{8,12},{9,13},{10,... | collective-permute-start | bytes 442376 | tf_op jit(solution)/shard_map/ppermute | solution.py:112
  103.5 3.9 %collective-permute-done.11 = f32[32,1152]{1,0:T(8,128)S(1)} collective-permute-done((f32[32,1152]{1,0:T(8,128)S(1)}, f32[32,1152]{1,0:T(8,128)S(1)}, u32[]{:S(2)}, u32[]{:S(2)}) %collective-permute-start.11) | collective-permute-done | bytes 147488 | tf_op jit(solution)/shard_map/ppermute | solution.py:112
  107.4 1.3 collective-permute-start.12
  108.7 2.0 %collective-permute-done.12 = bf16[32,1152]{1,0:T(8,128)(2,1)S(1)} collective-permute-done((bf16[32,1152]{1,0:T(8,128)(2,1)S(1)}, bf16[32,1152]{1,0:T(8,128)(2,1)S(1)}, u32[]{:S(2)}, u32[]{:S(2)}) %collective-permute-start.12) | collective-permute-done | bytes 73760 | tf_op jit(solution)/shard_map/ppermute | solution.py:116
  110.7 0.1 collective-permute-start.13
  110.8 5.6 %collective-permute-done.13 = bf16[64,1152]{1,0:T(8,128)(2,1)S(1)} collective-permute-done((bf16[64,1152]{1,0:T(8,128)(2,1)S(1)}, bf16[64,1152]{1,0:T(8,128)(2,1)S(1)}, u32[]{:S(2)}, u32[]{:S(2)}) %collective-permute-start.13) | collective-permute-done | bytes 147488 | tf_op jit(solution)/shard_map/ppermute | solution.py:116
  116.4 0.1 broadcast_select_fusion.5
  116.5 1.3 collective-permute-start.14
  117.8 4.4 %collective-permute-done.14 = bf16[128,1152]{1,0:T(8,128)(2,1)S(1)} collective-permute-done((bf16[128,1152]{1,0:T(8,128)(2,1)S(1)}, bf16[128,1152]{1,0:T(8,128)(2,1)S(1)}, u32[]{:S(2)}, u32[]{:S(2)}) %collective-permute-start.14) | collective-permute-done | bytes 294944 | tf_op jit(solution)/shard_map/ppermute | solution.py:116
  122.2 0.1 broadcast_select_fusion.3
  122.3 11.1 %collective-permute-start.15 = (bf16[256,1152]{1,0:T(8,128)(2,1)S(1)}, bf16[256,1152]{1,0:T(8,128)(2,1)S(1)}, u32[]{:S(2)}, u32[]{:S(2)}) collective-permute-start(bf16[256,1152]{1,0:T(8,128)(2,1)S(1)} %pad_maximum_fusion.1), channel_id=1, source_target_pairs={{0,32},{1,33},{2,34},{3,35},{4,36},{5,37},{6,38},{7,39},{8,40},{9,... | collective-permute-start | bytes 1769480 | tf_op jit(solution)/shard_map/ppermute | solution.py:116
  133.4 1.6 %collective-permute-done.15 = bf16[256,1152]{1,0:T(8,128)(2,1)S(1)} collective-permute-done((bf16[256,1152]{1,0:T(8,128)(2,1)S(1)}, bf16[256,1152]{1,0:T(8,128)(2,1)S(1)}, u32[]{:S(2)}, u32[]{:S(2)}) %collective-permute-start.15) | collective-permute-done | bytes 589856 | tf_op jit(solution)/shard_map/ppermute | solution.py:116
  135.1 0.2 broadcast_select_fusion.1
  135.3 0.7 maximum_convert_fusion.1
  136.0 0.2 maximum_convert_fusion
  136.2 1.1 reshape.546
  137.3 0.8 copy.15
  138.1 1.6 %fusion.27 = (f32[256,1024]{1,0:T(8,128)}, f32[256,1024]{1,0:T(8,128)}) fusion(f32[512,1152]{1,0:T(8,128)S(1)} %maximum_convert_fusion), kind=kLoop, calls=%fused_computation.71 | loop fusion | bytes 4194304 | tf_op jit(solution)/shard_map/slice | solution.py:173
  (26 shorter events, 0.4 us)
Async XLA Ops:
  0.6 44.2 %copy-start = (bf16[256,1024]{1,0:T(8,128)(2,1)S(1)}, bf16[256,1024]{1,0:T(8,128)(2,1)}, u32[]{:S(2)}) copy-start(bf16[256,1024]{1,0:T(8,128)(2,1)} %param.14) | copy-start | bytes 1572868
  18.9 8.2 %copy-start.5 = (s32[1,256,8]{1,2,0:T(8,128)S(1)}, s32[1,256,8]{1,2,0:T(8,128)}, u32[]{:S(2)}) copy-start(s32[1,256,8]{1,2,0:T(8,128)} %param.11) | copy-start | bytes 24580
  20.1 9.9 %collective-permute-start = (f32[256,384]{1,0:T(8,128)S(1)}, f32[256,384]{1,0:T(8,128)S(1)}, u32[]{:S(2)}, u32[]{:S(2)}) collective-permute-start(f32[256,384]{1,0:T(8,128)S(1)} %get-tuple-element.16), channel_id=1, source_target_pairs={{32,0},{64,32},{96,64},{128,96},{160,128},{192,160},{224,192},{33,... | collective-permute-start | bytes 1179656 | tf_op jit(solution)/shard_map/ppermute | solution.py:11
  25.2 6.6 %collective-permute-start.1 = (f32[256,384]{1,0:T(8,128)S(1)}, f32[256,384]{1,0:T(8,128)S(1)}, u32[]{:S(2)}, u32[]{:S(2)}) collective-permute-start(f32[256,384]{1,0:T(8,128)S(1)} %get-tuple-element.17), channel_id=1, source_target_pairs={{0,32},{32,64},{64,96},{96,128},{128,160},{160,192},{192,224},{1,3... | collective-permute-start | bytes 1179656 | tf_op jit(solution)/shard_map/ppermute | solution.py:11
  27.1 12.4 %copy-start.2 = (bf16[256,1024]{1,0:T(8,128)(2,1)S(1)}, bf16[256,1024]{1,0:T(8,128)(2,1)}, u32[]{:S(2)}) copy-start(bf16[256,1024]{1,0:T(8,128)(2,1)} %param.13) | copy-start | bytes 1572868
  33.2 6.6 %collective-permute-start.2 = (bf16[1,256,256]{2,1,0:T(8,128)(2,1)S(1)}, bf16[1,256,256]{2,1,0:T(8,128)(2,1)S(1)}, u32[]{:S(2)}, u32[]{:S(2)}) collective-permute-start(bf16[1,256,256]{2,1,0:T(8,128)(2,1)S(1)} %fusion.19), channel_id=1, source_target_pairs={{0,32},{32,64},{64,96},{96,128},{128,160},{160,192},{192,224},{1,3... | collective-permute-start | bytes 393224 | tf_op jit(solution)/shard_map/ppermute | solution.py:19
  37.6 6.3 %collective-permute-start.3 = (bf16[1,256,256]{2,1,0:T(8,128)(2,1)S(1)}, bf16[1,256,256]{2,1,0:T(8,128)(2,1)S(1)}, u32[]{:S(2)}, u32[]{:S(2)}) collective-permute-start(bf16[1,256,256]{2,1,0:T(8,128)(2,1)S(1)} %fusion.19), channel_id=1, source_target_pairs={{32,0},{64,32},{96,64},{128,96},{160,128},{192,160},{224,192},{33,... | collective-permute-start | bytes 393224 | tf_op jit(solution)/shard_map/ppermute | solution.py:22
  44.9 0.7 copy-start.4
  44.9 0.9 copy-start.6
  45.8 0.9 copy-start.3
  52.8 3.2 %collective-permute-start.4 = (f32[256,1152]{1,0:T(8,128)}, f32[256,1152]{1,0:T(8,128)}, u32[]{:S(2)}, u32[]{:S(2)}) collective-permute-start(f32[256,1152]{1,0:T(8,128)} %slice_select_fusion), channel_id=1, source_target_pairs={{0,32},{1,33},{2,34},{3,35},{4,36},{5,37},{6,38},{7,39},{8,40},{9,... | collective-permute-start | bytes 3538952 | tf_op jit(solution)/shard_map/ppermute | solution.py:109
  57.4 1.0 copy-start.1
  58.5 9.1 %collective-permute-start.5 = (f32[128,1152]{1,0:T(8,128)S(1)}, f32[128,1152]{1,0:T(8,128)S(1)}, u32[]{:S(2)}, u32[]{:S(2)}) collective-permute-start(f32[128,1152]{1,0:T(8,128)S(1)} %slice_select_fusion.1), channel_id=1, source_target_pairs={{0,64},{1,65},{2,66},{3,67},{4,68},{5,69},{6,70},{7,71},{8,72},{9,... | collective-permute-start | bytes 1769480 | tf_op jit(solution)/shard_map/ppermute | solution.py:109
  69.0 6.0 %collective-permute-start.6 = (f32[64,1152]{1,0:T(8,128)S(1)}, f32[64,1152]{1,0:T(8,128)S(1)}, u32[]{:S(2)}, u32[]{:S(2)}) collective-permute-start(f32[64,1152]{1,0:T(8,128)S(1)} %slice_select_fusion.2), channel_id=1, source_target_pairs={{0,8},{1,9},{2,10},{3,11},{4,12},{5,13},{6,14},{7,15},{8,0},{9,1},... | collective-permute-start | bytes 884744 | tf_op jit(solution)/shard_map/ppermute | solution.py:109
  75.1 4.1 %collective-permute-start.7 = (f32[32,1152]{1,0:T(8,128)S(1)}, f32[32,1152]{1,0:T(8,128)S(1)}, u32[]{:S(2)}, u32[]{:S(2)}) collective-permute-start(f32[32,1152]{1,0:T(8,128)S(1)} %slice_select_fusion.3), channel_id=1, source_target_pairs={{0,1},{1,0},{2,3},{3,2},{4,5},{5,4},{6,7},{7,6},{8,9},{9,8},{10,11... | collective-permute-start | bytes 442376 | tf_op jit(solution)/shard_map/ppermute | solution.py:109
  79.2 5.6 %collective-permute-start.8 = (f32[32,1152]{1,0:T(8,128)S(1)}, f32[32,1152]{1,0:T(8,128)S(1)}, u32[]{:S(2)}, u32[]{:S(2)}) collective-permute-start(f32[32,1152]{1,0:T(8,128)S(1)} %select_add_fusion.3), channel_id=1, source_target_pairs={{0,128},{1,129},{2,130},{3,131},{4,132},{5,133},{6,134},{7,135},{8... | collective-permute-start | bytes 442376 | tf_op jit(solution)/shard_map/ppermute | solution.py:112
  84.8 6.7 %collective-permute-start.9 = (f32[32,1152]{1,0:T(8,128)S(1)}, f32[32,1152]{1,0:T(8,128)S(1)}, u32[]{:S(2)}, u32[]{:S(2)}) collective-permute-start(f32[32,1152]{1,0:T(8,128)S(1)} %add.252), channel_id=1, source_target_pairs={{0,16},{1,17},{2,18},{3,19},{4,20},{5,21},{6,22},{7,23},{8,24},{9,... | collective-permute-start | bytes 442376 | tf_op jit(solution)/shard_map/ppermute | solution.py:112
  91.5 5.8 %collective-permute-start.10 = (f32[32,1152]{1,0:T(8,128)S(1)}, f32[32,1152]{1,0:T(8,128)S(1)}, u32[]{:S(2)}, u32[]{:S(2)}) collective-permute-start(f32[32,1152]{1,0:T(8,128)S(1)} %add.253), channel_id=1, source_target_pairs={{0,2},{1,3},{2,0},{3,1},{4,6},{5,7},{6,4},{7,5},{8,10},{9,11},{10,... | collective-permute-start | bytes 442376 | tf_op jit(solution)/shard_map/ppermute | solution.py:112
  97.3 10.1 %collective-permute-start.11 = (f32[32,1152]{1,0:T(8,128)S(1)}, f32[32,1152]{1,0:T(8,128)S(1)}, u32[]{:S(2)}, u32[]{:S(2)}) collective-permute-start(f32[32,1152]{1,0:T(8,128)S(1)} %add.254), channel_id=1, source_target_pairs={{0,4},{1,5},{2,6},{3,7},{4,0},{5,1},{6,2},{7,3},{8,12},{9,13},{10,... | collective-permute-start | bytes 442376 | tf_op jit(solution)/shard_map/ppermute | solution.py:112
  107.4 3.3 %collective-permute-start.12 = (bf16[32,1152]{1,0:T(8,128)(2,1)S(1)}, bf16[32,1152]{1,0:T(8,128)(2,1)S(1)}, u32[]{:S(2)}, u32[]{:S(2)}) collective-permute-start(bf16[32,1152]{1,0:T(8,128)(2,1)S(1)} %add_convert_fusion.1), channel_id=1, source_target_pairs={{0,1},{1,0},{2,3},{3,2},{4,5},{5,4},{6,7},{7,6},{8,9},{9,8},{10,11... | collective-permute-start | bytes 221192 | tf_op jit(solution)/shard_map/ppermute | solution.py:116
  110.7 5.7 %collective-permute-start.13 = (bf16[64,1152]{1,0:T(8,128)(2,1)S(1)}, bf16[64,1152]{1,0:T(8,128)(2,1)S(1)}, u32[]{:S(2)}, u32[]{:S(2)}) collective-permute-start(bf16[64,1152]{1,0:T(8,128)(2,1)S(1)} %pad_maximum_fusion.3), channel_id=1, source_target_pairs={{0,8},{1,9},{2,10},{3,11},{4,12},{5,13},{6,14},{7,15},{8,0},{9,1},... | collective-permute-start | bytes 442376 | tf_op jit(solution)/shard_map/ppermute | solution.py:116
  116.5 5.7 %collective-permute-start.14 = (bf16[128,1152]{1,0:T(8,128)(2,1)S(1)}, bf16[128,1152]{1,0:T(8,128)(2,1)S(1)}, u32[]{:S(2)}, u32[]{:S(2)}) collective-permute-start(bf16[128,1152]{1,0:T(8,128)(2,1)S(1)} %pad_maximum_fusion.2), channel_id=1, source_target_pairs={{0,64},{1,65},{2,66},{3,67},{4,68},{5,69},{6,70},{7,71},{8,72},{9,... | collective-permute-start | bytes 884744 | tf_op jit(solution)/shard_map/ppermute | solution.py:116
  122.3 12.7 %collective-permute-start.15 = (bf16[256,1152]{1,0:T(8,128)(2,1)S(1)}, bf16[256,1152]{1,0:T(8,128)(2,1)S(1)}, u32[]{:S(2)}, u32[]{:S(2)}) collective-permute-start(bf16[256,1152]{1,0:T(8,128)(2,1)S(1)} %pad_maximum_fusion.1), channel_id=1, source_target_pairs={{0,32},{1,33},{2,34},{3,35},{4,36},{5,37},{6,38},{7,39},{8,40},{9,... | collective-permute-start | bytes 1769480 | tf_op jit(solution)/shard_map/ppermute | solution.py:116

commit v13 on v12

--- a/solution.py
+++ b/solution.py
@@ -157,16 +157,16 @@
     grad_head = jnp.einsum("ekh,ekc->hc", units, d_logits, preferred_element_type=jnp.float32)
     d_units = jnp.einsum("ekc,hc->ekh", d_logits, w_out, preferred_element_type=jnp.float32)
     d_z = (d_units * sig * (1.0 + zval * (1.0 - sig))).astype(jnp.bfloat16)
-    grad_own = jnp.einsum("ekf,ekh->fh", pooled, d_z, preferred_element_type=jnp.float32)
-    grad_side = jnp.einsum("ekf,ekh->fh", agg, d_z, preferred_element_type=jnp.float32)
+    both = jnp.concatenate([pooled, agg], axis=2)
+    grads = jnp.einsum("ekf,ekh->fh", both, d_z, preferred_element_type=jnp.float32)
     sizes = {"region": lax.axis_size("region"), "dp": lax.axis_size("dp")}
-    feats, hid = grad_own.shape
-    rows = 2 * feats
+    rows, hid = grads.shape
+    feats = rows // 2
     head = grad_head.reshape(rows, -1)
     lanes = 128
     spare = jnp.zeros((rows, lanes - head.shape[1]), jnp.float32)
     packed = jnp.concatenate(
-        [jnp.concatenate([grad_own, grad_side], axis=0), head, spare], axis=1
+        [grads, head, spare], axis=1
     )
     packed = all_sum(packed, sizes, 4)
     packed = packed.astype(jnp.float32)

time: 140 us -> 140 us (level)
  other arithmetic: 8.42 us -> 6.94 us
    concatenate x1 -> x0, other arithmetic: 1.48 us -> none  [local(): jnp.concatenate([grad_own, grad_side], axis=0)]
where the time goes in v13:
time: 140 us; the launch traced here: 139 us
  waiting for transfers between devices  55.5 us (40%)
  starting transfers between devices  44.4 us (32%)
  Pallas kernels  17.6 us (13%)
  local copies, waits for them, and re-layouts  9.29 us (7%)
  other arithmetic  6.94 us (5%)
  matrix products  4.52 us (3%)
    ppermute x4, waiting for transfers between devices, all_sum(): got = lax.ppermute(jnp.where(upper, low, high), axes, perm)  19.6 us
    pallas_call x1, Pallas kernels, accumulate(): pl.pallas_call(pooled_sums_kernel, grid=(length // block,), in_specs=[pl....  17.6 us
    ppermute x4, starting transfers between devices, all_sum(): value = value + lax.ppermute(value, axes, perm)  14.3 us
    ppermute x4, starting transfers between devices, all_sum(): got = lax.ppermute(value, axes, perm)  14 us
    ppermute x4, waiting for transfers between devices, all_sum(): value = value + lax.ppermute(value, axes, perm)  13.8 us
    ppermute x4, waiting for transfers between devices, all_sum(): got = lax.ppermute(value, axes, perm)  13.4 us
    ppermute x2, starting transfers between devices, passed_along(): lax.ppermute(value, axis, [(source, source + steps) for source in range(i...  7.02 us
    ppermute x2, waiting for transfers between devices, passed_along(): lax.ppermute(value, axis, [(source, source + steps) for source in range(i...  4.64 us
  transfers between devices with their start and end apart: 16, of which 15 were waited for; matrix products, arithmetic and copies ran while one was open for 0% of the time, Pallas kernels for 0%

profile of v13, /device:TPU:1, one launch (start us, length us, event | category | flops | bytes accessed | tf_op | source)
XLA Modules:
  0.0 139.2 jit_solution(13115748813639361731)
XLA Ops:
  0.6 0.0 copy-start
  0.7 0.6 broadcast_in_dim.6.offset_ref
  1.2 17.6 %shard_map.111 = f32[768,384]{1,0:T(8,128)} custom-call(s32[8,128]{1,0:T(8,128)} %broadcast_in_dim.6.offset_ref, s32[1,16384]{1,0:T(1,128)} %ids_ref.1, f32[1,16384]{1,0:T(1,128)} %weight_ref.1, bf16[16384,256]{1,0:T(8,128)(2,1)} %bitcast.44), custom_call_target="tpu_custom_call" | custom-call | flops 9663676416 | bytes 9699328 | tf_op jit(solution)/shard_map/pallas_call | solution.py:58
  18.9 1.2 fusion.35
  20.1 5.1 %collective-permute-start = (f32[256,384]{1,0:T(8,128)S(1)}, f32[256,384]{1,0:T(8,128)S(1)}, u32[]{:S(2)}, u32[]{:S(2)}) collective-permute-start(f32[256,384]{1,0:T(8,128)S(1)} %get-tuple-element.16), channel_id=1, source_target_pairs={{32,0},{64,32},{96,64},{128,96},{160,128},{192,160},{224,192},{33,... | collective-permute-start | bytes 1179656 | tf_op jit(solution)/shard_map/ppermute | solution.py:11
  25.2 1.9 %collective-permute-start.1 = (f32[256,384]{1,0:T(8,128)S(1)}, f32[256,384]{1,0:T(8,128)S(1)}, u32[]{:S(2)}, u32[]{:S(2)}) collective-permute-start(f32[256,384]{1,0:T(8,128)S(1)} %get-tuple-element.17), channel_id=1, source_target_pairs={{0,32},{32,64},{64,96},{96,128},{128,160},{160,192},{192,224},{1,3... | collective-permute-start | bytes 1179656 | tf_op jit(solution)/shard_map/ppermute | solution.py:11
  27.1 0.0 copy-start.2
  27.2 2.8 %collective-permute-done = f32[256,384]{1,0:T(8,128)S(1)} collective-permute-done((f32[256,384]{1,0:T(8,128)S(1)}, f32[256,384]{1,0:T(8,128)S(1)}, u32[]{:S(2)}, u32[]{:S(2)}) %collective-permute-start) | collective-permute-done | bytes 393248 | tf_op jit(solution)/shard_map/ppermute | solution.py:11
  30.0 1.8 %collective-permute-done.1 = f32[256,384]{1,0:T(8,128)S(1)} collective-permute-done((f32[256,384]{1,0:T(8,128)S(1)}, f32[256,384]{1,0:T(8,128)S(1)}, u32[]{:S(2)}, u32[]{:S(2)}) %collective-permute-start.1) | collective-permute-done | bytes 393248 | tf_op jit(solution)/shard_map/ppermute | solution.py:11
  31.8 1.1 fusion.11
  32.9 0.2 fusion.27
  33.1 0.1 fusion.24
  33.2 4.4 %collective-permute-start.2 = (bf16[1,256,256]{2,1,0:T(8,128)(2,1)S(1)}, bf16[1,256,256]{2,1,0:T(8,128)(2,1)S(1)}, u32[]{:S(2)}, u32[]{:S(2)}) collective-permute-start(bf16[1,256,256]{2,1,0:T(8,128)(2,1)S(1)} %fusion.24), channel_id=1, source_target_pairs={{0,32},{32,64},{64,96},{96,128},{128,160},{160,192},{192,224},{1,3... | collective-permute-start | bytes 393224 | tf_op jit(solution)/shard_map/ppermute | solution.py:19
  37.6 1.9 %collective-permute-start.3 = (bf16[1,256,256]{2,1,0:T(8,128)(2,1)S(1)}, bf16[1,256,256]{2,1,0:T(8,128)(2,1)S(1)}, u32[]{:S(2)}, u32[]{:S(2)}) collective-permute-start(bf16[1,256,256]{2,1,0:T(8,128)(2,1)S(1)} %fusion.24), channel_id=1, source_target_pairs={{32,0},{64,32},{96,64},{128,96},{160,128},{192,160},{224,192},{33,... | collective-permute-start | bytes 393224 | tf_op jit(solution)/shard_map/ppermute | solution.py:22
  39.5 0.3 fusion.28
  39.8 0.0 collective-permute-done.2
  39.8 4.0 %collective-permute-done.3 = bf16[1,256,256]{2,1,0:T(8,128)(2,1)S(1)} collective-permute-done((bf16[1,256,256]{2,1,0:T(8,128)(2,1)S(1)}, bf16[1,256,256]{2,1,0:T(8,128)(2,1)S(1)}, u32[]{:S(2)}, u32[]{:S(2)}) %collective-permute-start.3) | collective-permute-done | bytes 131104 | tf_op jit(solution)/shard_map/ppermute | solution.py:22
  43.9 1.0 fusion.3
  44.9 0.0 copy-start.4
  44.9 0.0 copy-start.6
  44.9 0.5 multiply_convert_fusion
  45.3 0.2 copy-done.4
  45.6 0.2 fusion.37
  45.8 0.4 fusion.33
  46.2 0.1 reshape.544
  46.3 2.2 %fusion.2 = f32[512,1024]{1,0:T(8,128)} fusion(bf16[1024,8]{0,1:T(8,128)(2,1)S(1)} %copy-done.4, f32[256,1024]{1,0:T(8,128)S(1)} %get-tuple-element.33, bf16[1,256,256]{2,1,0:T(8,128)(2,1)S(1)} %bitcast.45, bf16[1,256,256]{2,1,0:T(8,128)(2,1)S(1)} %fusion.24, f32[256,8]{0,1:T(8,128)S(1)} %fusion.37, s32[256]{0:T(256)S(1)} %bitcast.35), kind=kOutput, calls=%fused_computation.4 | convolution fusion | flops 275529728 | bytes 3433472 | tf_op jit(solution)/shard_map/ekf,ekh->fh/dot_general | solution.py:161
  48.6 2.6 %concatenate.23 = f32[512,1152]{1,0:T(8,128)S(1)} concatenate(f32[512,1024]{1,0:T(8,128)} %fusion.2, f32[512,16]{1,0:T(8,128)S(1)} %reshape.544, f32[512,112]{1,0:T(8,128)S(1)} %broadcast_in_dim.8), dimensions={1} | concatenate | bytes 4718592 | tf_op jit(solution)/shard_map/concatenate | solution.py:168
  51.1 1.2 slice_select_fusion
  52.3 0.0 collective-permute-start.4
  52.3 3.2 %collective-permute-done.4 = f32[256,1152]{1,0:T(8,128)} collective-permute-done((f32[256,1152]{1,0:T(8,128)}, f32[256,1152]{1,0:T(8,128)}, u32[]{:S(2)}, u32[]{:S(2)}) %collective-permute-start.4) | collective-permute-done | bytes 1179680 | tf_op jit(solution)/shard_map/ppermute | solution.py:109
  55.5 1.4 %select_add_fusion = f32[256,1152]{1,0:T(8,128)S(1)} fusion(f32[256,1152]{1,0:T(8,128)} %collective-permute-done.4, f32[512,1152]{1,0:T(8,128)S(1)} %concatenate.23, pred[]{:T(512)S(6)} %eq.321), kind=kLoop, calls=%fused_computation.6 | loop fusion | flops 589824 | bytes 4718593 | tf_op jit(solution)/shard_map/add | solution.py:110
  56.9 1.0 copy-done.1
  58.0 0.1 slice_select_fusion.1
  58.1 0.8 collective-permute-start.5
  58.8 8.4 %collective-permute-done.5 = f32[128,1152]{1,0:T(8,128)S(1)} collective-permute-done((f32[128,1152]{1,0:T(8,128)S(1)}, f32[128,1152]{1,0:T(8,128)S(1)}, u32[]{:S(2)}, u32[]{:S(2)}) %collective-permute-start.5) | collective-permute-done | bytes 589856 | tf_op jit(solution)/shard_map/ppermute | solution.py:109
  67.2 1.3 select_add_fusion.1
  68.5 1.1 collective-permute-start.6
  69.6 4.9 %collective-permute-done.6 = f32[64,1152]{1,0:T(8,128)S(1)} collective-permute-done((f32[64,1152]{1,0:T(8,128)S(1)}, f32[64,1152]{1,0:T(8,128)S(1)}, u32[]{:S(2)}, u32[]{:S(2)}) %collective-permute-start.6) | collective-permute-done | bytes 294944 | tf_op jit(solution)/shard_map/ppermute | solution.py:109
  74.6 0.9 collective-permute-start.7
  75.4 3.2 %collective-permute-done.7 = f32[32,1152]{1,0:T(8,128)S(1)} collective-permute-done((f32[32,1152]{1,0:T(8,128)S(1)}, f32[32,1152]{1,0:T(8,128)S(1)}, u32[]{:S(2)}, u32[]{:S(2)}) %collective-permute-start.7) | collective-permute-done | bytes 147488 | tf_op jit(solution)/shard_map/ppermute | solution.py:109
  78.7 2.6 %collective-permute-start.8 = (f32[32,1152]{1,0:T(8,128)S(1)}, f32[32,1152]{1,0:T(8,128)S(1)}, u32[]{:S(2)}, u32[]{:S(2)}) collective-permute-start(f32[32,1152]{1,0:T(8,128)S(1)} %select_add_fusion.3), channel_id=1, source_target_pairs={{0,128},{1,129},{2,130},{3,131},{4,132},{5,133},{6,134},{7,135},{8... | collective-permute-start | bytes 442376 | tf_op jit(solution)/shard_map/ppermute | solution.py:112
  81.2 3.0 %collective-permute-done.8 = f32[32,1152]{1,0:T(8,128)S(1)} collective-permute-done((f32[32,1152]{1,0:T(8,128)S(1)}, f32[32,1152]{1,0:T(8,128)S(1)}, u32[]{:S(2)}, u32[]{:S(2)}) %collective-permute-start.8) | collective-permute-done | bytes 147488 | tf_op jit(solution)/shard_map/ppermute | solution.py:112
  84.3 2.6 %collective-permute-start.9 = (f32[32,1152]{1,0:T(8,128)S(1)}, f32[32,1152]{1,0:T(8,128)S(1)}, u32[]{:S(2)}, u32[]{:S(2)}) collective-permute-start(f32[32,1152]{1,0:T(8,128)S(1)} %add.252), channel_id=1, source_target_pairs={{0,16},{1,17},{2,18},{3,19},{4,20},{5,21},{6,22},{7,23},{8,24},{9,... | collective-permute-start | bytes 442376 | tf_op jit(solution)/shard_map/ppermute | solution.py:112
  86.9 4.1 %collective-permute-done.9 = f32[32,1152]{1,0:T(8,128)S(1)} collective-permute-done((f32[32,1152]{1,0:T(8,128)S(1)}, f32[32,1152]{1,0:T(8,128)S(1)}, u32[]{:S(2)}, u32[]{:S(2)}) %collective-permute-start.9) | collective-permute-done | bytes 147488 | tf_op jit(solution)/shard_map/ppermute | solution.py:112
  91.0 3.0 %collective-permute-start.10 = (f32[32,1152]{1,0:T(8,128)S(1)}, f32[32,1152]{1,0:T(8,128)S(1)}, u32[]{:S(2)}, u32[]{:S(2)}) collective-permute-start(f32[32,1152]{1,0:T(8,128)S(1)} %add.253), channel_id=1, source_target_pairs={{0,2},{1,3},{2,0},{3,1},{4,6},{5,7},{6,4},{7,5},{8,10},{9,11},{10,... | collective-permute-start | bytes 442376 | tf_op jit(solution)/shard_map/ppermute | solution.py:112
  94.0 2.8 %collective-permute-done.10 = f32[32,1152]{1,0:T(8,128)S(1)} collective-permute-done((f32[32,1152]{1,0:T(8,128)S(1)}, f32[32,1152]{1,0:T(8,128)S(1)}, u32[]{:S(2)}, u32[]{:S(2)}) %collective-permute-start.10) | collective-permute-done | bytes 147488 | tf_op jit(solution)/shard_map/ppermute | solution.py:112
  96.8 6.2 %collective-permute-start.11 = (f32[32,1152]{1,0:T(8,128)S(1)}, f32[32,1152]{1,0:T(8,128)S(1)}, u32[]{:S(2)}, u32[]{:S(2)}) collective-permute-start(f32[32,1152]{1,0:T(8,128)S(1)} %add.254), channel_id=1, source_target_pairs={{0,4},{1,5},{2,6},{3,7},{4,0},{5,1},{6,2},{7,3},{8,12},{9,13},{10,... | collective-permute-start | bytes 442376 | tf_op jit(solution)/shard_map/ppermute | solution.py:112
  103.0 3.9 %collective-permute-done.11 = f32[32,1152]{1,0:T(8,128)S(1)} collective-permute-done((f32[32,1152]{1,0:T(8,128)S(1)}, f32[32,1152]{1,0:T(8,128)S(1)}, u32[]{:S(2)}, u32[]{:S(2)}) %collective-permute-start.11) | collective-permute-done | bytes 147488 | tf_op jit(solution)/shard_map/ppermute | solution.py:112
  106.9 1.3 collective-permute-start.12
  108.2 2.0 %collective-permute-done.12 = bf16[32,1152]{1,0:T(8,128)(2,1)S(1)} collective-permute-done((bf16[32,1152]{1,0:T(8,128)(2,1)S(1)}, bf16[32,1152]{1,0:T(8,128)(2,1)S(1)}, u32[]{:S(2)}, u32[]{:S(2)}) %collective-permute-start.12) | collective-permute-done | bytes 73760 | tf_op jit(solution)/shard_map/ppermute | solution.py:116
  110.2 0.1 collective-permute-start.13
  110.3 5.5 %collective-permute-done.13 = bf16[64,1152]{1,0:T(8,128)(2,1)S(1)} collective-permute-done((bf16[64,1152]{1,0:T(8,128)(2,1)S(1)}, bf16[64,1152]{1,0:T(8,128)(2,1)S(1)}, u32[]{:S(2)}, u32[]{:S(2)}) %collective-permute-start.13) | collective-permute-done | bytes 147488 | tf_op jit(solution)/shard_map/ppermute | solution.py:116
  115.8 0.1 broadcast_select_fusion.5
  115.9 1.4 collective-permute-start.14
  117.3 4.3 %collective-permute-done.14 = bf16[128,1152]{1,0:T(8,128)(2,1)S(1)} collective-permute-done((bf16[128,1152]{1,0:T(8,128)(2,1)S(1)}, bf16[128,1152]{1,0:T(8,128)(2,1)S(1)}, u32[]{:S(2)}, u32[]{:S(2)}) %collective-permute-start.14) | collective-permute-done | bytes 294944 | tf_op jit(solution)/shard_map/ppermute | solution.py:116
  121.6 0.1 broadcast_select_fusion.3
  121.8 11.2 %collective-permute-start.15 = (bf16[256,1152]{1,0:T(8,128)(2,1)S(1)}, bf16[256,1152]{1,0:T(8,128)(2,1)S(1)}, u32[]{:S(2)}, u32[]{:S(2)}) collective-permute-start(bf16[256,1152]{1,0:T(8,128)(2,1)S(1)} %pad_maximum_fusion), channel_id=1, source_target_pairs={{0,32},{1,33},{2,34},{3,35},{4,36},{5,37},{6,38},{7,39},{8,40},{9,... | collective-permute-start | bytes 1769480 | tf_op jit(solution)/shard_map/ppermute | solution.py:116
  132.9 1.6 %collective-permute-done.15 = bf16[256,1152]{1,0:T(8,128)(2,1)S(1)} collective-permute-done((bf16[256,1152]{1,0:T(8,128)(2,1)S(1)}, bf16[256,1152]{1,0:T(8,128)(2,1)S(1)}, u32[]{:S(2)}, u32[]{:S(2)}) %collective-permute-start.15) | collective-permute-done | bytes 589856 | tf_op jit(solution)/shard_map/ppermute | solution.py:116
  134.6 0.2 broadcast_select_fusion.1
  134.8 0.7 maximum_convert_fusion.1
  135.5 0.2 maximum_convert_fusion
  135.7 1.1 reshape.545
  136.8 0.8 copy.17
  137.6 1.6 %fusion.34 = (f32[256,1024]{1,0:T(8,128)}, f32[256,1024]{1,0:T(8,128)}) fusion(f32[512,1152]{1,0:T(8,128)S(1)} %maximum_convert_fusion), kind=kLoop, calls=%fused_computation.78 | loop fusion | bytes 4194304 | tf_op jit(solution)/shard_map/slice | solution.py:173
  (23 shorter events, 0.3 us)
Async XLA Ops:
  0.6 44.2 %copy-start = (bf16[256,1024]{1,0:T(8,128)(2,1)S(1)}, bf16[256,1024]{1,0:T(8,128)(2,1)}, u32[]{:S(2)}) copy-start(bf16[256,1024]{1,0:T(8,128)(2,1)} %param.14) | copy-start | bytes 1572868
  18.9 8.2 %copy-start.5 = (s32[1,256,8]{1,2,0:T(8,128)S(1)}, s32[1,256,8]{1,2,0:T(8,128)}, u32[]{:S(2)}) copy-start(s32[1,256,8]{1,2,0:T(8,128)} %param.11) | copy-start | bytes 24580
  20.1 9.9 %collective-permute-start = (f32[256,384]{1,0:T(8,128)S(1)}, f32[256,384]{1,0:T(8,128)S(1)}, u32[]{:S(2)}, u32[]{:S(2)}) collective-permute-start(f32[256,384]{1,0:T(8,128)S(1)} %get-tuple-element.16), channel_id=1, source_target_pairs={{32,0},{64,32},{96,64},{128,96},{160,128},{192,160},{224,192},{33,... | collective-permute-start | bytes 1179656 | tf_op jit(solution)/shard_map/ppermute | solution.py:11
  25.2 6.6 %collective-permute-start.1 = (f32[256,384]{1,0:T(8,128)S(1)}, f32[256,384]{1,0:T(8,128)S(1)}, u32[]{:S(2)}, u32[]{:S(2)}) collective-permute-start(f32[256,384]{1,0:T(8,128)S(1)} %get-tuple-element.17), channel_id=1, source_target_pairs={{0,32},{32,64},{64,96},{96,128},{128,160},{160,192},{192,224},{1,3... | collective-permute-start | bytes 1179656 | tf_op jit(solution)/shard_map/ppermute | solution.py:11
  27.1 12.4 %copy-start.2 = (bf16[256,1024]{1,0:T(8,128)(2,1)S(1)}, bf16[256,1024]{1,0:T(8,128)(2,1)}, u32[]{:S(2)}) copy-start(bf16[256,1024]{1,0:T(8,128)(2,1)} %param.13) | copy-start | bytes 1572868
  33.2 6.6 %collective-permute-start.2 = (bf16[1,256,256]{2,1,0:T(8,128)(2,1)S(1)}, bf16[1,256,256]{2,1,0:T(8,128)(2,1)S(1)}, u32[]{:S(2)}, u32[]{:S(2)}) collective-permute-start(bf16[1,256,256]{2,1,0:T(8,128)(2,1)S(1)} %fusion.24), channel_id=1, source_target_pairs={{0,32},{32,64},{64,96},{96,128},{128,160},{160,192},{192,224},{1,3... | collective-permute-start | bytes 393224 | tf_op jit(solution)/shard_map/ppermute | solution.py:19
  37.6 6.3 %collective-permute-start.3 = (bf16[1,256,256]{2,1,0:T(8,128)(2,1)S(1)}, bf16[1,256,256]{2,1,0:T(8,128)(2,1)S(1)}, u32[]{:S(2)}, u32[]{:S(2)}) collective-permute-start(bf16[1,256,256]{2,1,0:T(8,128)(2,1)S(1)} %fusion.24), channel_id=1, source_target_pairs={{32,0},{64,32},{96,64},{128,96},{160,128},{192,160},{224,192},{33,... | collective-permute-start | bytes 393224 | tf_op jit(solution)/shard_map/ppermute | solution.py:22
  44.9 0.7 copy-start.4
  44.9 0.9 copy-start.6
  45.8 2.7 %copy-start.3 = (f32[256,8]{0,1:T(8,128)}, f32[256,8]{0,1:T(8,128)S(1)}, u32[]{:S(2)}) copy-start(f32[256,8]{0,1:T(8,128)S(1)} %fusion.37) | copy-start | bytes 24580
  52.3 3.2 %collective-permute-start.4 = (f32[256,1152]{1,0:T(8,128)}, f32[256,1152]{1,0:T(8,128)}, u32[]{:S(2)}, u32[]{:S(2)}) collective-permute-start(f32[256,1152]{1,0:T(8,128)} %slice_select_fusion), channel_id=1, source_target_pairs={{0,32},{1,33},{2,34},{3,35},{4,36},{5,37},{6,38},{7,39},{8,40},{9,... | collective-permute-start | bytes 3538952 | tf_op jit(solution)/shard_map/ppermute | solution.py:109
  56.9 1.0 copy-start.1
  58.1 9.1 %collective-permute-start.5 = (f32[128,1152]{1,0:T(8,128)S(1)}, f32[128,1152]{1,0:T(8,128)S(1)}, u32[]{:S(2)}, u32[]{:S(2)}) collective-permute-start(f32[128,1152]{1,0:T(8,128)S(1)} %slice_select_fusion.1), channel_id=1, source_target_pairs={{0,64},{1,65},{2,66},{3,67},{4,68},{5,69},{6,70},{7,71},{8,72},{9,... | collective-permute-start | bytes 1769480 | tf_op jit(solution)/shard_map/ppermute | solution.py:109
  68.5 6.0 %collective-permute-start.6 = (f32[64,1152]{1,0:T(8,128)S(1)}, f32[64,1152]{1,0:T(8,128)S(1)}, u32[]{:S(2)}, u32[]{:S(2)}) collective-permute-start(f32[64,1152]{1,0:T(8,128)S(1)} %slice_select_fusion.2), channel_id=1, source_target_pairs={{0,8},{1,9},{2,10},{3,11},{4,12},{5,13},{6,14},{7,15},{8,0},{9,1},... | collective-permute-start | bytes 884744 | tf_op jit(solution)/shard_map/ppermute | solution.py:109
  74.6 4.1 %collective-permute-start.7 = (f32[32,1152]{1,0:T(8,128)S(1)}, f32[32,1152]{1,0:T(8,128)S(1)}, u32[]{:S(2)}, u32[]{:S(2)}) collective-permute-start(f32[32,1152]{1,0:T(8,128)S(1)} %slice_select_fusion.3), channel_id=1, source_target_pairs={{0,1},{1,0},{2,3},{3,2},{4,5},{5,4},{6,7},{7,6},{8,9},{9,8},{10,11... | collective-permute-start | bytes 442376 | tf_op jit(solution)/shard_map/ppermute | solution.py:109
  78.7 5.6 %collective-permute-start.8 = (f32[32,1152]{1,0:T(8,128)S(1)}, f32[32,1152]{1,0:T(8,128)S(1)}, u32[]{:S(2)}, u32[]{:S(2)}) collective-permute-start(f32[32,1152]{1,0:T(8,128)S(1)} %select_add_fusion.3), channel_id=1, source_target_pairs={{0,128},{1,129},{2,130},{3,131},{4,132},{5,133},{6,134},{7,135},{8... | collective-permute-start | bytes 442376 | tf_op jit(solution)/shard_map/ppermute | solution.py:112
  84.3 6.7 %collective-permute-start.9 = (f32[32,1152]{1,0:T(8,128)S(1)}, f32[32,1152]{1,0:T(8,128)S(1)}, u32[]{:S(2)}, u32[]{:S(2)}) collective-permute-start(f32[32,1152]{1,0:T(8,128)S(1)} %add.252), channel_id=1, source_target_pairs={{0,16},{1,17},{2,18},{3,19},{4,20},{5,21},{6,22},{7,23},{8,24},{9,... | collective-permute-start | bytes 442376 | tf_op jit(solution)/shard_map/ppermute | solution.py:112
  91.0 5.8 %collective-permute-start.10 = (f32[32,1152]{1,0:T(8,128)S(1)}, f32[32,1152]{1,0:T(8,128)S(1)}, u32[]{:S(2)}, u32[]{:S(2)}) collective-permute-start(f32[32,1152]{1,0:T(8,128)S(1)} %add.253), channel_id=1, source_target_pairs={{0,2},{1,3},{2,0},{3,1},{4,6},{5,7},{6,4},{7,5},{8,10},{9,11},{10,... | collective-permute-start | bytes 442376 | tf_op jit(solution)/shard_map/ppermute | solution.py:112
  96.8 10.0 %collective-permute-start.11 = (f32[32,1152]{1,0:T(8,128)S(1)}, f32[32,1152]{1,0:T(8,128)S(1)}, u32[]{:S(2)}, u32[]{:S(2)}) collective-permute-start(f32[32,1152]{1,0:T(8,128)S(1)} %add.254), channel_id=1, source_target_pairs={{0,4},{1,5},{2,6},{3,7},{4,0},{5,1},{6,2},{7,3},{8,12},{9,13},{10,... | collective-permute-start | bytes 442376 | tf_op jit(solution)/shard_map/ppermute | solution.py:112
  106.9 3.3 %collective-permute-start.12 = (bf16[32,1152]{1,0:T(8,128)(2,1)S(1)}, bf16[32,1152]{1,0:T(8,128)(2,1)S(1)}, u32[]{:S(2)}, u32[]{:S(2)}) collective-permute-start(bf16[32,1152]{1,0:T(8,128)(2,1)S(1)} %add_convert_fusion.1), channel_id=1, source_target_pairs={{0,1},{1,0},{2,3},{3,2},{4,5},{5,4},{6,7},{7,6},{8,9},{9,8},{10,11... | collective-permute-start | bytes 221192 | tf_op jit(solution)/shard_map/ppermute | solution.py:116
  110.2 5.6 %collective-permute-start.13 = (bf16[64,1152]{1,0:T(8,128)(2,1)S(1)}, bf16[64,1152]{1,0:T(8,128)(2,1)S(1)}, u32[]{:S(2)}, u32[]{:S(2)}) collective-permute-start(bf16[64,1152]{1,0:T(8,128)(2,1)S(1)} %pad_maximum_fusion.2), channel_id=1, source_target_pairs={{0,8},{1,9},{2,10},{3,11},{4,12},{5,13},{6,14},{7,15},{8,0},{9,1},... | collective-permute-start | bytes 442376 | tf_op jit(solution)/shard_map/ppermute | solution.py:116
  115.9 5.7 %collective-permute-start.14 = (bf16[128,1152]{1,0:T(8,128)(2,1)S(1)}, bf16[128,1152]{1,0:T(8,128)(2,1)S(1)}, u32[]{:S(2)}, u32[]{:S(2)}) collective-permute-start(bf16[128,1152]{1,0:T(8,128)(2,1)S(1)} %pad_maximum_fusion.1), channel_id=1, source_target_pairs={{0,64},{1,65},{2,66},{3,67},{4,68},{5,69},{6,70},{7,71},{8,72},{9,... | collective-permute-start | bytes 884744 | tf_op jit(solution)/shard_map/ppermute | solution.py:116
  121.8 12.8 %collective-permute-start.15 = (bf16[256,1152]{1,0:T(8,128)(2,1)S(1)}, bf16[256,1152]{1,0:T(8,128)(2,1)S(1)}, u32[]{:S(2)}, u32[]{:S(2)}) collective-permute-start(bf16[256,1152]{1,0:T(8,128)(2,1)S(1)} %pad_maximum_fusion), channel_id=1, source_target_pairs={{0,32},{1,33},{2,34},{3,35},{4,36},{5,37},{6,38},{7,39},{8,40},{9,... | collective-permute-start | bytes 1769480 | tf_op jit(solution)/shard_map/ppermute | solution.py:116
